TPU v7x, 512 devices: a whole 4x8x8 slice. The times are simulated.
512 devices in a mesh: shot: 32 (over z_lo, y), recv: 16 (over z_hi, x, core).
Axes of the slice: x: 4, y: 8, z: 8 (z_hi: 2, z_lo: 4; z = z_hi * 4 + z_lo), core: 2. Of those that a mesh axis runs over, the one named last changes fastest.
Arguments:
- traces: bfloat16 [2, 2, 4096, 4096], P(None, None, 'shot', 'recv'), may hold values from -6 to 6
Outputs:
- multiples: float32 [2, 2, 4096, 4096], P(None, None, 'shot', 'recv')
All inputs are finite; a program needn't handle non-finite values.
Results may differ from a plain program's by a relative error of at most 0.0044.
Values may be sent and summed in bfloat16 or wider, within the bound.
No kernel may reach another device: no remote copies, remote signals or barrier semaphores. Data moves between devices by JAX's collectives and lax.ppermute only.
A program may use at most 64 MiB of HBM per device.

v0:
```python
import jax
import jax.numpy as jnp
from jax import lax
from jax.sharding import PartitionSpec as P

NS = 4096


def complex_product(left_block, right_block, form):
    real_real = jnp.einsum(
        form, left_block[:, 0], right_block[:, 0], preferred_element_type=jnp.float32
    )
    imag_imag = jnp.einsum(
        form, left_block[:, 1], right_block[:, 1], preferred_element_type=jnp.float32
    )
    real_imag = jnp.einsum(
        form, left_block[:, 0], right_block[:, 1], preferred_element_type=jnp.float32
    )
    imag_real = jnp.einsum(
        form, left_block[:, 1], right_block[:, 0], preferred_element_type=jnp.float32
    )
    return jnp.stack((real_real - imag_imag, real_imag + imag_real), axis=1)


def per_device(traces):
    freqs = traces.shape[0]
    block_rows = traces.shape[2]
    col_width = traces.shape[3]
    recv_count = lax.axis_size("recv")
    shot_count = lax.axis_size("shot")
    group_blocks = shot_count // recv_count
    piece_len = block_rows // recv_count
    total = shot_count * block_rows
    row_split = traces.reshape(freqs, 2, recv_count, piece_len, col_width)
    col_split = traces.reshape(freqs, 2, block_rows, group_blocks, recv_count, piece_len)
    col_split = jnp.transpose(col_split, (0, 1, 4, 2, 3, 5))
    got_rows, got_cols = (
        lax.all_to_all(row_split, "recv", split_axis=2, concat_axis=2, tiled=True),
        lax.all_to_all(col_split, "recv", split_axis=2, concat_axis=2, tiled=True),
    )
    wide_rows = jnp.transpose(got_rows, (0, 1, 3, 2, 4)).reshape(freqs, 2, piece_len, total)
    own_cols = jnp.transpose(got_cols, (0, 1, 3, 2, 4, 5)).reshape(freqs, 2, block_rows, col_width)
    mirrored = lax.all_to_all(wide_rows, "shot", split_axis=3, concat_axis=2, tiled=True)
    summed = own_cols.astype(jnp.float32) + jnp.swapaxes(mirrored, 2, 3).astype(jnp.float32)
    averaged = (summed * 0.5).astype(jnp.bfloat16)
    spread = lax.all_gather(averaged, "recv", axis=3, tiled=True)
    spread = spread.reshape(freqs, 2, block_rows, recv_count, shot_count, piece_len)
    panel = jnp.transpose(spread, (0, 1, 2, 4, 3, 5)).reshape(freqs, 2, block_rows, total)
    recv_index = lax.axis_index("recv")
    own_tile = lax.dynamic_slice_in_dim(panel, recv_index * col_width, col_width, 3)
    product = complex_product(
        panel, lax.all_gather(own_tile, "shot", axis=2, tiled=True), "fik,fkj->fij"
    )
    scale_factor = jnp.float32(float(NS) ** (-0.5))
    return product * scale_factor


def solution(mesh):
    placed = (P(None, None, "shot", "recv"),)
    return jax.shard_map(
        per_device,
        mesh=mesh,
        in_specs=placed,
        out_specs=P(None, None, "shot", "recv"),
        check_vma=False,
    )
```

profile of v0, /device:TPU:2, one launch (start us, length us, event | category | flops | bytes accessed | tf_op | source)
XLA Modules:
  0.0 359.7 jit_solution(880751011759938663)
XLA Ops:
  6.5 1.7 copy.37
  8.2 13.3 %all-to-all-start.1 = ((bf16[2,2,16,8,256]{4,3,1,0,2:T(8,128)(2,1)}), bf16[2,2,16,8,256]{4,3,1,0,2:T(8,128)(2,1)S(1)}, u32[]{:S(2)}, u32[]{:S(2)}) async-start(bf16[2,2,16,8,256]{4,3,1,0,2:T(8,128)(2,1)} %copy.37), calls=%async_computation.1 | async-start | bytes 524288 | tf_op jit(solution)/shard_map/all_to_all | solution.py:38
  21.5 1.1 copy.34
  22.6 0.8 copy.35
  23.4 7.5 %all-to-all-done.1 = bf16[2,2,16,8,256]{4,3,1,0,2:T(8,128)(2,1)S(1)} async-done(((bf16[2,2,16,8,256]{4,3,1,0,2:T(8,128)(2,1)}), bf16[2,2,16,8,256]{4,3,1,0,2:T(8,128)(2,1)S(1)}, u32[]{:S(2)}, u32[]{:S(2)}) %all-to-all-start.1) | async-done | bytes 262176 | tf_op jit(solution)/shard_map/all_to_all | solution.py:38
  30.9 6.7 %all-to-all-start = ((bf16[2,2,16,128,2,8]{3,5,4,1,0,2:T(8,128)(2,1)}), bf16[2,2,16,128,2,8]{3,5,4,1,0,2:T(8,128)(2,1)S(1)}, u32[]{:S(2)}, u32[]{:S(2)}) async-start(bf16[2,2,16,128,2,8]{3,5,4,1,0,2:T(8,128)(2,1)} %copy.35), calls=%async_computation | async-start | bytes 524288 | tf_op jit(solution)/shard_map/all_to_all | solution.py:39
  37.6 7.2 %copy.47 = bf16[2,2,8,16,256]{2,1,0,4,3:T(2,128)(2,1)} copy(bf16[2,2,8,16,256]{4,2,1,0,3:T(8,128)(2,1)S(1)} %bitcast.82) | data formatting | bytes 524288 | tf_op jit(solution)/shard_map/reshape | solution.py:41
  44.8 6.4 %reshape.30 = bf16[32,2,2048]{2,1,0:T(2,128)(2,1)} reshape(bf16[4096,2,2,8]{3,2,1,0:T(2,128)(2,1)} %bitcast.72) | data formatting | bytes 524288
  51.3 11.3 %all-to-all-start.2 = ((bf16[32,2,2048]{2,1,0:T(2,128)(2,1)}), bf16[32,2,2048]{2,1,0:T(2,128)(2,1)S(1)}, u32[]{:S(2)}, u32[]{:S(2)}) async-start(bf16[32,2,2048]{2,1,0:T(2,128)(2,1)} %reshape.30), calls=%async_computation.2 | async-start | bytes 524288 | tf_op jit(solution)/shard_map/all_to_all | solution.py:43
  62.7 12.1 %all-to-all-done.2 = bf16[32,2,2048]{2,1,0:T(2,128)(2,1)S(1)} async-done(((bf16[32,2,2048]{2,1,0:T(2,128)(2,1)}), bf16[32,2,2048]{2,1,0:T(2,128)(2,1)S(1)}, u32[]{:S(2)}, u32[]{:S(2)}) %all-to-all-start.2) | async-done | bytes 262176 | tf_op jit(solution)/shard_map/all_to_all | solution.py:43
  74.8 5.9 %reshape.31 = bf16[4096,2,2,8]{3,2,1,0:T(2,128)(2,1)} reshape(bf16[32,2,2048]{2,1,0:T(2,128)(2,1)S(1)} %all-to-all-done.2) | data formatting | bytes 524288
  80.7 8.2 %copy.40 = bf16[2,2,8,4096]{3,2,1,0:T(8,128)(2,1)S(1)} copy(bf16[2,2,8,4096]{2,1,0,3:T(2,128)(2,1)} %bitcast.73) | data formatting | bytes 524288 | tf_op jit(solution)/shard_map/all_to_all | solution.py:43
  89.1 1.1 fusion.9
  90.2 81.0 %all-gather.3.cloned.1.call-done = bf16[2,2,128,4096]{2,3,1,0:T(8,128)(2,1)} async-done(((bf16[2,2,128,256]{2,3,1,0:T(8,128)(2,1)}), bf16[2,2,128,4096]{2,3,1,0:T(8,128)(2,1)}) %all-gather.3.cloned.1.call-update) | async-done | bytes 4194320 | tf_op jit(solution)/shard_map/all_gather | solution.py:46
  171.2 3.4 copy.42
  174.6 2.0 copy-done
  176.6 0.9 copy.50
  177.4 164.6 %all-gather.5.cloned.1.call-done = bf16[2,2,4096,256]{3,2,0,1:T(8,128)(2,1)} async-done(((bf16[2,2,128,256]{3,2,0,1:T(8,128)(2,1)}), bf16[2,2,4096,256]{3,2,0,1:T(8,128)(2,1)}) %all-gather.5.cloned.1.call-update) | async-done | bytes 8388624 | tf_op jit(solution)/shard_map/all_gather | solution.py:52
  342.0 4.0 %fusion = f32[2,128,256]{2,1,0:T(8,128)S(1)} fusion(bf16[2,2,4096,256]{3,2,0,1:T(8,128)(2,1)} %all-gather.5.cloned.1.call-done, bf16[2,2,128,4096]{2,3,1,0:T(8,128)(2,1)} %bitcast.75), kind=kOutput, calls=%fused_computation.2 | convolution fusion | flops 536870912 | bytes 6553600 | tf_op jit(solution)/shard_map/fik,fkj->fij/dot_general | solution.py:19
  346.0 0.1 copy-done.1
  346.1 3.9 %fusion.1 = f32[2,128,256]{2,1,0:T(8,128)S(1)} fusion(bf16[2,2,4096,256]{3,2,0,1:T(8,128)(2,1)} %all-gather.5.cloned.1.call-done, bf16[2,2,128,4096]{2,3,1,0:T(8,128)(2,1)S(1)} %bitcast.76), kind=kOutput, calls=%fused_computation.3 | convolution fusion | flops 536870912 | bytes 6553600 | tf_op jit(solution)/shard_map/fik,fkj->fij/dot_general | solution.py:10
  350.0 1.0 fusion.7
  351.0 1.0 fusion.5
  352.1 0.8 copy.46
  (13 shorter events, 0.3 us)
Async XLA Ops:
  8.2 22.7 %all-to-all-start.1 = ((bf16[2,2,16,8,256]{4,3,1,0,2:T(8,128)(2,1)}), bf16[2,2,16,8,256]{4,3,1,0,2:T(8,128)(2,1)S(1)}, u32[]{:S(2)}, u32[]{:S(2)}) async-start(bf16[2,2,16,8,256]{4,3,1,0,2:T(8,128)(2,1)} %copy.37), calls=%async_computation.1 | async-start | bytes 524288 | tf_op jit(solution)/shard_map/all_to_all | solution.py:38
  30.9 20.4 %all-to-all-start = ((bf16[2,2,16,128,2,8]{3,5,4,1,0,2:T(8,128)(2,1)}), bf16[2,2,16,128,2,8]{3,5,4,1,0,2:T(8,128)(2,1)S(1)}, u32[]{:S(2)}, u32[]{:S(2)}) async-start(bf16[2,2,16,128,2,8]{3,5,4,1,0,2:T(8,128)(2,1)} %copy.35), calls=%async_computation | async-start | bytes 524288 | tf_op jit(solution)/shard_map/all_to_all | solution.py:39
  51.3 23.5 %all-to-all-start.2 = ((bf16[32,2,2048]{2,1,0:T(2,128)(2,1)}), bf16[32,2,2048]{2,1,0:T(2,128)(2,1)S(1)}, u32[]{:S(2)}, u32[]{:S(2)}) async-start(bf16[32,2,2048]{2,1,0:T(2,128)(2,1)} %reshape.30), calls=%async_computation.2 | async-start | bytes 524288 | tf_op jit(solution)/shard_map/all_to_all | solution.py:43
  62.6 108.6 %all-gather.3.cloned.1.call-start = ((), (), s32[]{:S(2)}) async-start(), calls=%async_computation.3 | async-start | bytes 4456448 | tf_op jit(solution)/shard_map/all_gather | solution.py:46
  90.1 251.9 %all-gather.5.cloned.1.call-start = ((), (), s32[]{:S(2)}) async-start(), calls=%async_computation.4 | async-start | bytes 8650752 | tf_op jit(solution)/shard_map/all_gather | solution.py:52
  174.6 2.0 copy-start
  342.0 4.0 %copy-start.1 = (bf16[2,2,128,32,16,8]{2,5,4,3,1,0:T(8,128)(2,1)S(1)}, bf16[2,2,128,32,16,8]{2,5,4,3,1,0:T(8,128)(2,1)}, u32[]{:S(2)}) copy-start(bf16[2,2,128,32,16,8]{2,5,4,3,1,0:T(8,128)(2,1)} %copy-done) | copy-start | bytes 12582916
  342.0 8.0 %copy-start.2 = (bf16[2,2,4096,256]{3,2,0,1:T(8,128)(2,1)S(1)}, bf16[2,2,4096,256]{3,2,0,1:T(8,128)(2,1)}, u32[]{:S(2)}) copy-start(bf16[2,2,4096,256]{3,2,0,1:T(8,128)(2,1)} %all-gather.5.cloned.1.call-done) | copy-start | bytes 25165828
Sparse Core Ops, SparseCore 0:
  90.3 80.9 all-gather.2
  177.6 164.4 all-gather.4
where the time goes:
time: 360 us
  waiting for transfers between devices  265 us (74%)
  local copies, waits for them, and re-layouts  38.5 us (11%)
  starting transfers between devices  31.4 us (9%)
  between operations  13.5 us (4%)
  matrix products  9.86 us (3%)
    all_gather x1, waiting for transfers between devices, per_device(): lax.all_gather(own_tile, 'shot', axis=2, tiled=True)  165 us
    all_gather x1, waiting for transfers between devices, per_device(): spread = lax.all_gather(averaged, 'recv', axis=3, tiled=True)  81 us
    unnamed x11, local copies, waits for them, and re-layouts  16.4 us
    all_to_all x1, starting transfers between devices, per_device(): lax.all_to_all(row_split, 'recv', split_axis=2, concat_axis=2, tiled=True)  13.3 us
    all_to_all x1, waiting for transfers between devices, per_device(): lax.all_to_all(wide_rows, 'shot', split_axis=3, concat_axis=2, tiled=True)  12.1 us
    all_to_all x1, starting transfers between devices, per_device(): lax.all_to_all(wide_rows, 'shot', split_axis=3, concat_axis=2, tiled=True)  11.3 us
    all_to_all x1, local copies, waits for them, and re-layouts, per_device(): lax.all_to_all(wide_rows, 'shot', split_axis=3, concat_axis=2, tiled=True)  8.24 us
    all_to_all x1, waiting for transfers between devices, per_device(): lax.all_to_all(row_split, 'recv', split_axis=2, concat_axis=2, tiled=True)  7.48 us
  transfers between devices with their start and end apart: 5, of which 4 were waited for; matrix products, arithmetic and copies ran while one was open for 4% of the time, Pallas kernels for 0%

commit v1 on v0

v1 whole, which is shorter than its diff:
```python
import jax
import jax.numpy as jnp
from jax import lax
from jax.sharding import PartitionSpec as P

NS = 4096


def complex_product(left_block, right_block, form):
    real_real = jnp.einsum(
        form, left_block[:, 0], right_block[:, 0], preferred_element_type=jnp.float32
    )
    imag_imag = jnp.einsum(
        form, left_block[:, 1], right_block[:, 1], preferred_element_type=jnp.float32
    )
    real_imag = jnp.einsum(
        form, left_block[:, 0], right_block[:, 1], preferred_element_type=jnp.float32
    )
    imag_real = jnp.einsum(
        form, left_block[:, 1], right_block[:, 0], preferred_element_type=jnp.float32
    )
    return jnp.stack((real_real - imag_imag, real_imag + imag_real), axis=1)


def mirrored_pieces(traces, shot_count, recv_count):
    block_rows = traces.shape[2]
    g = traces.shape[3] // block_rows
    me_shot = lax.axis_index("shot")
    pieces = []
    for a in range(g):
        got = []
        for h in range(g):
            perm = [
                (s * recv_count + r, (g * r + h) * recv_count + s // g)
                for s in range(a, shot_count, g)
                for r in range(recv_count)
            ]
            part = traces[:, :, :, h * block_rows:(h + 1) * block_rows]
            got.append(lax.ppermute(part, ("shot", "recv"), perm))
        pieces.append(jnp.stack(got)[me_shot % g])
    return jnp.concatenate(pieces, axis=2)


def per_device(traces):
    recv_count = lax.axis_size("recv")
    shot_count = lax.axis_size("shot")
    mirrored = mirrored_pieces(traces, shot_count, recv_count)
    summed = traces.astype(jnp.float32) + jnp.swapaxes(mirrored, 2, 3).astype(jnp.float32)
    averaged = (summed * 0.5).astype(jnp.bfloat16)
    row_panel = lax.all_gather(averaged, "recv", axis=3, tiled=True)
    col_panel = lax.all_gather(averaged, "shot", axis=2, tiled=True)
    product = complex_product(row_panel, col_panel, "fik,fkj->fij")
    scale_factor = jnp.float32(float(NS) ** (-0.5))
    return product * scale_factor


def solution(mesh):
    placed = (P(None, None, "shot", "recv"),)
    return jax.shard_map(
        per_device,
        mesh=mesh,
        in_specs=placed,
        out_specs=P(None, None, "shot", "recv"),
        check_vma=False,
    )
```

time: 360 us -> 322 us (0.89)
  local copies, waits for them, and re-layouts: 38.5 us -> 2.77 us
  starting transfers between devices: 31.4 us -> 18.9 us
  waiting for transfers between devices: 265 us -> 276 us
    all_to_all x3 -> x0, starting transfers between devices: 31.4 us -> none  [the longest x1 13.3 us: per_device(): lax.all_to_all(row_split, 'recv', split_axis=2, concat_axis=2, tiled=True)]
    all_gather x2, waiting for transfers between devices: 246 us -> 269 us  [the longest x1 167 us: per_device(): col_panel = lax.all_gather(averaged, 'shot', axis=2, tiled=True)]
    all_to_all x3 -> x0, waiting for transfers between devices: 19.6 us -> none  [the longest x1 12.1 us: per_device(): lax.all_to_all(wide_rows, 'shot', split_axis=3, concat_axis=2, tiled=True)]
    ppermute x0 -> x4, starting transfers between devices: none -> 18.9 us  [mirrored_pieces(): got.append(lax.ppermute(part, ('shot', 'recv'), perm))]
    unnamed x11 -> x6, local copies, waits for them, and re-layouts: 16.4 us -> 0.69 us
    reshape x2 -> x0, local copies, waits for them, and re-layouts: 8.89 us -> none  [the longest x1 7.21 us: per_device(): jnp.transpose(got_rows, (0, 1, 3, 2, 4)).reshape(freqs, 2, piece_len, total)]
    all_to_all x1 -> x0, local copies, waits for them, and re-layouts: 8.24 us -> none  [per_device(): lax.all_to_all(wide_rows, 'shot', split_axis=3, concat_axis=2, tiled=True)]
    ppermute x0 -> x4, waiting for transfers between devices: none -> 6.08 us  [mirrored_pieces(): got.append(lax.ppermute(part, ('shot', 'recv'), perm))]
  transfers between devices with their start and end apart: 5 -> 6, of which waited for: 4 -> 4; matrix products, arithmetic and copies ran while one was open for 4% -> 0% of each run, Pallas kernels for 0% -> 0%
where the time goes in v1:
time: 322 us
  waiting for transfers between devices  276 us (86%)
  starting transfers between devices  18.9 us (6%)
  between operations  13.5 us (4%)
  matrix products  9.24 us (3%)
    all_gather x1, waiting for transfers between devices, per_device(): col_panel = lax.all_gather(averaged, 'shot', axis=2, tiled=True)  167 us
    all_gather x1, waiting for transfers between devices, per_device(): row_panel = lax.all_gather(averaged, 'recv', axis=3, tiled=True)  102 us
    ppermute x4, starting transfers between devices, mirrored_pieces(): got.append(lax.ppermute(part, ('shot', 'recv'), perm))  18.9 us
  transfers between devices with their start and end apart: 6, of which 4 were waited for; matrix products, arithmetic and copies ran while one was open for 0% of the time, Pallas kernels for 0%

profile of v1, /device:TPU:2, one launch (start us, length us, event | category | flops | bytes accessed | tf_op | source)
XLA Modules:
  0.0 322.0 jit_solution(6613637756357751815)
XLA Ops:
  6.5 1.0 fusion.12
  7.5 0.7 collective-permute-start.3
  8.2 10.1 %collective-permute-start.1 = (bf16[2,2,128,128]{3,2,1,0:T(8,128)(2,1)S(1)}, bf16[2,2,128,128]{3,2,1,0:T(8,128)(2,1)S(1)}, u32[]{:S(2)}, u32[]{:S(2)}) collective-permute-start(bf16[2,2,128,128]{3,2,1,0:T(8,128)(2,1)S(1)} %get-tuple-element.5), channel_id=1, source_target_pairs={{0,16},{1,48},{2,80},{3,112},{4,144},{5,176},{6,208},{7,240},{8,27... | collective-permute-start | bytes 393224 | tf_op jit(solution)/shard_map/ppermute | solution.py:39
  18.3 1.3 collective-permute-start.2
  19.6 6.8 %collective-permute-start = (bf16[2,2,128,128]{3,2,1,0:T(8,128)(2,1)S(1)}, bf16[2,2,128,128]{3,2,1,0:T(8,128)(2,1)S(1)}, u32[]{:S(2)}, u32[]{:S(2)}) collective-permute-start(bf16[2,2,128,128]{3,2,1,0:T(8,128)(2,1)S(1)} %get-tuple-element.6), channel_id=1, source_target_pairs={{0,0},{1,32},{2,64},{3,96},{4,128},{5,160},{6,192},{7,224},{8,256}... | collective-permute-start | bytes 393224 | tf_op jit(solution)/shard_map/ppermute | solution.py:39
  26.4 0.0 collective-permute-done.1
  26.5 3.8 %collective-permute-done.2 = bf16[2,2,128,128]{3,2,1,0:T(8,128)(2,1)S(1)} collective-permute-done((bf16[2,2,128,128]{3,2,1,0:T(8,128)(2,1)S(1)}, bf16[2,2,128,128]{3,2,1,0:T(8,128)(2,1)S(1)}, u32[]{:S(2)}, u32[]{:S(2)}) %collective-permute-start.2) | collective-permute-done | bytes 131104 | tf_op jit(solution)/shard_map/ppermute | solution.py:39
  30.2 2.3 collective-permute-done
  32.5 0.1 fusion.10
  32.6 0.1 copy.4
  32.8 0.1 copy.3
  32.9 1.7 fusion.9
  34.6 0.0 all-gather.3.cloned.1.call-update
  34.7 0.0 all-gather.5.cloned.1.call-start
  34.7 0.7 all-gather.5.cloned.1.call-update
  35.4 101.9 %all-gather.3.cloned.1.call-done = bf16[2,2,128,4096]{3,2,0,1:T(8,128)(2,1)} async-done(((bf16[2,2,128,256]{3,2,0,1:T(8,128)(2,1)}), bf16[2,2,128,4096]{3,2,0,1:T(8,128)(2,1)}) %all-gather.3.cloned.1.call-update) | async-done | bytes 4194320 | tf_op jit(solution)/shard_map/all_gather | solution.py:50
  137.3 167.0 %all-gather.5.cloned.1.call-done = bf16[2,2,4096,256]{3,2,0,1:T(8,128)(2,1)} async-done(((bf16[2,2,128,256]{3,2,0,1:T(8,128)(2,1)}), bf16[2,2,4096,256]{3,2,0,1:T(8,128)(2,1)}) %all-gather.5.cloned.1.call-update) | async-done | bytes 8388624 | tf_op jit(solution)/shard_map/all_gather | solution.py:51
  304.3 3.7 %fusion = f32[2,128,256]{2,1,0:T(8,128)S(1)} fusion(bf16[2,2,4096,256]{3,2,0,1:T(8,128)(2,1)} %all-gather.5.cloned.1.call-done, bf16[2,2,128,4096]{3,2,0,1:T(8,128)(2,1)} %all-gather.3.cloned.1.call-done), kind=kOutput, calls=%fused_computation.2 | convolution fusion | flops 536870912 | bytes 6553600 | tf_op jit(solution)/shard_map/fik,fkj->fij/dot_general | solution.py:19
  308.0 0.0 slice-start.1
  308.0 4.1 %fusion.1 = f32[2,128,256]{2,1,0:T(8,128)S(1)} fusion(bf16[2,2,4096,256]{3,2,0,1:T(8,128)(2,1)} %all-gather.5.cloned.1.call-done, bf16[2,2,128,4096]{3,2,0,1:T(8,128)(2,1)} %all-gather.3.cloned.1.call-done), kind=kOutput, calls=%fused_computation.3 | convolution fusion | flops 536870912 | bytes 6553600 | tf_op jit(solution)/shard_map/fik,fkj->fij/dot_general | solution.py:10
  312.2 0.7 slice-done.1
  312.9 0.7 fusion.7
  313.6 0.7 fusion.5
  314.4 0.8 copy.5
  (8 shorter events, 0.1 us)
Async XLA Ops:
  6.5 130.8 %all-gather.3.cloned.1.call-start = ((), (), s32[]{:S(2)}) async-start(), calls=%async_computation | async-start | bytes 4456448 | tf_op jit(solution)/shard_map/all_gather | solution.py:50
  7.5 18.9 %collective-permute-start.3 = (bf16[2,2,128,128]{3,2,1,0:T(8,128)(2,1)S(1)}, bf16[2,2,128,128]{3,2,1,0:T(8,128)(2,1)S(1)}, u32[]{:S(2)}, u32[]{:S(2)}) collective-permute-start(bf16[2,2,128,128]{3,2,1,0:T(8,128)(2,1)S(1)} %get-tuple-element.5), channel_id=1, source_target_pairs={{16,16},{17,48},{18,80},{19,112},{20,144},{21,176},{22,208},{23,24... | collective-permute-start | bytes 393224 | tf_op jit(solution)/shard_map/ppermute | solution.py:39
  8.2 18.2 %collective-permute-start.1 = (bf16[2,2,128,128]{3,2,1,0:T(8,128)(2,1)S(1)}, bf16[2,2,128,128]{3,2,1,0:T(8,128)(2,1)S(1)}, u32[]{:S(2)}, u32[]{:S(2)}) collective-permute-start(bf16[2,2,128,128]{3,2,1,0:T(8,128)(2,1)S(1)} %get-tuple-element.5), channel_id=1, source_target_pairs={{0,16},{1,48},{2,80},{3,112},{4,144},{5,176},{6,208},{7,240},{8,27... | collective-permute-start | bytes 393224 | tf_op jit(solution)/shard_map/ppermute | solution.py:39
  18.3 11.9 %collective-permute-start.2 = (bf16[2,2,128,128]{3,2,1,0:T(8,128)(2,1)S(1)}, bf16[2,2,128,128]{3,2,1,0:T(8,128)(2,1)S(1)}, u32[]{:S(2)}, u32[]{:S(2)}) collective-permute-start(bf16[2,2,128,128]{3,2,1,0:T(8,128)(2,1)S(1)} %get-tuple-element.6), channel_id=1, source_target_pairs={{16,0},{17,32},{18,64},{19,96},{20,128},{21,160},{22,192},{23,224}... | collective-permute-start | bytes 393224 | tf_op jit(solution)/shard_map/ppermute | solution.py:39
  19.6 12.9 %collective-permute-start = (bf16[2,2,128,128]{3,2,1,0:T(8,128)(2,1)S(1)}, bf16[2,2,128,128]{3,2,1,0:T(8,128)(2,1)S(1)}, u32[]{:S(2)}, u32[]{:S(2)}) collective-permute-start(bf16[2,2,128,128]{3,2,1,0:T(8,128)(2,1)S(1)} %get-tuple-element.6), channel_id=1, source_target_pairs={{0,0},{1,32},{2,64},{3,96},{4,128},{5,160},{6,192},{7,224},{8,256}... | collective-permute-start | bytes 393224 | tf_op jit(solution)/shard_map/ppermute | solution.py:39
  34.7 269.7 %all-gather.5.cloned.1.call-start = ((), (), s32[]{:S(2)}) async-start(), calls=%async_computation.1 | async-start | bytes 8650752 | tf_op jit(solution)/shard_map/all_gather | solution.py:51
  304.3 7.9 %slice-start = ((s8[8388608]{0:T(1024)(128)(4,1)}), s8[4194304]{0:T(1024)(128)(4,1)S(1)}, s32[]{:S(2)}) async-start(s8[8388608]{0:T(1024)(128)(4,1)} %bitcast.54), calls=%async_computation.2 | async-start | bytes 8388608
  304.3 7.9 %copy-start = (bf16[2,2,128,4096]{3,2,0,1:T(8,128)(2,1)S(1)}, bf16[2,2,128,4096]{3,2,0,1:T(8,128)(2,1)}, u32[]{:S(2)}) copy-start(bf16[2,2,128,4096]{3,2,0,1:T(8,128)(2,1)} %all-gather.3.cloned.1.call-done) | copy-start | bytes 12582916
  308.0 4.9 %slice-start.1 = ((s8[8388608]{0:T(1024)(128)(4,1)}), s8[4194304]{0:T(1024)(128)(4,1)S(1)}, s32[]{:S(2)}) async-start(s8[8388608]{0:T(1024)(128)(4,1)} %bitcast.54), calls=%async_computation.3 | async-start | bytes 8388608
Sparse Core Ops, SparseCore 0:
  34.8 102.4 all-gather.2
  139.4 164.8 all-gather.4

commit v2 on v1

--- a/solution.py
+++ b/solution.py
@@ -20,6 +20,43 @@
         form, left_block[:, 1], right_block[:, 0], preferred_element_type=jnp.float32
     )
     return jnp.stack((real_real - imag_imag, real_imag + imag_real), axis=1)
+
+
+def stream_gather(block, axis, stride, n, wrap):
+    axis_size = lax.axis_size(axis)
+    pos = (lax.axis_index(axis) // stride) % n
+    k_up = n // 2 if wrap else n - 1
+    k_dn = n - 1 - k_up if wrap else n - 1
+
+    def perm(step, direction):
+        pairs = []
+        for i in range(axis_size):
+            p = (i // stride) % n
+            q = (p + direction) % n if wrap else p + direction
+            origin = p - direction * (step - 1)
+            if not wrap and not (0 <= q < n and 0 <= origin < n):
+                continue
+            pairs.append((i, i + (q - p) * stride))
+        return pairs
+
+    ups, dns = [], []
+    up = dn = block
+    for k in range(1, max(k_up, k_dn) + 1):
+        if k <= k_up:
+            up = lax.ppermute(up, axis, perm(k, 1))
+            ups.append(up)
+        if k <= k_dn:
+            dn = lax.ppermute(dn, axis, perm(k, -1))
+            dns.append(dn)
+    stacked = jnp.stack([block] + ups + dns)
+    j = jnp.arange(n)
+    if wrap:
+        d = (pos - j) % n
+        sel = jnp.where(d == 0, 0, jnp.where(d <= k_up, d, k_up + n - d))
+    else:
+        d = pos - j
+        sel = jnp.where(d == 0, 0, jnp.where(d > 0, d, k_up - d))
+    return jnp.take(stacked, sel, axis=0)
 
 
 def mirrored_pieces(traces, shot_count, recv_count):
@@ -47,8 +84,19 @@
     mirrored = mirrored_pieces(traces, shot_count, recv_count)
     summed = traces.astype(jnp.float32) + jnp.swapaxes(mirrored, 2, 3).astype(jnp.float32)
     averaged = (summed * 0.5).astype(jnp.bfloat16)
-    row_panel = lax.all_gather(averaged, "recv", axis=3, tiled=True)
-    col_panel = lax.all_gather(averaged, "shot", axis=2, tiled=True)
+    freqs, _, block_rows, col_width = averaged.shape
+    y_n, z_n = 8, shot_count // 8
+    x_n, zh_n = 4, recv_count // 8
+    first = stream_gather(averaged[:1], "shot", 1, y_n, True)
+    first = stream_gather(first, "shot", y_n, z_n, False)
+    second = stream_gather(averaged[1:], "shot", y_n, z_n, False)
+    second = jnp.swapaxes(stream_gather(second, "shot", 1, y_n, True), 0, 1)
+    cols = jnp.concatenate((first, second), axis=2)
+    col_panel = jnp.transpose(cols, (2, 3, 0, 1, 4, 5)).reshape(freqs, 2, shot_count * block_rows, col_width)
+    rows = stream_gather(averaged, "recv", 8, zh_n, True)
+    rows = stream_gather(rows, "recv", 2, x_n, True)
+    rows = stream_gather(rows, "recv", 1, 2, True)
+    row_panel = jnp.transpose(rows, (3, 4, 5, 2, 1, 0, 6)).reshape(freqs, 2, block_rows, recv_count * col_width)
     product = complex_product(row_panel, col_panel, "fik,fkj->fij")
     scale_factor = jnp.float32(float(NS) ** (-0.5))
     return product * scale_factor

time: 322 us -> 282 us (0.88)
  the two profiles are of different devices: /device:TPU:2 before, /device:TPU:134 now
where the time goes in v2:
time: 282 us; the launch traced here: 280 us
  starting transfers between devices  125 us (44%)
  local copies, waits for them, and re-layouts  77 us (27%)
  other arithmetic  38.8 us (14%)
  waiting for transfers between devices  30.4 us (11%)
  matrix products  7.78 us (3%)
    ppermute x18, starting transfers between devices, stream_gather(): up = lax.ppermute(up, axis, perm(k, 1))  48.2 us
    ppermute x13, starting transfers between devices, stream_gather(): dn = lax.ppermute(dn, axis, perm(k, -1))  47.4 us
    ppermute x4, starting transfers between devices, mirrored_pieces(): got.append(lax.ppermute(part, ('shot', 'recv'), perm))  29.7 us
    unnamed x39, local copies, waits for them, and re-layouts  28.5 us
    ppermute x18, waiting for transfers between devices, stream_gather(): up = lax.ppermute(up, axis, perm(k, 1))  22.6 us
    gather x8, local copies, waits for them, and re-layouts, stream_gather(): return jnp.take(stacked, sel, axis=0)  21.3 us
    select_n x13, other arithmetic, stream_gather(): return jnp.take(stacked, sel, axis=0)  14.6 us
    transpose x1, local copies, waits for them, and re-layouts, per_device(): jnp.transpose(cols, (2, 3, 0, 1, 4, 5))  7.9 us
  transfers between devices with their start and end apart: 35, of which 5 were waited for; matrix products, arithmetic and copies ran while one was open for 30% of the time, Pallas kernels for 0%

profile of v2, /device:TPU:134, one launch (start us, length us, event | category | flops | bytes accessed | tf_op | source)
XLA Modules:
  0.0 280.0 jit_solution(15841952010585205870)
XLA Ops:
  1.7 15.2 %collective-permute-start.1 = (bf16[2,2,128,128]{3,2,1,0:T(8,128)(2,1)S(1)}, bf16[2,2,128,128]{3,2,1,0:T(8,128)(2,1)S(1)}, u32[]{:S(2)}, u32[]{:S(2)}) collective-permute-start(bf16[2,2,128,128]{3,2,1,0:T(8,128)(2,1)S(1)} %get-tuple-element.11), channel_id=1, source_target_pairs={{0,16},{1,48},{2,80},{3,112},{4,144},{5,176},{6,208},{7,240},{8,27... | collective-permute-start | bytes 393224 | tf_op jit(solution)/shard_map/ppermute | solution.py:76
  18.2 12.5 %collective-permute-start = (bf16[2,2,128,128]{3,2,1,0:T(8,128)(2,1)S(1)}, bf16[2,2,128,128]{3,2,1,0:T(8,128)(2,1)S(1)}, u32[]{:S(2)}, u32[]{:S(2)}) collective-permute-start(bf16[2,2,128,128]{3,2,1,0:T(8,128)(2,1)S(1)} %get-tuple-element.12), channel_id=1, source_target_pairs={{0,0},{1,32},{2,64},{3,96},{4,128},{5,160},{6,192},{7,224},{8,256}... | collective-permute-start | bytes 393224 | tf_op jit(solution)/shard_map/ppermute | solution.py:76
  33.8 5.9 %collective-permute-done.2 = bf16[2,2,128,128]{3,2,1,0:T(8,128)(2,1)S(1)} collective-permute-done((bf16[2,2,128,128]{3,2,1,0:T(8,128)(2,1)S(1)}, bf16[2,2,128,128]{3,2,1,0:T(8,128)(2,1)S(1)}, u32[]{:S(2)}, u32[]{:S(2)}) %collective-permute-start.2) | collective-permute-done | bytes 131104 | tf_op jit(solution)/shard_map/ppermute | solution.py:76
  50.8 5.1 %collective-permute-start.13 = (bf16[1,2,128,256]{3,2,1,0:T(8,128)(2,1)S(1)}, bf16[1,2,128,256]{3,2,1,0:T(8,128)(2,1)}, u32[]{:S(2)}, u32[]{:S(2)}) collective-permute-start(bf16[1,2,128,256]{3,2,1,0:T(8,128)(2,1)S(1)} %get-tuple-element.7), channel_id=1, source_target_pairs={{0,112},{16,0},{32,16},{48,32},{64,48},{80,64},{96,80},{112,96},{1... | collective-permute-start | bytes 393224 | tf_op jit(solution)/shard_map/ppermute | solution.py:49
  62.2 4.2 %collective-permute-start.26 = (bf16[1,2,128,256]{3,2,1,0:T(8,128)(2,1)}, bf16[1,2,128,256]{3,2,1,0:T(8,128)(2,1)}, u32[]{:S(2)}, u32[]{:S(2)}) collective-permute-start(bf16[1,2,128,256]{3,2,1,0:T(8,128)(2,1)} %collective-permute-done.25), channel_id=1, source_target_pairs={{128,0},{144,16},{160,32},{176,48},{192,64},{208,80},{224,96},{240... | collective-permute-start | bytes 393224 | tf_op jit(solution)/shard_map/ppermute | solution.py:49
  68.3 5.1 %collective-permute-start.14 = (bf16[1,2,128,256]{3,2,1,0:T(8,128)(2,1)}, bf16[1,2,128,256]{3,2,1,0:T(8,128)(2,1)}, u32[]{:S(2)}, u32[]{:S(2)}) collective-permute-start(bf16[1,2,128,256]{3,2,1,0:T(8,128)(2,1)} %collective-permute-done.13), channel_id=1, source_target_pairs={{0,112},{16,0},{32,16},{48,32},{64,48},{80,64},{96,80},{112,96},{1... | collective-permute-start | bytes 393224 | tf_op jit(solution)/shard_map/ppermute | solution.py:49
  76.7 5.4 %collective-permute-start.7 = (bf16[2,2,2,128,256]{4,3,2,1,0:T(8,128)(2,1)}, bf16[2,2,2,128,256]{4,3,2,1,0:T(8,128)(2,1)}, u32[]{:S(2)}, u32[]{:S(2)}) collective-permute-start(bf16[2,2,2,128,256]{4,3,2,1,0:T(8,128)(2,1)} %broadcast_select_fusion.1), channel_id=1, source_target_pairs={{0,6},{1,7},{2,0},{3,1},{4,2},{5,3},{6,4},{7,5},{8,14},{9,15},{10,... | collective-permute-start | bytes 1572872 | tf_op jit(solution)/shard_map/ppermute | solution.py:49
  82.8 6.6 %collective-permute-start.5 = (bf16[2,2,2,128,256]{4,3,2,1,0:T(8,128)(2,1)}, bf16[2,2,2,128,256]{4,3,2,1,0:T(8,128)(2,1)}, u32[]{:S(2)}, u32[]{:S(2)}) collective-permute-start(bf16[2,2,2,128,256]{4,3,2,1,0:T(8,128)(2,1)} %broadcast_select_fusion.1), channel_id=1, source_target_pairs={{0,2},{1,3},{2,4},{3,5},{4,6},{5,7},{6,0},{7,1},{8,10},{9,11},{10,... | collective-permute-start | bytes 1572872 | tf_op jit(solution)/shard_map/ppermute | solution.py:46
  95.3 5.1 %collective-permute-start.15 = (bf16[1,2,128,256]{3,2,1,0:T(8,128)(2,1)}, bf16[1,2,128,256]{3,2,1,0:T(8,128)(2,1)S(1)}, u32[]{:S(2)}, u32[]{:S(2)}) collective-permute-start(bf16[1,2,128,256]{3,2,1,0:T(8,128)(2,1)} %collective-permute-done.14), channel_id=1, source_target_pairs={{0,112},{16,0},{32,16},{48,32},{64,48},{80,64},{96,80},{112,96},{1... | collective-permute-start | bytes 393224 | tf_op jit(solution)/shard_map/ppermute | solution.py:49
  108.7 10.4 %collective-permute-done.12 = bf16[1,2,128,256]{3,2,1,0:T(8,128)(2,1)S(1)} collective-permute-done((bf16[1,2,128,256]{3,2,1,0:T(8,128)(2,1)S(1)}, bf16[1,2,128,256]{3,2,1,0:T(8,128)(2,1)S(1)}, u32[]{:S(2)}, u32[]{:S(2)}) %collective-permute-start.12) | collective-permute-done | bytes 131104 | tf_op jit(solution)/shard_map/ppermute | solution.py:46
  131.2 3.9 %collective-permute-start.29 = (bf16[4,1,2,128,256]{4,3,2,0,1:T(8,128)(2,1)}, bf16[4,1,2,128,256]{4,3,2,0,1:T(8,128)(2,1)}, u32[]{:S(2)}, u32[]{:S(2)}) collective-permute-start(bf16[4,1,2,128,256]{4,3,2,0,1:T(8,128)(2,1)} %collective-permute-done.28), channel_id=1, source_target_pairs={{0,16},{16,32},{32,48},{48,64},{64,80},{80,96},{96,112},{112,0},{1... | collective-permute-start | bytes 1572872 | tf_op jit(solution)/shard_map/ppermute | solution.py:46
  157.3 4.3 %collective-permute-start.34 = (bf16[4,1,2,128,256]{4,3,2,0,1:T(8,128)(2,1)}, bf16[4,1,2,128,256]{4,3,2,0,1:T(8,128)(2,1)S(1)}, u32[]{:S(2)}, u32[]{:S(2)}) collective-permute-start(bf16[4,1,2,128,256]{4,3,2,0,1:T(8,128)(2,1)} %collective-permute-done.33), channel_id=1, source_target_pairs={{0,112},{16,0},{32,16},{48,32},{64,48},{80,64},{96,80},{112,96},{1... | collective-permute-start | bytes 1572872 | tf_op jit(solution)/shard_map/ppermute | solution.py:49
  166.4 4.2 %collective-permute-done.30 = bf16[4,1,2,128,256]{4,3,2,0,1:T(8,128)(2,1)S(1)} collective-permute-done((bf16[4,1,2,128,256]{4,3,2,0,1:T(8,128)(2,1)}, bf16[4,1,2,128,256]{4,3,2,0,1:T(8,128)(2,1)S(1)}, u32[]{:S(2)}, u32[]{:S(2)}) %collective-permute-start.30) | collective-permute-done | bytes 524320 | tf_op jit(solution)/shard_map/ppermute | solution.py:46
  179.2 8.0 %collective-permute-done.31 = bf16[4,1,2,128,256]{4,3,2,0,1:T(8,128)(2,1)S(1)} collective-permute-done((bf16[4,1,2,128,256]{4,3,2,0,1:T(8,128)(2,1)S(1)}, bf16[4,1,2,128,256]{4,3,2,0,1:T(8,128)(2,1)S(1)}, u32[]{:S(2)}, u32[]{:S(2)}) %collective-permute-start.31) | collective-permute-done | bytes 524320 | tf_op jit(solution)/shard_map/ppermute | solution.py:46
  192.6 4.9 %gather_fusion.5 = bf16[8,4,2,128,256]{4,3,2,1,0:T(8,128)(2,1)} fusion(bf16[8,4,2,128,256]{4,3,2,1,0:T(8,128)(2,1)} %bitcast.71, s32[1024]{0:T(1024)S(1)} %pad_clamp_fusion.1), kind=kCustom, calls=%fused_computation.5 | custom fusion | bytes 8388640 | tf_op jit(solution)/shard_map/jit(_take)/gather | solution.py:59
  197.5 4.0 %collective-permute-start.18 = (bf16[8,1,2,128,256]{4,3,2,0,1:T(8,128)(2,1)}, bf16[8,1,2,128,256]{4,3,2,0,1:T(8,128)(2,1)}, u32[]{:S(2)}, u32[]{:S(2)}) collective-permute-start(bf16[8,1,2,128,256]{4,3,2,0,1:T(8,128)(2,1)} %collective-permute-done.17), channel_id=1, source_target_pairs={{256,384},{272,400},{288,416},{304,432},{320,448},{336,464},{352,4... | collective-permute-start | bytes 3145736 | tf_op jit(solution)/shard_map/ppermute | solution.py:46
  201.5 4.6 %fusion.1 = bf16[4,8,1,2,128,256]{5,4,3,1,0,2:T(8,128)(2,1)} fusion(bf16[8,4,2,128,256]{4,3,2,1,0:T(8,128)(2,1)} %gather_fusion.5, pred[8]{0:T(512)(128)(4,1)S(1)} %copy-done.3), kind=kLoop, calls=%fused_computation.16 | loop fusion | flops 2097152 | bytes 8388616 | tf_op jit(solution)/shard_map/transpose | solution.py:93
  210.1 4.0 %fusion.6 = (bf16[2,4,2,2,2,128,128]{6,5,4,3,2,1,0:T(8,128)(2,1)}, bf16[2,4,2,2,2,128,128]{6,5,4,3,2,1,0:T(8,128)(2,1)}) fusion(bf16[1,4,2,2,2,128,256]{6,5,4,3,2,1,0:T(8,128)(2,1)S(1)} %copy-done.1, bf16[1,4,2,2,2,128,256]{6,5,4,3,2,1,0:T(8,128)(2,1)} %bitcast.16), kind=kLoop, calls=%fused_computation.22 | loop fusion | flops 8388608 | bytes 8388608 | tf_op jit(solution)/shard_map/stack | solution.py:51
  222.9 6.3 %copy.20 = bf16[2,2,128,2,4,2,256]{6,5,4,3,2,0,1:T(2,128)(2,1)} copy(bf16[2,2,128,2,4,2,256]{6,2,1,0,3,4,5:T(8,128)(2,1)S(1)} %fusion) | data formatting | bytes 8388608 | tf_op jit(solution)/shard_map/jit(_take)/select_n | solution.py:59
  229.2 7.8 %reshape.384 = bf16[2,2,128,4096]{3,2,0,1:T(8,128)(2,1)} reshape(bf16[2,2,128,2,4,2,256]{6,5,4,3,2,0,1:T(2,128)(2,1)} %copy.20) | data formatting | bytes 8388608 | tf_op jit(solution)/shard_map/reshape | solution.py:99
  246.2 5.8 %gather_fusion.3 = bf16[4,8,2,128,256]{4,3,2,1,0:T(8,128)(2,1)} fusion(bf16[7,8,2,128,256]{4,3,2,1,0:T(8,128)(2,1)} %bitcast.188, s32[1024]{0:T(1024)S(1)} %pad_clamp_fusion), kind=kCustom, calls=%fused_computation.3 | custom fusion | bytes 8388624 | tf_op jit(solution)/shard_map/jit(_take)/gather | solution.py:59
  252.0 4.7 %bitcast_select_fusion.1 = bf16[4,8,1,2,128,256]{5,4,3,1,0,2:T(8,128)(2,1)} fusion(bf16[4,8,2,128,256]{4,3,2,1,0:T(8,128)(2,1)} %gather_fusion.3, pred[4]{0:T(512)(128)(4,1)S(1)} %get-tuple-element.13), kind=kLoop, calls=%fused_computation.17 | loop fusion | flops 2097152 | bytes 8388612 | tf_op jit(solution)/shard_map/jit(_take)/select_n | solution.py:59
  256.8 6.3 %maximum_bitcast_fusion = bf16[2,2,4,8,128,256]{5,4,1,3,2,0:T(8,128)(2,1)} fusion(bf16[4,8,1,2,128,256]{5,4,3,1,0,2:T(8,128)(2,1)S(1)} %copy-done, bf16[4,8,1,2,128,256]{5,4,3,1,0,2:T(8,128)(2,1)} %bitcast_select_fusion.1), kind=kLoop, calls=%fused_computation.8 | loop fusion | flops 4194304 | bytes 16777216 | tf_op jit(solution)/shard_map/transpose | solution.py:95
  263.0 7.9 %copy.35 = bf16[2,2,4,8,128,256]{5,4,3,2,0,1:T(8,128)(2,1)} copy(bf16[2,2,4,8,128,256]{5,4,1,3,2,0:T(8,128)(2,1)} %maximum_bitcast_fusion) | data formatting | bytes 16777216 | tf_op jit(solution)/shard_map/transpose | solution.py:95
  (141 shorter events, 126.9 us)
Async XLA Ops:
  1.0 38.8 %collective-permute-start.3 = (bf16[2,2,128,128]{3,2,1,0:T(8,128)(2,1)S(1)}, bf16[2,2,128,128]{3,2,1,0:T(8,128)(2,1)S(1)}, u32[]{:S(2)}, u32[]{:S(2)}) collective-permute-start(bf16[2,2,128,128]{3,2,1,0:T(8,128)(2,1)S(1)} %get-tuple-element.11), channel_id=1, source_target_pairs={{16,16},{17,48},{18,80},{19,112},{20,144},{21,176},{22,208},{23,24... | collective-permute-start | bytes 393224 | tf_op jit(solution)/shard_map/ppermute | solution.py:76
  1.7 38.1 %collective-permute-start.1 = (bf16[2,2,128,128]{3,2,1,0:T(8,128)(2,1)S(1)}, bf16[2,2,128,128]{3,2,1,0:T(8,128)(2,1)S(1)}, u32[]{:S(2)}, u32[]{:S(2)}) collective-permute-start(bf16[2,2,128,128]{3,2,1,0:T(8,128)(2,1)S(1)} %get-tuple-element.11), channel_id=1, source_target_pairs={{0,16},{1,48},{2,80},{3,112},{4,144},{5,176},{6,208},{7,240},{8,27... | collective-permute-start | bytes 393224 | tf_op jit(solution)/shard_map/ppermute | solution.py:76
  16.9 22.9 %collective-permute-start.2 = (bf16[2,2,128,128]{3,2,1,0:T(8,128)(2,1)S(1)}, bf16[2,2,128,128]{3,2,1,0:T(8,128)(2,1)S(1)}, u32[]{:S(2)}, u32[]{:S(2)}) collective-permute-start(bf16[2,2,128,128]{3,2,1,0:T(8,128)(2,1)S(1)} %get-tuple-element.12), channel_id=1, source_target_pairs={{16,0},{17,32},{18,64},{19,96},{20,128},{21,160},{22,192},{23,224}... | collective-permute-start | bytes 393224 | tf_op jit(solution)/shard_map/ppermute | solution.py:76
  18.2 23.4 %collective-permute-start = (bf16[2,2,128,128]{3,2,1,0:T(8,128)(2,1)S(1)}, bf16[2,2,128,128]{3,2,1,0:T(8,128)(2,1)S(1)}, u32[]{:S(2)}, u32[]{:S(2)}) collective-permute-start(bf16[2,2,128,128]{3,2,1,0:T(8,128)(2,1)S(1)} %get-tuple-element.12), channel_id=1, source_target_pairs={{0,0},{1,32},{2,64},{3,96},{4,128},{5,160},{6,192},{7,224},{8,256}... | collective-permute-start | bytes 393224 | tf_op jit(solution)/shard_map/ppermute | solution.py:76
  56.0 18.4 %collective-permute-start.4 = (bf16[2,2,128,256]{3,2,1,0:T(8,128)(2,1)S(1)}, bf16[2,2,128,256]{3,2,1,0:T(8,128)(2,1)S(1)}, u32[]{:S(2)}, u32[]{:S(2)}) collective-permute-start(bf16[2,2,128,256]{3,2,1,0:T(8,128)(2,1)S(1)} %fusion.12), channel_id=1, source_target_pairs={{0,8},{1,9},{2,10},{3,11},{4,12},{5,13},{6,14},{7,15},{8,0},{9,1},... | collective-permute-start | bytes 786440 | tf_op jit(solution)/shard_map/ppermute | solution.py:46
  58.2 24.6 %collective-permute-start.23 = (bf16[1,2,128,256]{3,2,1,0:T(8,128)(2,1)}, bf16[1,2,128,256]{3,2,1,0:T(8,128)(2,1)}, u32[]{:S(2)}, u32[]{:S(2)}) collective-permute-start(bf16[1,2,128,256]{3,2,1,0:T(8,128)(2,1)} %collective-permute-done.22), channel_id=1, source_target_pairs={{128,256},{144,272},{160,288},{176,304},{192,320},{208,336},{224,3... | collective-permute-start | bytes 393224 | tf_op jit(solution)/shard_map/ppermute | solution.py:46
  62.2 30.5 %collective-permute-start.26 = (bf16[1,2,128,256]{3,2,1,0:T(8,128)(2,1)}, bf16[1,2,128,256]{3,2,1,0:T(8,128)(2,1)}, u32[]{:S(2)}, u32[]{:S(2)}) collective-permute-start(bf16[1,2,128,256]{3,2,1,0:T(8,128)(2,1)} %collective-permute-done.25), channel_id=1, source_target_pairs={{128,0},{144,16},{160,32},{176,48},{192,64},{208,80},{224,96},{240... | collective-permute-start | bytes 393224 | tf_op jit(solution)/shard_map/ppermute | solution.py:49
  66.4 24.0 %collective-permute-start.10 = (bf16[1,2,128,256]{3,2,1,0:T(8,128)(2,1)}, bf16[1,2,128,256]{3,2,1,0:T(8,128)(2,1)}, u32[]{:S(2)}, u32[]{:S(2)}) collective-permute-start(bf16[1,2,128,256]{3,2,1,0:T(8,128)(2,1)} %collective-permute-done.9), channel_id=1, source_target_pairs={{0,16},{16,32},{32,48},{48,64},{64,80},{80,96},{96,112},{112,0},{1... | collective-permute-start | bytes 393224 | tf_op jit(solution)/shard_map/ppermute | solution.py:46
  68.3 26.3 %collective-permute-start.14 = (bf16[1,2,128,256]{3,2,1,0:T(8,128)(2,1)}, bf16[1,2,128,256]{3,2,1,0:T(8,128)(2,1)}, u32[]{:S(2)}, u32[]{:S(2)}) collective-permute-start(bf16[1,2,128,256]{3,2,1,0:T(8,128)(2,1)} %collective-permute-done.13), channel_id=1, source_target_pairs={{0,112},{16,0},{32,16},{48,32},{64,48},{80,64},{96,80},{112,96},{1... | collective-permute-start | bytes 393224 | tf_op jit(solution)/shard_map/ppermute | solution.py:49
  76.7 60.4 %collective-permute-start.7 = (bf16[2,2,2,128,256]{4,3,2,1,0:T(8,128)(2,1)}, bf16[2,2,2,128,256]{4,3,2,1,0:T(8,128)(2,1)}, u32[]{:S(2)}, u32[]{:S(2)}) collective-permute-start(bf16[2,2,2,128,256]{4,3,2,1,0:T(8,128)(2,1)} %broadcast_select_fusion.1), channel_id=1, source_target_pairs={{0,6},{1,7},{2,0},{3,1},{4,2},{5,3},{6,4},{7,5},{8,14},{9,15},{10,... | collective-permute-start | bytes 1572872 | tf_op jit(solution)/shard_map/ppermute | solution.py:49
  82.8 43.5 %collective-permute-start.5 = (bf16[2,2,2,128,256]{4,3,2,1,0:T(8,128)(2,1)}, bf16[2,2,2,128,256]{4,3,2,1,0:T(8,128)(2,1)}, u32[]{:S(2)}, u32[]{:S(2)}) collective-permute-start(bf16[2,2,2,128,256]{4,3,2,1,0:T(8,128)(2,1)} %broadcast_select_fusion.1), channel_id=1, source_target_pairs={{0,2},{1,3},{2,4},{3,5},{4,6},{5,7},{6,0},{7,1},{8,10},{9,11},{10,... | collective-permute-start | bytes 1572872 | tf_op jit(solution)/shard_map/ppermute | solution.py:46
  95.3 27.6 %collective-permute-start.15 = (bf16[1,2,128,256]{3,2,1,0:T(8,128)(2,1)}, bf16[1,2,128,256]{3,2,1,0:T(8,128)(2,1)S(1)}, u32[]{:S(2)}, u32[]{:S(2)}) collective-permute-start(bf16[1,2,128,256]{3,2,1,0:T(8,128)(2,1)} %collective-permute-done.14), channel_id=1, source_target_pairs={{0,112},{16,0},{32,16},{48,32},{64,48},{80,64},{96,80},{112,96},{1... | collective-permute-start | bytes 393224 | tf_op jit(solution)/shard_map/ppermute | solution.py:49
  103.8 27.4 %collective-permute-start.28 = (bf16[4,1,2,128,256]{4,3,2,0,1:T(8,128)(2,1)}, bf16[4,1,2,128,256]{4,3,2,0,1:T(8,128)(2,1)}, u32[]{:S(2)}, u32[]{:S(2)}) collective-permute-start(bf16[4,1,2,128,256]{4,3,2,0,1:T(8,128)(2,1)} %bitcast_select_fusion.5), channel_id=1, source_target_pairs={{0,16},{16,32},{32,48},{48,64},{64,80},{80,96},{96,112},{112,0},{1... | collective-permute-start | bytes 1572872 | tf_op jit(solution)/shard_map/ppermute | solution.py:46
  119.1 21.9 %collective-permute-start.32 = (bf16[4,1,2,128,256]{4,3,2,0,1:T(8,128)(2,1)}, bf16[4,1,2,128,256]{4,3,2,0,1:T(8,128)(2,1)}, u32[]{:S(2)}, u32[]{:S(2)}) collective-permute-start(bf16[4,1,2,128,256]{4,3,2,0,1:T(8,128)(2,1)} %bitcast_select_fusion.5), channel_id=1, source_target_pairs={{0,112},{16,0},{32,16},{48,32},{64,48},{80,64},{96,80},{112,96},{1... | collective-permute-start | bytes 1572872 | tf_op jit(solution)/shard_map/ppermute | solution.py:49
  124.4 39.2 %collective-permute-start.16 = (bf16[8,1,2,128,256]{4,3,2,0,1:T(8,128)(2,1)S(1)}, bf16[8,1,2,128,256]{4,3,2,0,1:T(8,128)(2,1)}, u32[]{:S(2)}, u32[]{:S(2)}) collective-permute-start(bf16[8,1,2,128,256]{4,3,2,0,1:T(8,128)(2,1)S(1)} %bitcast_select_fusion.3), channel_id=1, source_target_pairs={{0,128},{16,144},{32,160},{48,176},{64,192},{80,208},{96,224},{112... | collective-permute-start | bytes 3145736 | tf_op jit(solution)/shard_map/ppermute | solution.py:46
  126.3 17.9 %collective-permute-start.6 = (bf16[2,2,2,128,256]{4,3,2,1,0:T(8,128)(2,1)}, bf16[2,2,2,128,256]{4,3,2,1,0:T(8,128)(2,1)S(1)}, u32[]{:S(2)}, u32[]{:S(2)}) collective-permute-start(bf16[2,2,2,128,256]{4,3,2,1,0:T(8,128)(2,1)} %collective-permute-done.5), channel_id=1, source_target_pairs={{0,2},{1,3},{2,4},{3,5},{4,6},{5,7},{6,0},{7,1},{8,10},{9,11},{10,... | collective-permute-start | bytes 1572872 | tf_op jit(solution)/shard_map/ppermute | solution.py:46
  131.2 21.7 %collective-permute-start.29 = (bf16[4,1,2,128,256]{4,3,2,0,1:T(8,128)(2,1)}, bf16[4,1,2,128,256]{4,3,2,0,1:T(8,128)(2,1)}, u32[]{:S(2)}, u32[]{:S(2)}) collective-permute-start(bf16[4,1,2,128,256]{4,3,2,0,1:T(8,128)(2,1)} %collective-permute-done.28), channel_id=1, source_target_pairs={{0,16},{16,32},{32,48},{48,64},{64,80},{80,96},{96,112},{112,0},{1... | collective-permute-start | bytes 1572872 | tf_op jit(solution)/shard_map/ppermute | solution.py:46
  137.1 37.7 %collective-permute-start.19 = (bf16[8,1,2,128,256]{4,3,2,0,1:T(8,128)(2,1)S(1)}, bf16[8,1,2,128,256]{4,3,2,0,1:T(8,128)(2,1)}, u32[]{:S(2)}, u32[]{:S(2)}) collective-permute-start(bf16[8,1,2,128,256]{4,3,2,0,1:T(8,128)(2,1)S(1)} %bitcast_select_fusion.3), channel_id=1, source_target_pairs={{128,0},{144,16},{160,32},{176,48},{192,64},{208,80},{224,96},{240... | collective-permute-start | bytes 3145736 | tf_op jit(solution)/shard_map/ppermute | solution.py:49
  151.0 59.1 %collective-permute-start.8 = (bf16[4,2,2,2,128,256]{5,4,3,2,1,0:T(8,128)(2,1)}, bf16[4,2,2,2,128,256]{5,4,3,2,1,0:T(8,128)(2,1)}, u32[]{:S(2)}, u32[]{:S(2)}) collective-permute-start(bf16[4,2,2,2,128,256]{5,4,3,2,1,0:T(8,128)(2,1)} %broadcast_select_fusion), channel_id=1, source_target_pairs={{0,1},{1,0},{2,3},{3,2},{4,5},{5,4},{6,7},{7,6},{8,9},{9,8},{10,11... | collective-permute-start | bytes 6291464 | tf_op jit(solution)/shard_map/ppermute | solution.py:46
  157.3 34.4 %collective-permute-start.34 = (bf16[4,1,2,128,256]{4,3,2,0,1:T(8,128)(2,1)}, bf16[4,1,2,128,256]{4,3,2,0,1:T(8,128)(2,1)S(1)}, u32[]{:S(2)}, u32[]{:S(2)}) collective-permute-start(bf16[4,1,2,128,256]{4,3,2,0,1:T(8,128)(2,1)} %collective-permute-done.33), channel_id=1, source_target_pairs={{0,112},{16,0},{32,16},{48,32},{64,48},{80,64},{96,80},{112,96},{1... | collective-permute-start | bytes 1572872 | tf_op jit(solution)/shard_map/ppermute | solution.py:49
  163.5 34.0 %collective-permute-start.17 = (bf16[8,1,2,128,256]{4,3,2,0,1:T(8,128)(2,1)}, bf16[8,1,2,128,256]{4,3,2,0,1:T(8,128)(2,1)}, u32[]{:S(2)}, u32[]{:S(2)}) collective-permute-start(bf16[8,1,2,128,256]{4,3,2,0,1:T(8,128)(2,1)} %collective-permute-done.16), channel_id=1, source_target_pairs={{128,256},{144,272},{160,288},{176,304},{192,320},{208,336},{224,3... | collective-permute-start | bytes 3145736 | tf_op jit(solution)/shard_map/ppermute | solution.py:46
  174.8 31.3 %collective-permute-start.20 = (bf16[8,1,2,128,256]{4,3,2,0,1:T(8,128)(2,1)}, bf16[8,1,2,128,256]{4,3,2,0,1:T(8,128)(2,1)}, u32[]{:S(2)}, u32[]{:S(2)}) collective-permute-start(bf16[8,1,2,128,256]{4,3,2,0,1:T(8,128)(2,1)} %collective-permute-done.19), channel_id=1, source_target_pairs={{128,0},{144,16},{160,32},{176,48},{192,64},{208,80},{224,96},{240... | collective-permute-start | bytes 3145736 | tf_op jit(solution)/shard_map/ppermute | solution.py:49
  197.5 39.5 %collective-permute-start.18 = (bf16[8,1,2,128,256]{4,3,2,0,1:T(8,128)(2,1)}, bf16[8,1,2,128,256]{4,3,2,0,1:T(8,128)(2,1)}, u32[]{:S(2)}, u32[]{:S(2)}) collective-permute-start(bf16[8,1,2,128,256]{4,3,2,0,1:T(8,128)(2,1)} %collective-permute-done.17), channel_id=1, source_target_pairs={{256,384},{272,400},{288,416},{304,432},{320,448},{336,464},{352,4... | collective-permute-start | bytes 3145736 | tf_op jit(solution)/shard_map/ppermute | solution.py:46
  206.1 37.8 %collective-permute-start.21 = (bf16[8,1,2,128,256]{4,3,2,0,1:T(8,128)(2,1)}, bf16[8,1,2,128,256]{4,3,2,0,1:T(8,128)(2,1)}, u32[]{:S(2)}, u32[]{:S(2)}) collective-permute-start(bf16[8,1,2,128,256]{4,3,2,0,1:T(8,128)(2,1)} %collective-permute-done.20), channel_id=1, source_target_pairs={{128,0},{144,16},{160,32},{176,48},{192,64},{208,80},{224,96},{240... | collective-permute-start | bytes 3145736 | tf_op jit(solution)/shard_map/ppermute | solution.py:49
  (19 other events, 229.7 us)

commit v3 on v2

--- a/solution.py
+++ b/solution.py
@@ -1,9 +1,11 @@
 import jax
 import jax.numpy as jnp
 from jax import lax
-from jax.sharding import PartitionSpec as P
+from jax.sharding import Mesh, PartitionSpec as P
 
 NS = 4096
+SHOT = ("z_lo", "y")
+RECV = ("z_hi", "x", "core")
 
 
 def complex_product(left_block, right_block, form):
@@ -22,9 +24,10 @@
     return jnp.stack((real_real - imag_imag, real_imag + imag_real), axis=1)
 
 
-def stream_gather(block, axis, stride, n, wrap):
-    axis_size = lax.axis_size(axis)
-    pos = (lax.axis_index(axis) // stride) % n
+def stream_gather(block, axis, wrap):
+    n = lax.axis_size(axis)
+    axis_size, stride = n, 1
+    pos = lax.axis_index(axis)
     k_up = n // 2 if wrap else n - 1
     k_dn = n - 1 - k_up if wrap else n - 1
 
@@ -62,7 +65,7 @@
 def mirrored_pieces(traces, shot_count, recv_count):
     block_rows = traces.shape[2]
     g = traces.shape[3] // block_rows
-    me_shot = lax.axis_index("shot")
+    me_shot = lax.axis_index(SHOT)
     pieces = []
     for a in range(g):
         got = []
@@ -73,41 +76,38 @@
                 for r in range(recv_count)
             ]
             part = traces[:, :, :, h * block_rows:(h + 1) * block_rows]
-            got.append(lax.ppermute(part, ("shot", "recv"), perm))
+            got.append(lax.ppermute(part, SHOT + RECV, perm))
         pieces.append(jnp.stack(got)[me_shot % g])
     return jnp.concatenate(pieces, axis=2)
 
 
 def per_device(traces):
-    recv_count = lax.axis_size("recv")
-    shot_count = lax.axis_size("shot")
+    recv_count = lax.axis_size(RECV)
+    shot_count = lax.axis_size(SHOT)
     mirrored = mirrored_pieces(traces, shot_count, recv_count)
     summed = traces.astype(jnp.float32) + jnp.swapaxes(mirrored, 2, 3).astype(jnp.float32)
     averaged = (summed * 0.5).astype(jnp.bfloat16)
     freqs, _, block_rows, col_width = averaged.shape
-    y_n, z_n = 8, shot_count // 8
-    x_n, zh_n = 4, recv_count // 8
-    first = stream_gather(averaged[:1], "shot", 1, y_n, True)
-    first = stream_gather(first, "shot", y_n, z_n, False)
-    second = stream_gather(averaged[1:], "shot", y_n, z_n, False)
-    second = jnp.swapaxes(stream_gather(second, "shot", 1, y_n, True), 0, 1)
+    first = stream_gather(stream_gather(averaged[:1], "y", True), "z_lo", False)
+    second = jnp.swapaxes(stream_gather(stream_gather(averaged[1:], "z_lo", False), "y", True), 0, 1)
     cols = jnp.concatenate((first, second), axis=2)
     col_panel = jnp.transpose(cols, (2, 3, 0, 1, 4, 5)).reshape(freqs, 2, shot_count * block_rows, col_width)
-    rows = stream_gather(averaged, "recv", 8, zh_n, True)
-    rows = stream_gather(rows, "recv", 2, x_n, True)
-    rows = stream_gather(rows, "recv", 1, 2, True)
-    row_panel = jnp.transpose(rows, (3, 4, 5, 2, 1, 0, 6)).reshape(freqs, 2, block_rows, recv_count * col_width)
+    rows = lax.all_gather(averaged, "z_hi", axis=0)
+    rows = lax.all_gather(rows, "x", axis=1)
+    rows = lax.all_gather(rows, "core", axis=2)
+    row_panel = jnp.transpose(rows, (3, 4, 5, 0, 1, 2, 6)).reshape(freqs, 2, block_rows, recv_count * col_width)
     product = complex_product(row_panel, col_panel, "fik,fkj->fij")
     scale_factor = jnp.float32(float(NS) ** (-0.5))
     return product * scale_factor
 
 
 def solution(mesh):
-    placed = (P(None, None, "shot", "recv"),)
+    fine = Mesh(mesh.devices.reshape(4, 8, 2, 4, 2), SHOT + RECV)
+    placed = P(None, None, SHOT, RECV)
     return jax.shard_map(
         per_device,
-        mesh=mesh,
-        in_specs=placed,
-        out_specs=P(None, None, "shot", "recv"),
+        mesh=fine,
+        in_specs=(placed,),
+        out_specs=placed,
         check_vma=False,
     )

time: 282 us -> 277 us (0.982)
  the two profiles are of different devices: /device:TPU:134 before, /device:TPU:2 now
where the time goes in v3:
time: 277 us; the launch traced here: 275 us
  starting transfers between devices  86 us (31%)
  local copies, waits for them, and re-layouts  60.1 us (22%)
  waiting for transfers between devices  55.5 us (20%)
  blocking collectives  30.7 us (11%)
  other arithmetic  20.3 us (7%)
  between operations  14 us (5%)
  matrix products  8.3 us (3%)
    ppermute x12, starting transfers between devices, stream_gather(): dn = lax.ppermute(dn, axis, perm(k, -1))  35.2 us
    ppermute x14, starting transfers between devices, stream_gather(): up = lax.ppermute(up, axis, perm(k, 1))  32.7 us
    all_gather x1, blocking collectives, per_device(): rows = lax.all_gather(averaged, 'z_hi', axis=0)  30.7 us
    ppermute x12, waiting for transfers between devices, stream_gather(): dn = lax.ppermute(dn, axis, perm(k, -1))  27.1 us
    ppermute x14, waiting for transfers between devices, stream_gather(): up = lax.ppermute(up, axis, perm(k, 1))  23.1 us
    unnamed x31, local copies, waits for them, and re-layouts  18.4 us
    ppermute x4, starting transfers between devices, mirrored_pieces(): got.append(lax.ppermute(part, SHOT + RECV, perm))  18.1 us
    gather x4, local copies, waits for them, and re-layouts, stream_gather(): return jnp.take(stacked, sel, axis=0)  12.5 us
  transfers between devices with their start and end apart: 32, of which 8 were waited for; matrix products, arithmetic and copies ran while one was open for 22% of the time, Pallas kernels for 0%

profile of v3, /device:TPU:2, one launch (start us, length us, event | category | flops | bytes accessed | tf_op | source)
XLA Modules:
  0.0 275.0 jit_solution(3014148296014578824)
XLA Ops:
  7.5 7.7 %collective-permute-start = (bf16[2,2,128,128]{3,2,1,0:T(8,128)(2,1)S(1)}, bf16[2,2,128,128]{3,2,1,0:T(8,128)(2,1)S(1)}, u32[]{:S(2)}, u32[]{:S(2)}) collective-permute-start(bf16[2,2,128,128]{3,2,1,0:T(8,128)(2,1)S(1)} %get-tuple-element.10), channel_id=1, source_target_pairs={{0,0},{1,32},{2,64},{3,96},{4,128},{5,160},{6,192},{7,224},{8,256}... | collective-permute-start | bytes 393224 | tf_op jit(solution)/shard_map/ppermute | solution.py:79
  16.5 8.5 %collective-permute-start.1 = (bf16[2,2,128,128]{3,2,1,0:T(8,128)(2,1)S(1)}, bf16[2,2,128,128]{3,2,1,0:T(8,128)(2,1)S(1)}, u32[]{:S(2)}, u32[]{:S(2)}) collective-permute-start(bf16[2,2,128,128]{3,2,1,0:T(8,128)(2,1)S(1)} %get-tuple-element.9), channel_id=1, source_target_pairs={{0,16},{1,48},{2,80},{3,112},{4,144},{5,176},{6,208},{7,240},{8,27... | collective-permute-start | bytes 393224 | tf_op jit(solution)/shard_map/ppermute | solution.py:79
  25.8 5.3 %collective-permute-done.1 = bf16[2,2,128,128]{3,2,1,0:T(8,128)(2,1)S(1)} collective-permute-done((bf16[2,2,128,128]{3,2,1,0:T(8,128)(2,1)S(1)}, bf16[2,2,128,128]{3,2,1,0:T(8,128)(2,1)S(1)}, u32[]{:S(2)}, u32[]{:S(2)}) %collective-permute-start.1) | collective-permute-done | bytes 131104 | tf_op jit(solution)/shard_map/ppermute | solution.py:79
  32.6 7.0 %collective-permute-start.4 = (bf16[1,2,128,256]{3,2,1,0:T(8,128)(2,1)S(1)}, bf16[1,2,128,256]{3,2,1,0:T(8,128)(2,1)S(1)}, u32[]{:S(2)}, u32[]{:S(2)}) collective-permute-start(bf16[1,2,128,256]{3,2,1,0:T(8,128)(2,1)S(1)} %get-tuple-element.5), channel_id=1, source_target_pairs={{0,16},{16,32},{32,48},{48,64},{64,80},{80,96},{96,112},{112,0},{1... | collective-permute-start | bytes 393224 | tf_op jit(solution)/shard_map/ppermute | solution.py:49
  41.5 6.1 %collective-permute-start.17 = (bf16[1,2,128,256]{3,2,1,0:T(8,128)(2,1)S(1)}, bf16[1,2,128,256]{3,2,1,0:T(8,128)(2,1)S(1)}, u32[]{:S(2)}, u32[]{:S(2)}) collective-permute-start(bf16[1,2,128,256]{3,2,1,0:T(8,128)(2,1)S(1)} %get-tuple-element.6), channel_id=1, source_target_pairs={{0,128},{128,256},{256,384},{1,129},{129,257},{257,385},{2,130},{1... | collective-permute-start | bytes 393224 | tf_op jit(solution)/shard_map/ppermute | solution.py:49
  48.9 30.7 %all-gather = bf16[4,2,128,256]{3,2,1,0:T(8,128)(2,1)} all-gather(bf16[2,2,128,256]{3,2,1,0:T(8,128)(2,1)S(1)} %fusion.10), channel_id=2, replica_groups=mesh['z_lo'=4,'y'=8,'z_hi'=2,'x'=4,'core'=2] {'z_hi'}, dimensions={0}, use_global_device_ids=true | all-gather | bytes 786432 | tf_op jit(solution)/shard_map/all_gather | solution.py:95
  81.7 5.1 %collective-permute-start.9 = (bf16[1,2,128,256]{3,2,1,0:T(8,128)(2,1)S(1)}, bf16[1,2,128,256]{3,2,1,0:T(8,128)(2,1)S(1)}, u32[]{:S(2)}, u32[]{:S(2)}) collective-permute-start(bf16[1,2,128,256]{3,2,1,0:T(8,128)(2,1)S(1)} %collective-permute-done.8), channel_id=1, source_target_pairs={{0,112},{16,0},{32,16},{48,32},{64,48},{80,64},{96,80},{112,96},{1... | collective-permute-start | bytes 393224 | tf_op jit(solution)/shard_map/ppermute | solution.py:52
  90.8 5.1 %collective-permute-start.10 = (bf16[1,2,128,256]{3,2,1,0:T(8,128)(2,1)S(1)}, bf16[1,2,128,256]{3,2,1,0:T(8,128)(2,1)S(1)}, u32[]{:S(2)}, u32[]{:S(2)}) collective-permute-start(bf16[1,2,128,256]{3,2,1,0:T(8,128)(2,1)S(1)} %collective-permute-done.9), channel_id=1, source_target_pairs={{0,112},{16,0},{32,16},{48,32},{64,48},{80,64},{96,80},{112,96},{1... | collective-permute-start | bytes 393224 | tf_op jit(solution)/shard_map/ppermute | solution.py:52
  101.5 7.8 %collective-permute-done.22 = bf16[1,2,128,256]{3,2,1,0:T(8,128)(2,1)S(1)} collective-permute-done((bf16[1,2,128,256]{3,2,1,0:T(8,128)(2,1)S(1)}, bf16[1,2,128,256]{3,2,1,0:T(8,128)(2,1)S(1)}, u32[]{:S(2)}, u32[]{:S(2)}) %collective-permute-start.22) | collective-permute-done | bytes 131104 | tf_op jit(solution)/shard_map/ppermute | solution.py:52
  112.7 5.1 %collective-permute-start.27 = (bf16[4,1,2,128,256]{4,3,2,0,1:T(8,128)(2,1)}, bf16[4,1,2,128,256]{4,3,2,0,1:T(8,128)(2,1)S(1)}, u32[]{:S(2)}, u32[]{:S(2)}) collective-permute-start(bf16[4,1,2,128,256]{4,3,2,0,1:T(8,128)(2,1)} %bitcast_select_fusion.4), channel_id=1, source_target_pairs={{0,112},{16,0},{32,16},{48,32},{64,48},{80,64},{96,80},{112,96},{1... | collective-permute-start | bytes 1572872 | tf_op jit(solution)/shard_map/ppermute | solution.py:52
  119.8 9.1 %collective-permute-done.7 = bf16[1,2,128,256]{3,2,1,0:T(8,128)(2,1)S(1)} collective-permute-done((bf16[1,2,128,256]{3,2,1,0:T(8,128)(2,1)S(1)}, bf16[1,2,128,256]{3,2,1,0:T(8,128)(2,1)S(1)}, u32[]{:S(2)}, u32[]{:S(2)}) %collective-permute-start.7) | collective-permute-done | bytes 131104 | tf_op jit(solution)/shard_map/ppermute | solution.py:49
  136.4 5.1 %collective-permute-start.28 = (bf16[4,1,2,128,256]{4,3,2,0,1:T(8,128)(2,1)S(1)}, bf16[4,1,2,128,256]{4,3,2,0,1:T(8,128)(2,1)S(1)}, u32[]{:S(2)}, u32[]{:S(2)}) collective-permute-start(bf16[4,1,2,128,256]{4,3,2,0,1:T(8,128)(2,1)S(1)} %collective-permute-done.27), channel_id=1, source_target_pairs={{0,112},{16,0},{32,16},{48,32},{64,48},{80,64},{96,80},{112,96},{1... | collective-permute-start | bytes 1572872 | tf_op jit(solution)/shard_map/ppermute | solution.py:52
  149.3 4.0 %collective-permute-done.11 = bf16[8,1,2,128,256]{4,3,2,0,1:T(8,128)(2,1)} collective-permute-done((bf16[8,1,2,128,256]{4,3,2,0,1:T(8,128)(2,1)S(1)}, bf16[8,1,2,128,256]{4,3,2,0,1:T(8,128)(2,1)}, u32[]{:S(2)}, u32[]{:S(2)}) %collective-permute-start.11) | collective-permute-done | bytes 1048608 | tf_op jit(solution)/shard_map/ppermute | solution.py:49
  154.9 4.8 %collective-permute-start.29 = (bf16[4,1,2,128,256]{4,3,2,0,1:T(8,128)(2,1)S(1)}, bf16[4,1,2,128,256]{4,3,2,0,1:T(8,128)(2,1)}, u32[]{:S(2)}, u32[]{:S(2)}) collective-permute-start(bf16[4,1,2,128,256]{4,3,2,0,1:T(8,128)(2,1)S(1)} %collective-permute-done.28), channel_id=1, source_target_pairs={{0,112},{16,0},{32,16},{48,32},{64,48},{80,64},{96,80},{112,96},{1... | collective-permute-start | bytes 1572872 | tf_op jit(solution)/shard_map/ppermute | solution.py:52
  167.2 7.3 %collective-permute-done.26 = bf16[4,1,2,128,256]{4,3,2,0,1:T(8,128)(2,1)} collective-permute-done((bf16[4,1,2,128,256]{4,3,2,0,1:T(8,128)(2,1)}, bf16[4,1,2,128,256]{4,3,2,0,1:T(8,128)(2,1)}, u32[]{:S(2)}, u32[]{:S(2)}) %collective-permute-start.26) | collective-permute-done | bytes 524320 | tf_op jit(solution)/shard_map/ppermute | solution.py:49
  181.7 5.4 %gather_fusion.3 = bf16[8,4,2,128,256]{4,3,2,1,0:T(8,128)(2,1)} fusion(bf16[8,4,2,128,256]{4,3,2,1,0:T(8,128)(2,1)} %bitcast.63, s32[1024]{0:T(1024)S(1)} %pad_clamp_fusion.1), kind=kCustom, calls=%fused_computation.3 | custom fusion | bytes 8388640 | tf_op jit(solution)/shard_map/jit(_take)/gather | solution.py:62
  187.1 4.6 %fusion = bf16[4,8,1,2,128,256]{5,4,3,1,0,2:T(8,128)(2,1)} fusion(bf16[8,4,2,128,256]{4,3,2,1,0:T(8,128)(2,1)} %gather_fusion.3, pred[8]{0:T(512)(128)(4,1)S(1)} %compare_and_fusion), kind=kLoop, calls=%fused_computation.8 | loop fusion | flops 2097152 | bytes 8388616 | tf_op jit(solution)/shard_map/transpose | solution.py:92
  199.9 15.8 %collective-permute-done.16 = bf16[8,1,2,128,256]{4,3,2,0,1:T(8,128)(2,1)S(1)} collective-permute-done((bf16[8,1,2,128,256]{4,3,2,0,1:T(8,128)(2,1)}, bf16[8,1,2,128,256]{4,3,2,0,1:T(8,128)(2,1)S(1)}, u32[]{:S(2)}, u32[]{:S(2)}) %collective-permute-start.16) | collective-permute-done | bytes 1048608 | tf_op jit(solution)/shard_map/ppermute | solution.py:52
  216.8 5.9 %gather_fusion.1 = bf16[4,8,2,128,256]{4,3,2,1,0:T(8,128)(2,1)} fusion(bf16[7,8,2,128,256]{4,3,2,1,0:T(8,128)(2,1)} %bitcast.36, s32[1024]{0:T(1024)S(1)} %pad_clamp_fusion), kind=kCustom, calls=%fused_computation.1 | custom fusion | bytes 8388624 | tf_op jit(solution)/shard_map/jit(_take)/gather | solution.py:62
  222.7 4.8 %bitcast_select_fusion.1 = bf16[4,8,1,2,128,256]{5,4,3,1,0,2:T(8,128)(2,1)} fusion(bf16[4,8,2,128,256]{4,3,2,1,0:T(8,128)(2,1)} %gather_fusion.1, pred[4]{0:T(512)(128)(4,1)S(1)} %compare_and_fusion.1), kind=kLoop, calls=%fused_computation.9 | loop fusion | flops 2097152 | bytes 8388612 | tf_op jit(solution)/shard_map/jit(_take)/select_n | solution.py:62
  227.5 6.2 %maximum_bitcast_fusion = bf16[2,2,4,8,128,256]{5,4,1,3,2,0:T(8,128)(2,1)} fusion(bf16[4,8,1,2,128,256]{5,4,3,1,0,2:T(8,128)(2,1)S(1)} %copy-done, bf16[4,8,1,2,128,256]{5,4,3,1,0,2:T(8,128)(2,1)} %bitcast_select_fusion.1), kind=kLoop, calls=%fused_computation.4 | loop fusion | flops 4194304 | bytes 16777216 | tf_op jit(solution)/shard_map/transpose | solution.py:94
  233.8 7.8 %copy.53 = bf16[2,2,4,8,128,256]{5,4,3,2,0,1:T(8,128)(2,1)} copy(bf16[2,2,4,8,128,256]{5,4,1,3,2,0:T(8,128)(2,1)} %maximum_bitcast_fusion) | data formatting | bytes 16777216 | tf_op jit(solution)/shard_map/transpose | solution.py:94
  241.5 8.5 %copy.38 = bf16[2,2,128,2,4,2,256]{6,5,4,3,2,0,1:T(2,128)(2,1)} copy(bf16[2,2,128,2,4,2,256]{6,2,1,0,5,4,3:T(8,128)(2,1)} %bitcast.174) | data formatting | bytes 8388608 | tf_op jit(solution)/shard_map/transpose | solution.py:98
  250.0 7.8 %reshape.163 = bf16[2,2,128,4096]{3,2,0,1:T(8,128)(2,1)} reshape(bf16[2,2,128,2,4,2,256]{6,5,4,3,2,0,1:T(2,128)(2,1)} %copy.38) | data formatting | bytes 8388608 | tf_op jit(solution)/shard_map/reshape | solution.py:98
  (111 shorter events, 75.3 us)
Async XLA Ops:
  6.5 156.5 %all-gather.6.cloned.1.call-start = ((), (), s32[]{:S(2)}) async-start(), calls=%async_computation | async-start | bytes 2621440 | tf_op jit(solution)/shard_map/all_gather | solution.py:96
  7.5 18.3 %collective-permute-start = (bf16[2,2,128,128]{3,2,1,0:T(8,128)(2,1)S(1)}, bf16[2,2,128,128]{3,2,1,0:T(8,128)(2,1)S(1)}, u32[]{:S(2)}, u32[]{:S(2)}) collective-permute-start(bf16[2,2,128,128]{3,2,1,0:T(8,128)(2,1)S(1)} %get-tuple-element.10), channel_id=1, source_target_pairs={{0,0},{1,32},{2,64},{3,96},{4,128},{5,160},{6,192},{7,224},{8,256}... | collective-permute-start | bytes 393224 | tf_op jit(solution)/shard_map/ppermute | solution.py:79
  15.2 15.9 %collective-permute-start.2 = (bf16[2,2,128,128]{3,2,1,0:T(8,128)(2,1)S(1)}, bf16[2,2,128,128]{3,2,1,0:T(8,128)(2,1)S(1)}, u32[]{:S(2)}, u32[]{:S(2)}) collective-permute-start(bf16[2,2,128,128]{3,2,1,0:T(8,128)(2,1)S(1)} %get-tuple-element.10), channel_id=1, source_target_pairs={{16,0},{17,32},{18,64},{19,96},{20,128},{21,160},{22,192},{23,224}... | collective-permute-start | bytes 393224 | tf_op jit(solution)/shard_map/ppermute | solution.py:79
  16.5 14.6 %collective-permute-start.1 = (bf16[2,2,128,128]{3,2,1,0:T(8,128)(2,1)S(1)}, bf16[2,2,128,128]{3,2,1,0:T(8,128)(2,1)S(1)}, u32[]{:S(2)}, u32[]{:S(2)}) collective-permute-start(bf16[2,2,128,128]{3,2,1,0:T(8,128)(2,1)S(1)} %get-tuple-element.9), channel_id=1, source_target_pairs={{0,16},{1,48},{2,80},{3,112},{4,144},{5,176},{6,208},{7,240},{8,27... | collective-permute-start | bytes 393224 | tf_op jit(solution)/shard_map/ppermute | solution.py:79
  32.6 47.2 %collective-permute-start.4 = (bf16[1,2,128,256]{3,2,1,0:T(8,128)(2,1)S(1)}, bf16[1,2,128,256]{3,2,1,0:T(8,128)(2,1)S(1)}, u32[]{:S(2)}, u32[]{:S(2)}) collective-permute-start(bf16[1,2,128,256]{3,2,1,0:T(8,128)(2,1)S(1)} %get-tuple-element.5), channel_id=1, source_target_pairs={{0,16},{16,32},{32,48},{48,64},{64,80},{80,96},{96,112},{112,0},{1... | collective-permute-start | bytes 393224 | tf_op jit(solution)/shard_map/ppermute | solution.py:49
  39.6 42.1 %collective-permute-start.8 = (bf16[1,2,128,256]{3,2,1,0:T(8,128)(2,1)S(1)}, bf16[1,2,128,256]{3,2,1,0:T(8,128)(2,1)S(1)}, u32[]{:S(2)}, u32[]{:S(2)}) collective-permute-start(bf16[1,2,128,256]{3,2,1,0:T(8,128)(2,1)S(1)} %get-tuple-element.5), channel_id=1, source_target_pairs={{0,112},{16,0},{32,16},{48,32},{64,48},{80,64},{96,80},{112,96},{1... | collective-permute-start | bytes 393224 | tf_op jit(solution)/shard_map/ppermute | solution.py:52
  41.5 45.3 %collective-permute-start.17 = (bf16[1,2,128,256]{3,2,1,0:T(8,128)(2,1)S(1)}, bf16[1,2,128,256]{3,2,1,0:T(8,128)(2,1)S(1)}, u32[]{:S(2)}, u32[]{:S(2)}) collective-permute-start(bf16[1,2,128,256]{3,2,1,0:T(8,128)(2,1)S(1)} %get-tuple-element.6), channel_id=1, source_target_pairs={{0,128},{128,256},{256,384},{1,129},{129,257},{257,385},{2,130},{1... | collective-permute-start | bytes 393224 | tf_op jit(solution)/shard_map/ppermute | solution.py:49
  47.6 39.9 %collective-permute-start.20 = (bf16[1,2,128,256]{3,2,1,0:T(8,128)(2,1)S(1)}, bf16[1,2,128,256]{3,2,1,0:T(8,128)(2,1)S(1)}, u32[]{:S(2)}, u32[]{:S(2)}) collective-permute-start(bf16[1,2,128,256]{3,2,1,0:T(8,128)(2,1)S(1)} %get-tuple-element.6), channel_id=1, source_target_pairs={{128,0},{256,128},{384,256},{129,1},{257,129},{385,257},{130,2},{2... | collective-permute-start | bytes 393224 | tf_op jit(solution)/shard_map/ppermute | solution.py:52
  79.6 161.9 %all-gather.8.cloned.1.call-start = ((), (), s32[]{:S(2)}) async-start(), calls=%async_computation.1 | async-start | bytes 6291456 | tf_op jit(solution)/shard_map/all_gather | solution.py:97
  88.8 29.0 %collective-permute-start.6 = (bf16[1,2,128,256]{3,2,1,0:T(8,128)(2,1)S(1)}, bf16[1,2,128,256]{3,2,1,0:T(8,128)(2,1)S(1)}, u32[]{:S(2)}, u32[]{:S(2)}) collective-permute-start(bf16[1,2,128,256]{3,2,1,0:T(8,128)(2,1)S(1)} %collective-permute-done.5), channel_id=1, source_target_pairs={{0,16},{16,32},{32,48},{48,64},{64,80},{80,96},{96,112},{112,0},{1... | collective-permute-start | bytes 393224 | tf_op jit(solution)/shard_map/ppermute | solution.py:49
  90.8 38.2 %collective-permute-start.10 = (bf16[1,2,128,256]{3,2,1,0:T(8,128)(2,1)S(1)}, bf16[1,2,128,256]{3,2,1,0:T(8,128)(2,1)S(1)}, u32[]{:S(2)}, u32[]{:S(2)}) collective-permute-start(bf16[1,2,128,256]{3,2,1,0:T(8,128)(2,1)S(1)} %collective-permute-done.9), channel_id=1, source_target_pairs={{0,112},{16,0},{32,16},{48,32},{64,48},{80,64},{96,80},{112,96},{1... | collective-permute-start | bytes 393224 | tf_op jit(solution)/shard_map/ppermute | solution.py:52
  110.8 18.8 %collective-permute-start.23 = (bf16[4,1,2,128,256]{4,3,2,0,1:T(8,128)(2,1)}, bf16[4,1,2,128,256]{4,3,2,0,1:T(8,128)(2,1)}, u32[]{:S(2)}, u32[]{:S(2)}) collective-permute-start(bf16[4,1,2,128,256]{4,3,2,0,1:T(8,128)(2,1)} %bitcast_select_fusion.4), channel_id=1, source_target_pairs={{0,16},{16,32},{32,48},{48,64},{64,80},{80,96},{96,112},{112,0},{1... | collective-permute-start | bytes 1572872 | tf_op jit(solution)/shard_map/ppermute | solution.py:49
  112.7 23.7 %collective-permute-start.27 = (bf16[4,1,2,128,256]{4,3,2,0,1:T(8,128)(2,1)}, bf16[4,1,2,128,256]{4,3,2,0,1:T(8,128)(2,1)S(1)}, u32[]{:S(2)}, u32[]{:S(2)}) collective-permute-start(bf16[4,1,2,128,256]{4,3,2,0,1:T(8,128)(2,1)} %bitcast_select_fusion.4), channel_id=1, source_target_pairs={{0,112},{16,0},{32,16},{48,32},{64,48},{80,64},{96,80},{112,96},{1... | collective-permute-start | bytes 1572872 | tf_op jit(solution)/shard_map/ppermute | solution.py:52
  129.6 14.6 %collective-permute-start.24 = (bf16[4,1,2,128,256]{4,3,2,0,1:T(8,128)(2,1)}, bf16[4,1,2,128,256]{4,3,2,0,1:T(8,128)(2,1)S(1)}, u32[]{:S(2)}, u32[]{:S(2)}) collective-permute-start(bf16[4,1,2,128,256]{4,3,2,0,1:T(8,128)(2,1)} %collective-permute-done.23), channel_id=1, source_target_pairs={{0,16},{16,32},{32,48},{48,64},{64,80},{80,96},{96,112},{112,0},{1... | collective-permute-start | bytes 1572872 | tf_op jit(solution)/shard_map/ppermute | solution.py:49
  131.7 21.6 %collective-permute-start.11 = (bf16[8,1,2,128,256]{4,3,2,0,1:T(8,128)(2,1)S(1)}, bf16[8,1,2,128,256]{4,3,2,0,1:T(8,128)(2,1)}, u32[]{:S(2)}, u32[]{:S(2)}) collective-permute-start(bf16[8,1,2,128,256]{4,3,2,0,1:T(8,128)(2,1)S(1)} %bitcast_select_fusion.2), channel_id=1, source_target_pairs={{0,128},{128,256},{256,384},{1,129},{129,257},{257,385},{2,130},{1... | collective-permute-start | bytes 3145736 | tf_op jit(solution)/shard_map/ppermute | solution.py:49
  134.1 25.6 %collective-permute-start.14 = (bf16[8,1,2,128,256]{4,3,2,0,1:T(8,128)(2,1)S(1)}, bf16[8,1,2,128,256]{4,3,2,0,1:T(8,128)(2,1)S(1)}, u32[]{:S(2)}, u32[]{:S(2)}) collective-permute-start(bf16[8,1,2,128,256]{4,3,2,0,1:T(8,128)(2,1)S(1)} %bitcast_select_fusion.2), channel_id=1, source_target_pairs={{128,0},{256,128},{384,256},{129,1},{257,129},{385,257},{130,2},{2... | collective-permute-start | bytes 3145736 | tf_op jit(solution)/shard_map/ppermute | solution.py:52
  136.4 18.5 %collective-permute-start.28 = (bf16[4,1,2,128,256]{4,3,2,0,1:T(8,128)(2,1)S(1)}, bf16[4,1,2,128,256]{4,3,2,0,1:T(8,128)(2,1)S(1)}, u32[]{:S(2)}, u32[]{:S(2)}) collective-permute-start(bf16[4,1,2,128,256]{4,3,2,0,1:T(8,128)(2,1)S(1)} %collective-permute-done.27), channel_id=1, source_target_pairs={{0,112},{16,0},{32,16},{48,32},{64,48},{80,64},{96,80},{112,96},{1... | collective-permute-start | bytes 1572872 | tf_op jit(solution)/shard_map/ppermute | solution.py:52
  144.2 16.9 %collective-permute-start.25 = (bf16[4,1,2,128,256]{4,3,2,0,1:T(8,128)(2,1)S(1)}, bf16[4,1,2,128,256]{4,3,2,0,1:T(8,128)(2,1)}, u32[]{:S(2)}, u32[]{:S(2)}) collective-permute-start(bf16[4,1,2,128,256]{4,3,2,0,1:T(8,128)(2,1)S(1)} %collective-permute-done.24), channel_id=1, source_target_pairs={{0,16},{16,32},{32,48},{48,64},{64,80},{80,96},{96,112},{112,0},{1... | collective-permute-start | bytes 1572872 | tf_op jit(solution)/shard_map/ppermute | solution.py:49
  153.3 24.0 %collective-permute-start.12 = (bf16[8,1,2,128,256]{4,3,2,0,1:T(8,128)(2,1)}, bf16[8,1,2,128,256]{4,3,2,0,1:T(8,128)(2,1)S(1)}, u32[]{:S(2)}, u32[]{:S(2)}) collective-permute-start(bf16[8,1,2,128,256]{4,3,2,0,1:T(8,128)(2,1)} %collective-permute-done.11), channel_id=1, source_target_pairs={{128,256},{256,384},{129,257},{257,385},{130,258},{258,386},{131,2... | collective-permute-start | bytes 3145736 | tf_op jit(solution)/shard_map/ppermute | solution.py:49
  154.9 24.9 %collective-permute-start.29 = (bf16[4,1,2,128,256]{4,3,2,0,1:T(8,128)(2,1)S(1)}, bf16[4,1,2,128,256]{4,3,2,0,1:T(8,128)(2,1)}, u32[]{:S(2)}, u32[]{:S(2)}) collective-permute-start(bf16[4,1,2,128,256]{4,3,2,0,1:T(8,128)(2,1)S(1)} %collective-permute-done.28), channel_id=1, source_target_pairs={{0,112},{16,0},{32,16},{48,32},{64,48},{80,64},{96,80},{112,96},{1... | collective-permute-start | bytes 1572872 | tf_op jit(solution)/shard_map/ppermute | solution.py:52
  159.8 32.0 %collective-permute-start.15 = (bf16[8,1,2,128,256]{4,3,2,0,1:T(8,128)(2,1)S(1)}, bf16[8,1,2,128,256]{4,3,2,0,1:T(8,128)(2,1)}, u32[]{:S(2)}, u32[]{:S(2)}) collective-permute-start(bf16[8,1,2,128,256]{4,3,2,0,1:T(8,128)(2,1)S(1)} %collective-permute-done.14), channel_id=1, source_target_pairs={{128,0},{256,128},{129,1},{257,129},{130,2},{258,130},{131,3},{259... | collective-permute-start | bytes 3145736 | tf_op jit(solution)/shard_map/ppermute | solution.py:52
  161.1 13.5 %collective-permute-start.26 = (bf16[4,1,2,128,256]{4,3,2,0,1:T(8,128)(2,1)}, bf16[4,1,2,128,256]{4,3,2,0,1:T(8,128)(2,1)}, u32[]{:S(2)}, u32[]{:S(2)}) collective-permute-start(bf16[4,1,2,128,256]{4,3,2,0,1:T(8,128)(2,1)} %collective-permute-done.25), channel_id=1, source_target_pairs={{0,16},{16,32},{32,48},{48,64},{64,80},{80,96},{96,112},{112,0},{1... | collective-permute-start | bytes 1572872 | tf_op jit(solution)/shard_map/ppermute | solution.py:49
  177.3 17.0 %collective-permute-start.13 = (bf16[8,1,2,128,256]{4,3,2,0,1:T(8,128)(2,1)S(1)}, bf16[8,1,2,128,256]{4,3,2,0,1:T(8,128)(2,1)}, u32[]{:S(2)}, u32[]{:S(2)}) collective-permute-start(bf16[8,1,2,128,256]{4,3,2,0,1:T(8,128)(2,1)S(1)} %collective-permute-done.12), channel_id=1, source_target_pairs={{256,384},{257,385},{258,386},{259,387},{260,388},{261,389},{262,3... | collective-permute-start | bytes 3145736 | tf_op jit(solution)/shard_map/ppermute | solution.py:49
  191.7 24.0 %collective-permute-start.16 = (bf16[8,1,2,128,256]{4,3,2,0,1:T(8,128)(2,1)}, bf16[8,1,2,128,256]{4,3,2,0,1:T(8,128)(2,1)S(1)}, u32[]{:S(2)}, u32[]{:S(2)}) collective-permute-start(bf16[8,1,2,128,256]{4,3,2,0,1:T(8,128)(2,1)} %collective-permute-done.15), channel_id=1, source_target_pairs={{128,0},{129,1},{130,2},{131,3},{132,4},{133,5},{134,6},{135,7},{1... | collective-permute-start | bytes 3145736 | tf_op jit(solution)/shard_map/ppermute | solution.py:52
  (12 other events, 91.8 us)
Sparse Core Ops, SparseCore 0:
  79.8 34.4 all-gather.5
  163.2 23.7 all-gather.7

commit v4 on v3

--- a/solution.py
+++ b/solution.py
@@ -88,11 +88,9 @@
     summed = traces.astype(jnp.float32) + jnp.swapaxes(mirrored, 2, 3).astype(jnp.float32)
     averaged = (summed * 0.5).astype(jnp.bfloat16)
     freqs, _, block_rows, col_width = averaged.shape
-    first = stream_gather(stream_gather(averaged[:1], "y", True), "z_lo", False)
-    second = jnp.swapaxes(stream_gather(stream_gather(averaged[1:], "z_lo", False), "y", True), 0, 1)
-    cols = jnp.concatenate((first, second), axis=2)
-    col_panel = jnp.transpose(cols, (2, 3, 0, 1, 4, 5)).reshape(freqs, 2, shot_count * block_rows, col_width)
-    rows = lax.all_gather(averaged, "z_hi", axis=0)
+    cols = stream_gather(stream_gather(averaged, "z_lo", False), "y", True)
+    col_panel = jnp.transpose(cols, (2, 3, 1, 0, 4, 5)).reshape(freqs, 2, shot_count * block_rows, col_width)
+    rows = stream_gather(averaged, "z_hi", True)
     rows = lax.all_gather(rows, "x", axis=1)
     rows = lax.all_gather(rows, "core", axis=2)
     row_panel = jnp.transpose(rows, (3, 4, 5, 0, 1, 2, 6)).reshape(freqs, 2, block_rows, recv_count * col_width)

time: 277 us -> 265 us (0.957)
  the two profiles are of different devices: /device:TPU:2 before, /device:TPU:56 now
where the time goes in v4:
time: 265 us; the launch traced here: 260 us
  waiting for transfers between devices  102 us (38%)
  starting transfers between devices  75 us (28%)
  local copies, waits for them, and re-layouts  49.7 us (19%)
  between operations  13.8 us (5%)
  other arithmetic  11.2 us (4%)
  matrix products  8.3 us (3%)
    ppermute x8, waiting for transfers between devices, stream_gather(): up = lax.ppermute(up, axis, perm(k, 1))  75.1 us
    ppermute x8, starting transfers between devices, stream_gather(): up = lax.ppermute(up, axis, perm(k, 1))  51.9 us
    ppermute x6, waiting for transfers between devices, stream_gather(): dn = lax.ppermute(dn, axis, perm(k, -1))  17.4 us
    unnamed x19, local copies, waits for them, and re-layouts  13.1 us
    ppermute x4, starting transfers between devices, mirrored_pieces(): got.append(lax.ppermute(part, SHOT + RECV, perm))  12.8 us
    ppermute x6, starting transfers between devices, stream_gather(): dn = lax.ppermute(dn, axis, perm(k, -1))  10.3 us
    gather x3, local copies, waits for them, and re-layouts, stream_gather(): return jnp.take(stacked, sel, axis=0)  9.26 us
    ppermute x4, waiting for transfers between devices, mirrored_pieces(): got.append(lax.ppermute(part, SHOT + RECV, perm))  9.24 us
  transfers between devices with their start and end apart: 20, of which 10 were waited for; matrix products, arithmetic and copies ran while one was open for 15% of the time, Pallas kernels for 0%

profile of v4, /device:TPU:56, one launch (start us, length us, event | category | flops | bytes accessed | tf_op | source)
XLA Modules:
  0.0 259.8 jit_solution(5697723452965426026)
XLA Ops:
  8.2 7.8 %collective-permute-start.2 = (bf16[2,2,128,128]{3,2,1,0:T(8,128)(2,1)S(1)}, bf16[2,2,128,128]{3,2,1,0:T(8,128)(2,1)S(1)}, u32[]{:S(2)}, u32[]{:S(2)}) collective-permute-start(bf16[2,2,128,128]{3,2,1,0:T(8,128)(2,1)S(1)} %get-tuple-element.8), channel_id=1, source_target_pairs={{16,0},{17,32},{18,64},{19,96},{20,128},{21,160},{22,192},{23,224}... | collective-permute-start | bytes 393224 | tf_op jit(solution)/shard_map/ppermute | solution.py:79
  17.3 3.1 %collective-permute-start.3 = (bf16[2,2,128,128]{3,2,1,0:T(8,128)(2,1)S(1)}, bf16[2,2,128,128]{3,2,1,0:T(8,128)(2,1)S(1)}, u32[]{:S(2)}, u32[]{:S(2)}) collective-permute-start(bf16[2,2,128,128]{3,2,1,0:T(8,128)(2,1)S(1)} %get-tuple-element.7), channel_id=1, source_target_pairs={{16,16},{17,48},{18,80},{19,112},{20,144},{21,176},{22,208},{23,24... | collective-permute-start | bytes 393224 | tf_op jit(solution)/shard_map/ppermute | solution.py:79
  20.4 4.6 %collective-permute-done.1 = bf16[2,2,128,128]{3,2,1,0:T(8,128)(2,1)S(1)} collective-permute-done((bf16[2,2,128,128]{3,2,1,0:T(8,128)(2,1)S(1)}, bf16[2,2,128,128]{3,2,1,0:T(8,128)(2,1)S(1)}, u32[]{:S(2)}, u32[]{:S(2)}) %collective-permute-start.1) | collective-permute-done | bytes 131104 | tf_op jit(solution)/shard_map/ppermute | solution.py:79
  25.1 4.6 %collective-permute-done.3 = bf16[2,2,128,128]{3,2,1,0:T(8,128)(2,1)S(1)} collective-permute-done((bf16[2,2,128,128]{3,2,1,0:T(8,128)(2,1)S(1)}, bf16[2,2,128,128]{3,2,1,0:T(8,128)(2,1)S(1)}, u32[]{:S(2)}, u32[]{:S(2)}) %collective-permute-start.3) | collective-permute-done | bytes 131104 | tf_op jit(solution)/shard_map/ppermute | solution.py:79
  31.1 9.4 %collective-permute-start.5 = (bf16[2,2,128,256]{3,2,1,0:T(8,128)(2,1)S(1)}, bf16[2,2,128,256]{3,2,1,0:T(8,128)(2,1)}, u32[]{:S(2)}, u32[]{:S(2)}) collective-permute-start(bf16[2,2,128,256]{3,2,1,0:T(8,128)(2,1)S(1)} %get-tuple-element.6), channel_id=1, source_target_pairs={{0,128},{128,256},{256,384},{1,129},{129,257},{257,385},{2,130},{1... | collective-permute-start | bytes 786440 | tf_op jit(solution)/shard_map/ppermute | solution.py:49
  40.5 24.6 %collective-permute-start.4 = (bf16[2,2,128,256]{3,2,1,0:T(8,128)(2,1)S(1)}, bf16[2,2,128,256]{3,2,1,0:T(8,128)(2,1)S(1)}, u32[]{:S(2)}, u32[]{:S(2)}) collective-permute-start(bf16[2,2,128,256]{3,2,1,0:T(8,128)(2,1)S(1)} %get-tuple-element.6), channel_id=1, source_target_pairs={{0,8},{8,0},{1,9},{9,1},{2,10},{10,2},{3,11},{11,3},{4,12},{12,4},... | collective-permute-start | bytes 786440 | tf_op jit(solution)/shard_map/ppermute | solution.py:49
  67.9 8.8 %collective-permute-done.4 = bf16[2,2,128,256]{3,2,1,0:T(8,128)(2,1)S(1)} collective-permute-done((bf16[2,2,128,256]{3,2,1,0:T(8,128)(2,1)S(1)}, bf16[2,2,128,256]{3,2,1,0:T(8,128)(2,1)S(1)}, u32[]{:S(2)}, u32[]{:S(2)}) %collective-permute-start.4) | collective-permute-done | bytes 262176 | tf_op jit(solution)/shard_map/ppermute | solution.py:49
  81.3 5.6 %collective-permute-done.9 = bf16[2,2,128,256]{3,2,1,0:T(8,128)(2,1)S(1)} collective-permute-done((bf16[2,2,128,256]{3,2,1,0:T(8,128)(2,1)S(1)}, bf16[2,2,128,256]{3,2,1,0:T(8,128)(2,1)S(1)}, u32[]{:S(2)}, u32[]{:S(2)}) %collective-permute-start.9) | collective-permute-done | bytes 262176 | tf_op jit(solution)/shard_map/ppermute | solution.py:52
  89.3 6.4 %collective-permute-done.10 = bf16[2,2,128,256]{3,2,1,0:T(8,128)(2,1)S(1)} collective-permute-done((bf16[2,2,128,256]{3,2,1,0:T(8,128)(2,1)S(1)}, bf16[2,2,128,256]{3,2,1,0:T(8,128)(2,1)S(1)}, u32[]{:S(2)}, u32[]{:S(2)}) %collective-permute-start.10) | collective-permute-done | bytes 262176 | tf_op jit(solution)/shard_map/ppermute | solution.py:52
  98.4 22.8 %collective-permute-done.11 = bf16[4,2,2,128,256]{4,3,2,1,0:T(8,128)(2,1)S(1)} collective-permute-done((bf16[4,2,2,128,256]{4,3,2,1,0:T(8,128)(2,1)S(1)}, bf16[4,2,2,128,256]{4,3,2,1,0:T(8,128)(2,1)S(1)}, u32[]{:S(2)}, u32[]{:S(2)}) %collective-permute-start.11) | collective-permute-done | bytes 1048608 | tf_op jit(solution)/shard_map/ppermute | solution.py:49
  121.3 3.4 %collective-permute-start.12 = (bf16[4,2,2,128,256]{4,3,2,1,0:T(8,128)(2,1)S(1)}, bf16[4,2,2,128,256]{4,3,2,1,0:T(8,128)(2,1)}, u32[]{:S(2)}, u32[]{:S(2)}) collective-permute-start(bf16[4,2,2,128,256]{4,3,2,1,0:T(8,128)(2,1)S(1)} %collective-permute-done.11), channel_id=1, source_target_pairs={{0,16},{16,32},{32,48},{48,64},{64,80},{80,96},{96,112},{112,0},{1... | collective-permute-start | bytes 3145736 | tf_op jit(solution)/shard_map/ppermute | solution.py:49
  127.1 18.1 %collective-permute-done.12 = bf16[4,2,2,128,256]{4,3,2,1,0:T(8,128)(2,1)} collective-permute-done((bf16[4,2,2,128,256]{4,3,2,1,0:T(8,128)(2,1)S(1)}, bf16[4,2,2,128,256]{4,3,2,1,0:T(8,128)(2,1)}, u32[]{:S(2)}, u32[]{:S(2)}) %collective-permute-start.12) | collective-permute-done | bytes 1048608 | tf_op jit(solution)/shard_map/ppermute | solution.py:49
  145.2 4.9 %collective-permute-start.13 = (bf16[4,2,2,128,256]{4,3,2,1,0:T(8,128)(2,1)}, bf16[4,2,2,128,256]{4,3,2,1,0:T(8,128)(2,1)}, u32[]{:S(2)}, u32[]{:S(2)}) collective-permute-start(bf16[4,2,2,128,256]{4,3,2,1,0:T(8,128)(2,1)} %collective-permute-done.12), channel_id=1, source_target_pairs={{0,16},{16,32},{32,48},{48,64},{64,80},{80,96},{96,112},{112,0},{1... | collective-permute-start | bytes 3145736 | tf_op jit(solution)/shard_map/ppermute | solution.py:49
  152.2 17.2 %collective-permute-done.13 = bf16[4,2,2,128,256]{4,3,2,1,0:T(8,128)(2,1)} collective-permute-done((bf16[4,2,2,128,256]{4,3,2,1,0:T(8,128)(2,1)}, bf16[4,2,2,128,256]{4,3,2,1,0:T(8,128)(2,1)}, u32[]{:S(2)}, u32[]{:S(2)}) %collective-permute-start.13) | collective-permute-done | bytes 1048608 | tf_op jit(solution)/shard_map/ppermute | solution.py:49
  169.4 5.6 %collective-permute-start.14 = (bf16[4,2,2,128,256]{4,3,2,1,0:T(8,128)(2,1)}, bf16[4,2,2,128,256]{4,3,2,1,0:T(8,128)(2,1)S(1)}, u32[]{:S(2)}, u32[]{:S(2)}) collective-permute-start(bf16[4,2,2,128,256]{4,3,2,1,0:T(8,128)(2,1)} %collective-permute-done.13), channel_id=1, source_target_pairs={{0,16},{16,32},{32,48},{48,64},{64,80},{80,96},{96,112},{112,0},{1... | collective-permute-start | bytes 3145736 | tf_op jit(solution)/shard_map/ppermute | solution.py:49
  185.2 8.1 %collective-permute-done.14 = bf16[4,2,2,128,256]{4,3,2,1,0:T(8,128)(2,1)S(1)} collective-permute-done((bf16[4,2,2,128,256]{4,3,2,1,0:T(8,128)(2,1)}, bf16[4,2,2,128,256]{4,3,2,1,0:T(8,128)(2,1)S(1)}, u32[]{:S(2)}, u32[]{:S(2)}) %collective-permute-start.14) | collective-permute-done | bytes 1048608 | tf_op jit(solution)/shard_map/ppermute | solution.py:49
  196.5 5.4 %collective-permute-done.17 = bf16[4,2,2,128,256]{4,3,2,1,0:T(8,128)(2,1)S(1)} collective-permute-done((bf16[4,2,2,128,256]{4,3,2,1,0:T(8,128)(2,1)S(1)}, bf16[4,2,2,128,256]{4,3,2,1,0:T(8,128)(2,1)S(1)}, u32[]{:S(2)}, u32[]{:S(2)}) %collective-permute-start.17) | collective-permute-done | bytes 1048608 | tf_op jit(solution)/shard_map/ppermute | solution.py:52
  203.0 8.1 %gather_fusion.2 = bf16[8,4,2,2,128,256]{5,4,3,2,1,0:T(8,128)(2,1)} fusion(bf16[8,4,2,2,128,256]{5,4,3,2,1,0:T(8,128)(2,1)} %bitcast_dynamic-update-slice_fusion, s32[1024]{0:T(1024)S(1)} %pad_clamp_fusion), kind=kCustom, calls=%fused_computation.2 | custom fusion | bytes 16777248 | tf_op jit(solution)/shard_map/jit(_take)/gather | solution.py:62
  211.1 7.5 %select_bitcast_fusion = bf16[2,2,4,8,128,256]{5,4,1,0,2,3:T(8,128)(2,1)} fusion(bf16[8,4,2,2,128,256]{5,4,3,2,1,0:T(8,128)(2,1)} %gather_fusion.2, pred[8]{0:T(512)(128)(4,1)S(1)} %compare_and_fusion.1), kind=kLoop, calls=%fused_computation.3 | loop fusion | flops 4194304 | bytes 16777224 | tf_op jit(solution)/shard_map/jit(_take)/select_n | solution.py:62
  218.6 7.8 %copy.10 = bf16[2,2,4,8,128,256]{5,4,3,2,0,1:T(8,128)(2,1)} copy(bf16[2,2,4,8,128,256]{5,4,1,0,2,3:T(8,128)(2,1)} %select_bitcast_fusion) | data formatting | bytes 16777216 | tf_op jit(solution)/shard_map/jit(_take)/select_n | solution.py:62
  226.3 8.5 %copy.13 = bf16[2,4,2,2,2,128,256]{6,2,1,0,5,3,4:T(2,128)(2,1)} copy(bf16[2,4,2,2,2,128,256]{6,5,4,3,2,0,1:T(8,128)(2,1)} %bitcast.106) | data formatting | bytes 8388608 | tf_op jit(solution)/shard_map/all_gather | solution.py:95
  234.9 7.8 %reshape.194 = bf16[2,2,128,4096]{3,2,0,1:T(8,128)(2,1)} reshape(bf16[2,2,128,2,4,2,256]{6,5,4,3,2,0,1:T(2,128)(2,1)} %bitcast.99) | data formatting | bytes 8388608 | tf_op jit(solution)/shard_map/reshape | solution.py:96
  242.7 3.7 %fusion.1 = f32[2,128,256]{2,1,0:T(8,128)S(1)} fusion(bf16[2,2,4096,256]{3,2,0,1:T(8,128)(2,1)} %bitcast.100, bf16[2,2,128,4096]{3,2,0,1:T(8,128)(2,1)} %reshape.194), kind=kOutput, calls=%fused_computation.8 | convolution fusion | flops 536870912 | bytes 6553600 | tf_op jit(solution)/shard_map/fik,fkj->fij/dot_general | solution.py:12
  246.7 3.2 %fusion = f32[2,128,256]{2,1,0:T(8,128)S(1)} fusion(bf16[2,2,4096,256]{3,2,0,1:T(8,128)(2,1)} %bitcast.101, bf16[2,2,128,4096]{3,2,0,1:T(8,128)(2,1)S(1)} %copy-done), kind=kOutput, calls=%fused_computation.7 | convolution fusion | flops 536870912 | bytes 6553600 | tf_op jit(solution)/shard_map/fik,fkj->fij/dot_general | solution.py:21
  (71 shorter events, 39.0 us)
Async XLA Ops:
  6.5 143.6 %all-gather.4.cloned.1.call-start = ((), (), s32[]{:S(2)}) async-start(), calls=%async_computation | async-start | bytes 2621440 | tf_op jit(solution)/shard_map/all_gather | solution.py:94
  7.5 12.9 %collective-permute-start = (bf16[2,2,128,128]{3,2,1,0:T(8,128)(2,1)S(1)}, bf16[2,2,128,128]{3,2,1,0:T(8,128)(2,1)S(1)}, u32[]{:S(2)}, u32[]{:S(2)}) collective-permute-start(bf16[2,2,128,128]{3,2,1,0:T(8,128)(2,1)S(1)} %get-tuple-element.8), channel_id=1, source_target_pairs={{0,0},{1,32},{2,64},{3,96},{4,128},{5,160},{6,192},{7,224},{8,256}... | collective-permute-start | bytes 393224 | tf_op jit(solution)/shard_map/ppermute | solution.py:79
  8.2 16.9 %collective-permute-start.2 = (bf16[2,2,128,128]{3,2,1,0:T(8,128)(2,1)S(1)}, bf16[2,2,128,128]{3,2,1,0:T(8,128)(2,1)S(1)}, u32[]{:S(2)}, u32[]{:S(2)}) collective-permute-start(bf16[2,2,128,128]{3,2,1,0:T(8,128)(2,1)S(1)} %get-tuple-element.8), channel_id=1, source_target_pairs={{16,0},{17,32},{18,64},{19,96},{20,128},{21,160},{22,192},{23,224}... | collective-permute-start | bytes 393224 | tf_op jit(solution)/shard_map/ppermute | solution.py:79
  16.0 9.1 %collective-permute-start.1 = (bf16[2,2,128,128]{3,2,1,0:T(8,128)(2,1)S(1)}, bf16[2,2,128,128]{3,2,1,0:T(8,128)(2,1)S(1)}, u32[]{:S(2)}, u32[]{:S(2)}) collective-permute-start(bf16[2,2,128,128]{3,2,1,0:T(8,128)(2,1)S(1)} %get-tuple-element.7), channel_id=1, source_target_pairs={{0,16},{1,48},{2,80},{3,112},{4,144},{5,176},{6,208},{7,240},{8,27... | collective-permute-start | bytes 393224 | tf_op jit(solution)/shard_map/ppermute | solution.py:79
  17.3 12.4 %collective-permute-start.3 = (bf16[2,2,128,128]{3,2,1,0:T(8,128)(2,1)S(1)}, bf16[2,2,128,128]{3,2,1,0:T(8,128)(2,1)S(1)}, u32[]{:S(2)}, u32[]{:S(2)}) collective-permute-start(bf16[2,2,128,128]{3,2,1,0:T(8,128)(2,1)S(1)} %get-tuple-element.7), channel_id=1, source_target_pairs={{16,16},{17,48},{18,80},{19,112},{20,144},{21,176},{22,208},{23,24... | collective-permute-start | bytes 393224 | tf_op jit(solution)/shard_map/ppermute | solution.py:79
  31.1 35.4 %collective-permute-start.5 = (bf16[2,2,128,256]{3,2,1,0:T(8,128)(2,1)S(1)}, bf16[2,2,128,256]{3,2,1,0:T(8,128)(2,1)}, u32[]{:S(2)}, u32[]{:S(2)}) collective-permute-start(bf16[2,2,128,256]{3,2,1,0:T(8,128)(2,1)S(1)} %get-tuple-element.6), channel_id=1, source_target_pairs={{0,128},{128,256},{256,384},{1,129},{129,257},{257,385},{2,130},{1... | collective-permute-start | bytes 786440 | tf_op jit(solution)/shard_map/ppermute | solution.py:49
  40.5 36.2 %collective-permute-start.4 = (bf16[2,2,128,256]{3,2,1,0:T(8,128)(2,1)S(1)}, bf16[2,2,128,256]{3,2,1,0:T(8,128)(2,1)S(1)}, u32[]{:S(2)}, u32[]{:S(2)}) collective-permute-start(bf16[2,2,128,256]{3,2,1,0:T(8,128)(2,1)S(1)} %get-tuple-element.6), channel_id=1, source_target_pairs={{0,8},{8,0},{1,9},{9,1},{2,10},{10,2},{3,11},{11,3},{4,12},{12,4},... | collective-permute-start | bytes 786440 | tf_op jit(solution)/shard_map/ppermute | solution.py:49
  65.2 12.2 %collective-permute-start.8 = (bf16[2,2,128,256]{3,2,1,0:T(8,128)(2,1)S(1)}, bf16[2,2,128,256]{3,2,1,0:T(8,128)(2,1)S(1)}, u32[]{:S(2)}, u32[]{:S(2)}) collective-permute-start(bf16[2,2,128,256]{3,2,1,0:T(8,128)(2,1)S(1)} %get-tuple-element.6), channel_id=1, source_target_pairs={{128,0},{256,128},{384,256},{129,1},{257,129},{385,257},{130,2},{2... | collective-permute-start | bytes 786440 | tf_op jit(solution)/shard_map/ppermute | solution.py:52
  66.5 13.1 %collective-permute-start.6 = (bf16[2,2,128,256]{3,2,1,0:T(8,128)(2,1)}, bf16[2,2,128,256]{3,2,1,0:T(8,128)(2,1)}, u32[]{:S(2)}, u32[]{:S(2)}) collective-permute-start(bf16[2,2,128,256]{3,2,1,0:T(8,128)(2,1)} %collective-permute-done.5), channel_id=1, source_target_pairs={{128,256},{256,384},{129,257},{257,385},{130,258},{258,386},{131,2... | collective-permute-start | bytes 786440 | tf_op jit(solution)/shard_map/ppermute | solution.py:49
  77.4 9.6 %collective-permute-start.9 = (bf16[2,2,128,256]{3,2,1,0:T(8,128)(2,1)S(1)}, bf16[2,2,128,256]{3,2,1,0:T(8,128)(2,1)S(1)}, u32[]{:S(2)}, u32[]{:S(2)}) collective-permute-start(bf16[2,2,128,256]{3,2,1,0:T(8,128)(2,1)S(1)} %collective-permute-done.8), channel_id=1, source_target_pairs={{128,0},{256,128},{129,1},{257,129},{130,2},{258,130},{131,3},{259... | collective-permute-start | bytes 786440 | tf_op jit(solution)/shard_map/ppermute | solution.py:52
  79.6 146.7 %all-gather.6.cloned.1.call-start = ((), (), s32[]{:S(2)}) async-start(), calls=%async_computation.1 | async-start | bytes 6291456 | tf_op jit(solution)/shard_map/all_gather | solution.py:95
  79.7 9.6 %collective-permute-start.7 = (bf16[2,2,128,256]{3,2,1,0:T(8,128)(2,1)}, bf16[2,2,128,256]{3,2,1,0:T(8,128)(2,1)S(1)}, u32[]{:S(2)}, u32[]{:S(2)}) collective-permute-start(bf16[2,2,128,256]{3,2,1,0:T(8,128)(2,1)} %collective-permute-done.6), channel_id=1, source_target_pairs={{256,384},{257,385},{258,386},{259,387},{260,388},{261,389},{262,3... | collective-permute-start | bytes 786440 | tf_op jit(solution)/shard_map/ppermute | solution.py:49
  87.0 8.7 %collective-permute-start.10 = (bf16[2,2,128,256]{3,2,1,0:T(8,128)(2,1)S(1)}, bf16[2,2,128,256]{3,2,1,0:T(8,128)(2,1)S(1)}, u32[]{:S(2)}, u32[]{:S(2)}) collective-permute-start(bf16[2,2,128,256]{3,2,1,0:T(8,128)(2,1)S(1)} %collective-permute-done.9), channel_id=1, source_target_pairs={{128,0},{129,1},{130,2},{131,3},{132,4},{133,5},{134,6},{135,7},{1... | collective-permute-start | bytes 786440 | tf_op jit(solution)/shard_map/ppermute | solution.py:52
  96.5 24.7 %collective-permute-start.11 = (bf16[4,2,2,128,256]{4,3,2,1,0:T(8,128)(2,1)S(1)}, bf16[4,2,2,128,256]{4,3,2,1,0:T(8,128)(2,1)S(1)}, u32[]{:S(2)}, u32[]{:S(2)}) collective-permute-start(bf16[4,2,2,128,256]{4,3,2,1,0:T(8,128)(2,1)S(1)} %broadcast_select_fusion), channel_id=1, source_target_pairs={{0,16},{16,32},{32,48},{48,64},{64,80},{80,96},{96,112},{112,0},{1... | collective-permute-start | bytes 3145736 | tf_op jit(solution)/shard_map/ppermute | solution.py:49
  121.3 5.9 %copy-start.1 = (bf16[4,2,2,128,256]{4,3,2,1,0:T(8,128)(2,1)}, bf16[4,2,2,128,256]{4,3,2,1,0:T(8,128)(2,1)S(1)}, u32[]{:S(2)}) copy-start(bf16[4,2,2,128,256]{4,3,2,1,0:T(8,128)(2,1)S(1)} %collective-permute-done.11) | copy-start | bytes 3145732
  121.3 24.0 %collective-permute-start.12 = (bf16[4,2,2,128,256]{4,3,2,1,0:T(8,128)(2,1)S(1)}, bf16[4,2,2,128,256]{4,3,2,1,0:T(8,128)(2,1)}, u32[]{:S(2)}, u32[]{:S(2)}) collective-permute-start(bf16[4,2,2,128,256]{4,3,2,1,0:T(8,128)(2,1)S(1)} %collective-permute-done.11), channel_id=1, source_target_pairs={{0,16},{16,32},{32,48},{48,64},{64,80},{80,96},{96,112},{112,0},{1... | collective-permute-start | bytes 3145736 | tf_op jit(solution)/shard_map/ppermute | solution.py:49
  124.7 25.5 %collective-permute-start.15 = (bf16[4,2,2,128,256]{4,3,2,1,0:T(8,128)(2,1)S(1)}, bf16[4,2,2,128,256]{4,3,2,1,0:T(8,128)(2,1)S(1)}, u32[]{:S(2)}, u32[]{:S(2)}) collective-permute-start(bf16[4,2,2,128,256]{4,3,2,1,0:T(8,128)(2,1)S(1)} %broadcast_select_fusion), channel_id=1, source_target_pairs={{0,112},{16,0},{32,16},{48,32},{64,48},{80,64},{96,80},{112,96},{1... | collective-permute-start | bytes 3145736 | tf_op jit(solution)/shard_map/ppermute | solution.py:52
  145.2 24.1 %collective-permute-start.13 = (bf16[4,2,2,128,256]{4,3,2,1,0:T(8,128)(2,1)}, bf16[4,2,2,128,256]{4,3,2,1,0:T(8,128)(2,1)}, u32[]{:S(2)}, u32[]{:S(2)}) collective-permute-start(bf16[4,2,2,128,256]{4,3,2,1,0:T(8,128)(2,1)} %collective-permute-done.12), channel_id=1, source_target_pairs={{0,16},{16,32},{32,48},{48,64},{64,80},{80,96},{96,112},{112,0},{1... | collective-permute-start | bytes 3145736 | tf_op jit(solution)/shard_map/ppermute | solution.py:49
  150.2 28.3 %collective-permute-start.16 = (bf16[4,2,2,128,256]{4,3,2,1,0:T(8,128)(2,1)S(1)}, bf16[4,2,2,128,256]{4,3,2,1,0:T(8,128)(2,1)S(1)}, u32[]{:S(2)}, u32[]{:S(2)}) collective-permute-start(bf16[4,2,2,128,256]{4,3,2,1,0:T(8,128)(2,1)S(1)} %collective-permute-done.15), channel_id=1, source_target_pairs={{0,112},{16,0},{32,16},{48,32},{64,48},{80,64},{96,80},{112,96},{1... | collective-permute-start | bytes 3145736 | tf_op jit(solution)/shard_map/ppermute | solution.py:52
  169.4 24.0 %collective-permute-start.14 = (bf16[4,2,2,128,256]{4,3,2,1,0:T(8,128)(2,1)}, bf16[4,2,2,128,256]{4,3,2,1,0:T(8,128)(2,1)S(1)}, u32[]{:S(2)}, u32[]{:S(2)}) collective-permute-start(bf16[4,2,2,128,256]{4,3,2,1,0:T(8,128)(2,1)} %collective-permute-done.13), channel_id=1, source_target_pairs={{0,16},{16,32},{32,48},{48,64},{64,80},{80,96},{96,112},{112,0},{1... | collective-permute-start | bytes 3145736 | tf_op jit(solution)/shard_map/ppermute | solution.py:49
  178.5 23.4 %collective-permute-start.17 = (bf16[4,2,2,128,256]{4,3,2,1,0:T(8,128)(2,1)S(1)}, bf16[4,2,2,128,256]{4,3,2,1,0:T(8,128)(2,1)S(1)}, u32[]{:S(2)}, u32[]{:S(2)}) collective-permute-start(bf16[4,2,2,128,256]{4,3,2,1,0:T(8,128)(2,1)S(1)} %collective-permute-done.16), channel_id=1, source_target_pairs={{0,112},{16,0},{32,16},{48,32},{64,48},{80,64},{96,80},{112,96},{1... | collective-permute-start | bytes 3145736 | tf_op jit(solution)/shard_map/ppermute | solution.py:52
  242.7 4.0 %copy-start = (bf16[2,2,128,4096]{3,2,0,1:T(8,128)(2,1)S(1)}, bf16[2,2,128,4096]{3,2,0,1:T(8,128)(2,1)}, u32[]{:S(2)}) copy-start(bf16[2,2,128,4096]{3,2,0,1:T(8,128)(2,1)} %reshape.194) | copy-start | bytes 12582916
  242.7 7.2 %slice-start = ((s8[8388608]{0:T(1024)(128)(4,1)}), s8[4194304]{0:T(1024)(128)(4,1)S(1)}, s32[]{:S(2)}) async-start(s8[8388608]{0:T(1024)(128)(4,1)} %bitcast.102), calls=%async_computation.2 | async-start | bytes 8388608
  246.7 3.9 %slice-start.1 = ((s8[8388608]{0:T(1024)(128)(4,1)}), s8[4194304]{0:T(1024)(128)(4,1)S(1)}, s32[]{:S(2)}) async-start(s8[8388608]{0:T(1024)(128)(4,1)} %bitcast.102), calls=%async_computation.3 | async-start | bytes 8388608
Sparse Core Ops, SparseCore 0:
  79.7 35.6 all-gather.3
  150.3 18.2 all-gather.5

commit v5 on v4

--- a/solution.py
+++ b/solution.py
@@ -62,6 +62,21 @@
     return jnp.take(stacked, sel, axis=0)
 
 
+def ring_blocks(block, axis):
+    n = lax.axis_size(axis)
+    right = [(i, (i + 1) % n) for i in range(n)]
+    left = [(d, s) for s, d in right]
+    got = [(0, block)]
+    up = dn = block
+    for k in range(1, n // 2 + 1):
+        up = lax.ppermute(up, axis, right)
+        got.append((k, up))
+        if k < n - n // 2:
+            dn = lax.ppermute(dn, axis, left)
+            got.append((-k, dn))
+    return got
+
+
 def mirrored_pieces(traces, shot_count, recv_count):
     block_rows = traces.shape[2]
     g = traces.shape[3] // block_rows
@@ -88,13 +103,19 @@
     summed = traces.astype(jnp.float32) + jnp.swapaxes(mirrored, 2, 3).astype(jnp.float32)
     averaged = (summed * 0.5).astype(jnp.bfloat16)
     freqs, _, block_rows, col_width = averaged.shape
-    cols = stream_gather(stream_gather(averaged, "z_lo", False), "y", True)
-    col_panel = jnp.transpose(cols, (2, 3, 1, 0, 4, 5)).reshape(freqs, 2, shot_count * block_rows, col_width)
+    z_cols = jnp.moveaxis(stream_gather(averaged, "z_lo", False), 0, 2)
     rows = stream_gather(averaged, "z_hi", True)
     rows = lax.all_gather(rows, "x", axis=1)
     rows = lax.all_gather(rows, "core", axis=2)
-    row_panel = jnp.transpose(rows, (3, 4, 5, 0, 1, 2, 6)).reshape(freqs, 2, block_rows, recv_count * col_width)
-    product = complex_product(row_panel, col_panel, "fik,fkj->fij")
+    y_n = lax.axis_size("y")
+    z_n = z_cols.shape[2]
+    row_panel = jnp.transpose(rows, (3, 4, 5, 0, 1, 2, 6)).reshape(freqs, 2, block_rows, z_n, y_n, block_rows)
+    me_y = lax.axis_index("y")
+    product = None
+    for offset, col_block in ring_blocks(z_cols, "y"):
+        row_block = lax.dynamic_index_in_dim(row_panel, (me_y - offset) % y_n, axis=4, keepdims=False)
+        part = complex_product(row_block, col_block, "fizk,fzkj->fij")
+        product = part if product is None else product + part
     scale_factor = jnp.float32(float(NS) ** (-0.5))
     return product * scale_factor
 

time: 265 us -> 261 us (0.985)
  matrix products: 8.3 us -> 26.4 us
  local copies, waits for them, and re-layouts: 49.7 us -> 33.9 us
  waiting for transfers between devices: 102 us -> 111 us
  other arithmetic: 11.2 us -> 2.36 us
  starting transfers between devices: 75 us -> 69.4 us
    ppermute x8 -> x4, waiting for transfers between devices: 75.1 us -> 9.63 us  [stream_gather(): up = lax.ppermute(up, axis, perm(k, 1))]
    ppermute x0 -> x7, waiting for transfers between devices: none -> 59.1 us  [the longest x4 59.1 us: ring_blocks(): up = lax.ppermute(up, axis, right)]
    all_gather x1, waiting for transfers between devices: 0.02 us -> 27.6 us  [per_device(): rows = lax.all_gather(rows, 'x', axis=1)]
    ppermute x0 -> x7, starting transfers between devices: none -> 24 us  [the longest x4 16.2 us: ring_blocks(): up = lax.ppermute(up, axis, right)]
    ppermute x8 -> x4, starting transfers between devices: 51.9 us -> 30 us  [stream_gather(): up = lax.ppermute(up, axis, perm(k, 1))]
    dynamic_slice x0 -> x9, local copies, waits for them, and re-layouts: none -> 14.1 us  [per_device(): lax.dynamic_index_in_dim(row_panel, (me_y - offset) % y_n, axis=4, keepdi...]
    unnamed x19 -> x27, local copies, waits for them, and re-layouts: 13.1 us -> 3.69 us
    ppermute x6 -> x3, waiting for transfers between devices: 17.4 us -> 8.95 us  [stream_gather(): dn = lax.ppermute(dn, axis, perm(k, -1))]
  transfers between devices with their start and end apart: 20 -> 20, of which waited for: 10 -> 10; matrix products, arithmetic and copies ran while one was open for 15% -> 17% of each run, Pallas kernels for 0% -> 0%
where the time goes in v5:
time: 261 us; the launch traced here: 257 us
  waiting for transfers between devices  111 us (43%)
  starting transfers between devices  69.4 us (27%)
  local copies, waits for them, and re-layouts  33.9 us (13%)
  matrix products  26.4 us (10%)
  between operations  14.2 us (5%)
    ppermute x4, waiting for transfers between devices, ring_blocks(): up = lax.ppermute(up, axis, right)  59.1 us
    ppermute x4, starting transfers between devices, stream_gather(): up = lax.ppermute(up, axis, perm(k, 1))  30 us
    all_gather x1, waiting for transfers between devices, per_device(): rows = lax.all_gather(rows, 'x', axis=1)  27.6 us
    ppermute x4, starting transfers between devices, ring_blocks(): up = lax.ppermute(up, axis, right)  16.2 us
    dynamic_slice x9, local copies, waits for them, and re-layouts, per_device(): lax.dynamic_index_in_dim(row_panel, (me_y - offset) % y_n, axis=4, keepdi...  14.1 us
    ppermute x4, starting transfers between devices, mirrored_pieces(): got.append(lax.ppermute(part, SHOT + RECV, perm))  11.4 us
    ppermute x4, waiting for transfers between devices, stream_gather(): up = lax.ppermute(up, axis, perm(k, 1))  9.63 us
    ppermute x3, waiting for transfers between devices, stream_gather(): dn = lax.ppermute(dn, axis, perm(k, -1))  8.95 us
  transfers between devices with their start and end apart: 20, of which 10 were waited for; matrix products, arithmetic and copies ran while one was open for 17% of the time, Pallas kernels for 0%

profile of v5, /device:TPU:56, one launch (start us, length us, event | category | flops | bytes accessed | tf_op | source)
XLA Modules:
  0.0 256.8 jit_solution(3260523224798214723)
XLA Ops:
  7.6 3.1 %collective-permute-start.3 = (bf16[2,2,128,128]{3,2,1,0:T(8,128)(2,1)S(1)}, bf16[2,2,128,128]{3,2,1,0:T(8,128)(2,1)S(1)}, u32[]{:S(2)}, u32[]{:S(2)}) collective-permute-start(bf16[2,2,128,128]{3,2,1,0:T(8,128)(2,1)S(1)} %get-tuple-element.15), channel_id=1, source_target_pairs={{16,16},{17,48},{18,80},{19,112},{20,144},{21,176},{22,208},{23,24... | collective-permute-start | bytes 393224 | tf_op jit(solution)/shard_map/ppermute | solution.py:94
  11.9 6.4 %collective-permute-start.2 = (bf16[2,2,128,128]{3,2,1,0:T(8,128)(2,1)S(1)}, bf16[2,2,128,128]{3,2,1,0:T(8,128)(2,1)S(1)}, u32[]{:S(2)}, u32[]{:S(2)}) collective-permute-start(bf16[2,2,128,128]{3,2,1,0:T(8,128)(2,1)S(1)} %get-tuple-element.16), channel_id=1, source_target_pairs={{16,0},{17,32},{18,64},{19,96},{20,128},{21,160},{22,192},{23,224}... | collective-permute-start | bytes 393224 | tf_op jit(solution)/shard_map/ppermute | solution.py:94
  20.1 4.2 %collective-permute-done.1 = bf16[2,2,128,128]{3,2,1,0:T(8,128)(2,1)S(1)} collective-permute-done((bf16[2,2,128,128]{3,2,1,0:T(8,128)(2,1)S(1)}, bf16[2,2,128,128]{3,2,1,0:T(8,128)(2,1)S(1)}, u32[]{:S(2)}, u32[]{:S(2)}) %collective-permute-start.1) | collective-permute-done | bytes 131104 | tf_op jit(solution)/shard_map/ppermute | solution.py:94
  25.5 23.6 %collective-permute-start.4 = (bf16[2,2,128,256]{3,2,1,0:T(8,128)(2,1)S(1)}, bf16[2,2,128,256]{3,2,1,0:T(8,128)(2,1)S(1)}, u32[]{:S(2)}, u32[]{:S(2)}) collective-permute-start(bf16[2,2,128,256]{3,2,1,0:T(8,128)(2,1)S(1)} %get-tuple-element.6), channel_id=1, source_target_pairs={{0,8},{8,0},{1,9},{9,1},{2,10},{10,2},{3,11},{11,3},{4,12},{12,4},... | collective-permute-start | bytes 786440 | tf_op jit(solution)/shard_map/ppermute | solution.py:49
  49.1 6.2 %collective-permute-done.4 = bf16[2,2,128,256]{3,2,1,0:T(8,128)(2,1)S(1)} collective-permute-done((bf16[2,2,128,256]{3,2,1,0:T(8,128)(2,1)S(1)}, bf16[2,2,128,256]{3,2,1,0:T(8,128)(2,1)S(1)}, u32[]{:S(2)}, u32[]{:S(2)}) %collective-permute-start.4) | collective-permute-done | bytes 262176 | tf_op jit(solution)/shard_map/ppermute | solution.py:49
  56.9 5.1 %collective-permute-start.5 = (bf16[2,2,128,256]{3,2,1,0:T(8,128)(2,1)S(1)}, bf16[2,2,128,256]{3,2,1,0:T(8,128)(2,1)S(1)}, u32[]{:S(2)}, u32[]{:S(2)}) collective-permute-start(bf16[2,2,128,256]{3,2,1,0:T(8,128)(2,1)S(1)} %get-tuple-element.6), channel_id=1, source_target_pairs={{0,128},{128,256},{256,384},{1,129},{129,257},{257,385},{2,130},{1... | collective-permute-start | bytes 786440 | tf_op jit(solution)/shard_map/ppermute | solution.py:49
  63.3 3.5 %collective-permute-done.5 = bf16[2,2,128,256]{3,2,1,0:T(8,128)(2,1)S(1)} collective-permute-done((bf16[2,2,128,256]{3,2,1,0:T(8,128)(2,1)S(1)}, bf16[2,2,128,256]{3,2,1,0:T(8,128)(2,1)S(1)}, u32[]{:S(2)}, u32[]{:S(2)}) %collective-permute-start.5) | collective-permute-done | bytes 262176 | tf_op jit(solution)/shard_map/ppermute | solution.py:49
  67.5 3.4 %collective-permute-done.8 = bf16[2,2,128,256]{3,2,1,0:T(8,128)(2,1)S(1)} collective-permute-done((bf16[2,2,128,256]{3,2,1,0:T(8,128)(2,1)S(1)}, bf16[2,2,128,256]{3,2,1,0:T(8,128)(2,1)S(1)}, u32[]{:S(2)}, u32[]{:S(2)}) %collective-permute-start.8) | collective-permute-done | bytes 262176 | tf_op jit(solution)/shard_map/ppermute | solution.py:52
  73.7 5.5 %collective-permute-done.9 = bf16[2,2,128,256]{3,2,1,0:T(8,128)(2,1)S(1)} collective-permute-done((bf16[2,2,128,256]{3,2,1,0:T(8,128)(2,1)S(1)}, bf16[2,2,128,256]{3,2,1,0:T(8,128)(2,1)S(1)}, u32[]{:S(2)}, u32[]{:S(2)}) %collective-permute-start.9) | collective-permute-done | bytes 262176 | tf_op jit(solution)/shard_map/ppermute | solution.py:52
  81.2 27.6 %all-gather.4.cloned.1.call-done = bf16[2,4,2,2,128,256]{5,4,3,2,0,1:T(8,128)(2,1)} async-done(((bf16[2,1,2,2,128,256]{5,4,3,2,0,1:T(8,128)(2,1)}), bf16[2,4,2,2,128,256]{5,4,3,2,0,1:T(8,128)(2,1)}) %all-gather.4.cloned.1.call-update) | async-done | bytes 2097168 | tf_op jit(solution)/shard_map/all_gather | solution.py:108
  108.8 3.2 %copy.32 = bf16[2,4,2,2,128,256]{5,4,3,2,1,0:T(8,128)(2,1)} copy(bf16[2,4,2,2,128,256]{5,4,3,2,0,1:T(8,128)(2,1)} %all-gather.4.cloned.1.call-done) | data formatting | bytes 4194304 | tf_op jit(solution)/shard_map/all_gather | solution.py:108
  114.9 2.1 gather_fusion.1
  117.2 2.3 collective-permute-start.11
  119.5 3.5 %collective-permute-start.12 = (bf16[2,2,4,128,256]{4,3,2,0,1:T(8,128)(2,1)S(1)}, bf16[2,2,4,128,256]{4,3,2,0,1:T(8,128)(2,1)S(1)}, u32[]{:S(2)}, u32[]{:S(2)}) collective-permute-start(bf16[2,2,4,128,256]{4,3,2,0,1:T(8,128)(2,1)S(1)} %fusion.32), channel_id=1, source_target_pairs={{16,0},{32,16},{48,32},{64,48},{80,64},{96,80},{112,96},{0,112},{1... | collective-permute-start | bytes 3145736 | tf_op jit(solution)/shard_map/ppermute | solution.py:75
  123.1 20.8 %collective-permute-done.11 = bf16[2,2,4,128,256]{4,3,2,0,1:T(8,128)(2,1)S(1)} collective-permute-done((bf16[2,2,4,128,256]{4,3,2,0,1:T(8,128)(2,1)S(1)}, bf16[2,2,4,128,256]{4,3,2,0,1:T(8,128)(2,1)S(1)}, u32[]{:S(2)}, u32[]{:S(2)}) %collective-permute-start.11) | collective-permute-done | bytes 1048608 | tf_op jit(solution)/shard_map/ppermute | solution.py:72
  143.8 3.5 %collective-permute-start.13 = (bf16[2,2,4,128,256]{4,3,2,0,1:T(8,128)(2,1)S(1)}, bf16[2,2,4,128,256]{4,3,2,0,1:T(8,128)(2,1)S(1)}, u32[]{:S(2)}, u32[]{:S(2)}) collective-permute-start(bf16[2,2,4,128,256]{4,3,2,0,1:T(8,128)(2,1)S(1)} %collective-permute-done.11), channel_id=1, source_target_pairs={{0,16},{16,32},{32,48},{48,64},{64,80},{80,96},{96,112},{112,0},{1... | collective-permute-start | bytes 3145736 | tf_op jit(solution)/shard_map/ppermute | solution.py:72
  147.4 2.3 collective-permute-start.14
  149.7 19.9 %collective-permute-done.13 = bf16[2,2,4,128,256]{4,3,2,0,1:T(8,128)(2,1)S(1)} collective-permute-done((bf16[2,2,4,128,256]{4,3,2,0,1:T(8,128)(2,1)S(1)}, bf16[2,2,4,128,256]{4,3,2,0,1:T(8,128)(2,1)S(1)}, u32[]{:S(2)}, u32[]{:S(2)}) %collective-permute-start.13) | collective-permute-done | bytes 1048608 | tf_op jit(solution)/shard_map/ppermute | solution.py:72
  169.6 4.7 %collective-permute-start.15 = (bf16[2,2,4,128,256]{4,3,2,0,1:T(8,128)(2,1)S(1)}, bf16[2,2,4,128,256]{4,3,2,0,1:T(8,128)(2,1)}, u32[]{:S(2)}, u32[]{:S(2)}) collective-permute-start(bf16[2,2,4,128,256]{4,3,2,0,1:T(8,128)(2,1)S(1)} %collective-permute-done.13), channel_id=1, source_target_pairs={{0,16},{16,32},{32,48},{48,64},{64,80},{80,96},{96,112},{112,0},{1... | collective-permute-start | bytes 3145736 | tf_op jit(solution)/shard_map/ppermute | solution.py:72
  176.4 18.4 %collective-permute-done.15 = bf16[2,2,4,128,256]{4,3,2,0,1:T(8,128)(2,1)} collective-permute-done((bf16[2,2,4,128,256]{4,3,2,0,1:T(8,128)(2,1)S(1)}, bf16[2,2,4,128,256]{4,3,2,0,1:T(8,128)(2,1)}, u32[]{:S(2)}, u32[]{:S(2)}) %collective-permute-start.15) | collective-permute-done | bytes 1048608 | tf_op jit(solution)/shard_map/ppermute | solution.py:72
  194.9 5.7 %collective-permute-start.17 = (bf16[2,2,4,128,256]{4,3,2,0,1:T(8,128)(2,1)}, bf16[2,2,4,128,256]{4,3,2,0,1:T(8,128)(2,1)}, u32[]{:S(2)}, u32[]{:S(2)}) collective-permute-start(bf16[2,2,4,128,256]{4,3,2,0,1:T(8,128)(2,1)} %collective-permute-done.15), channel_id=1, source_target_pairs={{0,16},{16,32},{32,48},{48,64},{64,80},{80,96},{96,112},{112,0},{1... | collective-permute-start | bytes 3145736 | tf_op jit(solution)/shard_map/ppermute | solution.py:72
  200.6 7.3 %copy.33 = bf16[2,2,128,2,4,2,256]{2,6,5,4,3,1,0:T(8,128)(2,1)} copy(bf16[2,2,128,2,4,2,256]{6,2,1,0,5,4,3:T(8,128)(2,1)} %bitcast.369) | data formatting | bytes 8388608 | tf_op jit(solution)/shard_map/transpose | solution.py:112
  207.9 3.8 %constant_dynamic-slice_fusion = (bf16[2,2,128,4,1,128]{2,5,4,3,1,0:T(8,128)(2,1)S(1)}, bf16[2,2,128,4,1,128]{2,5,4,3,1,0:T(8,128)(2,1)S(1)}, bf16[2,2,128,4,1,1...) fusion(bf16[2,2,128,4,8,128]{2,5,4,3,1,0:T(8,128)(2,1)} %bitcas, ...), kind=kLoop, calls=%fused_computation.128 | loop fusion | bytes 8388640 | tf_op jit(solution)/shard_map/jit(dynamic_index_in_dim)/dynamic_slice | solution.py:116
  215.9 2.1 copy.37
  (107 shorter events, 54.5 us)
Async XLA Ops:
  6.5 18.1 %copy-start.10 = (bf16[2,2,128,256]{3,2,1,0:T(8,128)(2,1)S(1)}, bf16[2,2,128,256]{3,2,1,0:T(8,128)(2,1)}, u32[]{:S(2)}) copy-start(bf16[2,2,128,256]{3,2,1,0:T(8,128)(2,1)} %param.1) | copy-start | bytes 786436
  6.5 102.2 %all-gather.4.cloned.1.call-start = ((), (), s32[]{:S(2)}) async-start(), calls=%async_computation | async-start | bytes 2621440 | tf_op jit(solution)/shard_map/all_gather | solution.py:108
  7.6 12.5 %collective-permute-start.3 = (bf16[2,2,128,128]{3,2,1,0:T(8,128)(2,1)S(1)}, bf16[2,2,128,128]{3,2,1,0:T(8,128)(2,1)S(1)}, u32[]{:S(2)}, u32[]{:S(2)}) collective-permute-start(bf16[2,2,128,128]{3,2,1,0:T(8,128)(2,1)S(1)} %get-tuple-element.15), channel_id=1, source_target_pairs={{16,16},{17,48},{18,80},{19,112},{20,144},{21,176},{22,208},{23,24... | collective-permute-start | bytes 393224 | tf_op jit(solution)/shard_map/ppermute | solution.py:94
  10.6 13.6 %collective-permute-start.1 = (bf16[2,2,128,128]{3,2,1,0:T(8,128)(2,1)S(1)}, bf16[2,2,128,128]{3,2,1,0:T(8,128)(2,1)S(1)}, u32[]{:S(2)}, u32[]{:S(2)}) collective-permute-start(bf16[2,2,128,128]{3,2,1,0:T(8,128)(2,1)S(1)} %get-tuple-element.15), channel_id=1, source_target_pairs={{0,16},{1,48},{2,80},{3,112},{4,144},{5,176},{6,208},{7,240},{8,27... | collective-permute-start | bytes 393224 | tf_op jit(solution)/shard_map/ppermute | solution.py:94
  11.9 12.3 %collective-permute-start.2 = (bf16[2,2,128,128]{3,2,1,0:T(8,128)(2,1)S(1)}, bf16[2,2,128,128]{3,2,1,0:T(8,128)(2,1)S(1)}, u32[]{:S(2)}, u32[]{:S(2)}) collective-permute-start(bf16[2,2,128,128]{3,2,1,0:T(8,128)(2,1)S(1)} %get-tuple-element.16), channel_id=1, source_target_pairs={{16,0},{17,32},{18,64},{19,96},{20,128},{21,160},{22,192},{23,224}... | collective-permute-start | bytes 393224 | tf_op jit(solution)/shard_map/ppermute | solution.py:94
  18.3 6.0 %collective-permute-start = (bf16[2,2,128,128]{3,2,1,0:T(8,128)(2,1)S(1)}, bf16[2,2,128,128]{3,2,1,0:T(8,128)(2,1)S(1)}, u32[]{:S(2)}, u32[]{:S(2)}) collective-permute-start(bf16[2,2,128,128]{3,2,1,0:T(8,128)(2,1)S(1)} %get-tuple-element.16), channel_id=1, source_target_pairs={{0,0},{1,32},{2,64},{3,96},{4,128},{5,160},{6,192},{7,224},{8,256}... | collective-permute-start | bytes 393224 | tf_op jit(solution)/shard_map/ppermute | solution.py:94
  25.5 29.8 %collective-permute-start.4 = (bf16[2,2,128,256]{3,2,1,0:T(8,128)(2,1)S(1)}, bf16[2,2,128,256]{3,2,1,0:T(8,128)(2,1)S(1)}, u32[]{:S(2)}, u32[]{:S(2)}) collective-permute-start(bf16[2,2,128,256]{3,2,1,0:T(8,128)(2,1)S(1)} %get-tuple-element.6), channel_id=1, source_target_pairs={{0,8},{8,0},{1,9},{9,1},{2,10},{10,2},{3,11},{11,3},{4,12},{12,4},... | collective-permute-start | bytes 786440 | tf_op jit(solution)/shard_map/ppermute | solution.py:49
  56.8 143.7 %all-gather.6.cloned.1.call-start = ((), (), s32[]{:S(2)}) async-start(), calls=%async_computation.1 | async-start | bytes 6291456 | tf_op jit(solution)/shard_map/all_gather | solution.py:109
  56.9 9.9 %collective-permute-start.5 = (bf16[2,2,128,256]{3,2,1,0:T(8,128)(2,1)S(1)}, bf16[2,2,128,256]{3,2,1,0:T(8,128)(2,1)S(1)}, u32[]{:S(2)}, u32[]{:S(2)}) collective-permute-start(bf16[2,2,128,256]{3,2,1,0:T(8,128)(2,1)S(1)} %get-tuple-element.6), channel_id=1, source_target_pairs={{0,128},{128,256},{256,384},{1,129},{129,257},{257,385},{2,130},{1... | collective-permute-start | bytes 786440 | tf_op jit(solution)/shard_map/ppermute | solution.py:49
  62.0 8.9 %collective-permute-start.8 = (bf16[2,2,128,256]{3,2,1,0:T(8,128)(2,1)S(1)}, bf16[2,2,128,256]{3,2,1,0:T(8,128)(2,1)S(1)}, u32[]{:S(2)}, u32[]{:S(2)}) collective-permute-start(bf16[2,2,128,256]{3,2,1,0:T(8,128)(2,1)S(1)} %get-tuple-element.6), channel_id=1, source_target_pairs={{128,0},{256,128},{384,256},{129,1},{257,129},{385,257},{130,2},{2... | collective-permute-start | bytes 786440 | tf_op jit(solution)/shard_map/ppermute | solution.py:52
  66.8 5.4 %collective-permute-start.6 = (bf16[2,2,128,256]{3,2,1,0:T(8,128)(2,1)S(1)}, bf16[2,2,128,256]{3,2,1,0:T(8,128)(2,1)S(1)}, u32[]{:S(2)}, u32[]{:S(2)}) collective-permute-start(bf16[2,2,128,256]{3,2,1,0:T(8,128)(2,1)S(1)} %collective-permute-done.5), channel_id=1, source_target_pairs={{128,256},{256,384},{129,257},{257,385},{130,258},{258,386},{131,2... | collective-permute-start | bytes 786440 | tf_op jit(solution)/shard_map/ppermute | solution.py:49
  70.9 8.3 %collective-permute-start.9 = (bf16[2,2,128,256]{3,2,1,0:T(8,128)(2,1)S(1)}, bf16[2,2,128,256]{3,2,1,0:T(8,128)(2,1)S(1)}, u32[]{:S(2)}, u32[]{:S(2)}) collective-permute-start(bf16[2,2,128,256]{3,2,1,0:T(8,128)(2,1)S(1)} %collective-permute-done.8), channel_id=1, source_target_pairs={{128,0},{256,128},{129,1},{257,129},{130,2},{258,130},{131,3},{259... | collective-permute-start | bytes 786440 | tf_op jit(solution)/shard_map/ppermute | solution.py:52
  72.2 39.7 %collective-permute-start.7 = (bf16[2,2,128,256]{3,2,1,0:T(8,128)(2,1)S(1)}, bf16[2,2,128,256]{3,2,1,0:T(8,128)(2,1)S(1)}, u32[]{:S(2)}, u32[]{:S(2)}) collective-permute-start(bf16[2,2,128,256]{3,2,1,0:T(8,128)(2,1)S(1)} %collective-permute-done.6), channel_id=1, source_target_pairs={{256,384},{257,385},{258,386},{259,387},{260,388},{261,389},{262,3... | collective-permute-start | bytes 786440 | tf_op jit(solution)/shard_map/ppermute | solution.py:49
  79.2 35.0 %collective-permute-start.10 = (bf16[2,2,128,256]{3,2,1,0:T(8,128)(2,1)S(1)}, bf16[2,2,128,256]{3,2,1,0:T(8,128)(2,1)S(1)}, u32[]{:S(2)}, u32[]{:S(2)}) collective-permute-start(bf16[2,2,128,256]{3,2,1,0:T(8,128)(2,1)S(1)} %collective-permute-done.9), channel_id=1, source_target_pairs={{128,0},{129,1},{130,2},{131,3},{132,4},{133,5},{134,6},{135,7},{1... | collective-permute-start | bytes 786440 | tf_op jit(solution)/shard_map/ppermute | solution.py:52
  117.2 26.6 %collective-permute-start.11 = (bf16[2,2,4,128,256]{4,3,2,0,1:T(8,128)(2,1)S(1)}, bf16[2,2,4,128,256]{4,3,2,0,1:T(8,128)(2,1)S(1)}, u32[]{:S(2)}, u32[]{:S(2)}) collective-permute-start(bf16[2,2,4,128,256]{4,3,2,0,1:T(8,128)(2,1)S(1)} %fusion.32), channel_id=1, source_target_pairs={{0,16},{16,32},{32,48},{48,64},{64,80},{80,96},{96,112},{112,0},{1... | collective-permute-start | bytes 3145736 | tf_op jit(solution)/shard_map/ppermute | solution.py:72
  119.5 27.8 %collective-permute-start.12 = (bf16[2,2,4,128,256]{4,3,2,0,1:T(8,128)(2,1)S(1)}, bf16[2,2,4,128,256]{4,3,2,0,1:T(8,128)(2,1)S(1)}, u32[]{:S(2)}, u32[]{:S(2)}) collective-permute-start(bf16[2,2,4,128,256]{4,3,2,0,1:T(8,128)(2,1)S(1)} %fusion.32), channel_id=1, source_target_pairs={{16,0},{32,16},{48,32},{64,48},{80,64},{96,80},{112,96},{0,112},{1... | collective-permute-start | bytes 3145736 | tf_op jit(solution)/shard_map/ppermute | solution.py:75
  143.8 25.8 %collective-permute-start.13 = (bf16[2,2,4,128,256]{4,3,2,0,1:T(8,128)(2,1)S(1)}, bf16[2,2,4,128,256]{4,3,2,0,1:T(8,128)(2,1)S(1)}, u32[]{:S(2)}, u32[]{:S(2)}) collective-permute-start(bf16[2,2,4,128,256]{4,3,2,0,1:T(8,128)(2,1)S(1)} %collective-permute-done.11), channel_id=1, source_target_pairs={{0,16},{16,32},{32,48},{48,64},{64,80},{80,96},{96,112},{112,0},{1... | collective-permute-start | bytes 3145736 | tf_op jit(solution)/shard_map/ppermute | solution.py:72
  147.4 60.5 %copy-start.8 = (bf16[2,2,4,128,256]{4,3,2,0,1:T(8,128)(2,1)}, bf16[2,2,4,128,256]{4,3,2,0,1:T(8,128)(2,1)S(1)}, u32[]{:S(2)}) copy-start(bf16[2,2,4,128,256]{4,3,2,0,1:T(8,128)(2,1)S(1)} %collective-permute-done.12) | copy-start | bytes 3145732
  147.4 27.1 %collective-permute-start.14 = (bf16[2,2,4,128,256]{4,3,2,0,1:T(8,128)(2,1)S(1)}, bf16[2,2,4,128,256]{4,3,2,0,1:T(8,128)(2,1)}, u32[]{:S(2)}, u32[]{:S(2)}) collective-permute-start(bf16[2,2,4,128,256]{4,3,2,0,1:T(8,128)(2,1)S(1)} %collective-permute-done.12), channel_id=1, source_target_pairs={{16,0},{32,16},{48,32},{64,48},{80,64},{96,80},{112,96},{0,112},{1... | collective-permute-start | bytes 3145736 | tf_op jit(solution)/shard_map/ppermute | solution.py:75
  169.6 38.3 %copy-start.6 = (bf16[2,2,4,128,256]{4,3,2,0,1:T(8,128)(2,1)}, bf16[2,2,4,128,256]{4,3,2,0,1:T(8,128)(2,1)S(1)}, u32[]{:S(2)}) copy-start(bf16[2,2,4,128,256]{4,3,2,0,1:T(8,128)(2,1)S(1)} %collective-permute-done.13) | copy-start | bytes 3145732
  169.6 25.2 %collective-permute-start.15 = (bf16[2,2,4,128,256]{4,3,2,0,1:T(8,128)(2,1)S(1)}, bf16[2,2,4,128,256]{4,3,2,0,1:T(8,128)(2,1)}, u32[]{:S(2)}, u32[]{:S(2)}) collective-permute-start(bf16[2,2,4,128,256]{4,3,2,0,1:T(8,128)(2,1)S(1)} %collective-permute-done.13), channel_id=1, source_target_pairs={{0,16},{16,32},{32,48},{48,64},{64,80},{80,96},{96,112},{112,0},{1... | collective-permute-start | bytes 3145736 | tf_op jit(solution)/shard_map/ppermute | solution.py:72
  174.5 53.3 %collective-permute-start.16 = (bf16[2,2,4,128,256]{4,3,2,0,1:T(8,128)(2,1)}, bf16[2,2,4,128,256]{4,3,2,0,1:T(8,128)(2,1)}, u32[]{:S(2)}, u32[]{:S(2)}) collective-permute-start(bf16[2,2,4,128,256]{4,3,2,0,1:T(8,128)(2,1)} %collective-permute-done.14), channel_id=1, source_target_pairs={{16,0},{32,16},{48,32},{64,48},{80,64},{96,80},{112,96},{0,112},{1... | collective-permute-start | bytes 3145736 | tf_op jit(solution)/shard_map/ppermute | solution.py:75
  194.9 39.7 %collective-permute-start.17 = (bf16[2,2,4,128,256]{4,3,2,0,1:T(8,128)(2,1)}, bf16[2,2,4,128,256]{4,3,2,0,1:T(8,128)(2,1)}, u32[]{:S(2)}, u32[]{:S(2)}) collective-permute-start(bf16[2,2,4,128,256]{4,3,2,0,1:T(8,128)(2,1)} %collective-permute-done.15), channel_id=1, source_target_pairs={{0,16},{16,32},{32,48},{48,64},{64,80},{80,96},{96,112},{112,0},{1... | collective-permute-start | bytes 3145736 | tf_op jit(solution)/shard_map/ppermute | solution.py:72
  226.4 4.1 %copy-start = (bf16[2,2,128,4,1,128]{5,2,3,0,1,4:T(8,128)(2,1)S(1)}, bf16[2,2,128,4,1,128]{5,2,3,0,1,4:T(8,128)(2,1)}, u32[]{:S(2)}) copy-start(bf16[2,2,128,4,1,128]{5,2,3,0,1,4:T(8,128)(2,1)} %copy.36) | copy-start | bytes 1572868
  (7 other events, 19.2 us)
Sparse Core Ops, SparseCore 0:
  57.0 51.7 all-gather.3
  112.1 21.8 all-gather.5

commit v6 on v5

--- a/solution.py
+++ b/solution.py
@@ -62,7 +62,7 @@
     return jnp.take(stacked, sel, axis=0)
 
 
-def ring_blocks(block, axis):
+def ring_blocks(block, axis, held):
     n = lax.axis_size(axis)
     right = [(i, (i + 1) % n) for i in range(n)]
     left = [(d, s) for s, d in right]
@@ -74,7 +74,9 @@
         if k < n - n // 2:
             dn = lax.ppermute(dn, axis, left)
             got.append((-k, dn))
-    return got
+        if k == 1:
+            up, dn, held = lax.optimization_barrier((up, dn, held))
+    return got, held
 
 
 def mirrored_pieces(traces, shot_count, recv_count):
@@ -103,19 +105,26 @@
     summed = traces.astype(jnp.float32) + jnp.swapaxes(mirrored, 2, 3).astype(jnp.float32)
     averaged = (summed * 0.5).astype(jnp.bfloat16)
     freqs, _, block_rows, col_width = averaged.shape
-    z_cols = jnp.moveaxis(stream_gather(averaged, "z_lo", False), 0, 2)
     rows = stream_gather(averaged, "z_hi", True)
     rows = lax.all_gather(rows, "x", axis=1)
     rows = lax.all_gather(rows, "core", axis=2)
     y_n = lax.axis_size("y")
-    z_n = z_cols.shape[2]
+    z_n = lax.axis_size("z_lo")
     row_panel = jnp.transpose(rows, (3, 4, 5, 0, 1, 2, 6)).reshape(freqs, 2, block_rows, z_n, y_n, block_rows)
     me_y = lax.axis_index("y")
-    product = None
-    for offset, col_block in ring_blocks(z_cols, "y"):
-        row_block = lax.dynamic_index_in_dim(row_panel, (me_y - offset) % y_n, axis=4, keepdims=False)
-        part = complex_product(row_block, col_block, "fizk,fzkj->fij")
-        product = part if product is None else product + part
+    products = []
+    rest = averaged
+    for f in range(freqs):
+        z_cols = jnp.moveaxis(stream_gather(rest[:1], "z_lo", False), 0, 2)
+        z_cols, rest = lax.optimization_barrier((z_cols, rest[1:]))
+        blocks, panel = ring_blocks(z_cols, "y", row_panel[f:f + 1])
+        product = None
+        for offset, col_block in blocks:
+            row_block = lax.dynamic_index_in_dim(panel, (me_y - offset) % y_n, axis=4, keepdims=False)
+            part = complex_product(row_block, col_block, "fizk,fzkj->fij")
+            product = part if product is None else product + part
+        products.append(product)
+    product = jnp.concatenate(products, axis=0)
     scale_factor = jnp.float32(float(NS) ** (-0.5))
     return product * scale_factor
 

time: 261 us -> 305 us (1.17)
  starting transfers between devices: 69.4 us -> 96.4 us
  matrix products: 26.4 us -> 49.7 us
  waiting for transfers between devices: 111 us -> 102 us
    ppermute x4 -> x8, waiting for transfers between devices: 59.1 us -> 10.3 us  [ring_blocks(): up = lax.ppermute(up, axis, right)]
    ppermute x3 -> x6, waiting for transfers between devices: 8.95 us -> 29.7 us  [stream_gather(): dn = lax.ppermute(dn, axis, perm(k, -1))]
    ppermute x4 -> x8, starting transfers between devices: 16.2 us -> 33.8 us  [ring_blocks(): up = lax.ppermute(up, axis, right)]
    all_gather x1, waiting for transfers between devices: 27.6 us -> 43.6 us  [per_device(): rows = lax.all_gather(rows, 'x', axis=1)]
    slice x0 -> x4, local copies, waits for them, and re-layouts: none -> 10.8 us  [the longest x3 10.8 us: per_device(): blocks, panel = ring_blocks(z_cols, 'y', row_panel[f:f + 1])]
    transpose x1 -> x0, local copies, waits for them, and re-layouts: 7.33 us -> none  [per_device(): jnp.transpose(rows, (3, 4, 5, 0, 1, 2, 6))]
    dot_general x8 -> x16, matrix products: 6.05 us -> 13.1 us  [complex_product(): jnp.einsum(form, left_block[:, 0], right_block[:, 1], preferred_element_t...]
    dot_general x8 -> x16, matrix products: 6.05 us -> 12.5 us  [complex_product(): jnp.einsum(form, left_block[:, 0], right_block[:, 0], preferred_element_t...]
  transfers between devices with their start and end apart: 20 -> 33, of which waited for: 10 -> 15; matrix products, arithmetic and copies ran while one was open for 17% -> 24% of each run, Pallas kernels for 0% -> 0%
where the time goes in v6:
time: 305 us; the launch traced here: 300 us
  waiting for transfers between devices  102 us (33%)
  starting transfers between devices  96.4 us (32%)
  matrix products  49.7 us (16%)
  local copies, waits for them, and re-layouts  34 us (11%)
  between operations  14.9 us (5%)
  other arithmetic  3.51 us (1%)
    all_gather x1, waiting for transfers between devices, per_device(): rows = lax.all_gather(rows, 'x', axis=1)  43.6 us
    ppermute x8, starting transfers between devices, ring_blocks(): up = lax.ppermute(up, axis, right)  33.8 us
    ppermute x6, waiting for transfers between devices, stream_gather(): dn = lax.ppermute(dn, axis, perm(k, -1))  29.7 us
    ppermute x7, starting transfers between devices, stream_gather(): up = lax.ppermute(up, axis, perm(k, 1))  27.4 us
    dynamic_slice x18, local copies, waits for them, and re-layouts, per_device(): lax.dynamic_index_in_dim(panel, (me_y - offset) % y_n, axis=4, keepdims=F...  16.9 us
    ppermute x6, starting transfers between devices, ring_blocks(): dn = lax.ppermute(dn, axis, left)  14.2 us
    ppermute x4, starting transfers between devices, mirrored_pieces(): got.append(lax.ppermute(part, SHOT + RECV, perm))  13.2 us
    dot_general x16, matrix products, complex_product(): jnp.einsum(form, left_block[:, 0], right_block[:, 1], preferred_element_t...  13.1 us
  transfers between devices with their start and end apart: 33, of which 15 were waited for; matrix products, arithmetic and copies ran while one was open for 24% of the time, Pallas kernels for 0%

profile of v6, /device:TPU:56, one launch (start us, length us, event | category | flops | bytes accessed | tf_op | source)
XLA Modules:
  0.0 300.2 jit_solution(5018368933851019126)
XLA Ops:
  9.5 7.8 %collective-permute-start.2 = (bf16[2,2,128,128]{3,2,1,0:T(8,128)(2,1)S(1)}, bf16[2,2,128,128]{3,2,1,0:T(8,128)(2,1)S(1)}, u32[]{:S(2)}, u32[]{:S(2)}) collective-permute-start(bf16[2,2,128,128]{3,2,1,0:T(8,128)(2,1)S(1)} %get-tuple-element.43), channel_id=1, source_target_pairs={{16,0},{17,32},{18,64},{19,96},{20,128},{21,160},{22,192},{23,224}... | collective-permute-start | bytes 393224 | tf_op jit(solution)/shard_map/ppermute | solution.py:96
  17.3 3.4 %collective-permute-start.3 = (bf16[2,2,128,128]{3,2,1,0:T(8,128)(2,1)S(1)}, bf16[2,2,128,128]{3,2,1,0:T(8,128)(2,1)S(1)}, u32[]{:S(2)}, u32[]{:S(2)}) collective-permute-start(bf16[2,2,128,128]{3,2,1,0:T(8,128)(2,1)S(1)} %get-tuple-element.42), channel_id=1, source_target_pairs={{16,16},{17,48},{18,80},{19,112},{20,144},{21,176},{22,208},{23,24... | collective-permute-start | bytes 393224 | tf_op jit(solution)/shard_map/ppermute | solution.py:96
  21.5 5.4 %collective-permute-done.3 = bf16[2,2,128,128]{3,2,1,0:T(8,128)(2,1)S(1)} collective-permute-done((bf16[2,2,128,128]{3,2,1,0:T(8,128)(2,1)S(1)}, bf16[2,2,128,128]{3,2,1,0:T(8,128)(2,1)S(1)}, u32[]{:S(2)}, u32[]{:S(2)}) %collective-permute-start.3) | collective-permute-done | bytes 131104 | tf_op jit(solution)/shard_map/ppermute | solution.py:96
  28.4 19.7 %collective-permute-start.12 = (bf16[2,2,128,256]{3,2,1,0:T(8,128)(2,1)S(1)}, bf16[2,2,128,256]{3,2,1,0:T(8,128)(2,1)S(1)}, u32[]{:S(2)}, u32[]{:S(2)}) collective-permute-start(bf16[2,2,128,256]{3,2,1,0:T(8,128)(2,1)S(1)} %fusion.67), channel_id=1, source_target_pairs={{0,8},{8,0},{1,9},{9,1},{2,10},{10,2},{3,11},{11,3},{4,12},{12,4},... | collective-permute-start | bytes 786440 | tf_op jit(solution)/shard_map/ppermute | solution.py:49
  48.1 9.5 %collective-permute-done.12 = bf16[2,2,128,256]{3,2,1,0:T(8,128)(2,1)S(1)} collective-permute-done((bf16[2,2,128,256]{3,2,1,0:T(8,128)(2,1)S(1)}, bf16[2,2,128,256]{3,2,1,0:T(8,128)(2,1)S(1)}, u32[]{:S(2)}, u32[]{:S(2)}) %collective-permute-start.12) | collective-permute-done | bytes 262176 | tf_op jit(solution)/shard_map/ppermute | solution.py:49
  59.3 43.6 %all-gather.4.cloned.1.call-done = bf16[2,4,2,2,128,256]{5,4,3,2,0,1:T(8,128)(2,1)} async-done(((bf16[2,1,2,2,128,256]{5,4,3,2,0,1:T(8,128)(2,1)}), bf16[2,4,2,2,128,256]{5,4,3,2,0,1:T(8,128)(2,1)}) %all-gather.4.cloned.1.call-update) | async-done | bytes 2097168 | tf_op jit(solution)/shard_map/all_gather | solution.py:109
  106.2 3.6 %collective-permute-start.4 = (bf16[1,2,128,256]{3,2,1,0:T(8,128)(2,1)S(1)}, bf16[1,2,128,256]{3,2,1,0:T(8,128)(2,1)S(1)}, u32[]{:S(2)}, u32[]{:S(2)}) collective-permute-start(bf16[1,2,128,256]{3,2,1,0:T(8,128)(2,1)S(1)} %get-tuple-element.41), channel_id=1, source_target_pairs={{0,128},{128,256},{256,384},{1,129},{129,257},{257,385},{2,130},{1... | collective-permute-start | bytes 393224 | tf_op jit(solution)/shard_map/ppermute | solution.py:49
  113.0 3.6 %collective-permute-done.7 = bf16[1,2,128,256]{3,2,1,0:T(8,128)(2,1)S(1)} collective-permute-done((bf16[1,2,128,256]{3,2,1,0:T(8,128)(2,1)S(1)}, bf16[1,2,128,256]{3,2,1,0:T(8,128)(2,1)S(1)}, u32[]{:S(2)}, u32[]{:S(2)}) %collective-permute-start.7) | collective-permute-done | bytes 131104 | tf_op jit(solution)/shard_map/ppermute | solution.py:52
  118.7 4.9 %collective-permute-done.8 = bf16[1,2,128,256]{3,2,1,0:T(8,128)(2,1)S(1)} collective-permute-done((bf16[1,2,128,256]{3,2,1,0:T(8,128)(2,1)S(1)}, bf16[1,2,128,256]{3,2,1,0:T(8,128)(2,1)S(1)}, u32[]{:S(2)}, u32[]{:S(2)}) %collective-permute-start.8) | collective-permute-done | bytes 131104 | tf_op jit(solution)/shard_map/ppermute | solution.py:52
  124.9 5.5 %collective-permute-done.9 = bf16[1,2,128,256]{3,2,1,0:T(8,128)(2,1)S(1)} collective-permute-done((bf16[1,2,128,256]{3,2,1,0:T(8,128)(2,1)S(1)}, bf16[1,2,128,256]{3,2,1,0:T(8,128)(2,1)S(1)}, u32[]{:S(2)}, u32[]{:S(2)}) %collective-permute-start.9) | collective-permute-done | bytes 131104 | tf_op jit(solution)/shard_map/ppermute | solution.py:52
  133.4 3.5 %collective-permute-start.11 = (bf16[1,2,4,128,256]{4,3,2,1,0:T(8,128)(2,1)S(1)}, bf16[1,2,4,128,256]{4,3,2,1,0:T(8,128)(2,1)}, u32[]{:S(2)}, u32[]{:S(2)}) collective-permute-start(bf16[1,2,4,128,256]{4,3,2,1,0:T(8,128)(2,1)S(1)} %fusion.65), channel_id=1, source_target_pairs={{16,0},{32,16},{48,32},{64,48},{80,64},{96,80},{112,96},{0,112},{1... | collective-permute-start | bytes 1572872 | tf_op jit(solution)/shard_map/ppermute | solution.py:75
  141.6 4.3 %collective-permute-done.21 = bf16[1,2,128,256]{3,2,1,0:T(8,128)(2,1)S(1)} collective-permute-done((bf16[1,2,128,256]{3,2,1,0:T(8,128)(2,1)S(1)}, bf16[1,2,128,256]{3,2,1,0:T(8,128)(2,1)S(1)}, u32[]{:S(2)}, u32[]{:S(2)}) %collective-permute-start.21) | collective-permute-done | bytes 131104 | tf_op jit(solution)/shard_map/ppermute | solution.py:52
  147.9 6.0 %collective-permute-done.22 = bf16[1,2,128,256]{3,2,1,0:T(8,128)(2,1)S(1)} collective-permute-done((bf16[1,2,128,256]{3,2,1,0:T(8,128)(2,1)S(1)}, bf16[1,2,128,256]{3,2,1,0:T(8,128)(2,1)S(1)}, u32[]{:S(2)}, u32[]{:S(2)}) %collective-permute-start.22) | collective-permute-done | bytes 131104 | tf_op jit(solution)/shard_map/ppermute | solution.py:52
  155.2 5.5 %collective-permute-done.23 = bf16[1,2,128,256]{3,2,1,0:T(8,128)(2,1)S(1)} collective-permute-done((bf16[1,2,128,256]{3,2,1,0:T(8,128)(2,1)S(1)}, bf16[1,2,128,256]{3,2,1,0:T(8,128)(2,1)S(1)}, u32[]{:S(2)}, u32[]{:S(2)}) %collective-permute-start.23) | collective-permute-done | bytes 131104 | tf_op jit(solution)/shard_map/ppermute | solution.py:52
  161.4 3.5 %collective-permute-start.24 = (bf16[1,2,4,128,256]{4,3,2,1,0:T(8,128)(2,1)S(1)}, bf16[1,2,4,128,256]{4,3,2,1,0:T(8,128)(2,1)}, u32[]{:S(2)}, u32[]{:S(2)}) collective-permute-start(bf16[1,2,4,128,256]{4,3,2,1,0:T(8,128)(2,1)S(1)} %fusion.64), channel_id=1, source_target_pairs={{0,16},{16,32},{32,48},{48,64},{64,80},{80,96},{96,112},{112,0},{1... | collective-permute-start | bytes 1572872 | tf_op jit(solution)/shard_map/ppermute | solution.py:72
  167.3 4.8 %fusion.93 = (bf16[1,2,128,2,4,2,256]{6,2,1,0,5,4,3:T(8,128)(2,1)}, bf16[1,2,128,2,4,2,256]{6,2,1,0,5,4,3:T(8,128)(2,1)}) fusion(bf16[2,2,128,2,4,2,256]{6,2,1,0,5,4,3:T(8,128)(2,1)} %bitcast.673), kind=kLoop, calls=%fused_computation.283 | loop fusion | bytes 8388608 | tf_op jit(solution)/shard_map/slice | solution.py:120
  187.7 4.7 %collective-permute-start.13 = (bf16[1,2,4,128,256]{4,3,2,1,0:T(8,128)(2,1)}, bf16[1,2,4,128,256]{4,3,2,1,0:T(8,128)(2,1)}, u32[]{:S(2)}, u32[]{:S(2)}) collective-permute-start(bf16[1,2,4,128,256]{4,3,2,1,0:T(8,128)(2,1)} %collective-permute-done.10), channel_id=1, source_target_pairs={{0,16},{16,32},{32,48},{48,64},{64,80},{80,96},{96,112},{112,0},{1... | collective-permute-start | bytes 1572872 | tf_op jit(solution)/shard_map/ppermute | solution.py:72
  200.9 5.1 %collective-permute-start.26 = (bf16[1,2,4,128,256]{4,3,2,1,0:T(8,128)(2,1)}, bf16[1,2,4,128,256]{4,3,2,1,0:T(8,128)(2,1)}, u32[]{:S(2)}, u32[]{:S(2)}) collective-permute-start(bf16[1,2,4,128,256]{4,3,2,1,0:T(8,128)(2,1)} %collective-permute-done.24), channel_id=1, source_target_pairs={{0,16},{16,32},{32,48},{48,64},{64,80},{80,96},{96,112},{112,0},{1... | collective-permute-start | bytes 1572872 | tf_op jit(solution)/shard_map/ppermute | solution.py:72
  236.0 5.1 %collective-permute-start.15 = (bf16[1,2,4,128,256]{4,3,2,1,0:T(8,128)(2,1)}, bf16[1,2,4,128,256]{4,3,2,1,0:T(8,128)(2,1)S(1)}, u32[]{:S(2)}, u32[]{:S(2)}) collective-permute-start(bf16[1,2,4,128,256]{4,3,2,1,0:T(8,128)(2,1)} %collective-permute-done.13), channel_id=1, source_target_pairs={{0,16},{16,32},{32,48},{48,64},{64,80},{80,96},{96,112},{112,0},{1... | collective-permute-start | bytes 1572872 | tf_op jit(solution)/shard_map/ppermute | solution.py:72
  257.2 4.5 %collective-permute-start.28 = (bf16[1,2,4,128,256]{4,3,2,1,0:T(8,128)(2,1)}, bf16[1,2,4,128,256]{4,3,2,1,0:T(8,128)(2,1)S(1)}, u32[]{:S(2)}, u32[]{:S(2)}) collective-permute-start(bf16[1,2,4,128,256]{4,3,2,1,0:T(8,128)(2,1)} %collective-permute-done.26), channel_id=1, source_target_pairs={{0,16},{16,32},{32,48},{48,64},{64,80},{80,96},{96,112},{112,0},{1... | collective-permute-start | bytes 1572872 | tf_op jit(solution)/shard_map/ppermute | solution.py:72
  268.6 4.1 %collective-permute-start.17 = (bf16[1,2,4,128,256]{4,3,2,1,0:T(8,128)(2,1)S(1)}, bf16[1,2,4,128,256]{4,3,2,1,0:T(8,128)(2,1)S(1)}, u32[]{:S(2)}, u32[]{:S(2)}) collective-permute-start(bf16[1,2,4,128,256]{4,3,2,1,0:T(8,128)(2,1)S(1)} %collective-permute-done.15), channel_id=1, source_target_pairs={{0,16},{16,32},{32,48},{48,64},{64,80},{80,96},{96,112},{112,0},{1... | collective-permute-start | bytes 1572872 | tf_op jit(solution)/shard_map/ppermute | solution.py:72
  275.3 4.4 %collective-permute-start.30 = (bf16[1,2,4,128,256]{4,3,2,1,0:T(8,128)(2,1)S(1)}, bf16[1,2,4,128,256]{4,3,2,1,0:T(8,128)(2,1)S(1)}, u32[]{:S(2)}, u32[]{:S(2)}) collective-permute-start(bf16[1,2,4,128,256]{4,3,2,1,0:T(8,128)(2,1)S(1)} %collective-permute-done.28), channel_id=1, source_target_pairs={{0,16},{16,32},{32,48},{48,64},{64,80},{80,96},{96,112},{112,0},{1... | collective-permute-start | bytes 1572872 | tf_op jit(solution)/shard_map/ppermute | solution.py:72
  281.0 5.0 %collective-permute-done.17 = bf16[1,2,4,128,256]{4,3,2,1,0:T(8,128)(2,1)S(1)} collective-permute-done((bf16[1,2,4,128,256]{4,3,2,1,0:T(8,128)(2,1)S(1)}, bf16[1,2,4,128,256]{4,3,2,1,0:T(8,128)(2,1)S(1)}, u32[]{:S(2)}, u32[]{:S(2)}) %collective-permute-start.17) | collective-permute-done | bytes 524320 | tf_op jit(solution)/shard_map/ppermute | solution.py:72
  286.9 4.7 %collective-permute-done.30 = bf16[1,2,4,128,256]{4,3,2,1,0:T(8,128)(2,1)S(1)} collective-permute-done((bf16[1,2,4,128,256]{4,3,2,1,0:T(8,128)(2,1)S(1)}, bf16[1,2,4,128,256]{4,3,2,1,0:T(8,128)(2,1)S(1)}, u32[]{:S(2)}, u32[]{:S(2)}) %collective-permute-start.30) | collective-permute-done | bytes 524320 | tf_op jit(solution)/shard_map/ppermute | solution.py:72
  (194 shorter events, 113.2 us)
Async XLA Ops:
  6.5 96.3 %all-gather.4.cloned.1.call-start = ((), (), s32[]{:S(2)}) async-start(), calls=%async_computation | async-start | bytes 2621440 | tf_op jit(solution)/shard_map/all_gather | solution.py:109
  7.5 13.3 %collective-permute-start = (bf16[2,2,128,128]{3,2,1,0:T(8,128)(2,1)S(1)}, bf16[2,2,128,128]{3,2,1,0:T(8,128)(2,1)S(1)}, u32[]{:S(2)}, u32[]{:S(2)}) collective-permute-start(bf16[2,2,128,128]{3,2,1,0:T(8,128)(2,1)S(1)} %get-tuple-element.43), channel_id=1, source_target_pairs={{0,0},{1,32},{2,64},{3,96},{4,128},{5,160},{6,192},{7,224},{8,256}... | collective-permute-start | bytes 393224 | tf_op jit(solution)/shard_map/ppermute | solution.py:96
  8.2 13.3 %collective-permute-start.1 = (bf16[2,2,128,128]{3,2,1,0:T(8,128)(2,1)S(1)}, bf16[2,2,128,128]{3,2,1,0:T(8,128)(2,1)S(1)}, u32[]{:S(2)}, u32[]{:S(2)}) collective-permute-start(bf16[2,2,128,128]{3,2,1,0:T(8,128)(2,1)S(1)} %get-tuple-element.42), channel_id=1, source_target_pairs={{0,16},{1,48},{2,80},{3,112},{4,144},{5,176},{6,208},{7,240},{8,27... | collective-permute-start | bytes 393224 | tf_op jit(solution)/shard_map/ppermute | solution.py:96
  9.5 12.0 %collective-permute-start.2 = (bf16[2,2,128,128]{3,2,1,0:T(8,128)(2,1)S(1)}, bf16[2,2,128,128]{3,2,1,0:T(8,128)(2,1)S(1)}, u32[]{:S(2)}, u32[]{:S(2)}) collective-permute-start(bf16[2,2,128,128]{3,2,1,0:T(8,128)(2,1)S(1)} %get-tuple-element.43), channel_id=1, source_target_pairs={{16,0},{17,32},{18,64},{19,96},{20,128},{21,160},{22,192},{23,224}... | collective-permute-start | bytes 393224 | tf_op jit(solution)/shard_map/ppermute | solution.py:96
  17.3 9.6 %collective-permute-start.3 = (bf16[2,2,128,128]{3,2,1,0:T(8,128)(2,1)S(1)}, bf16[2,2,128,128]{3,2,1,0:T(8,128)(2,1)S(1)}, u32[]{:S(2)}, u32[]{:S(2)}) collective-permute-start(bf16[2,2,128,128]{3,2,1,0:T(8,128)(2,1)S(1)} %get-tuple-element.42), channel_id=1, source_target_pairs={{16,16},{17,48},{18,80},{19,112},{20,144},{21,176},{22,208},{23,24... | collective-permute-start | bytes 393224 | tf_op jit(solution)/shard_map/ppermute | solution.py:96
  28.4 29.2 %collective-permute-start.12 = (bf16[2,2,128,256]{3,2,1,0:T(8,128)(2,1)S(1)}, bf16[2,2,128,256]{3,2,1,0:T(8,128)(2,1)S(1)}, u32[]{:S(2)}, u32[]{:S(2)}) collective-permute-start(bf16[2,2,128,256]{3,2,1,0:T(8,128)(2,1)S(1)} %fusion.67), channel_id=1, source_target_pairs={{0,8},{8,0},{1,9},{9,1},{2,10},{10,2},{3,11},{11,3},{4,12},{12,4},... | collective-permute-start | bytes 786440 | tf_op jit(solution)/shard_map/ppermute | solution.py:49
  59.2 108.1 %all-gather.6.cloned.1.call-start = ((), (), s32[]{:S(2)}) async-start(), calls=%async_computation.1 | async-start | bytes 6291456 | tf_op jit(solution)/shard_map/all_gather | solution.py:110
  131.1 44.0 %collective-permute-start.10 = (bf16[1,2,4,128,256]{4,3,2,1,0:T(8,128)(2,1)S(1)}, bf16[1,2,4,128,256]{4,3,2,1,0:T(8,128)(2,1)}, u32[]{:S(2)}, u32[]{:S(2)}) collective-permute-start(bf16[1,2,4,128,256]{4,3,2,1,0:T(8,128)(2,1)S(1)} %fusion.65), channel_id=1, source_target_pairs={{0,16},{16,32},{32,48},{48,64},{64,80},{80,96},{96,112},{112,0},{1... | collective-permute-start | bytes 1572872 | tf_op jit(solution)/shard_map/ppermute | solution.py:72
  133.4 41.6 %collective-permute-start.11 = (bf16[1,2,4,128,256]{4,3,2,1,0:T(8,128)(2,1)S(1)}, bf16[1,2,4,128,256]{4,3,2,1,0:T(8,128)(2,1)}, u32[]{:S(2)}, u32[]{:S(2)}) collective-permute-start(bf16[1,2,4,128,256]{4,3,2,1,0:T(8,128)(2,1)S(1)} %fusion.65), channel_id=1, source_target_pairs={{16,0},{32,16},{48,32},{64,48},{80,64},{96,80},{112,96},{0,112},{1... | collective-permute-start | bytes 1572872 | tf_op jit(solution)/shard_map/ppermute | solution.py:75
  138.4 7.4 %collective-permute-start.21 = (bf16[1,2,128,256]{3,2,1,0:T(8,128)(2,1)S(1)}, bf16[1,2,128,256]{3,2,1,0:T(8,128)(2,1)S(1)}, u32[]{:S(2)}, u32[]{:S(2)}) collective-permute-start(bf16[1,2,128,256]{3,2,1,0:T(8,128)(2,1)S(1)} %get-tuple-element.18), channel_id=1, source_target_pairs={{128,0},{256,128},{384,256},{129,1},{257,129},{385,257},{130,2},{2... | collective-permute-start | bytes 393224 | tf_op jit(solution)/shard_map/ppermute | solution.py:52
  145.9 8.0 %collective-permute-start.22 = (bf16[1,2,128,256]{3,2,1,0:T(8,128)(2,1)S(1)}, bf16[1,2,128,256]{3,2,1,0:T(8,128)(2,1)S(1)}, u32[]{:S(2)}, u32[]{:S(2)}) collective-permute-start(bf16[1,2,128,256]{3,2,1,0:T(8,128)(2,1)S(1)} %collective-permute-done.21), channel_id=1, source_target_pairs={{128,0},{256,128},{129,1},{257,129},{130,2},{258,130},{131,3},{259... | collective-permute-start | bytes 393224 | tf_op jit(solution)/shard_map/ppermute | solution.py:52
  147.2 8.0 %collective-permute-start.20 = (bf16[1,2,128,256]{3,2,1,0:T(8,128)(2,1)S(1)}, bf16[1,2,128,256]{3,2,1,0:T(8,128)(2,1)S(1)}, u32[]{:S(2)}, u32[]{:S(2)}) collective-permute-start(bf16[1,2,128,256]{3,2,1,0:T(8,128)(2,1)S(1)} %collective-permute-done.19), channel_id=1, source_target_pairs={{256,384},{257,385},{258,386},{259,387},{260,388},{261,389},{262,3... | collective-permute-start | bytes 393224 | tf_op jit(solution)/shard_map/ppermute | solution.py:49
  161.4 20.9 %collective-permute-start.24 = (bf16[1,2,4,128,256]{4,3,2,1,0:T(8,128)(2,1)S(1)}, bf16[1,2,4,128,256]{4,3,2,1,0:T(8,128)(2,1)}, u32[]{:S(2)}, u32[]{:S(2)}) collective-permute-start(bf16[1,2,4,128,256]{4,3,2,1,0:T(8,128)(2,1)S(1)} %fusion.64), channel_id=1, source_target_pairs={{0,16},{16,32},{32,48},{48,64},{64,80},{80,96},{96,112},{112,0},{1... | collective-permute-start | bytes 1572872 | tf_op jit(solution)/shard_map/ppermute | solution.py:72
  164.9 17.4 %collective-permute-start.25 = (bf16[1,2,4,128,256]{4,3,2,1,0:T(8,128)(2,1)S(1)}, bf16[1,2,4,128,256]{4,3,2,1,0:T(8,128)(2,1)}, u32[]{:S(2)}, u32[]{:S(2)}) collective-permute-start(bf16[1,2,4,128,256]{4,3,2,1,0:T(8,128)(2,1)S(1)} %fusion.64), channel_id=1, source_target_pairs={{16,0},{32,16},{48,32},{64,48},{80,64},{96,80},{112,96},{0,112},{1... | collective-permute-start | bytes 1572872 | tf_op jit(solution)/shard_map/ppermute | solution.py:75
  187.7 48.3 %collective-permute-start.13 = (bf16[1,2,4,128,256]{4,3,2,1,0:T(8,128)(2,1)}, bf16[1,2,4,128,256]{4,3,2,1,0:T(8,128)(2,1)}, u32[]{:S(2)}, u32[]{:S(2)}) collective-permute-start(bf16[1,2,4,128,256]{4,3,2,1,0:T(8,128)(2,1)} %collective-permute-done.10), channel_id=1, source_target_pairs={{0,16},{16,32},{32,48},{48,64},{64,80},{80,96},{96,112},{112,0},{1... | collective-permute-start | bytes 1572872 | tf_op jit(solution)/shard_map/ppermute | solution.py:72
  192.6 48.6 %collective-permute-start.14 = (bf16[1,2,4,128,256]{4,3,2,1,0:T(8,128)(2,1)}, bf16[1,2,4,128,256]{4,3,2,1,0:T(8,128)(2,1)}, u32[]{:S(2)}, u32[]{:S(2)}) collective-permute-start(bf16[1,2,4,128,256]{4,3,2,1,0:T(8,128)(2,1)} %collective-permute-done.11), channel_id=1, source_target_pairs={{16,0},{32,16},{48,32},{64,48},{80,64},{96,80},{112,96},{0,112},{1... | collective-permute-start | bytes 1572872 | tf_op jit(solution)/shard_map/ppermute | solution.py:75
  200.9 56.3 %collective-permute-start.26 = (bf16[1,2,4,128,256]{4,3,2,1,0:T(8,128)(2,1)}, bf16[1,2,4,128,256]{4,3,2,1,0:T(8,128)(2,1)}, u32[]{:S(2)}, u32[]{:S(2)}) collective-permute-start(bf16[1,2,4,128,256]{4,3,2,1,0:T(8,128)(2,1)} %collective-permute-done.24), channel_id=1, source_target_pairs={{0,16},{16,32},{32,48},{48,64},{64,80},{80,96},{96,112},{112,0},{1... | collective-permute-start | bytes 1572872 | tf_op jit(solution)/shard_map/ppermute | solution.py:72
  206.3 42.6 %collective-permute-start.27 = (bf16[1,2,4,128,256]{4,3,2,1,0:T(8,128)(2,1)}, bf16[1,2,4,128,256]{4,3,2,1,0:T(8,128)(2,1)}, u32[]{:S(2)}, u32[]{:S(2)}) collective-permute-start(bf16[1,2,4,128,256]{4,3,2,1,0:T(8,128)(2,1)} %collective-permute-done.25), channel_id=1, source_target_pairs={{16,0},{32,16},{48,32},{64,48},{80,64},{96,80},{112,96},{0,112},{1... | collective-permute-start | bytes 1572872 | tf_op jit(solution)/shard_map/ppermute | solution.py:75
  236.0 32.5 %collective-permute-start.15 = (bf16[1,2,4,128,256]{4,3,2,1,0:T(8,128)(2,1)}, bf16[1,2,4,128,256]{4,3,2,1,0:T(8,128)(2,1)S(1)}, u32[]{:S(2)}, u32[]{:S(2)}) collective-permute-start(bf16[1,2,4,128,256]{4,3,2,1,0:T(8,128)(2,1)} %collective-permute-done.13), channel_id=1, source_target_pairs={{0,16},{16,32},{32,48},{48,64},{64,80},{80,96},{96,112},{112,0},{1... | collective-permute-start | bytes 1572872 | tf_op jit(solution)/shard_map/ppermute | solution.py:72
  241.2 31.5 %collective-permute-start.16 = (bf16[1,2,4,128,256]{4,3,2,1,0:T(8,128)(2,1)}, bf16[1,2,4,128,256]{4,3,2,1,0:T(8,128)(2,1)S(1)}, u32[]{:S(2)}, u32[]{:S(2)}) collective-permute-start(bf16[1,2,4,128,256]{4,3,2,1,0:T(8,128)(2,1)} %collective-permute-done.14), channel_id=1, source_target_pairs={{16,0},{32,16},{48,32},{64,48},{80,64},{96,80},{112,96},{0,112},{1... | collective-permute-start | bytes 1572872 | tf_op jit(solution)/shard_map/ppermute | solution.py:75
  248.9 24.8 %collective-permute-start.29 = (bf16[1,2,4,128,256]{4,3,2,1,0:T(8,128)(2,1)}, bf16[1,2,4,128,256]{4,3,2,1,0:T(8,128)(2,1)S(1)}, u32[]{:S(2)}, u32[]{:S(2)}) collective-permute-start(bf16[1,2,4,128,256]{4,3,2,1,0:T(8,128)(2,1)} %collective-permute-done.27), channel_id=1, source_target_pairs={{16,0},{32,16},{48,32},{64,48},{80,64},{96,80},{112,96},{0,112},{1... | collective-permute-start | bytes 1572872 | tf_op jit(solution)/shard_map/ppermute | solution.py:75
  257.2 18.1 %collective-permute-start.28 = (bf16[1,2,4,128,256]{4,3,2,1,0:T(8,128)(2,1)}, bf16[1,2,4,128,256]{4,3,2,1,0:T(8,128)(2,1)S(1)}, u32[]{:S(2)}, u32[]{:S(2)}) collective-permute-start(bf16[1,2,4,128,256]{4,3,2,1,0:T(8,128)(2,1)} %collective-permute-done.26), channel_id=1, source_target_pairs={{0,16},{16,32},{32,48},{48,64},{64,80},{80,96},{96,112},{112,0},{1... | collective-permute-start | bytes 1572872 | tf_op jit(solution)/shard_map/ppermute | solution.py:72
  268.6 17.4 %collective-permute-start.17 = (bf16[1,2,4,128,256]{4,3,2,1,0:T(8,128)(2,1)S(1)}, bf16[1,2,4,128,256]{4,3,2,1,0:T(8,128)(2,1)S(1)}, u32[]{:S(2)}, u32[]{:S(2)}) collective-permute-start(bf16[1,2,4,128,256]{4,3,2,1,0:T(8,128)(2,1)S(1)} %collective-permute-done.15), channel_id=1, source_target_pairs={{0,16},{16,32},{32,48},{48,64},{64,80},{80,96},{96,112},{112,0},{1... | collective-permute-start | bytes 1572872 | tf_op jit(solution)/shard_map/ppermute | solution.py:72
  275.3 16.3 %collective-permute-start.30 = (bf16[1,2,4,128,256]{4,3,2,1,0:T(8,128)(2,1)S(1)}, bf16[1,2,4,128,256]{4,3,2,1,0:T(8,128)(2,1)S(1)}, u32[]{:S(2)}, u32[]{:S(2)}) collective-permute-start(bf16[1,2,4,128,256]{4,3,2,1,0:T(8,128)(2,1)S(1)} %collective-permute-done.28), channel_id=1, source_target_pairs={{0,16},{16,32},{32,48},{48,64},{64,80},{80,96},{96,112},{112,0},{1... | collective-permute-start | bytes 1572872 | tf_op jit(solution)/shard_map/ppermute | solution.py:72
  (23 other events, 184.8 us)
Sparse Core Ops, SparseCore 0:
  59.3 43.5 all-gather.3
  106.2 21.8 all-gather.5

commit v7 on v5

--- a/solution.py
+++ b/solution.py
@@ -62,7 +62,7 @@
     return jnp.take(stacked, sel, axis=0)
 
 
-def ring_blocks(block, axis):
+def ring_blocks(block, axis, held):
     n = lax.axis_size(axis)
     right = [(i, (i + 1) % n) for i in range(n)]
     left = [(d, s) for s, d in right]
@@ -74,7 +74,9 @@
         if k < n - n // 2:
             dn = lax.ppermute(dn, axis, left)
             got.append((-k, dn))
-    return got
+        if k == 3:
+            up, dn, held = lax.optimization_barrier((up, dn, held))
+    return got, held
 
 
 def mirrored_pieces(traces, shot_count, recv_count):
@@ -103,16 +105,17 @@
     summed = traces.astype(jnp.float32) + jnp.swapaxes(mirrored, 2, 3).astype(jnp.float32)
     averaged = (summed * 0.5).astype(jnp.bfloat16)
     freqs, _, block_rows, col_width = averaged.shape
-    z_cols = jnp.moveaxis(stream_gather(averaged, "z_lo", False), 0, 2)
     rows = stream_gather(averaged, "z_hi", True)
     rows = lax.all_gather(rows, "x", axis=1)
     rows = lax.all_gather(rows, "core", axis=2)
     y_n = lax.axis_size("y")
-    z_n = z_cols.shape[2]
+    z_n = lax.axis_size("z_lo")
     row_panel = jnp.transpose(rows, (3, 4, 5, 0, 1, 2, 6)).reshape(freqs, 2, block_rows, z_n, y_n, block_rows)
     me_y = lax.axis_index("y")
+    z_cols = jnp.moveaxis(stream_gather(averaged, "z_lo", False), 0, 2)
+    blocks, row_panel = ring_blocks(z_cols, "y", row_panel)
     product = None
-    for offset, col_block in ring_blocks(z_cols, "y"):
+    for offset, col_block in blocks:
         row_block = lax.dynamic_index_in_dim(row_panel, (me_y - offset) % y_n, axis=4, keepdims=False)
         part = complex_product(row_block, col_block, "fizk,fzkj->fij")
         product = part if product is None else product + part

time: 261 us -> 263 us (level); the launches traced: 257 us -> 262 us
  matrix products: 26.4 us -> 35.6 us
  waiting for transfers between devices: 111 us -> 104 us
  starting transfers between devices: 69.4 us -> 72.6 us
    ppermute x4, waiting for transfers between devices: 59.1 us -> 1.99 us  [ring_blocks(): up = lax.ppermute(up, axis, right)]
    ppermute x3, waiting for transfers between devices: 0.01 us -> 50.7 us  [ring_blocks(): dn = lax.ppermute(dn, axis, left)]
    dot_general x8, matrix products: 6.05 us -> 10.2 us  [complex_product(): jnp.einsum(form, left_block[:, 0], right_block[:, 0], preferred_element_t...]
    ppermute x4, starting transfers between devices: 16.2 us -> 19.9 us  [ring_blocks(): up = lax.ppermute(up, axis, right)]
    dot_general x8, matrix products: 6.05 us -> 9.4 us  [complex_product(): jnp.einsum(form, left_block[:, 0], right_block[:, 1], preferred_element_t...]
  transfers between devices with their start and end apart: 20 -> 20, of which waited for: 10 -> 12; matrix products, arithmetic and copies ran while one was open for 17% -> 16% of each run, Pallas kernels for 0% -> 0%
where the time goes in v7:
time: 263 us; the launch traced here: 262 us
  waiting for transfers between devices  104 us (40%)
  starting transfers between devices  72.6 us (28%)
  matrix products  35.6 us (14%)
  local copies, waits for them, and re-layouts  32.5 us (12%)
  between operations  14.3 us (5%)
    ppermute x3, waiting for transfers between devices, ring_blocks(): dn = lax.ppermute(dn, axis, left)  50.7 us
    ppermute x4, starting transfers between devices, stream_gather(): up = lax.ppermute(up, axis, perm(k, 1))  30 us
    all_gather x1, waiting for transfers between devices, per_device(): rows = lax.all_gather(rows, 'x', axis=1)  27.6 us
    ppermute x4, starting transfers between devices, ring_blocks(): up = lax.ppermute(up, axis, right)  19.9 us
    dynamic_slice x9, local copies, waits for them, and re-layouts, per_device(): lax.dynamic_index_in_dim(row_panel, (me_y - offset) % y_n, axis=4, keepdi...  11.6 us
    ppermute x4, starting transfers between devices, mirrored_pieces(): got.append(lax.ppermute(part, SHOT + RECV, perm))  11.4 us
    dot_general x8, matrix products, complex_product(): jnp.einsum(form, left_block[:, 0], right_block[:, 0], preferred_element_t...  10.2 us
    ppermute x4, waiting for transfers between devices, stream_gather(): up = lax.ppermute(up, axis, perm(k, 1))  9.63 us
  transfers between devices with their start and end apart: 20, of which 12 were waited for; matrix products, arithmetic and copies ran while one was open for 16% of the time, Pallas kernels for 0%

profile of v7, /device:TPU:56, one launch (start us, length us, event | category | flops | bytes accessed | tf_op | source)
XLA Modules:
  0.0 261.5 jit_solution(16481584086391862798)
XLA Ops:
  7.6 3.1 %collective-permute-start.3 = (bf16[2,2,128,128]{3,2,1,0:T(8,128)(2,1)S(1)}, bf16[2,2,128,128]{3,2,1,0:T(8,128)(2,1)S(1)}, u32[]{:S(2)}, u32[]{:S(2)}) collective-permute-start(bf16[2,2,128,128]{3,2,1,0:T(8,128)(2,1)S(1)} %get-tuple-element.19), channel_id=1, source_target_pairs={{16,16},{17,48},{18,80},{19,112},{20,144},{21,176},{22,208},{23,24... | collective-permute-start | bytes 393224 | tf_op jit(solution)/shard_map/ppermute | solution.py:96
  11.9 6.4 %collective-permute-start.2 = (bf16[2,2,128,128]{3,2,1,0:T(8,128)(2,1)S(1)}, bf16[2,2,128,128]{3,2,1,0:T(8,128)(2,1)S(1)}, u32[]{:S(2)}, u32[]{:S(2)}) collective-permute-start(bf16[2,2,128,128]{3,2,1,0:T(8,128)(2,1)S(1)} %get-tuple-element.20), channel_id=1, source_target_pairs={{16,0},{17,32},{18,64},{19,96},{20,128},{21,160},{22,192},{23,224}... | collective-permute-start | bytes 393224 | tf_op jit(solution)/shard_map/ppermute | solution.py:96
  20.1 4.2 %collective-permute-done.1 = bf16[2,2,128,128]{3,2,1,0:T(8,128)(2,1)S(1)} collective-permute-done((bf16[2,2,128,128]{3,2,1,0:T(8,128)(2,1)S(1)}, bf16[2,2,128,128]{3,2,1,0:T(8,128)(2,1)S(1)}, u32[]{:S(2)}, u32[]{:S(2)}) %collective-permute-start.1) | collective-permute-done | bytes 131104 | tf_op jit(solution)/shard_map/ppermute | solution.py:96
  25.5 23.6 %collective-permute-start.16 = (bf16[2,2,128,256]{3,2,1,0:T(8,128)(2,1)S(1)}, bf16[2,2,128,256]{3,2,1,0:T(8,128)(2,1)S(1)}, u32[]{:S(2)}, u32[]{:S(2)}) collective-permute-start(bf16[2,2,128,256]{3,2,1,0:T(8,128)(2,1)S(1)} %get-tuple-element.10), channel_id=1, source_target_pairs={{0,8},{8,0},{1,9},{9,1},{2,10},{10,2},{3,11},{11,3},{4,12},{12,4},... | collective-permute-start | bytes 786440 | tf_op jit(solution)/shard_map/ppermute | solution.py:49
  49.1 6.2 %collective-permute-done.16 = bf16[2,2,128,256]{3,2,1,0:T(8,128)(2,1)S(1)} collective-permute-done((bf16[2,2,128,256]{3,2,1,0:T(8,128)(2,1)S(1)}, bf16[2,2,128,256]{3,2,1,0:T(8,128)(2,1)S(1)}, u32[]{:S(2)}, u32[]{:S(2)}) %collective-permute-start.16) | collective-permute-done | bytes 262176 | tf_op jit(solution)/shard_map/ppermute | solution.py:49
  56.9 5.1 %collective-permute-start.4 = (bf16[2,2,128,256]{3,2,1,0:T(8,128)(2,1)S(1)}, bf16[2,2,128,256]{3,2,1,0:T(8,128)(2,1)S(1)}, u32[]{:S(2)}, u32[]{:S(2)}) collective-permute-start(bf16[2,2,128,256]{3,2,1,0:T(8,128)(2,1)S(1)} %get-tuple-element.10), channel_id=1, source_target_pairs={{0,128},{128,256},{256,384},{1,129},{129,257},{257,385},{2,130},{1... | collective-permute-start | bytes 786440 | tf_op jit(solution)/shard_map/ppermute | solution.py:49
  63.3 3.5 %collective-permute-done.4 = bf16[2,2,128,256]{3,2,1,0:T(8,128)(2,1)S(1)} collective-permute-done((bf16[2,2,128,256]{3,2,1,0:T(8,128)(2,1)S(1)}, bf16[2,2,128,256]{3,2,1,0:T(8,128)(2,1)S(1)}, u32[]{:S(2)}, u32[]{:S(2)}) %collective-permute-start.4) | collective-permute-done | bytes 262176 | tf_op jit(solution)/shard_map/ppermute | solution.py:49
  67.5 3.4 %collective-permute-done.7 = bf16[2,2,128,256]{3,2,1,0:T(8,128)(2,1)S(1)} collective-permute-done((bf16[2,2,128,256]{3,2,1,0:T(8,128)(2,1)S(1)}, bf16[2,2,128,256]{3,2,1,0:T(8,128)(2,1)S(1)}, u32[]{:S(2)}, u32[]{:S(2)}) %collective-permute-start.7) | collective-permute-done | bytes 262176 | tf_op jit(solution)/shard_map/ppermute | solution.py:52
  73.7 5.5 %collective-permute-done.8 = bf16[2,2,128,256]{3,2,1,0:T(8,128)(2,1)S(1)} collective-permute-done((bf16[2,2,128,256]{3,2,1,0:T(8,128)(2,1)S(1)}, bf16[2,2,128,256]{3,2,1,0:T(8,128)(2,1)S(1)}, u32[]{:S(2)}, u32[]{:S(2)}) %collective-permute-start.8) | collective-permute-done | bytes 262176 | tf_op jit(solution)/shard_map/ppermute | solution.py:52
  81.2 27.6 %all-gather.4.cloned.1.call-done = bf16[2,4,2,2,128,256]{5,4,3,2,0,1:T(8,128)(2,1)} async-done(((bf16[2,1,2,2,128,256]{5,4,3,2,0,1:T(8,128)(2,1)}), bf16[2,4,2,2,128,256]{5,4,3,2,0,1:T(8,128)(2,1)}) %all-gather.4.cloned.1.call-update) | async-done | bytes 2097168 | tf_op jit(solution)/shard_map/all_gather | solution.py:109
  108.8 3.2 %copy.33 = bf16[2,4,2,2,128,256]{5,4,3,2,1,0:T(8,128)(2,1)} copy(bf16[2,4,2,2,128,256]{5,4,3,2,0,1:T(8,128)(2,1)} %all-gather.4.cloned.1.call-done) | data formatting | bytes 4194304 | tf_op jit(solution)/shard_map/all_gather | solution.py:109
  114.9 2.1 gather_fusion
  117.2 3.3 %collective-permute-start.13 = (bf16[2,2,4,128,256]{4,3,2,0,1:T(8,128)(2,1)S(1)}, bf16[2,2,4,128,256]{4,3,2,0,1:T(8,128)(2,1)S(1)}, u32[]{:S(2)}, u32[]{:S(2)}) collective-permute-start(bf16[2,2,4,128,256]{4,3,2,0,1:T(8,128)(2,1)S(1)} %fusion.32), channel_id=1, source_target_pairs={{16,0},{32,16},{48,32},{64,48},{80,64},{96,80},{112,96},{0,112},{1... | collective-permute-start | bytes 3145736 | tf_op jit(solution)/shard_map/ppermute | solution.py:75
  120.6 3.7 %collective-permute-start.10 = (bf16[2,2,4,128,256]{4,3,2,0,1:T(8,128)(2,1)S(1)}, bf16[2,2,4,128,256]{4,3,2,0,1:T(8,128)(2,1)S(1)}, u32[]{:S(2)}, u32[]{:S(2)}) collective-permute-start(bf16[2,2,4,128,256]{4,3,2,0,1:T(8,128)(2,1)S(1)} %fusion.32), channel_id=1, source_target_pairs={{0,16},{16,32},{32,48},{48,64},{64,80},{80,96},{96,112},{112,0},{1... | collective-permute-start | bytes 3145736 | tf_op jit(solution)/shard_map/ppermute | solution.py:72
  124.3 20.8 %collective-permute-done.13 = bf16[2,2,4,128,256]{4,3,2,0,1:T(8,128)(2,1)S(1)} collective-permute-done((bf16[2,2,4,128,256]{4,3,2,0,1:T(8,128)(2,1)S(1)}, bf16[2,2,4,128,256]{4,3,2,0,1:T(8,128)(2,1)S(1)}, u32[]{:S(2)}, u32[]{:S(2)}) %collective-permute-start.13) | collective-permute-done | bytes 1048608 | tf_op jit(solution)/shard_map/ppermute | solution.py:75
  145.1 2.1 collective-permute-start.14
  148.2 4.9 %collective-permute-start.11 = (bf16[2,2,4,128,256]{4,3,2,0,1:T(8,128)(2,1)S(1)}, bf16[2,2,4,128,256]{4,3,2,0,1:T(8,128)(2,1)S(1)}, u32[]{:S(2)}, u32[]{:S(2)}) collective-permute-start(bf16[2,2,4,128,256]{4,3,2,0,1:T(8,128)(2,1)S(1)} %collective-permute-done.10), channel_id=1, source_target_pairs={{0,16},{16,32},{32,48},{48,64},{64,80},{80,96},{96,112},{112,0},{1... | collective-permute-start | bytes 3145736 | tf_op jit(solution)/shard_map/ppermute | solution.py:72
  153.1 19.0 %collective-permute-done.14 = bf16[2,2,4,128,256]{4,3,2,0,1:T(8,128)(2,1)S(1)} collective-permute-done((bf16[2,2,4,128,256]{4,3,2,0,1:T(8,128)(2,1)S(1)}, bf16[2,2,4,128,256]{4,3,2,0,1:T(8,128)(2,1)S(1)}, u32[]{:S(2)}, u32[]{:S(2)}) %collective-permute-start.14) | collective-permute-done | bytes 1048608 | tf_op jit(solution)/shard_map/ppermute | solution.py:75
  174.2 5.6 %collective-permute-start.12 = (bf16[2,2,4,128,256]{4,3,2,0,1:T(8,128)(2,1)S(1)}, bf16[2,2,4,128,256]{4,3,2,0,1:T(8,128)(2,1)}, u32[]{:S(2)}, u32[]{:S(2)}) collective-permute-start(bf16[2,2,4,128,256]{4,3,2,0,1:T(8,128)(2,1)S(1)} %collective-permute-done.11), channel_id=1, source_target_pairs={{0,16},{16,32},{32,48},{48,64},{64,80},{80,96},{96,112},{112,0},{1... | collective-permute-start | bytes 3145736 | tf_op jit(solution)/shard_map/ppermute | solution.py:72
  180.0 7.3 %copy.34 = bf16[2,2,128,2,4,2,256]{2,6,5,4,3,1,0:T(8,128)(2,1)} copy(bf16[2,2,128,2,4,2,256]{6,2,1,0,5,4,3:T(8,128)(2,1)} %bitcast.369) | data formatting | bytes 8388608 | tf_op jit(solution)/shard_map/transpose | solution.py:113
  187.3 11.0 %collective-permute-done.15 = bf16[2,2,4,128,256]{4,3,2,0,1:T(8,128)(2,1)} collective-permute-done((bf16[2,2,4,128,256]{4,3,2,0,1:T(8,128)(2,1)S(1)}, bf16[2,2,4,128,256]{4,3,2,0,1:T(8,128)(2,1)}, u32[]{:S(2)}, u32[]{:S(2)}) %collective-permute-start.15) | collective-permute-done | bytes 1048608 | tf_op jit(solution)/shard_map/ppermute | solution.py:75
  200.0 3.7 %constant_dynamic-slice_fusion = (bf16[2,2,128,4,1,128]{2,5,4,3,1,0:T(8,128)(2,1)}, bf16[2,2,128,4,1,128]{2,5,4,3,1,0:T(8,128)(2,1)}, bf16[2,2,128,4,1,128]{2,5,...) fusion(bf16[2,2,128,4,8,128]{2,5,4,3,1,0:T(8,128)(2,1)} %bitcas, ...), kind=kLoop, calls=%fused_computation.128 | loop fusion | bytes 8388640 | tf_op jit(solution)/shard_map/jit(dynamic_index_in_dim)/dynamic_slice | solution.py:119
  216.6 5.7 %collective-permute-start.17 = (bf16[2,2,4,128,256]{4,3,2,0,1:T(8,128)(2,1)}, bf16[2,2,4,128,256]{4,3,2,0,1:T(8,128)(2,1)}, u32[]{:S(2)}, u32[]{:S(2)}) collective-permute-start(bf16[2,2,4,128,256]{4,3,2,0,1:T(8,128)(2,1)} %collective-permute-done.12), channel_id=1, source_target_pairs={{0,16},{16,32},{32,48},{48,64},{64,80},{80,96},{96,112},{112,0},{1... | collective-permute-start | bytes 3145736 | tf_op jit(solution)/shard_map/ppermute | solution.py:72
  237.9 2.1 fusion.21
  (139 shorter events, 64.3 us)
Async XLA Ops:
  6.5 18.1 %copy-start.21 = (bf16[2,2,128,256]{3,2,1,0:T(8,128)(2,1)S(1)}, bf16[2,2,128,256]{3,2,1,0:T(8,128)(2,1)}, u32[]{:S(2)}) copy-start(bf16[2,2,128,256]{3,2,1,0:T(8,128)(2,1)} %param.1) | copy-start | bytes 786436
  6.5 102.2 %all-gather.4.cloned.1.call-start = ((), (), s32[]{:S(2)}) async-start(), calls=%async_computation | async-start | bytes 2621440 | tf_op jit(solution)/shard_map/all_gather | solution.py:109
  7.6 12.5 %collective-permute-start.3 = (bf16[2,2,128,128]{3,2,1,0:T(8,128)(2,1)S(1)}, bf16[2,2,128,128]{3,2,1,0:T(8,128)(2,1)S(1)}, u32[]{:S(2)}, u32[]{:S(2)}) collective-permute-start(bf16[2,2,128,128]{3,2,1,0:T(8,128)(2,1)S(1)} %get-tuple-element.19), channel_id=1, source_target_pairs={{16,16},{17,48},{18,80},{19,112},{20,144},{21,176},{22,208},{23,24... | collective-permute-start | bytes 393224 | tf_op jit(solution)/shard_map/ppermute | solution.py:96
  10.6 13.6 %collective-permute-start.1 = (bf16[2,2,128,128]{3,2,1,0:T(8,128)(2,1)S(1)}, bf16[2,2,128,128]{3,2,1,0:T(8,128)(2,1)S(1)}, u32[]{:S(2)}, u32[]{:S(2)}) collective-permute-start(bf16[2,2,128,128]{3,2,1,0:T(8,128)(2,1)S(1)} %get-tuple-element.19), channel_id=1, source_target_pairs={{0,16},{1,48},{2,80},{3,112},{4,144},{5,176},{6,208},{7,240},{8,27... | collective-permute-start | bytes 393224 | tf_op jit(solution)/shard_map/ppermute | solution.py:96
  11.9 12.3 %collective-permute-start.2 = (bf16[2,2,128,128]{3,2,1,0:T(8,128)(2,1)S(1)}, bf16[2,2,128,128]{3,2,1,0:T(8,128)(2,1)S(1)}, u32[]{:S(2)}, u32[]{:S(2)}) collective-permute-start(bf16[2,2,128,128]{3,2,1,0:T(8,128)(2,1)S(1)} %get-tuple-element.20), channel_id=1, source_target_pairs={{16,0},{17,32},{18,64},{19,96},{20,128},{21,160},{22,192},{23,224}... | collective-permute-start | bytes 393224 | tf_op jit(solution)/shard_map/ppermute | solution.py:96
  18.3 6.0 %collective-permute-start = (bf16[2,2,128,128]{3,2,1,0:T(8,128)(2,1)S(1)}, bf16[2,2,128,128]{3,2,1,0:T(8,128)(2,1)S(1)}, u32[]{:S(2)}, u32[]{:S(2)}) collective-permute-start(bf16[2,2,128,128]{3,2,1,0:T(8,128)(2,1)S(1)} %get-tuple-element.20), channel_id=1, source_target_pairs={{0,0},{1,32},{2,64},{3,96},{4,128},{5,160},{6,192},{7,224},{8,256}... | collective-permute-start | bytes 393224 | tf_op jit(solution)/shard_map/ppermute | solution.py:96
  25.5 29.8 %collective-permute-start.16 = (bf16[2,2,128,256]{3,2,1,0:T(8,128)(2,1)S(1)}, bf16[2,2,128,256]{3,2,1,0:T(8,128)(2,1)S(1)}, u32[]{:S(2)}, u32[]{:S(2)}) collective-permute-start(bf16[2,2,128,256]{3,2,1,0:T(8,128)(2,1)S(1)} %get-tuple-element.10), channel_id=1, source_target_pairs={{0,8},{8,0},{1,9},{9,1},{2,10},{10,2},{3,11},{11,3},{4,12},{12,4},... | collective-permute-start | bytes 786440 | tf_op jit(solution)/shard_map/ppermute | solution.py:49
  56.9 123.1 %all-gather.6.cloned.1.call-start = ((), (), s32[]{:S(2)}) async-start(), calls=%async_computation.1 | async-start | bytes 6291456 | tf_op jit(solution)/shard_map/all_gather | solution.py:110
  56.9 9.9 %collective-permute-start.4 = (bf16[2,2,128,256]{3,2,1,0:T(8,128)(2,1)S(1)}, bf16[2,2,128,256]{3,2,1,0:T(8,128)(2,1)S(1)}, u32[]{:S(2)}, u32[]{:S(2)}) collective-permute-start(bf16[2,2,128,256]{3,2,1,0:T(8,128)(2,1)S(1)} %get-tuple-element.10), channel_id=1, source_target_pairs={{0,128},{128,256},{256,384},{1,129},{129,257},{257,385},{2,130},{1... | collective-permute-start | bytes 786440 | tf_op jit(solution)/shard_map/ppermute | solution.py:49
  62.0 8.9 %collective-permute-start.7 = (bf16[2,2,128,256]{3,2,1,0:T(8,128)(2,1)S(1)}, bf16[2,2,128,256]{3,2,1,0:T(8,128)(2,1)S(1)}, u32[]{:S(2)}, u32[]{:S(2)}) collective-permute-start(bf16[2,2,128,256]{3,2,1,0:T(8,128)(2,1)S(1)} %get-tuple-element.10), channel_id=1, source_target_pairs={{128,0},{256,128},{384,256},{129,1},{257,129},{385,257},{130,2},{2... | collective-permute-start | bytes 786440 | tf_op jit(solution)/shard_map/ppermute | solution.py:52
  66.8 5.4 %collective-permute-start.5 = (bf16[2,2,128,256]{3,2,1,0:T(8,128)(2,1)S(1)}, bf16[2,2,128,256]{3,2,1,0:T(8,128)(2,1)S(1)}, u32[]{:S(2)}, u32[]{:S(2)}) collective-permute-start(bf16[2,2,128,256]{3,2,1,0:T(8,128)(2,1)S(1)} %collective-permute-done.4), channel_id=1, source_target_pairs={{128,256},{256,384},{129,257},{257,385},{130,258},{258,386},{131,2... | collective-permute-start | bytes 786440 | tf_op jit(solution)/shard_map/ppermute | solution.py:49
  70.9 8.3 %collective-permute-start.8 = (bf16[2,2,128,256]{3,2,1,0:T(8,128)(2,1)S(1)}, bf16[2,2,128,256]{3,2,1,0:T(8,128)(2,1)S(1)}, u32[]{:S(2)}, u32[]{:S(2)}) collective-permute-start(bf16[2,2,128,256]{3,2,1,0:T(8,128)(2,1)S(1)} %collective-permute-done.7), channel_id=1, source_target_pairs={{128,0},{256,128},{129,1},{257,129},{130,2},{258,130},{131,3},{259... | collective-permute-start | bytes 786440 | tf_op jit(solution)/shard_map/ppermute | solution.py:52
  72.3 39.7 %collective-permute-start.6 = (bf16[2,2,128,256]{3,2,1,0:T(8,128)(2,1)S(1)}, bf16[2,2,128,256]{3,2,1,0:T(8,128)(2,1)S(1)}, u32[]{:S(2)}, u32[]{:S(2)}) collective-permute-start(bf16[2,2,128,256]{3,2,1,0:T(8,128)(2,1)S(1)} %collective-permute-done.5), channel_id=1, source_target_pairs={{256,384},{257,385},{258,386},{259,387},{260,388},{261,389},{262,3... | collective-permute-start | bytes 786440 | tf_op jit(solution)/shard_map/ppermute | solution.py:49
  79.2 35.0 %collective-permute-start.9 = (bf16[2,2,128,256]{3,2,1,0:T(8,128)(2,1)S(1)}, bf16[2,2,128,256]{3,2,1,0:T(8,128)(2,1)S(1)}, u32[]{:S(2)}, u32[]{:S(2)}) collective-permute-start(bf16[2,2,128,256]{3,2,1,0:T(8,128)(2,1)S(1)} %collective-permute-done.8), channel_id=1, source_target_pairs={{128,0},{129,1},{130,2},{131,3},{132,4},{133,5},{134,6},{135,7},{1... | collective-permute-start | bytes 786440 | tf_op jit(solution)/shard_map/ppermute | solution.py:52
  117.2 27.8 %collective-permute-start.13 = (bf16[2,2,4,128,256]{4,3,2,0,1:T(8,128)(2,1)S(1)}, bf16[2,2,4,128,256]{4,3,2,0,1:T(8,128)(2,1)S(1)}, u32[]{:S(2)}, u32[]{:S(2)}) collective-permute-start(bf16[2,2,4,128,256]{4,3,2,0,1:T(8,128)(2,1)S(1)} %fusion.32), channel_id=1, source_target_pairs={{16,0},{32,16},{48,32},{64,48},{80,64},{96,80},{112,96},{0,112},{1... | collective-permute-start | bytes 3145736 | tf_op jit(solution)/shard_map/ppermute | solution.py:75
  120.6 26.6 %collective-permute-start.10 = (bf16[2,2,4,128,256]{4,3,2,0,1:T(8,128)(2,1)S(1)}, bf16[2,2,4,128,256]{4,3,2,0,1:T(8,128)(2,1)S(1)}, u32[]{:S(2)}, u32[]{:S(2)}) collective-permute-start(bf16[2,2,4,128,256]{4,3,2,0,1:T(8,128)(2,1)S(1)} %fusion.32), channel_id=1, source_target_pairs={{0,16},{16,32},{32,48},{48,64},{64,80},{80,96},{96,112},{112,0},{1... | collective-permute-start | bytes 3145736 | tf_op jit(solution)/shard_map/ppermute | solution.py:72
  145.1 29.1 %copy-start.14 = (bf16[2,2,4,128,256]{4,3,2,0,1:T(8,128)(2,1)}, bf16[2,2,4,128,256]{4,3,2,0,1:T(8,128)(2,1)S(1)}, u32[]{:S(2)}) copy-start(bf16[2,2,4,128,256]{4,3,2,0,1:T(8,128)(2,1)S(1)} %collective-permute-done.13) | copy-start | bytes 3145732
  145.1 27.0 %collective-permute-start.14 = (bf16[2,2,4,128,256]{4,3,2,0,1:T(8,128)(2,1)S(1)}, bf16[2,2,4,128,256]{4,3,2,0,1:T(8,128)(2,1)S(1)}, u32[]{:S(2)}, u32[]{:S(2)}) collective-permute-start(bf16[2,2,4,128,256]{4,3,2,0,1:T(8,128)(2,1)S(1)} %collective-permute-done.13), channel_id=1, source_target_pairs={{16,0},{32,16},{48,32},{64,48},{80,64},{96,80},{112,96},{0,112},{1... | collective-permute-start | bytes 3145736 | tf_op jit(solution)/shard_map/ppermute | solution.py:75
  148.2 26.0 %collective-permute-start.11 = (bf16[2,2,4,128,256]{4,3,2,0,1:T(8,128)(2,1)S(1)}, bf16[2,2,4,128,256]{4,3,2,0,1:T(8,128)(2,1)S(1)}, u32[]{:S(2)}, u32[]{:S(2)}) collective-permute-start(bf16[2,2,4,128,256]{4,3,2,0,1:T(8,128)(2,1)S(1)} %collective-permute-done.10), channel_id=1, source_target_pairs={{0,16},{16,32},{32,48},{48,64},{64,80},{80,96},{96,112},{112,0},{1... | collective-permute-start | bytes 3145736 | tf_op jit(solution)/shard_map/ppermute | solution.py:72
  172.0 15.2 %copy-start.19 = (bf16[2,2,4,128,256]{4,3,2,0,1:T(8,128)(2,1)}, bf16[2,2,4,128,256]{4,3,2,0,1:T(8,128)(2,1)S(1)}, u32[]{:S(2)}) copy-start(bf16[2,2,4,128,256]{4,3,2,0,1:T(8,128)(2,1)S(1)} %collective-permute-done.14) | copy-start | bytes 3145732
  172.0 26.2 %collective-permute-start.15 = (bf16[2,2,4,128,256]{4,3,2,0,1:T(8,128)(2,1)S(1)}, bf16[2,2,4,128,256]{4,3,2,0,1:T(8,128)(2,1)}, u32[]{:S(2)}, u32[]{:S(2)}) collective-permute-start(bf16[2,2,4,128,256]{4,3,2,0,1:T(8,128)(2,1)S(1)} %collective-permute-done.14), channel_id=1, source_target_pairs={{16,0},{32,16},{48,32},{64,48},{80,64},{96,80},{112,96},{0,112},{1... | collective-permute-start | bytes 3145736 | tf_op jit(solution)/shard_map/ppermute | solution.py:75
  174.2 13.1 %copy-start.17 = (bf16[2,2,4,128,256]{4,3,2,0,1:T(8,128)(2,1)}, bf16[2,2,4,128,256]{4,3,2,0,1:T(8,128)(2,1)S(1)}, u32[]{:S(2)}) copy-start(bf16[2,2,4,128,256]{4,3,2,0,1:T(8,128)(2,1)S(1)} %collective-permute-done.11) | copy-start | bytes 3145732
  174.2 25.8 %collective-permute-start.12 = (bf16[2,2,4,128,256]{4,3,2,0,1:T(8,128)(2,1)S(1)}, bf16[2,2,4,128,256]{4,3,2,0,1:T(8,128)(2,1)}, u32[]{:S(2)}, u32[]{:S(2)}) collective-permute-start(bf16[2,2,4,128,256]{4,3,2,0,1:T(8,128)(2,1)S(1)} %collective-permute-done.11), channel_id=1, source_target_pairs={{0,16},{16,32},{32,48},{48,64},{64,80},{80,96},{96,112},{112,0},{1... | collective-permute-start | bytes 3145736 | tf_op jit(solution)/shard_map/ppermute | solution.py:72
  216.6 31.6 %collective-permute-start.17 = (bf16[2,2,4,128,256]{4,3,2,0,1:T(8,128)(2,1)}, bf16[2,2,4,128,256]{4,3,2,0,1:T(8,128)(2,1)}, u32[]{:S(2)}, u32[]{:S(2)}) collective-permute-start(bf16[2,2,4,128,256]{4,3,2,0,1:T(8,128)(2,1)} %collective-permute-done.12), channel_id=1, source_target_pairs={{0,16},{16,32},{32,48},{48,64},{64,80},{80,96},{96,112},{112,0},{1... | collective-permute-start | bytes 3145736 | tf_op jit(solution)/shard_map/ppermute | solution.py:72
  (23 other events, 84.7 us)
Sparse Core Ops, SparseCore 0:
  57.0 51.7 all-gather.3
  112.1 21.8 all-gather.5

commit v8 on v7

--- a/solution.py
+++ b/solution.py
@@ -105,12 +105,11 @@
     summed = traces.astype(jnp.float32) + jnp.swapaxes(mirrored, 2, 3).astype(jnp.float32)
     averaged = (summed * 0.5).astype(jnp.bfloat16)
     freqs, _, block_rows, col_width = averaged.shape
-    rows = stream_gather(averaged, "z_hi", True)
-    rows = lax.all_gather(rows, "x", axis=1)
-    rows = lax.all_gather(rows, "core", axis=2)
+    rows = lax.all_gather(averaged, ("z_hi", "x"), axis=0)
+    rows = lax.all_gather(rows, "core", axis=1)
     y_n = lax.axis_size("y")
     z_n = lax.axis_size("z_lo")
-    row_panel = jnp.transpose(rows, (3, 4, 5, 0, 1, 2, 6)).reshape(freqs, 2, block_rows, z_n, y_n, block_rows)
+    row_panel = jnp.transpose(rows, (2, 3, 4, 0, 1, 5)).reshape(freqs, 2, block_rows, z_n, y_n, block_rows)
     me_y = lax.axis_index("y")
     z_cols = jnp.moveaxis(stream_gather(averaged, "z_lo", False), 0, 2)
     blocks, row_panel = ring_blocks(z_cols, "y", row_panel)

time: 263 us -> 283 us (1.076)
  waiting for transfers between devices: 104 us -> 152 us
  starting transfers between devices: 72.6 us -> 51.1 us
  local copies, waits for them, and re-layouts: 32.5 us -> 27.6 us
    all_gather x2, waiting for transfers between devices: 27.6 us -> 80.7 us  [the longest x1 80.6 us: per_device(): rows = lax.all_gather(averaged, ('z_hi', 'x'), axis=0)]
    ppermute x4 -> x3, starting transfers between devices: 30 us -> 8.48 us  [stream_gather(): up = lax.ppermute(up, axis, perm(k, 1))]
    ppermute x4 -> x3, waiting for transfers between devices: 9.63 us -> 2.88 us  [stream_gather(): up = lax.ppermute(up, axis, perm(k, 1))]
    ppermute x3, waiting for transfers between devices: 8.97 us -> 13.4 us  [stream_gather(): dn = lax.ppermute(dn, axis, perm(k, -1))]
    all_gather x1 -> x0, local copies, waits for them, and re-layouts: 3.16 us -> none  [per_device(): rows = lax.all_gather(rows, 'x', axis=1)]
    ppermute x3, waiting for transfers between devices: 50.7 us -> 47.6 us  [ring_blocks(): dn = lax.ppermute(dn, axis, left)]
  transfers between devices with their start and end apart: 20 -> 19, of which waited for: 12 -> 11; matrix products, arithmetic and copies ran while one was open for 16% -> 14% of each run, Pallas kernels for 0% -> 0%
where the time goes in v8:
time: 283 us; the launch traced here: 282 us
  waiting for transfers between devices  152 us (54%)
  starting transfers between devices  51.1 us (18%)
  matrix products  35.5 us (13%)
  local copies, waits for them, and re-layouts  27.6 us (10%)
  between operations  14.3 us (5%)
    all_gather x1, waiting for transfers between devices, per_device(): rows = lax.all_gather(averaged, ('z_hi', 'x'), axis=0)  80.6 us
    ppermute x3, waiting for transfers between devices, ring_blocks(): dn = lax.ppermute(dn, axis, left)  47.6 us
    ppermute x4, starting transfers between devices, ring_blocks(): up = lax.ppermute(up, axis, right)  19.9 us
    ppermute x3, waiting for transfers between devices, stream_gather(): dn = lax.ppermute(dn, axis, perm(k, -1))  13.4 us
    dynamic_slice x9, local copies, waits for them, and re-layouts, per_device(): lax.dynamic_index_in_dim(row_panel, (me_y - offset) % y_n, axis=4, keepdi...  11.5 us
    ppermute x4, starting transfers between devices, mirrored_pieces(): got.append(lax.ppermute(part, SHOT + RECV, perm))  11.4 us
    dot_general x8, matrix products, complex_product(): jnp.einsum(form, left_block[:, 0], right_block[:, 0], preferred_element_t...  10.2 us
    dot_general x8, matrix products, complex_product(): jnp.einsum(form, left_block[:, 0], right_block[:, 1], preferred_element_t...  9.36 us
  transfers between devices with their start and end apart: 19, of which 11 were waited for; matrix products, arithmetic and copies ran while one was open for 14% of the time, Pallas kernels for 0%

profile of v8, /device:TPU:56, one launch (start us, length us, event | category | flops | bytes accessed | tf_op | source)
XLA Modules:
  0.0 281.6 jit_solution(828964305346077373)
XLA Ops:
  7.6 3.1 %collective-permute-start.3 = (bf16[2,2,128,128]{3,2,1,0:T(8,128)(2,1)S(1)}, bf16[2,2,128,128]{3,2,1,0:T(8,128)(2,1)S(1)}, u32[]{:S(2)}, u32[]{:S(2)}) collective-permute-start(bf16[2,2,128,128]{3,2,1,0:T(8,128)(2,1)S(1)} %get-tuple-element.19), channel_id=1, source_target_pairs={{16,16},{17,48},{18,80},{19,112},{20,144},{21,176},{22,208},{23,24... | collective-permute-start | bytes 393224 | tf_op jit(solution)/shard_map/ppermute | solution.py:96
  11.9 6.4 %collective-permute-start.2 = (bf16[2,2,128,128]{3,2,1,0:T(8,128)(2,1)S(1)}, bf16[2,2,128,128]{3,2,1,0:T(8,128)(2,1)S(1)}, u32[]{:S(2)}, u32[]{:S(2)}) collective-permute-start(bf16[2,2,128,128]{3,2,1,0:T(8,128)(2,1)S(1)} %get-tuple-element.20), channel_id=1, source_target_pairs={{16,0},{17,32},{18,64},{19,96},{20,128},{21,160},{22,192},{23,224}... | collective-permute-start | bytes 393224 | tf_op jit(solution)/shard_map/ppermute | solution.py:96
  20.1 4.2 %collective-permute-done.1 = bf16[2,2,128,128]{3,2,1,0:T(8,128)(2,1)S(1)} collective-permute-done((bf16[2,2,128,128]{3,2,1,0:T(8,128)(2,1)S(1)}, bf16[2,2,128,128]{3,2,1,0:T(8,128)(2,1)S(1)}, u32[]{:S(2)}, u32[]{:S(2)}) %collective-permute-start.1) | collective-permute-done | bytes 131104 | tf_op jit(solution)/shard_map/ppermute | solution.py:96
  25.6 7.1 %collective-permute-start.4 = (bf16[2,2,128,256]{3,2,1,0:T(8,128)(2,1)}, bf16[2,2,128,256]{3,2,1,0:T(8,128)(2,1)S(1)}, u32[]{:S(2)}, u32[]{:S(2)}) collective-permute-start(bf16[2,2,128,256]{3,2,1,0:T(8,128)(2,1)} %get-tuple-element.10), channel_id=1, source_target_pairs={{0,128},{128,256},{256,384},{1,129},{129,257},{257,385},{2,130},{1... | collective-permute-start | bytes 786440 | tf_op jit(solution)/shard_map/ppermute | solution.py:49
  34.1 2.9 %collective-permute-done.4 = bf16[2,2,128,256]{3,2,1,0:T(8,128)(2,1)S(1)} collective-permute-done((bf16[2,2,128,256]{3,2,1,0:T(8,128)(2,1)}, bf16[2,2,128,256]{3,2,1,0:T(8,128)(2,1)S(1)}, u32[]{:S(2)}, u32[]{:S(2)}) %collective-permute-start.4) | collective-permute-done | bytes 262176 | tf_op jit(solution)/shard_map/ppermute | solution.py:49
  37.6 7.0 %collective-permute-done.7 = bf16[2,2,128,256]{3,2,1,0:T(8,128)(2,1)S(1)} collective-permute-done((bf16[2,2,128,256]{3,2,1,0:T(8,128)(2,1)}, bf16[2,2,128,256]{3,2,1,0:T(8,128)(2,1)S(1)}, u32[]{:S(2)}, u32[]{:S(2)}) %collective-permute-start.7) | collective-permute-done | bytes 262176 | tf_op jit(solution)/shard_map/ppermute | solution.py:52
  47.4 6.3 %collective-permute-done.8 = bf16[2,2,128,256]{3,2,1,0:T(8,128)(2,1)S(1)} collective-permute-done((bf16[2,2,128,256]{3,2,1,0:T(8,128)(2,1)S(1)}, bf16[2,2,128,256]{3,2,1,0:T(8,128)(2,1)S(1)}, u32[]{:S(2)}, u32[]{:S(2)}) %collective-permute-start.8) | collective-permute-done | bytes 262176 | tf_op jit(solution)/shard_map/ppermute | solution.py:52
  55.7 80.6 %all-gather.5.cloned.1.call-done = bf16[16,2,128,256]{3,2,1,0:T(8,128)(2,1)} async-done(((bf16[2,2,128,256]{3,2,1,0:T(8,128)(2,1)}), bf16[16,2,128,256]{3,2,1,0:T(8,128)(2,1)}) %all-gather.5.cloned.1.call-update) | async-done | bytes 2097168 | tf_op jit(solution)/shard_map/all_gather | solution.py:108
  139.4 2.1 gather_fusion
  141.6 3.3 %collective-permute-start.13 = (bf16[2,2,4,128,256]{4,3,2,0,1:T(8,128)(2,1)S(1)}, bf16[2,2,4,128,256]{4,3,2,0,1:T(8,128)(2,1)S(1)}, u32[]{:S(2)}, u32[]{:S(2)}) collective-permute-start(bf16[2,2,4,128,256]{4,3,2,0,1:T(8,128)(2,1)S(1)} %fusion.32), channel_id=1, source_target_pairs={{16,0},{32,16},{48,32},{64,48},{80,64},{96,80},{112,96},{0,112},{1... | collective-permute-start | bytes 3145736 | tf_op jit(solution)/shard_map/ppermute | solution.py:75
  145.0 3.7 %collective-permute-start.10 = (bf16[2,2,4,128,256]{4,3,2,0,1:T(8,128)(2,1)S(1)}, bf16[2,2,4,128,256]{4,3,2,0,1:T(8,128)(2,1)S(1)}, u32[]{:S(2)}, u32[]{:S(2)}) collective-permute-start(bf16[2,2,4,128,256]{4,3,2,0,1:T(8,128)(2,1)S(1)} %fusion.32), channel_id=1, source_target_pairs={{0,16},{16,32},{32,48},{48,64},{64,80},{80,96},{96,112},{112,0},{1... | collective-permute-start | bytes 3145736 | tf_op jit(solution)/shard_map/ppermute | solution.py:72
  148.7 19.4 %collective-permute-done.13 = bf16[2,2,4,128,256]{4,3,2,0,1:T(8,128)(2,1)S(1)} collective-permute-done((bf16[2,2,4,128,256]{4,3,2,0,1:T(8,128)(2,1)S(1)}, bf16[2,2,4,128,256]{4,3,2,0,1:T(8,128)(2,1)S(1)}, u32[]{:S(2)}, u32[]{:S(2)}) %collective-permute-start.13) | collective-permute-done | bytes 1048608 | tf_op jit(solution)/shard_map/ppermute | solution.py:75
  168.1 2.1 collective-permute-start.14
  171.2 4.9 %collective-permute-start.11 = (bf16[2,2,4,128,256]{4,3,2,0,1:T(8,128)(2,1)S(1)}, bf16[2,2,4,128,256]{4,3,2,0,1:T(8,128)(2,1)S(1)}, u32[]{:S(2)}, u32[]{:S(2)}) collective-permute-start(bf16[2,2,4,128,256]{4,3,2,0,1:T(8,128)(2,1)S(1)} %collective-permute-done.10), channel_id=1, source_target_pairs={{0,16},{16,32},{32,48},{48,64},{64,80},{80,96},{96,112},{112,0},{1... | collective-permute-start | bytes 3145736 | tf_op jit(solution)/shard_map/ppermute | solution.py:72
  176.1 17.5 %collective-permute-done.14 = bf16[2,2,4,128,256]{4,3,2,0,1:T(8,128)(2,1)S(1)} collective-permute-done((bf16[2,2,4,128,256]{4,3,2,0,1:T(8,128)(2,1)S(1)}, bf16[2,2,4,128,256]{4,3,2,0,1:T(8,128)(2,1)S(1)}, u32[]{:S(2)}, u32[]{:S(2)}) %collective-permute-start.14) | collective-permute-done | bytes 1048608 | tf_op jit(solution)/shard_map/ppermute | solution.py:75
  195.8 5.6 %collective-permute-start.12 = (bf16[2,2,4,128,256]{4,3,2,0,1:T(8,128)(2,1)S(1)}, bf16[2,2,4,128,256]{4,3,2,0,1:T(8,128)(2,1)}, u32[]{:S(2)}, u32[]{:S(2)}) collective-permute-start(bf16[2,2,4,128,256]{4,3,2,0,1:T(8,128)(2,1)S(1)} %collective-permute-done.11), channel_id=1, source_target_pairs={{0,16},{16,32},{32,48},{48,64},{64,80},{80,96},{96,112},{112,0},{1... | collective-permute-start | bytes 3145736 | tf_op jit(solution)/shard_map/ppermute | solution.py:72
  201.6 6.2 %copy.33 = bf16[2,2,128,8,2,256]{2,5,4,3,1,0:T(8,128)(2,1)} copy(bf16[2,2,128,8,2,256]{5,2,1,0,4,3:T(8,128)(2,1)} %bitcast.365) | data formatting | bytes 8388608 | tf_op jit(solution)/shard_map/transpose | solution.py:112
  207.8 10.7 %collective-permute-done.15 = bf16[2,2,4,128,256]{4,3,2,0,1:T(8,128)(2,1)} collective-permute-done((bf16[2,2,4,128,256]{4,3,2,0,1:T(8,128)(2,1)S(1)}, bf16[2,2,4,128,256]{4,3,2,0,1:T(8,128)(2,1)}, u32[]{:S(2)}, u32[]{:S(2)}) %collective-permute-start.15) | collective-permute-done | bytes 1048608 | tf_op jit(solution)/shard_map/ppermute | solution.py:75
  220.2 3.7 %constant_dynamic-slice_fusion = (bf16[2,2,128,4,1,128]{2,5,4,3,1,0:T(8,128)(2,1)}, bf16[2,2,128,4,1,128]{2,5,4,3,1,0:T(8,128)(2,1)}, bf16[2,2,128,4,1,128]{2,5,...) fusion(bf16[2,2,128,4,8,128]{2,5,4,3,1,0:T(8,128)(2,1)} %bitcas, ...), kind=kLoop, calls=%fused_computation.124 | loop fusion | bytes 8388640 | tf_op jit(solution)/shard_map/jit(dynamic_index_in_dim)/dynamic_slice | solution.py:118
  227.1 2.0 copy.40
  234.7 2.0 fusion.1
  236.8 5.7 %collective-permute-start.16 = (bf16[2,2,4,128,256]{4,3,2,0,1:T(8,128)(2,1)}, bf16[2,2,4,128,256]{4,3,2,0,1:T(8,128)(2,1)}, u32[]{:S(2)}, u32[]{:S(2)}) collective-permute-start(bf16[2,2,4,128,256]{4,3,2,0,1:T(8,128)(2,1)} %collective-permute-done.12), channel_id=1, source_target_pairs={{0,16},{16,32},{32,48},{48,64},{64,80},{80,96},{96,112},{112,0},{1... | collective-permute-start | bytes 3145736 | tf_op jit(solution)/shard_map/ppermute | solution.py:72
  256.0 2.0 fusion.23
  258.0 2.1 fusion.21
  (130 shorter events, 56.6 us)
Async XLA Ops:
  6.5 18.1 %copy-start.21 = (bf16[2,2,128,256]{3,2,1,0:T(8,128)(2,1)S(1)}, bf16[2,2,128,256]{3,2,1,0:T(8,128)(2,1)}, u32[]{:S(2)}) copy-start(bf16[2,2,128,256]{3,2,1,0:T(8,128)(2,1)} %param.1) | copy-start | bytes 786436
  6.5 129.8 %all-gather.5.cloned.1.call-start = ((), (), s32[]{:S(2)}) async-start(), calls=%async_computation | async-start | bytes 2359296 | tf_op jit(solution)/shard_map/all_gather | solution.py:108
  7.6 12.5 %collective-permute-start.3 = (bf16[2,2,128,128]{3,2,1,0:T(8,128)(2,1)S(1)}, bf16[2,2,128,128]{3,2,1,0:T(8,128)(2,1)S(1)}, u32[]{:S(2)}, u32[]{:S(2)}) collective-permute-start(bf16[2,2,128,128]{3,2,1,0:T(8,128)(2,1)S(1)} %get-tuple-element.19), channel_id=1, source_target_pairs={{16,16},{17,48},{18,80},{19,112},{20,144},{21,176},{22,208},{23,24... | collective-permute-start | bytes 393224 | tf_op jit(solution)/shard_map/ppermute | solution.py:96
  10.6 13.6 %collective-permute-start.1 = (bf16[2,2,128,128]{3,2,1,0:T(8,128)(2,1)S(1)}, bf16[2,2,128,128]{3,2,1,0:T(8,128)(2,1)S(1)}, u32[]{:S(2)}, u32[]{:S(2)}) collective-permute-start(bf16[2,2,128,128]{3,2,1,0:T(8,128)(2,1)S(1)} %get-tuple-element.19), channel_id=1, source_target_pairs={{0,16},{1,48},{2,80},{3,112},{4,144},{5,176},{6,208},{7,240},{8,27... | collective-permute-start | bytes 393224 | tf_op jit(solution)/shard_map/ppermute | solution.py:96
  11.9 12.3 %collective-permute-start.2 = (bf16[2,2,128,128]{3,2,1,0:T(8,128)(2,1)S(1)}, bf16[2,2,128,128]{3,2,1,0:T(8,128)(2,1)S(1)}, u32[]{:S(2)}, u32[]{:S(2)}) collective-permute-start(bf16[2,2,128,128]{3,2,1,0:T(8,128)(2,1)S(1)} %get-tuple-element.20), channel_id=1, source_target_pairs={{16,0},{17,32},{18,64},{19,96},{20,128},{21,160},{22,192},{23,224}... | collective-permute-start | bytes 393224 | tf_op jit(solution)/shard_map/ppermute | solution.py:96
  18.3 6.0 %collective-permute-start = (bf16[2,2,128,128]{3,2,1,0:T(8,128)(2,1)S(1)}, bf16[2,2,128,128]{3,2,1,0:T(8,128)(2,1)S(1)}, u32[]{:S(2)}, u32[]{:S(2)}) collective-permute-start(bf16[2,2,128,128]{3,2,1,0:T(8,128)(2,1)S(1)} %get-tuple-element.20), channel_id=1, source_target_pairs={{0,0},{1,32},{2,64},{3,96},{4,128},{5,160},{6,192},{7,224},{8,256}... | collective-permute-start | bytes 393224 | tf_op jit(solution)/shard_map/ppermute | solution.py:96
  25.6 176.0 %all-gather.7.cloned.1.call-start = ((), (), s32[]{:S(2)}) async-start(), calls=%async_computation.1 | async-start | bytes 6291456 | tf_op jit(solution)/shard_map/all_gather | solution.py:109
  25.6 11.3 %collective-permute-start.4 = (bf16[2,2,128,256]{3,2,1,0:T(8,128)(2,1)}, bf16[2,2,128,256]{3,2,1,0:T(8,128)(2,1)S(1)}, u32[]{:S(2)}, u32[]{:S(2)}) collective-permute-start(bf16[2,2,128,256]{3,2,1,0:T(8,128)(2,1)} %get-tuple-element.10), channel_id=1, source_target_pairs={{0,128},{128,256},{256,384},{1,129},{129,257},{257,385},{2,130},{1... | collective-permute-start | bytes 786440 | tf_op jit(solution)/shard_map/ppermute | solution.py:49
  32.8 11.9 %collective-permute-start.7 = (bf16[2,2,128,256]{3,2,1,0:T(8,128)(2,1)}, bf16[2,2,128,256]{3,2,1,0:T(8,128)(2,1)S(1)}, u32[]{:S(2)}, u32[]{:S(2)}) collective-permute-start(bf16[2,2,128,256]{3,2,1,0:T(8,128)(2,1)} %get-tuple-element.10), channel_id=1, source_target_pairs={{128,0},{256,128},{384,256},{129,1},{257,129},{385,257},{130,2},{2... | collective-permute-start | bytes 786440 | tf_op jit(solution)/shard_map/ppermute | solution.py:52
  36.9 9.1 %collective-permute-start.5 = (bf16[2,2,128,256]{3,2,1,0:T(8,128)(2,1)S(1)}, bf16[2,2,128,256]{3,2,1,0:T(8,128)(2,1)S(1)}, u32[]{:S(2)}, u32[]{:S(2)}) collective-permute-start(bf16[2,2,128,256]{3,2,1,0:T(8,128)(2,1)S(1)} %collective-permute-done.4), channel_id=1, source_target_pairs={{128,256},{256,384},{129,257},{257,385},{130,258},{258,386},{131,2... | collective-permute-start | bytes 786440 | tf_op jit(solution)/shard_map/ppermute | solution.py:49
  44.7 9.0 %collective-permute-start.8 = (bf16[2,2,128,256]{3,2,1,0:T(8,128)(2,1)S(1)}, bf16[2,2,128,256]{3,2,1,0:T(8,128)(2,1)S(1)}, u32[]{:S(2)}, u32[]{:S(2)}) collective-permute-start(bf16[2,2,128,256]{3,2,1,0:T(8,128)(2,1)S(1)} %collective-permute-done.7), channel_id=1, source_target_pairs={{128,0},{256,128},{129,1},{257,129},{130,2},{258,130},{131,3},{259... | collective-permute-start | bytes 786440 | tf_op jit(solution)/shard_map/ppermute | solution.py:52
  46.0 90.4 %collective-permute-start.6 = (bf16[2,2,128,256]{3,2,1,0:T(8,128)(2,1)S(1)}, bf16[2,2,128,256]{3,2,1,0:T(8,128)(2,1)S(1)}, u32[]{:S(2)}, u32[]{:S(2)}) collective-permute-start(bf16[2,2,128,256]{3,2,1,0:T(8,128)(2,1)S(1)} %collective-permute-done.5), channel_id=1, source_target_pairs={{256,384},{257,385},{258,386},{259,387},{260,388},{261,389},{262,3... | collective-permute-start | bytes 786440 | tf_op jit(solution)/shard_map/ppermute | solution.py:49
  53.7 84.9 %collective-permute-start.9 = (bf16[2,2,128,256]{3,2,1,0:T(8,128)(2,1)S(1)}, bf16[2,2,128,256]{3,2,1,0:T(8,128)(2,1)S(1)}, u32[]{:S(2)}, u32[]{:S(2)}) collective-permute-start(bf16[2,2,128,256]{3,2,1,0:T(8,128)(2,1)S(1)} %collective-permute-done.8), channel_id=1, source_target_pairs={{128,0},{129,1},{130,2},{131,3},{132,4},{133,5},{134,6},{135,7},{1... | collective-permute-start | bytes 786440 | tf_op jit(solution)/shard_map/ppermute | solution.py:52
  141.6 26.4 %collective-permute-start.13 = (bf16[2,2,4,128,256]{4,3,2,0,1:T(8,128)(2,1)S(1)}, bf16[2,2,4,128,256]{4,3,2,0,1:T(8,128)(2,1)S(1)}, u32[]{:S(2)}, u32[]{:S(2)}) collective-permute-start(bf16[2,2,4,128,256]{4,3,2,0,1:T(8,128)(2,1)S(1)} %fusion.32), channel_id=1, source_target_pairs={{16,0},{32,16},{48,32},{64,48},{80,64},{96,80},{112,96},{0,112},{1... | collective-permute-start | bytes 3145736 | tf_op jit(solution)/shard_map/ppermute | solution.py:75
  145.0 25.2 %collective-permute-start.10 = (bf16[2,2,4,128,256]{4,3,2,0,1:T(8,128)(2,1)S(1)}, bf16[2,2,4,128,256]{4,3,2,0,1:T(8,128)(2,1)S(1)}, u32[]{:S(2)}, u32[]{:S(2)}) collective-permute-start(bf16[2,2,4,128,256]{4,3,2,0,1:T(8,128)(2,1)S(1)} %fusion.32), channel_id=1, source_target_pairs={{0,16},{16,32},{32,48},{48,64},{64,80},{80,96},{96,112},{112,0},{1... | collective-permute-start | bytes 3145736 | tf_op jit(solution)/shard_map/ppermute | solution.py:72
  168.1 27.7 %copy-start.14 = (bf16[2,2,4,128,256]{4,3,2,0,1:T(8,128)(2,1)}, bf16[2,2,4,128,256]{4,3,2,0,1:T(8,128)(2,1)S(1)}, u32[]{:S(2)}) copy-start(bf16[2,2,4,128,256]{4,3,2,0,1:T(8,128)(2,1)S(1)} %collective-permute-done.13) | copy-start | bytes 3145732
  168.1 25.6 %collective-permute-start.14 = (bf16[2,2,4,128,256]{4,3,2,0,1:T(8,128)(2,1)S(1)}, bf16[2,2,4,128,256]{4,3,2,0,1:T(8,128)(2,1)S(1)}, u32[]{:S(2)}, u32[]{:S(2)}) collective-permute-start(bf16[2,2,4,128,256]{4,3,2,0,1:T(8,128)(2,1)S(1)} %collective-permute-done.13), channel_id=1, source_target_pairs={{16,0},{32,16},{48,32},{64,48},{80,64},{96,80},{112,96},{0,112},{1... | collective-permute-start | bytes 3145736 | tf_op jit(solution)/shard_map/ppermute | solution.py:75
  171.2 24.6 %collective-permute-start.11 = (bf16[2,2,4,128,256]{4,3,2,0,1:T(8,128)(2,1)S(1)}, bf16[2,2,4,128,256]{4,3,2,0,1:T(8,128)(2,1)S(1)}, u32[]{:S(2)}, u32[]{:S(2)}) collective-permute-start(bf16[2,2,4,128,256]{4,3,2,0,1:T(8,128)(2,1)S(1)} %collective-permute-done.10), channel_id=1, source_target_pairs={{0,16},{16,32},{32,48},{48,64},{64,80},{80,96},{96,112},{112,0},{1... | collective-permute-start | bytes 3145736 | tf_op jit(solution)/shard_map/ppermute | solution.py:72
  193.6 14.2 %copy-start.19 = (bf16[2,2,4,128,256]{4,3,2,0,1:T(8,128)(2,1)}, bf16[2,2,4,128,256]{4,3,2,0,1:T(8,128)(2,1)S(1)}, u32[]{:S(2)}) copy-start(bf16[2,2,4,128,256]{4,3,2,0,1:T(8,128)(2,1)S(1)} %collective-permute-done.14) | copy-start | bytes 3145732
  193.6 24.8 %collective-permute-start.15 = (bf16[2,2,4,128,256]{4,3,2,0,1:T(8,128)(2,1)S(1)}, bf16[2,2,4,128,256]{4,3,2,0,1:T(8,128)(2,1)}, u32[]{:S(2)}, u32[]{:S(2)}) collective-permute-start(bf16[2,2,4,128,256]{4,3,2,0,1:T(8,128)(2,1)S(1)} %collective-permute-done.14), channel_id=1, source_target_pairs={{16,0},{32,16},{48,32},{64,48},{80,64},{96,80},{112,96},{0,112},{1... | collective-permute-start | bytes 3145736 | tf_op jit(solution)/shard_map/ppermute | solution.py:75
  195.8 12.0 %copy-start.17 = (bf16[2,2,4,128,256]{4,3,2,0,1:T(8,128)(2,1)}, bf16[2,2,4,128,256]{4,3,2,0,1:T(8,128)(2,1)S(1)}, u32[]{:S(2)}) copy-start(bf16[2,2,4,128,256]{4,3,2,0,1:T(8,128)(2,1)S(1)} %collective-permute-done.11) | copy-start | bytes 3145732
  195.8 24.4 %collective-permute-start.12 = (bf16[2,2,4,128,256]{4,3,2,0,1:T(8,128)(2,1)S(1)}, bf16[2,2,4,128,256]{4,3,2,0,1:T(8,128)(2,1)}, u32[]{:S(2)}, u32[]{:S(2)}) collective-permute-start(bf16[2,2,4,128,256]{4,3,2,0,1:T(8,128)(2,1)S(1)} %collective-permute-done.11), channel_id=1, source_target_pairs={{0,16},{16,32},{32,48},{48,64},{64,80},{80,96},{96,112},{112,0},{1... | collective-permute-start | bytes 3145736 | tf_op jit(solution)/shard_map/ppermute | solution.py:72
  234.7 10.4 %copy-start = (bf16[2,2,128,4,1,128]{5,2,3,0,1,4:T(8,128)(2,1)S(1)}, bf16[2,2,128,4,1,128]{5,2,3,0,1,4:T(8,128)(2,1)}, u32[]{:S(2)}) copy-start(bf16[2,2,128,4,1,128]{5,2,3,0,1,4:T(8,128)(2,1)} %copy.39) | copy-start | bytes 1572868
  236.8 31.5 %collective-permute-start.16 = (bf16[2,2,4,128,256]{4,3,2,0,1:T(8,128)(2,1)}, bf16[2,2,4,128,256]{4,3,2,0,1:T(8,128)(2,1)}, u32[]{:S(2)}, u32[]{:S(2)}) collective-permute-start(bf16[2,2,4,128,256]{4,3,2,0,1:T(8,128)(2,1)} %collective-permute-done.12), channel_id=1, source_target_pairs={{0,16},{16,32},{32,48},{48,64},{64,80},{80,96},{96,112},{112,0},{1... | collective-permute-start | bytes 3145736 | tf_op jit(solution)/shard_map/ppermute | solution.py:72
  (22 other events, 74.2 us)
Sparse Core Ops, SparseCore 0:
  25.7 110.6 all-gather.4
  138.4 17.4 all-gather.6

commit v9 on v7

--- a/solution.py
+++ b/solution.py
@@ -79,6 +79,27 @@
     return got, held
 
 
+def z_hi_swap(block):
+    z_axes = ("z_lo", "z_hi")
+    lo_n = lax.axis_size("z_lo")
+    n = lax.axis_size(z_axes)
+
+    def at(z):
+        z %= n
+        return (z % lo_n) * (n // lo_n) + z // lo_n
+
+    ahead = [(at(z), at(z + 2)) for z in range(n)]
+    behind = [(at(z), at(z - 2)) for z in range(n)]
+    half = block.shape[0] // 2
+    one, other = block[:half], block[half:]
+    for _ in range(2):
+        one = lax.ppermute(one, z_axes, ahead)
+        other = lax.ppermute(other, z_axes, behind)
+    partner = jnp.concatenate((one, other), axis=0)
+    low = lax.axis_index("z_hi") == 0
+    return jnp.stack((jnp.where(low, block, partner), jnp.where(low, partner, block)))
+
+
 def mirrored_pieces(traces, shot_count, recv_count):
     block_rows = traces.shape[2]
     g = traces.shape[3] // block_rows
@@ -105,7 +126,7 @@
     summed = traces.astype(jnp.float32) + jnp.swapaxes(mirrored, 2, 3).astype(jnp.float32)
     averaged = (summed * 0.5).astype(jnp.bfloat16)
     freqs, _, block_rows, col_width = averaged.shape
-    rows = stream_gather(averaged, "z_hi", True)
+    rows = z_hi_swap(averaged)
     rows = lax.all_gather(rows, "x", axis=1)
     rows = lax.all_gather(rows, "core", axis=2)
     y_n = lax.axis_size("y")

time: 263 us -> 265 us (level)
  starting transfers between devices: 72.6 us -> 79 us
  local copies, waits for them, and re-layouts: 32.5 us -> 28.8 us
    ppermute x0 -> x4, starting transfers between devices: none -> 28.6 us  [the longest x2 24.7 us: z_hi_swap(): one = lax.ppermute(one, z_axes, ahead)]
    ppermute x4 -> x3, starting transfers between devices: 30 us -> 7.89 us  [stream_gather(): up = lax.ppermute(up, axis, perm(k, 1))]
    ppermute x0 -> x4, waiting for transfers between devices: none -> 10.9 us  [the longest x2 7.93 us: z_hi_swap(): other = lax.ppermute(other, z_axes, behind)]
    all_gather x1, waiting for transfers between devices: 27.6 us -> 19.4 us  [per_device(): rows = lax.all_gather(rows, 'x', axis=1)]
    ppermute x4 -> x3, waiting for transfers between devices: 9.63 us -> 2.56 us  [stream_gather(): up = lax.ppermute(up, axis, perm(k, 1))]
    ppermute x3, waiting for transfers between devices: 8.97 us -> 12.3 us  [stream_gather(): dn = lax.ppermute(dn, axis, perm(k, -1))]
    all_gather x1 -> x0, local copies, waits for them, and re-layouts: 3.16 us -> none  [per_device(): rows = lax.all_gather(rows, 'x', axis=1)]
  transfers between devices with their start and end apart: 20 -> 23, of which waited for: 12 -> 15; matrix products, arithmetic and copies ran while one was open for 16% -> 15% of each run, Pallas kernels for 0% -> 0%
where the time goes in v9:
time: 265 us; the launch traced here: 263 us
  waiting for transfers between devices  103 us (39%)
  starting transfers between devices  79 us (30%)
  matrix products  35.6 us (13%)
  local copies, waits for them, and re-layouts  28.8 us (11%)
  between operations  14.3 us (5%)
    ppermute x3, waiting for transfers between devices, ring_blocks(): dn = lax.ppermute(dn, axis, left)  50.7 us
    ppermute x2, starting transfers between devices, z_hi_swap(): one = lax.ppermute(one, z_axes, ahead)  24.7 us
    ppermute x4, starting transfers between devices, ring_blocks(): up = lax.ppermute(up, axis, right)  19.9 us
    all_gather x1, waiting for transfers between devices, per_device(): rows = lax.all_gather(rows, 'x', axis=1)  19.4 us
    ppermute x3, waiting for transfers between devices, stream_gather(): dn = lax.ppermute(dn, axis, perm(k, -1))  12.3 us
    dynamic_slice x9, local copies, waits for them, and re-layouts, per_device(): lax.dynamic_index_in_dim(row_panel, (me_y - offset) % y_n, axis=4, keepdi...  11.6 us
    ppermute x4, starting transfers between devices, mirrored_pieces(): got.append(lax.ppermute(part, SHOT + RECV, perm))  11.4 us
    dot_general x8, matrix products, complex_product(): jnp.einsum(form, left_block[:, 0], right_block[:, 0], preferred_element_t...  10.2 us
  transfers between devices with their start and end apart: 23, of which 15 were waited for; matrix products, arithmetic and copies ran while one was open for 15% of the time, Pallas kernels for 0%

profile of v9, /device:TPU:56, one launch (start us, length us, event | category | flops | bytes accessed | tf_op | source)
XLA Modules:
  0.0 263.2 jit_solution(9646010504706002373)
XLA Ops:
  7.6 3.1 %collective-permute-start.3 = (bf16[2,2,128,128]{3,2,1,0:T(8,128)(2,1)S(1)}, bf16[2,2,128,128]{3,2,1,0:T(8,128)(2,1)S(1)}, u32[]{:S(2)}, u32[]{:S(2)}) collective-permute-start(bf16[2,2,128,128]{3,2,1,0:T(8,128)(2,1)S(1)} %get-tuple-element.23), channel_id=1, source_target_pairs={{16,16},{17,48},{18,80},{19,112},{20,144},{21,176},{22,208},{23,24... | collective-permute-start | bytes 393224 | tf_op jit(solution)/shard_map/ppermute | solution.py:117
  11.9 6.4 %collective-permute-start.2 = (bf16[2,2,128,128]{3,2,1,0:T(8,128)(2,1)S(1)}, bf16[2,2,128,128]{3,2,1,0:T(8,128)(2,1)S(1)}, u32[]{:S(2)}, u32[]{:S(2)}) collective-permute-start(bf16[2,2,128,128]{3,2,1,0:T(8,128)(2,1)S(1)} %get-tuple-element.24), channel_id=1, source_target_pairs={{16,0},{17,32},{18,64},{19,96},{20,128},{21,160},{22,192},{23,224}... | collective-permute-start | bytes 393224 | tf_op jit(solution)/shard_map/ppermute | solution.py:117
  20.1 4.2 %collective-permute-done.1 = bf16[2,2,128,128]{3,2,1,0:T(8,128)(2,1)S(1)} collective-permute-done((bf16[2,2,128,128]{3,2,1,0:T(8,128)(2,1)S(1)}, bf16[2,2,128,128]{3,2,1,0:T(8,128)(2,1)S(1)}, u32[]{:S(2)}, u32[]{:S(2)}) %collective-permute-start.1) | collective-permute-done | bytes 131104 | tf_op jit(solution)/shard_map/ppermute | solution.py:117
  25.5 12.0 %collective-permute-start.16 = (bf16[1,2,128,256]{3,2,1,0:T(8,128)(2,1)S(1)}, bf16[1,2,128,256]{3,2,1,0:T(8,128)(2,1)S(1)}, u32[]{:S(2)}, u32[]{:S(2)}) collective-permute-start(bf16[1,2,128,256]{3,2,1,0:T(8,128)(2,1)S(1)} %get-tuple-element.22), channel_id=1, source_target_pairs={{0,256},{128,384},{256,8},{384,136},{8,264},{136,392},{264,0},{392... | collective-permute-start | bytes 393224 | tf_op jit(solution)/shard_map/ppermute | solution.py:96
  41.4 12.7 %collective-permute-start.17 = (bf16[1,2,128,256]{3,2,1,0:T(8,128)(2,1)S(1)}, bf16[1,2,128,256]{3,2,1,0:T(8,128)(2,1)S(1)}, u32[]{:S(2)}, u32[]{:S(2)}) collective-permute-start(bf16[1,2,128,256]{3,2,1,0:T(8,128)(2,1)S(1)} %collective-permute-done.16), channel_id=1, source_target_pairs={{0,256},{128,384},{256,8},{384,136},{8,264},{136,392},{264,0},{392... | collective-permute-start | bytes 393224 | tf_op jit(solution)/shard_map/ppermute | solution.py:96
  58.4 6.6 %collective-permute-done.19 = bf16[1,2,128,256]{3,2,1,0:T(8,128)(2,1)S(1)} collective-permute-done((bf16[1,2,128,256]{3,2,1,0:T(8,128)(2,1)S(1)}, bf16[1,2,128,256]{3,2,1,0:T(8,128)(2,1)S(1)}, u32[]{:S(2)}, u32[]{:S(2)}) %collective-permute-start.19) | collective-permute-done | bytes 131104 | tf_op jit(solution)/shard_map/ppermute | solution.py:97
  66.0 6.5 %collective-permute-start.4 = (bf16[2,2,128,256]{3,2,1,0:T(8,128)(2,1)S(1)}, bf16[2,2,128,256]{3,2,1,0:T(8,128)(2,1)S(1)}, u32[]{:S(2)}, u32[]{:S(2)}) collective-permute-start(bf16[2,2,128,256]{3,2,1,0:T(8,128)(2,1)S(1)} %get-tuple-element.10), channel_id=1, source_target_pairs={{0,128},{128,256},{256,384},{1,129},{129,257},{257,385},{2,130},{1... | collective-permute-start | bytes 786440 | tf_op jit(solution)/shard_map/ppermute | solution.py:49
  73.9 2.6 collective-permute-done.4
  77.1 4.7 %collective-permute-done.7 = bf16[2,2,128,256]{3,2,1,0:T(8,128)(2,1)S(1)} collective-permute-done((bf16[2,2,128,256]{3,2,1,0:T(8,128)(2,1)S(1)}, bf16[2,2,128,256]{3,2,1,0:T(8,128)(2,1)S(1)}, u32[]{:S(2)}, u32[]{:S(2)}) %collective-permute-start.7) | collective-permute-done | bytes 262176 | tf_op jit(solution)/shard_map/ppermute | solution.py:52
  84.5 7.7 %collective-permute-done.8 = bf16[2,2,128,256]{3,2,1,0:T(8,128)(2,1)S(1)} collective-permute-done((bf16[2,2,128,256]{3,2,1,0:T(8,128)(2,1)S(1)}, bf16[2,2,128,256]{3,2,1,0:T(8,128)(2,1)S(1)}, u32[]{:S(2)}, u32[]{:S(2)}) %collective-permute-start.8) | collective-permute-done | bytes 262176 | tf_op jit(solution)/shard_map/ppermute | solution.py:52
  94.2 19.4 %all-gather.5.cloned.1.call-done = bf16[2,8,2,128,256]{4,3,2,1,0:T(8,128)(2,1)} async-done(((bf16[2,2,2,128,256]{4,3,2,1,0:T(8,128)(2,1)}), bf16[2,8,2,128,256]{4,3,2,1,0:T(8,128)(2,1)}) %all-gather.5.cloned.1.call-update) | async-done | bytes 2097168 | tf_op jit(solution)/shard_map/all_gather | solution.py:130
  116.6 2.1 gather_fusion
  118.9 3.3 %collective-permute-start.13 = (bf16[2,2,4,128,256]{4,3,2,0,1:T(8,128)(2,1)S(1)}, bf16[2,2,4,128,256]{4,3,2,0,1:T(8,128)(2,1)S(1)}, u32[]{:S(2)}, u32[]{:S(2)}) collective-permute-start(bf16[2,2,4,128,256]{4,3,2,0,1:T(8,128)(2,1)S(1)} %fusion.32), channel_id=1, source_target_pairs={{16,0},{32,16},{48,32},{64,48},{80,64},{96,80},{112,96},{0,112},{1... | collective-permute-start | bytes 3145736 | tf_op jit(solution)/shard_map/ppermute | solution.py:75
  122.2 3.7 %collective-permute-start.10 = (bf16[2,2,4,128,256]{4,3,2,0,1:T(8,128)(2,1)S(1)}, bf16[2,2,4,128,256]{4,3,2,0,1:T(8,128)(2,1)S(1)}, u32[]{:S(2)}, u32[]{:S(2)}) collective-permute-start(bf16[2,2,4,128,256]{4,3,2,0,1:T(8,128)(2,1)S(1)} %fusion.32), channel_id=1, source_target_pairs={{0,16},{16,32},{32,48},{48,64},{64,80},{80,96},{96,112},{112,0},{1... | collective-permute-start | bytes 3145736 | tf_op jit(solution)/shard_map/ppermute | solution.py:72
  125.9 20.8 %collective-permute-done.13 = bf16[2,2,4,128,256]{4,3,2,0,1:T(8,128)(2,1)S(1)} collective-permute-done((bf16[2,2,4,128,256]{4,3,2,0,1:T(8,128)(2,1)S(1)}, bf16[2,2,4,128,256]{4,3,2,0,1:T(8,128)(2,1)S(1)}, u32[]{:S(2)}, u32[]{:S(2)}) %collective-permute-start.13) | collective-permute-done | bytes 1048608 | tf_op jit(solution)/shard_map/ppermute | solution.py:75
  146.7 2.1 collective-permute-start.14
  149.8 4.9 %collective-permute-start.11 = (bf16[2,2,4,128,256]{4,3,2,0,1:T(8,128)(2,1)S(1)}, bf16[2,2,4,128,256]{4,3,2,0,1:T(8,128)(2,1)S(1)}, u32[]{:S(2)}, u32[]{:S(2)}) collective-permute-start(bf16[2,2,4,128,256]{4,3,2,0,1:T(8,128)(2,1)S(1)} %collective-permute-done.10), channel_id=1, source_target_pairs={{0,16},{16,32},{32,48},{48,64},{64,80},{80,96},{96,112},{112,0},{1... | collective-permute-start | bytes 3145736 | tf_op jit(solution)/shard_map/ppermute | solution.py:72
  154.7 18.9 %collective-permute-done.14 = bf16[2,2,4,128,256]{4,3,2,0,1:T(8,128)(2,1)S(1)} collective-permute-done((bf16[2,2,4,128,256]{4,3,2,0,1:T(8,128)(2,1)S(1)}, bf16[2,2,4,128,256]{4,3,2,0,1:T(8,128)(2,1)S(1)}, u32[]{:S(2)}, u32[]{:S(2)}) %collective-permute-start.14) | collective-permute-done | bytes 1048608 | tf_op jit(solution)/shard_map/ppermute | solution.py:75
  175.8 5.6 %collective-permute-start.12 = (bf16[2,2,4,128,256]{4,3,2,0,1:T(8,128)(2,1)S(1)}, bf16[2,2,4,128,256]{4,3,2,0,1:T(8,128)(2,1)}, u32[]{:S(2)}, u32[]{:S(2)}) collective-permute-start(bf16[2,2,4,128,256]{4,3,2,0,1:T(8,128)(2,1)S(1)} %collective-permute-done.11), channel_id=1, source_target_pairs={{0,16},{16,32},{32,48},{48,64},{64,80},{80,96},{96,112},{112,0},{1... | collective-permute-start | bytes 3145736 | tf_op jit(solution)/shard_map/ppermute | solution.py:72
  181.6 7.3 %copy.20 = bf16[2,2,128,2,4,2,256]{2,6,5,4,3,1,0:T(8,128)(2,1)} copy(bf16[2,2,128,2,4,2,256]{6,2,1,0,5,4,3:T(8,128)(2,1)} %bitcast.369) | data formatting | bytes 8388608 | tf_op jit(solution)/shard_map/transpose | solution.py:134
  188.9 11.0 %collective-permute-done.15 = bf16[2,2,4,128,256]{4,3,2,0,1:T(8,128)(2,1)} collective-permute-done((bf16[2,2,4,128,256]{4,3,2,0,1:T(8,128)(2,1)S(1)}, bf16[2,2,4,128,256]{4,3,2,0,1:T(8,128)(2,1)}, u32[]{:S(2)}, u32[]{:S(2)}) %collective-permute-start.15) | collective-permute-done | bytes 1048608 | tf_op jit(solution)/shard_map/ppermute | solution.py:75
  201.7 3.7 %constant_dynamic-slice_fusion = (bf16[2,2,128,4,1,128]{2,5,4,3,1,0:T(8,128)(2,1)}, bf16[2,2,128,4,1,128]{2,5,4,3,1,0:T(8,128)(2,1)}, bf16[2,2,128,4,1,128]{2,5,...) fusion(bf16[2,2,128,4,8,128]{2,5,4,3,1,0:T(8,128)(2,1)} %bitcas, ...), kind=kLoop, calls=%fused_computation.129 | loop fusion | bytes 8388640 | tf_op jit(solution)/shard_map/jit(dynamic_index_in_dim)/dynamic_slice | solution.py:140
  218.3 5.7 %collective-permute-start.20 = (bf16[2,2,4,128,256]{4,3,2,0,1:T(8,128)(2,1)}, bf16[2,2,4,128,256]{4,3,2,0,1:T(8,128)(2,1)}, u32[]{:S(2)}, u32[]{:S(2)}) collective-permute-start(bf16[2,2,4,128,256]{4,3,2,0,1:T(8,128)(2,1)} %collective-permute-done.12), channel_id=1, source_target_pairs={{0,16},{16,32},{32,48},{48,64},{64,80},{80,96},{96,112},{112,0},{1... | collective-permute-start | bytes 3145736 | tf_op jit(solution)/shard_map/ppermute | solution.py:72
  239.6 2.1 fusion.21
  (143 shorter events, 71.7 us)
Async XLA Ops:
  6.5 107.0 %all-gather.5.cloned.1.call-start = ((), (), s32[]{:S(2)}) async-start(), calls=%async_computation | async-start | bytes 2621440 | tf_op jit(solution)/shard_map/all_gather | solution.py:130
  7.6 12.5 %collective-permute-start.3 = (bf16[2,2,128,128]{3,2,1,0:T(8,128)(2,1)S(1)}, bf16[2,2,128,128]{3,2,1,0:T(8,128)(2,1)S(1)}, u32[]{:S(2)}, u32[]{:S(2)}) collective-permute-start(bf16[2,2,128,128]{3,2,1,0:T(8,128)(2,1)S(1)} %get-tuple-element.23), channel_id=1, source_target_pairs={{16,16},{17,48},{18,80},{19,112},{20,144},{21,176},{22,208},{23,24... | collective-permute-start | bytes 393224 | tf_op jit(solution)/shard_map/ppermute | solution.py:117
  10.6 13.6 %collective-permute-start.1 = (bf16[2,2,128,128]{3,2,1,0:T(8,128)(2,1)S(1)}, bf16[2,2,128,128]{3,2,1,0:T(8,128)(2,1)S(1)}, u32[]{:S(2)}, u32[]{:S(2)}) collective-permute-start(bf16[2,2,128,128]{3,2,1,0:T(8,128)(2,1)S(1)} %get-tuple-element.23), channel_id=1, source_target_pairs={{0,16},{1,48},{2,80},{3,112},{4,144},{5,176},{6,208},{7,240},{8,27... | collective-permute-start | bytes 393224 | tf_op jit(solution)/shard_map/ppermute | solution.py:117
  11.9 12.3 %collective-permute-start.2 = (bf16[2,2,128,128]{3,2,1,0:T(8,128)(2,1)S(1)}, bf16[2,2,128,128]{3,2,1,0:T(8,128)(2,1)S(1)}, u32[]{:S(2)}, u32[]{:S(2)}) collective-permute-start(bf16[2,2,128,128]{3,2,1,0:T(8,128)(2,1)S(1)} %get-tuple-element.24), channel_id=1, source_target_pairs={{16,0},{17,32},{18,64},{19,96},{20,128},{21,160},{22,192},{23,224}... | collective-permute-start | bytes 393224 | tf_op jit(solution)/shard_map/ppermute | solution.py:117
  18.3 6.0 %collective-permute-start = (bf16[2,2,128,128]{3,2,1,0:T(8,128)(2,1)S(1)}, bf16[2,2,128,128]{3,2,1,0:T(8,128)(2,1)S(1)}, u32[]{:S(2)}, u32[]{:S(2)}) collective-permute-start(bf16[2,2,128,128]{3,2,1,0:T(8,128)(2,1)S(1)} %get-tuple-element.24), channel_id=1, source_target_pairs={{0,0},{1,32},{2,64},{3,96},{4,128},{5,160},{6,192},{7,224},{8,256}... | collective-permute-start | bytes 393224 | tf_op jit(solution)/shard_map/ppermute | solution.py:117
  25.5 15.9 %collective-permute-start.16 = (bf16[1,2,128,256]{3,2,1,0:T(8,128)(2,1)S(1)}, bf16[1,2,128,256]{3,2,1,0:T(8,128)(2,1)S(1)}, u32[]{:S(2)}, u32[]{:S(2)}) collective-permute-start(bf16[1,2,128,256]{3,2,1,0:T(8,128)(2,1)S(1)} %get-tuple-element.22), channel_id=1, source_target_pairs={{0,256},{128,384},{256,8},{384,136},{8,264},{136,392},{264,0},{392... | collective-permute-start | bytes 393224 | tf_op jit(solution)/shard_map/ppermute | solution.py:96
  37.5 17.8 %collective-permute-start.18 = (bf16[1,2,128,256]{3,2,1,0:T(8,128)(2,1)S(1)}, bf16[1,2,128,256]{3,2,1,0:T(8,128)(2,1)S(1)}, u32[]{:S(2)}, u32[]{:S(2)}) collective-permute-start(bf16[1,2,128,256]{3,2,1,0:T(8,128)(2,1)S(1)} %get-tuple-element.21), channel_id=1, source_target_pairs={{0,264},{128,392},{256,0},{384,128},{8,256},{136,384},{264,8},{392... | collective-permute-start | bytes 393224 | tf_op jit(solution)/shard_map/ppermute | solution.py:97
  41.4 17.0 %collective-permute-start.17 = (bf16[1,2,128,256]{3,2,1,0:T(8,128)(2,1)S(1)}, bf16[1,2,128,256]{3,2,1,0:T(8,128)(2,1)S(1)}, u32[]{:S(2)}, u32[]{:S(2)}) collective-permute-start(bf16[1,2,128,256]{3,2,1,0:T(8,128)(2,1)S(1)} %collective-permute-done.16), channel_id=1, source_target_pairs={{0,256},{128,384},{256,8},{384,136},{8,264},{136,392},{264,0},{392... | collective-permute-start | bytes 393224 | tf_op jit(solution)/shard_map/ppermute | solution.py:96
  55.4 9.6 %collective-permute-start.19 = (bf16[1,2,128,256]{3,2,1,0:T(8,128)(2,1)S(1)}, bf16[1,2,128,256]{3,2,1,0:T(8,128)(2,1)S(1)}, u32[]{:S(2)}, u32[]{:S(2)}) collective-permute-start(bf16[1,2,128,256]{3,2,1,0:T(8,128)(2,1)S(1)} %collective-permute-done.18), channel_id=1, source_target_pairs={{0,264},{128,392},{256,0},{384,128},{8,256},{136,384},{264,8},{392... | collective-permute-start | bytes 393224 | tf_op jit(solution)/shard_map/ppermute | solution.py:97
  66.0 115.6 %all-gather.7.cloned.1.call-start = ((), (), s32[]{:S(2)}) async-start(), calls=%async_computation.1 | async-start | bytes 6291456 | tf_op jit(solution)/shard_map/all_gather | solution.py:131
  66.0 10.4 %collective-permute-start.4 = (bf16[2,2,128,256]{3,2,1,0:T(8,128)(2,1)S(1)}, bf16[2,2,128,256]{3,2,1,0:T(8,128)(2,1)S(1)}, u32[]{:S(2)}, u32[]{:S(2)}) collective-permute-start(bf16[2,2,128,256]{3,2,1,0:T(8,128)(2,1)S(1)} %get-tuple-element.10), channel_id=1, source_target_pairs={{0,128},{128,256},{256,384},{1,129},{129,257},{257,385},{2,130},{1... | collective-permute-start | bytes 786440 | tf_op jit(solution)/shard_map/ppermute | solution.py:49
  72.6 9.2 %collective-permute-start.7 = (bf16[2,2,128,256]{3,2,1,0:T(8,128)(2,1)S(1)}, bf16[2,2,128,256]{3,2,1,0:T(8,128)(2,1)S(1)}, u32[]{:S(2)}, u32[]{:S(2)}) collective-permute-start(bf16[2,2,128,256]{3,2,1,0:T(8,128)(2,1)S(1)} %get-tuple-element.10), channel_id=1, source_target_pairs={{128,0},{256,128},{384,256},{129,1},{257,129},{385,257},{130,2},{2... | collective-permute-start | bytes 786440 | tf_op jit(solution)/shard_map/ppermute | solution.py:52
  76.4 6.7 %collective-permute-start.5 = (bf16[2,2,128,256]{3,2,1,0:T(8,128)(2,1)S(1)}, bf16[2,2,128,256]{3,2,1,0:T(8,128)(2,1)S(1)}, u32[]{:S(2)}, u32[]{:S(2)}) collective-permute-start(bf16[2,2,128,256]{3,2,1,0:T(8,128)(2,1)S(1)} %collective-permute-done.4), channel_id=1, source_target_pairs={{128,256},{256,384},{129,257},{257,385},{130,258},{258,386},{131,2... | collective-permute-start | bytes 786440 | tf_op jit(solution)/shard_map/ppermute | solution.py:49
  81.8 10.4 %collective-permute-start.8 = (bf16[2,2,128,256]{3,2,1,0:T(8,128)(2,1)S(1)}, bf16[2,2,128,256]{3,2,1,0:T(8,128)(2,1)S(1)}, u32[]{:S(2)}, u32[]{:S(2)}) collective-permute-start(bf16[2,2,128,256]{3,2,1,0:T(8,128)(2,1)S(1)} %collective-permute-done.7), channel_id=1, source_target_pairs={{128,0},{256,128},{129,1},{257,129},{130,2},{258,130},{131,3},{259... | collective-permute-start | bytes 786440 | tf_op jit(solution)/shard_map/ppermute | solution.py:52
  83.1 30.5 %collective-permute-start.6 = (bf16[2,2,128,256]{3,2,1,0:T(8,128)(2,1)S(1)}, bf16[2,2,128,256]{3,2,1,0:T(8,128)(2,1)S(1)}, u32[]{:S(2)}, u32[]{:S(2)}) collective-permute-start(bf16[2,2,128,256]{3,2,1,0:T(8,128)(2,1)S(1)} %collective-permute-done.5), channel_id=1, source_target_pairs={{256,384},{257,385},{258,386},{259,387},{260,388},{261,389},{262,3... | collective-permute-start | bytes 786440 | tf_op jit(solution)/shard_map/ppermute | solution.py:49
  92.2 23.7 %collective-permute-start.9 = (bf16[2,2,128,256]{3,2,1,0:T(8,128)(2,1)S(1)}, bf16[2,2,128,256]{3,2,1,0:T(8,128)(2,1)S(1)}, u32[]{:S(2)}, u32[]{:S(2)}) collective-permute-start(bf16[2,2,128,256]{3,2,1,0:T(8,128)(2,1)S(1)} %collective-permute-done.8), channel_id=1, source_target_pairs={{128,0},{129,1},{130,2},{131,3},{132,4},{133,5},{134,6},{135,7},{1... | collective-permute-start | bytes 786440 | tf_op jit(solution)/shard_map/ppermute | solution.py:52
  118.9 27.8 %collective-permute-start.13 = (bf16[2,2,4,128,256]{4,3,2,0,1:T(8,128)(2,1)S(1)}, bf16[2,2,4,128,256]{4,3,2,0,1:T(8,128)(2,1)S(1)}, u32[]{:S(2)}, u32[]{:S(2)}) collective-permute-start(bf16[2,2,4,128,256]{4,3,2,0,1:T(8,128)(2,1)S(1)} %fusion.32), channel_id=1, source_target_pairs={{16,0},{32,16},{48,32},{64,48},{80,64},{96,80},{112,96},{0,112},{1... | collective-permute-start | bytes 3145736 | tf_op jit(solution)/shard_map/ppermute | solution.py:75
  122.2 26.6 %collective-permute-start.10 = (bf16[2,2,4,128,256]{4,3,2,0,1:T(8,128)(2,1)S(1)}, bf16[2,2,4,128,256]{4,3,2,0,1:T(8,128)(2,1)S(1)}, u32[]{:S(2)}, u32[]{:S(2)}) collective-permute-start(bf16[2,2,4,128,256]{4,3,2,0,1:T(8,128)(2,1)S(1)} %fusion.32), channel_id=1, source_target_pairs={{0,16},{16,32},{32,48},{48,64},{64,80},{80,96},{96,112},{112,0},{1... | collective-permute-start | bytes 3145736 | tf_op jit(solution)/shard_map/ppermute | solution.py:72
  146.7 29.1 %copy-start.14 = (bf16[2,2,4,128,256]{4,3,2,0,1:T(8,128)(2,1)}, bf16[2,2,4,128,256]{4,3,2,0,1:T(8,128)(2,1)S(1)}, u32[]{:S(2)}) copy-start(bf16[2,2,4,128,256]{4,3,2,0,1:T(8,128)(2,1)S(1)} %collective-permute-done.13) | copy-start | bytes 3145732
  146.7 27.0 %collective-permute-start.14 = (bf16[2,2,4,128,256]{4,3,2,0,1:T(8,128)(2,1)S(1)}, bf16[2,2,4,128,256]{4,3,2,0,1:T(8,128)(2,1)S(1)}, u32[]{:S(2)}, u32[]{:S(2)}) collective-permute-start(bf16[2,2,4,128,256]{4,3,2,0,1:T(8,128)(2,1)S(1)} %collective-permute-done.13), channel_id=1, source_target_pairs={{16,0},{32,16},{48,32},{64,48},{80,64},{96,80},{112,96},{0,112},{1... | collective-permute-start | bytes 3145736 | tf_op jit(solution)/shard_map/ppermute | solution.py:75
  149.8 26.0 %collective-permute-start.11 = (bf16[2,2,4,128,256]{4,3,2,0,1:T(8,128)(2,1)S(1)}, bf16[2,2,4,128,256]{4,3,2,0,1:T(8,128)(2,1)S(1)}, u32[]{:S(2)}, u32[]{:S(2)}) collective-permute-start(bf16[2,2,4,128,256]{4,3,2,0,1:T(8,128)(2,1)S(1)} %collective-permute-done.10), channel_id=1, source_target_pairs={{0,16},{16,32},{32,48},{48,64},{64,80},{80,96},{96,112},{112,0},{1... | collective-permute-start | bytes 3145736 | tf_op jit(solution)/shard_map/ppermute | solution.py:72
  173.7 26.2 %collective-permute-start.15 = (bf16[2,2,4,128,256]{4,3,2,0,1:T(8,128)(2,1)S(1)}, bf16[2,2,4,128,256]{4,3,2,0,1:T(8,128)(2,1)}, u32[]{:S(2)}, u32[]{:S(2)}) collective-permute-start(bf16[2,2,4,128,256]{4,3,2,0,1:T(8,128)(2,1)S(1)} %collective-permute-done.14), channel_id=1, source_target_pairs={{16,0},{32,16},{48,32},{64,48},{80,64},{96,80},{112,96},{0,112},{1... | collective-permute-start | bytes 3145736 | tf_op jit(solution)/shard_map/ppermute | solution.py:75
  175.8 25.8 %collective-permute-start.12 = (bf16[2,2,4,128,256]{4,3,2,0,1:T(8,128)(2,1)S(1)}, bf16[2,2,4,128,256]{4,3,2,0,1:T(8,128)(2,1)}, u32[]{:S(2)}, u32[]{:S(2)}) collective-permute-start(bf16[2,2,4,128,256]{4,3,2,0,1:T(8,128)(2,1)S(1)} %collective-permute-done.11), channel_id=1, source_target_pairs={{0,16},{16,32},{32,48},{48,64},{64,80},{80,96},{96,112},{112,0},{1... | collective-permute-start | bytes 3145736 | tf_op jit(solution)/shard_map/ppermute | solution.py:72
  218.3 31.6 %collective-permute-start.20 = (bf16[2,2,4,128,256]{4,3,2,0,1:T(8,128)(2,1)}, bf16[2,2,4,128,256]{4,3,2,0,1:T(8,128)(2,1)}, u32[]{:S(2)}, u32[]{:S(2)}) collective-permute-start(bf16[2,2,4,128,256]{4,3,2,0,1:T(8,128)(2,1)} %collective-permute-done.12), channel_id=1, source_target_pairs={{0,16},{16,32},{32,48},{48,64},{64,80},{80,96},{96,112},{112,0},{1... | collective-permute-start | bytes 3145736 | tf_op jit(solution)/shard_map/ppermute | solution.py:72
  (26 other events, 131.1 us)
Sparse Core Ops, SparseCore 0:
  66.1 47.4 all-gather.4
  115.7 21.8 all-gather.6

commit v10 on v9

--- a/solution.py
+++ b/solution.py
@@ -133,13 +133,21 @@
     z_n = lax.axis_size("z_lo")
     row_panel = jnp.transpose(rows, (3, 4, 5, 0, 1, 2, 6)).reshape(freqs, 2, block_rows, z_n, y_n, block_rows)
     me_y = lax.axis_index("y")
-    z_cols = jnp.moveaxis(stream_gather(averaged, "z_lo", False), 0, 2)
-    blocks, row_panel = ring_blocks(z_cols, "y", row_panel)
+    z_first = jnp.moveaxis(stream_gather(averaged[:1], "z_lo", False), 0, 2)
+    blocks, row_panel = ring_blocks(z_first, "y", row_panel)
     product = None
     for offset, col_block in blocks:
-        row_block = lax.dynamic_index_in_dim(row_panel, (me_y - offset) % y_n, axis=4, keepdims=False)
+        row_block = lax.dynamic_index_in_dim(row_panel[:1], (me_y - offset) % y_n, axis=4, keepdims=False)
         part = complex_product(row_block, col_block, "fizk,fzkj->fij")
         product = part if product is None else product + part
+    y_blocks, _ = ring_blocks(averaged[1:], "y", averaged[1:])
+    y_first = stream_gather(jnp.stack([block for _, block in y_blocks], axis=0), "z_lo", False)
+    late = None
+    for t, (offset, _) in enumerate(y_blocks):
+        row_block = lax.dynamic_index_in_dim(row_panel[1:], (me_y - offset) % y_n, axis=4, keepdims=False)
+        part = complex_product(row_block, jnp.moveaxis(y_first[:, t], 0, 2), "fizk,fzkj->fij")
+        late = part if late is None else late + part
+    product = jnp.concatenate((product, late), axis=0)
     scale_factor = jnp.float32(float(NS) ** (-0.5))
     return product * scale_factor
 

time: 265 us -> 362 us (1.37)
  matrix products: 35.6 us -> 84 us
  starting transfers between devices: 79 us -> 114 us
  local copies, waits for them, and re-layouts: 28.8 us -> 56.5 us
  waiting for transfers between devices: 103 us -> 83.6 us
  other arithmetic: 2.28 us -> 5.96 us
    ppermute x3 -> x6, waiting for transfers between devices: 50.7 us -> 5.6 us  [ring_blocks(): dn = lax.ppermute(dn, axis, left)]
    ppermute x3 -> x6, waiting for transfers between devices: 12.3 us -> 45.9 us  [stream_gather(): dn = lax.ppermute(dn, axis, perm(k, -1))]
    all_gather x1, waiting for transfers between devices: 19.4 us -> 0.01 us  [per_device(): rows = lax.all_gather(rows, 'x', axis=1)]
    dot_general x8 -> x16, matrix products: 7.86 us -> 22.4 us  [complex_product(): jnp.einsum(form, left_block[:, 1], right_block[:, 0], preferred_element_t...]
    dot_general x8 -> x16, matrix products: 8.1 us -> 21.8 us  [complex_product(): jnp.einsum(form, left_block[:, 1], right_block[:, 1], preferred_element_t...]
    ppermute x3 -> x6, starting transfers between devices: 7.89 us -> 19.8 us  [stream_gather(): up = lax.ppermute(up, axis, perm(k, 1))]
    dot_general x8 -> x16, matrix products: 9.39 us -> 20.1 us  [complex_product(): jnp.einsum(form, left_block[:, 0], right_block[:, 1], preferred_element_t...]
    dynamic_slice x9 -> x18, local copies, waits for them, and re-layouts: 11.6 us -> 21.6 us  [the longest x9 11.3 us: per_device(): lax.dynamic_index_in_dim(row_panel[:1], (me_y - offset) % y_n, axis=4, ke...]
  transfers between devices with their start and end apart: 23 -> 36, of which waited for: 15 -> 17; matrix products, arithmetic and copies ran while one was open for 15% -> 15% of each run, Pallas kernels for 0% -> 0%
where the time goes in v10:
time: 362 us; the launch traced here: 358 us
  starting transfers between devices  114 us (31%)
  matrix products  84 us (23%)
  waiting for transfers between devices  83.6 us (23%)
  local copies, waits for them, and re-layouts  56.5 us (16%)
  between operations  14.8 us (4%)
  other arithmetic  5.96 us (2%)
    ppermute x6, waiting for transfers between devices, stream_gather(): dn = lax.ppermute(dn, axis, perm(k, -1))  45.9 us
    ppermute x8, starting transfers between devices, ring_blocks(): up = lax.ppermute(up, axis, right)  29.3 us
    ppermute x2, starting transfers between devices, z_hi_swap(): one = lax.ppermute(one, z_axes, ahead)  26.2 us
    dot_general x16, matrix products, complex_product(): jnp.einsum(form, left_block[:, 1], right_block[:, 0], preferred_element_t...  22.4 us
    dot_general x16, matrix products, complex_product(): jnp.einsum(form, left_block[:, 1], right_block[:, 1], preferred_element_t...  21.8 us
    dot_general x16, matrix products, complex_product(): jnp.einsum(form, left_block[:, 0], right_block[:, 1], preferred_element_t...  20.1 us
    ppermute x6, starting transfers between devices, stream_gather(): up = lax.ppermute(up, axis, perm(k, 1))  19.8 us
    dot_general x16, matrix products, complex_product(): jnp.einsum(form, left_block[:, 0], right_block[:, 0], preferred_element_t...  19.8 us
  transfers between devices with their start and end apart: 36, of which 17 were waited for; matrix products, arithmetic and copies ran while one was open for 15% of the time, Pallas kernels for 0%

profile of v10, /device:TPU:56, one launch (start us, length us, event | category | flops | bytes accessed | tf_op | source)
XLA Modules:
  0.0 358.5 jit_solution(1911550412756352231)
XLA Ops:
  9.6 7.3 %collective-permute-start.3 = (bf16[2,2,128,128]{3,2,1,0:T(8,128)(2,1)S(1)}, bf16[2,2,128,128]{3,2,1,0:T(8,128)(2,1)S(1)}, u32[]{:S(2)}, u32[]{:S(2)}) collective-permute-start(bf16[2,2,128,128]{3,2,1,0:T(8,128)(2,1)S(1)} %get-tuple-element.41), channel_id=1, source_target_pairs={{16,16},{17,48},{18,80},{19,112},{20,144},{21,176},{22,208},{23,24... | collective-permute-start | bytes 393224 | tf_op jit(solution)/shard_map/ppermute | solution.py:117
  19.5 6.8 %collective-permute-done.1 = bf16[2,2,128,128]{3,2,1,0:T(8,128)(2,1)S(1)} collective-permute-done((bf16[2,2,128,128]{3,2,1,0:T(8,128)(2,1)S(1)}, bf16[2,2,128,128]{3,2,1,0:T(8,128)(2,1)S(1)}, u32[]{:S(2)}, u32[]{:S(2)}) %collective-permute-start.1) | collective-permute-done | bytes 131104 | tf_op jit(solution)/shard_map/ppermute | solution.py:117
  27.7 21.0 %collective-permute-start.16 = (bf16[1,2,128,256]{3,2,1,0:T(8,128)(2,1)S(1)}, bf16[1,2,128,256]{3,2,1,0:T(8,128)(2,1)S(1)}, u32[]{:S(2)}, u32[]{:S(2)}) collective-permute-start(bf16[1,2,128,256]{3,2,1,0:T(8,128)(2,1)S(1)} %get-tuple-element.39), channel_id=1, source_target_pairs={{0,256},{128,384},{256,8},{384,136},{8,264},{136,392},{264,0},{392... | collective-permute-start | bytes 393224 | tf_op jit(solution)/shard_map/ppermute | solution.py:96
  51.2 5.2 %collective-permute-start.17 = (bf16[1,2,128,256]{3,2,1,0:T(8,128)(2,1)S(1)}, bf16[1,2,128,256]{3,2,1,0:T(8,128)(2,1)S(1)}, u32[]{:S(2)}, u32[]{:S(2)}) collective-permute-start(bf16[1,2,128,256]{3,2,1,0:T(8,128)(2,1)S(1)} %collective-permute-done.16), channel_id=1, source_target_pairs={{0,256},{128,384},{256,8},{384,136},{8,264},{136,392},{264,0},{392... | collective-permute-start | bytes 393224 | tf_op jit(solution)/shard_map/ppermute | solution.py:96
  60.6 5.2 %collective-permute-done.19 = bf16[1,2,128,256]{3,2,1,0:T(8,128)(2,1)S(1)} collective-permute-done((bf16[1,2,128,256]{3,2,1,0:T(8,128)(2,1)S(1)}, bf16[1,2,128,256]{3,2,1,0:T(8,128)(2,1)S(1)}, u32[]{:S(2)}, u32[]{:S(2)}) %collective-permute-start.19) | collective-permute-done | bytes 131104 | tf_op jit(solution)/shard_map/ppermute | solution.py:97
  68.8 3.9 %collective-permute-start.22 = (bf16[1,2,128,256]{3,2,1,0:T(8,128)(2,1)S(1)}, bf16[1,2,128,256]{3,2,1,0:T(8,128)(2,1)S(1)}, u32[]{:S(2)}, u32[]{:S(2)}) collective-permute-start(bf16[1,2,128,256]{3,2,1,0:T(8,128)(2,1)S(1)} %get-tuple-element.40), channel_id=1, source_target_pairs={{16,0},{32,16},{48,32},{64,48},{80,64},{96,80},{112,96},{0,112},{1... | collective-permute-start | bytes 393224 | tf_op jit(solution)/shard_map/ppermute | solution.py:75
  72.7 9.6 %collective-permute-start.4 = (bf16[1,2,128,256]{3,2,1,0:T(8,128)(2,1)S(1)}, bf16[1,2,128,256]{3,2,1,0:T(8,128)(2,1)S(1)}, u32[]{:S(2)}, u32[]{:S(2)}) collective-permute-start(bf16[1,2,128,256]{3,2,1,0:T(8,128)(2,1)S(1)} %get-tuple-element.39), channel_id=1, source_target_pairs={{0,128},{128,256},{256,384},{1,129},{129,257},{257,385},{2,130},{1... | collective-permute-start | bytes 393224 | tf_op jit(solution)/shard_map/ppermute | solution.py:49
  83.7 3.1 collective-permute-start.23
  90.6 4.3 %collective-permute-start.25 = (bf16[1,2,128,256]{3,2,1,0:T(8,128)(2,1)S(1)}, bf16[1,2,128,256]{3,2,1,0:T(8,128)(2,1)S(1)}, u32[]{:S(2)}, u32[]{:S(2)}) collective-permute-start(bf16[1,2,128,256]{3,2,1,0:T(8,128)(2,1)S(1)} %collective-permute-done.23), channel_id=1, source_target_pairs={{0,16},{16,32},{32,48},{48,64},{64,80},{80,96},{96,112},{112,0},{1... | collective-permute-start | bytes 393224 | tf_op jit(solution)/shard_map/ppermute | solution.py:72
  97.4 5.6 %collective-permute-done.26 = bf16[1,2,128,256]{3,2,1,0:T(8,128)(2,1)S(1)} collective-permute-done((bf16[1,2,128,256]{3,2,1,0:T(8,128)(2,1)S(1)}, bf16[1,2,128,256]{3,2,1,0:T(8,128)(2,1)S(1)}, u32[]{:S(2)}, u32[]{:S(2)}) %collective-permute-start.26) | collective-permute-done | bytes 131104 | tf_op jit(solution)/shard_map/ppermute | solution.py:75
  104.9 4.9 %collective-permute-done.27 = bf16[1,2,128,256]{3,2,1,0:T(8,128)(2,1)S(1)} collective-permute-done((bf16[1,2,128,256]{3,2,1,0:T(8,128)(2,1)S(1)}, bf16[1,2,128,256]{3,2,1,0:T(8,128)(2,1)S(1)}, u32[]{:S(2)}, u32[]{:S(2)}) %collective-permute-start.27) | collective-permute-done | bytes 131104 | tf_op jit(solution)/shard_map/ppermute | solution.py:72
  109.8 5.5 %collective-permute-start.28 = (bf16[8,1,2,128,256]{4,3,2,0,1:T(8,128)(2,1)S(1)}, bf16[8,1,2,128,256]{4,3,2,0,1:T(8,128)(2,1)}, u32[]{:S(2)}, u32[]{:S(2)}) collective-permute-start(bf16[8,1,2,128,256]{4,3,2,0,1:T(8,128)(2,1)S(1)} %bitcast.781), channel_id=1, source_target_pairs={{0,128},{128,256},{256,384},{1,129},{129,257},{257,385},{2,130},{1... | collective-permute-start | bytes 3145736 | tf_op jit(solution)/shard_map/ppermute | solution.py:49
  118.1 6.9 %collective-permute-done.8 = bf16[1,2,128,256]{3,2,1,0:T(8,128)(2,1)S(1)} collective-permute-done((bf16[1,2,128,256]{3,2,1,0:T(8,128)(2,1)S(1)}, bf16[1,2,128,256]{3,2,1,0:T(8,128)(2,1)S(1)}, u32[]{:S(2)}, u32[]{:S(2)}) %collective-permute-start.8) | collective-permute-done | bytes 131104 | tf_op jit(solution)/shard_map/ppermute | solution.py:52
  127.7 5.9 %collective-permute-done.28 = bf16[8,1,2,128,256]{4,3,2,0,1:T(8,128)(2,1)} collective-permute-done((bf16[8,1,2,128,256]{4,3,2,0,1:T(8,128)(2,1)S(1)}, bf16[8,1,2,128,256]{4,3,2,0,1:T(8,128)(2,1)}, u32[]{:S(2)}, u32[]{:S(2)}) %collective-permute-start.28) | collective-permute-done | bytes 1048608 | tf_op jit(solution)/shard_map/ppermute | solution.py:49
  135.3 11.7 %collective-permute-done.9 = bf16[1,2,128,256]{3,2,1,0:T(8,128)(2,1)S(1)} collective-permute-done((bf16[1,2,128,256]{3,2,1,0:T(8,128)(2,1)S(1)}, bf16[1,2,128,256]{3,2,1,0:T(8,128)(2,1)S(1)}, u32[]{:S(2)}, u32[]{:S(2)}) %collective-permute-start.9) | collective-permute-done | bytes 131104 | tf_op jit(solution)/shard_map/ppermute | solution.py:52
  147.7 3.7 %collective-permute-start.10 = (bf16[1,2,4,128,256]{4,3,2,1,0:T(8,128)(2,1)S(1)}, bf16[1,2,4,128,256]{4,3,2,1,0:T(8,128)(2,1)S(1)}, u32[]{:S(2)}, u32[]{:S(2)}) collective-permute-start(bf16[1,2,4,128,256]{4,3,2,1,0:T(8,128)(2,1)S(1)} %fusion.64), channel_id=1, source_target_pairs={{0,16},{16,32},{32,48},{48,64},{64,80},{80,96},{96,112},{112,0},{1... | collective-permute-start | bytes 1572872 | tf_op jit(solution)/shard_map/ppermute | solution.py:72
  153.6 13.8 %collective-permute-done.31 = bf16[8,1,2,128,256]{4,3,2,1,0:T(8,128)(2,1)} collective-permute-done((bf16[8,1,2,128,256]{4,3,2,1,0:T(8,128)(2,1)S(1)}, bf16[8,1,2,128,256]{4,3,2,1,0:T(8,128)(2,1)}, u32[]{:S(2)}, u32[]{:S(2)}) %collective-permute-start.31) | collective-permute-done | bytes 1048608 | tf_op jit(solution)/shard_map/ppermute | solution.py:52
  168.6 4.0 %collective-permute-start.11 = (bf16[1,2,4,128,256]{4,3,2,1,0:T(8,128)(2,1)S(1)}, bf16[1,2,4,128,256]{4,3,2,1,0:T(8,128)(2,1)S(1)}, u32[]{:S(2)}, u32[]{:S(2)}) collective-permute-start(bf16[1,2,4,128,256]{4,3,2,1,0:T(8,128)(2,1)S(1)} %collective-permute-done.10), channel_id=1, source_target_pairs={{0,16},{16,32},{32,48},{48,64},{64,80},{80,96},{96,112},{112,0},{1... | collective-permute-start | bytes 1572872 | tf_op jit(solution)/shard_map/ppermute | solution.py:72
  177.3 5.0 %collective-permute-done.11 = bf16[1,2,4,128,256]{4,3,2,1,0:T(8,128)(2,1)S(1)} collective-permute-done((bf16[1,2,4,128,256]{4,3,2,1,0:T(8,128)(2,1)S(1)}, bf16[1,2,4,128,256]{4,3,2,1,0:T(8,128)(2,1)S(1)}, u32[]{:S(2)}, u32[]{:S(2)}) %collective-permute-start.11) | collective-permute-done | bytes 524320 | tf_op jit(solution)/shard_map/ppermute | solution.py:72
  182.3 5.4 %collective-permute-start.12 = (bf16[1,2,4,128,256]{4,3,2,1,0:T(8,128)(2,1)S(1)}, bf16[1,2,4,128,256]{4,3,2,1,0:T(8,128)(2,1)S(1)}, u32[]{:S(2)}, u32[]{:S(2)}) collective-permute-start(bf16[1,2,4,128,256]{4,3,2,1,0:T(8,128)(2,1)S(1)} %collective-permute-done.11), channel_id=1, source_target_pairs={{0,16},{16,32},{32,48},{48,64},{64,80},{80,96},{96,112},{112,0},{1... | collective-permute-start | bytes 1572872 | tf_op jit(solution)/shard_map/ppermute | solution.py:72
  203.2 13.0 %collective-permute-done.33 = bf16[8,1,2,128,256]{4,3,2,1,0:T(8,128)(2,1)S(1)} collective-permute-done((bf16[8,1,2,128,256]{4,3,2,1,0:T(8,128)(2,1)}, bf16[8,1,2,128,256]{4,3,2,1,0:T(8,128)(2,1)S(1)}, u32[]{:S(2)}, u32[]{:S(2)}) %collective-permute-start.33) | collective-permute-done | bytes 1048608 | tf_op jit(solution)/shard_map/ppermute | solution.py:52
  217.3 5.8 %gather_fusion.1 = bf16[4,8,2,128,256]{4,3,2,1,0:T(8,128)(2,1)} fusion(bf16[7,8,2,128,256]{4,3,2,1,0:T(8,128)(2,1)} %bitcast.136, s32[1024]{0:T(1024)S(1)} %pad_clamp_fusion), kind=kCustom, calls=%fused_computation.1 | custom fusion | bytes 8388624 | tf_op jit(solution)/shard_map/jit(_take)/gather | solution.py:62
  227.5 7.3 %copy.41 = bf16[2,2,128,2,4,2,256]{2,6,5,4,3,1,0:T(8,128)(2,1)} copy(bf16[2,2,128,2,4,2,256]{6,2,1,0,5,4,3:T(8,128)(2,1)} %bitcast.715) | data formatting | bytes 8388608 | tf_op jit(solution)/shard_map/transpose | solution.py:134
  318.4 4.9 %collective-permute-start.20 = (bf16[1,2,4,128,256]{4,3,2,1,0:T(8,128)(2,1)}, bf16[1,2,4,128,256]{4,3,2,1,0:T(8,128)(2,1)}, u32[]{:S(2)}, u32[]{:S(2)}) collective-permute-start(bf16[1,2,4,128,256]{4,3,2,1,0:T(8,128)(2,1)} %copy-done.20), channel_id=1, source_target_pairs={{0,16},{16,32},{32,48},{48,64},{64,80},{80,96},{96,112},{112,0},{1... | collective-permute-start | bytes 1572872 | tf_op jit(solution)/shard_map/ppermute | solution.py:72
  (259 shorter events, 173.8 us)
Async XLA Ops:
  6.5 128.7 %all-gather.5.cloned.1.call-start = ((), (), s32[]{:S(2)}) async-start(), calls=%async_computation | async-start | bytes 2621440 | tf_op jit(solution)/shard_map/all_gather | solution.py:130
  7.5 11.4 %collective-permute-start.2 = (bf16[2,2,128,128]{3,2,1,0:T(8,128)(2,1)S(1)}, bf16[2,2,128,128]{3,2,1,0:T(8,128)(2,1)S(1)}, u32[]{:S(2)}, u32[]{:S(2)}) collective-permute-start(bf16[2,2,128,128]{3,2,1,0:T(8,128)(2,1)S(1)} %get-tuple-element.42), channel_id=1, source_target_pairs={{16,0},{17,32},{18,64},{19,96},{20,128},{21,160},{22,192},{23,224}... | collective-permute-start | bytes 393224 | tf_op jit(solution)/shard_map/ppermute | solution.py:117
  9.6 10.0 %collective-permute-start.3 = (bf16[2,2,128,128]{3,2,1,0:T(8,128)(2,1)S(1)}, bf16[2,2,128,128]{3,2,1,0:T(8,128)(2,1)S(1)}, u32[]{:S(2)}, u32[]{:S(2)}) collective-permute-start(bf16[2,2,128,128]{3,2,1,0:T(8,128)(2,1)S(1)} %get-tuple-element.41), channel_id=1, source_target_pairs={{16,16},{17,48},{18,80},{19,112},{20,144},{21,176},{22,208},{23,24... | collective-permute-start | bytes 393224 | tf_op jit(solution)/shard_map/ppermute | solution.py:117
  27.7 23.5 %collective-permute-start.16 = (bf16[1,2,128,256]{3,2,1,0:T(8,128)(2,1)S(1)}, bf16[1,2,128,256]{3,2,1,0:T(8,128)(2,1)S(1)}, u32[]{:S(2)}, u32[]{:S(2)}) collective-permute-start(bf16[1,2,128,256]{3,2,1,0:T(8,128)(2,1)S(1)} %get-tuple-element.39), channel_id=1, source_target_pairs={{0,256},{128,384},{256,8},{384,136},{8,264},{136,392},{264,0},{392... | collective-permute-start | bytes 393224 | tf_op jit(solution)/shard_map/ppermute | solution.py:96
  51.2 9.4 %collective-permute-start.17 = (bf16[1,2,128,256]{3,2,1,0:T(8,128)(2,1)S(1)}, bf16[1,2,128,256]{3,2,1,0:T(8,128)(2,1)S(1)}, u32[]{:S(2)}, u32[]{:S(2)}) collective-permute-start(bf16[1,2,128,256]{3,2,1,0:T(8,128)(2,1)S(1)} %collective-permute-done.16), channel_id=1, source_target_pairs={{0,256},{128,384},{256,8},{384,136},{8,264},{136,392},{264,0},{392... | collective-permute-start | bytes 393224 | tf_op jit(solution)/shard_map/ppermute | solution.py:96
  66.8 160.7 %all-gather.7.cloned.1.call-start = ((), (), s32[]{:S(2)}) async-start(), calls=%async_computation.1 | async-start | bytes 6291456 | tf_op jit(solution)/shard_map/all_gather | solution.py:131
  66.9 16.8 %collective-permute-start.21 = (bf16[1,2,128,256]{3,2,1,0:T(8,128)(2,1)S(1)}, bf16[1,2,128,256]{3,2,1,0:T(8,128)(2,1)S(1)}, u32[]{:S(2)}, u32[]{:S(2)}) collective-permute-start(bf16[1,2,128,256]{3,2,1,0:T(8,128)(2,1)S(1)} %get-tuple-element.40), channel_id=1, source_target_pairs={{0,16},{16,32},{32,48},{48,64},{64,80},{80,96},{96,112},{112,0},{1... | collective-permute-start | bytes 393224 | tf_op jit(solution)/shard_map/ppermute | solution.py:72
  68.8 18.0 %collective-permute-start.22 = (bf16[1,2,128,256]{3,2,1,0:T(8,128)(2,1)S(1)}, bf16[1,2,128,256]{3,2,1,0:T(8,128)(2,1)S(1)}, u32[]{:S(2)}, u32[]{:S(2)}) collective-permute-start(bf16[1,2,128,256]{3,2,1,0:T(8,128)(2,1)S(1)} %get-tuple-element.40), channel_id=1, source_target_pairs={{16,0},{32,16},{48,32},{64,48},{80,64},{96,80},{112,96},{0,112},{1... | collective-permute-start | bytes 393224 | tf_op jit(solution)/shard_map/ppermute | solution.py:75
  72.7 42.7 %collective-permute-start.4 = (bf16[1,2,128,256]{3,2,1,0:T(8,128)(2,1)S(1)}, bf16[1,2,128,256]{3,2,1,0:T(8,128)(2,1)S(1)}, u32[]{:S(2)}, u32[]{:S(2)}) collective-permute-start(bf16[1,2,128,256]{3,2,1,0:T(8,128)(2,1)S(1)} %get-tuple-element.39), channel_id=1, source_target_pairs={{0,128},{128,256},{256,384},{1,129},{129,257},{257,385},{2,130},{1... | collective-permute-start | bytes 393224 | tf_op jit(solution)/shard_map/ppermute | solution.py:49
  82.4 33.7 %collective-permute-start.7 = (bf16[1,2,128,256]{3,2,1,0:T(8,128)(2,1)S(1)}, bf16[1,2,128,256]{3,2,1,0:T(8,128)(2,1)S(1)}, u32[]{:S(2)}, u32[]{:S(2)}) collective-permute-start(bf16[1,2,128,256]{3,2,1,0:T(8,128)(2,1)S(1)} %get-tuple-element.39), channel_id=1, source_target_pairs={{128,0},{256,128},{384,256},{129,1},{257,129},{385,257},{130,2},{2... | collective-permute-start | bytes 393224 | tf_op jit(solution)/shard_map/ppermute | solution.py:52
  109.8 23.8 %collective-permute-start.28 = (bf16[8,1,2,128,256]{4,3,2,0,1:T(8,128)(2,1)S(1)}, bf16[8,1,2,128,256]{4,3,2,0,1:T(8,128)(2,1)}, u32[]{:S(2)}, u32[]{:S(2)}) collective-permute-start(bf16[8,1,2,128,256]{4,3,2,0,1:T(8,128)(2,1)S(1)} %bitcast.781), channel_id=1, source_target_pairs={{0,128},{128,256},{256,384},{1,129},{129,257},{257,385},{2,130},{1... | collective-permute-start | bytes 3145736 | tf_op jit(solution)/shard_map/ppermute | solution.py:49
  125.0 21.9 %collective-permute-start.9 = (bf16[1,2,128,256]{3,2,1,0:T(8,128)(2,1)S(1)}, bf16[1,2,128,256]{3,2,1,0:T(8,128)(2,1)S(1)}, u32[]{:S(2)}, u32[]{:S(2)}) collective-permute-start(bf16[1,2,128,256]{3,2,1,0:T(8,128)(2,1)S(1)} %collective-permute-done.8), channel_id=1, source_target_pairs={{128,0},{129,1},{130,2},{131,3},{132,4},{133,5},{134,6},{135,7},{1... | collective-permute-start | bytes 393224 | tf_op jit(solution)/shard_map/ppermute | solution.py:52
  126.4 41.0 %collective-permute-start.31 = (bf16[8,1,2,128,256]{4,3,2,1,0:T(8,128)(2,1)S(1)}, bf16[8,1,2,128,256]{4,3,2,1,0:T(8,128)(2,1)}, u32[]{:S(2)}, u32[]{:S(2)}) collective-permute-start(bf16[8,1,2,128,256]{4,3,2,1,0:T(8,128)(2,1)S(1)} %bitcast_dynamic-update-slice_fusion.13), channel_id=1, source_target_pairs={{128,0},{256,128},{384,256},{129,1},{257,129},{385,257},{130,2},{2... | collective-permute-start | bytes 3145736 | tf_op jit(solution)/shard_map/ppermute | solution.py:52
  133.6 41.0 %collective-permute-start.29 = (bf16[8,1,2,128,256]{4,3,2,0,1:T(8,128)(2,1)}, bf16[8,1,2,128,256]{4,3,2,0,1:T(8,128)(2,1)}, u32[]{:S(2)}, u32[]{:S(2)}) collective-permute-start(bf16[8,1,2,128,256]{4,3,2,0,1:T(8,128)(2,1)} %collective-permute-done.28), channel_id=1, source_target_pairs={{128,256},{256,384},{129,257},{257,385},{130,258},{258,386},{131,2... | collective-permute-start | bytes 3145736 | tf_op jit(solution)/shard_map/ppermute | solution.py:49
  147.7 20.9 %collective-permute-start.10 = (bf16[1,2,4,128,256]{4,3,2,1,0:T(8,128)(2,1)S(1)}, bf16[1,2,4,128,256]{4,3,2,1,0:T(8,128)(2,1)S(1)}, u32[]{:S(2)}, u32[]{:S(2)}) collective-permute-start(bf16[1,2,4,128,256]{4,3,2,1,0:T(8,128)(2,1)S(1)} %fusion.64), channel_id=1, source_target_pairs={{0,16},{16,32},{32,48},{48,64},{64,80},{80,96},{96,112},{112,0},{1... | collective-permute-start | bytes 1572872 | tf_op jit(solution)/shard_map/ppermute | solution.py:72
  151.4 21.2 %collective-permute-start.13 = (bf16[1,2,4,128,256]{4,3,2,1,0:T(8,128)(2,1)S(1)}, bf16[1,2,4,128,256]{4,3,2,1,0:T(8,128)(2,1)S(1)}, u32[]{:S(2)}, u32[]{:S(2)}) collective-permute-start(bf16[1,2,4,128,256]{4,3,2,1,0:T(8,128)(2,1)S(1)} %fusion.64), channel_id=1, source_target_pairs={{16,0},{32,16},{48,32},{64,48},{80,64},{96,80},{112,96},{0,112},{1... | collective-permute-start | bytes 1572872 | tf_op jit(solution)/shard_map/ppermute | solution.py:75
  167.3 25.2 %collective-permute-start.32 = (bf16[8,1,2,128,256]{4,3,2,1,0:T(8,128)(2,1)}, bf16[8,1,2,128,256]{4,3,2,1,0:T(8,128)(2,1)}, u32[]{:S(2)}, u32[]{:S(2)}) collective-permute-start(bf16[8,1,2,128,256]{4,3,2,1,0:T(8,128)(2,1)} %collective-permute-done.31), channel_id=1, source_target_pairs={{128,0},{256,128},{129,1},{257,129},{130,2},{258,130},{131,3},{259... | collective-permute-start | bytes 3145736 | tf_op jit(solution)/shard_map/ppermute | solution.py:52
  168.6 13.6 %collective-permute-start.11 = (bf16[1,2,4,128,256]{4,3,2,1,0:T(8,128)(2,1)S(1)}, bf16[1,2,4,128,256]{4,3,2,1,0:T(8,128)(2,1)S(1)}, u32[]{:S(2)}, u32[]{:S(2)}) collective-permute-start(bf16[1,2,4,128,256]{4,3,2,1,0:T(8,128)(2,1)S(1)} %collective-permute-done.10), channel_id=1, source_target_pairs={{0,16},{16,32},{32,48},{48,64},{64,80},{80,96},{96,112},{112,0},{1... | collective-permute-start | bytes 1572872 | tf_op jit(solution)/shard_map/ppermute | solution.py:72
  172.6 15.1 %collective-permute-start.14 = (bf16[1,2,4,128,256]{4,3,2,1,0:T(8,128)(2,1)S(1)}, bf16[1,2,4,128,256]{4,3,2,1,0:T(8,128)(2,1)S(1)}, u32[]{:S(2)}, u32[]{:S(2)}) collective-permute-start(bf16[1,2,4,128,256]{4,3,2,1,0:T(8,128)(2,1)S(1)} %collective-permute-done.13), channel_id=1, source_target_pairs={{16,0},{32,16},{48,32},{64,48},{80,64},{96,80},{112,96},{0,112},{1... | collective-permute-start | bytes 1572872 | tf_op jit(solution)/shard_map/ppermute | solution.py:75
  174.6 21.7 %collective-permute-start.30 = (bf16[8,1,2,128,256]{4,3,2,0,1:T(8,128)(2,1)}, bf16[8,1,2,128,256]{4,3,2,0,1:T(8,128)(2,1)}, u32[]{:S(2)}, u32[]{:S(2)}) collective-permute-start(bf16[8,1,2,128,256]{4,3,2,0,1:T(8,128)(2,1)} %collective-permute-done.29), channel_id=1, source_target_pairs={{256,384},{257,385},{258,386},{259,387},{260,388},{261,389},{262,3... | collective-permute-start | bytes 3145736 | tf_op jit(solution)/shard_map/ppermute | solution.py:49
  182.3 52.5 %collective-permute-start.12 = (bf16[1,2,4,128,256]{4,3,2,1,0:T(8,128)(2,1)S(1)}, bf16[1,2,4,128,256]{4,3,2,1,0:T(8,128)(2,1)S(1)}, u32[]{:S(2)}, u32[]{:S(2)}) collective-permute-start(bf16[1,2,4,128,256]{4,3,2,1,0:T(8,128)(2,1)S(1)} %collective-permute-done.11), channel_id=1, source_target_pairs={{0,16},{16,32},{32,48},{48,64},{64,80},{80,96},{96,112},{112,0},{1... | collective-permute-start | bytes 1572872 | tf_op jit(solution)/shard_map/ppermute | solution.py:72
  187.7 47.1 %collective-permute-start.15 = (bf16[1,2,4,128,256]{4,3,2,1,0:T(8,128)(2,1)S(1)}, bf16[1,2,4,128,256]{4,3,2,1,0:T(8,128)(2,1)S(1)}, u32[]{:S(2)}, u32[]{:S(2)}) collective-permute-start(bf16[1,2,4,128,256]{4,3,2,1,0:T(8,128)(2,1)S(1)} %collective-permute-done.14), channel_id=1, source_target_pairs={{16,0},{32,16},{48,32},{64,48},{80,64},{96,80},{112,96},{0,112},{1... | collective-permute-start | bytes 1572872 | tf_op jit(solution)/shard_map/ppermute | solution.py:75
  192.5 23.7 %collective-permute-start.33 = (bf16[8,1,2,128,256]{4,3,2,1,0:T(8,128)(2,1)}, bf16[8,1,2,128,256]{4,3,2,1,0:T(8,128)(2,1)S(1)}, u32[]{:S(2)}, u32[]{:S(2)}) collective-permute-start(bf16[8,1,2,128,256]{4,3,2,1,0:T(8,128)(2,1)} %collective-permute-done.32), channel_id=1, source_target_pairs={{128,0},{129,1},{130,2},{131,3},{132,4},{133,5},{134,6},{135,7},{1... | collective-permute-start | bytes 3145736 | tf_op jit(solution)/shard_map/ppermute | solution.py:52
  318.4 27.6 %collective-permute-start.20 = (bf16[1,2,4,128,256]{4,3,2,1,0:T(8,128)(2,1)}, bf16[1,2,4,128,256]{4,3,2,1,0:T(8,128)(2,1)}, u32[]{:S(2)}, u32[]{:S(2)}) collective-permute-start(bf16[1,2,4,128,256]{4,3,2,1,0:T(8,128)(2,1)} %copy-done.20), channel_id=1, source_target_pairs={{0,16},{16,32},{32,48},{48,64},{64,80},{80,96},{96,112},{112,0},{1... | collective-permute-start | bytes 1572872 | tf_op jit(solution)/shard_map/ppermute | solution.py:72
  (53 other events, 937.4 us)
Sparse Core Ops, SparseCore 0:
  66.9 40.5 all-gather.4
  135.4 34.2 all-gather.6

commit v11 on v7

--- a/solution.py
+++ b/solution.py
@@ -114,10 +114,12 @@
     me_y = lax.axis_index("y")
     z_cols = jnp.moveaxis(stream_gather(averaged, "z_lo", False), 0, 2)
     blocks, row_panel = ring_blocks(z_cols, "y", row_panel)
+    real, imag = row_panel[:, 0], row_panel[:, 1]
+    paired = jnp.stack((jnp.stack((real, -imag), axis=1), jnp.stack((imag, real), axis=1)), axis=1)
     product = None
     for offset, col_block in blocks:
-        row_block = lax.dynamic_index_in_dim(row_panel, (me_y - offset) % y_n, axis=4, keepdims=False)
-        part = complex_product(row_block, col_block, "fizk,fzkj->fij")
+        row_block = lax.dynamic_index_in_dim(paired, (me_y - offset) % y_n, axis=5, keepdims=False)
+        part = jnp.einsum("fgcizk,fczkj->fgij", row_block, col_block, preferred_element_type=jnp.float32)
         product = part if product is None else product + part
     scale_factor = jnp.float32(float(NS) ** (-0.5))
     return product * scale_factor

time: 263 us -> 255 us (0.970)
  matrix products: 35.6 us -> 9.64 us
  waiting for transfers between devices: 104 us -> 117 us
  other arithmetic: 2.38 us -> 11.4 us
  starting transfers between devices: 72.6 us -> 66.4 us
    ppermute x4, waiting for transfers between devices: 1.99 us -> 65.5 us  [ring_blocks(): up = lax.ppermute(up, axis, right)]
    ppermute x3, waiting for transfers between devices: 50.7 us -> 5.46 us  [ring_blocks(): dn = lax.ppermute(dn, axis, left)]
    dot_general x32 -> x8, matrix products: 35.6 us -> 9.64 us  [per_device(): jnp.einsum('fgcizk,fczkj->fgij', row_block, col_block, preferred_element_...]
    all_gather x1, waiting for transfers between devices: 27.6 us -> 15.7 us  [per_device(): rows = lax.all_gather(rows, 'x', axis=1)]
    ppermute x4, starting transfers between devices: 19.9 us -> 12.6 us  [ring_blocks(): up = lax.ppermute(up, axis, right)]
    another operation x0 -> x3, other arithmetic: none -> 6.28 us  [per_device(): jnp.stack((jnp.stack((real, -imag), axis=1), jnp.stack((imag, real), axis...]
    ppermute x4, waiting for transfers between devices: 9.63 us -> 14 us  [stream_gather(): up = lax.ppermute(up, axis, perm(k, 1))]
    dynamic_slice x9 -> x8, local copies, waits for them, and re-layouts: 11.6 us -> 15 us  [per_device(): lax.dynamic_index_in_dim(paired, (me_y - offset) % y_n, axis=5, keepdims=...]
  transfers between devices with their start and end apart: 20 -> 20, of which waited for: 12 -> 12; matrix products, arithmetic and copies ran while one was open for 16% -> 7% of each run, Pallas kernels for 0% -> 0%
where the time goes in v11:
time: 255 us; the launch traced here: 251 us
  waiting for transfers between devices  117 us (46%)
  starting transfers between devices  66.4 us (26%)
  local copies, waits for them, and re-layouts  32.7 us (13%)
  between operations  14.1 us (6%)
  other arithmetic  11.4 us (4%)
  matrix products  9.64 us (4%)
    ppermute x4, waiting for transfers between devices, ring_blocks(): up = lax.ppermute(up, axis, right)  65.5 us
    ppermute x4, starting transfers between devices, stream_gather(): up = lax.ppermute(up, axis, perm(k, 1))  28.9 us
    all_gather x1, waiting for transfers between devices, per_device(): rows = lax.all_gather(rows, 'x', axis=1)  15.7 us
    dynamic_slice x8, local copies, waits for them, and re-layouts, per_device(): lax.dynamic_index_in_dim(paired, (me_y - offset) % y_n, axis=5, keepdims=...  15 us
    ppermute x4, waiting for transfers between devices, stream_gather(): up = lax.ppermute(up, axis, perm(k, 1))  14 us
    ppermute x4, starting transfers between devices, mirrored_pieces(): got.append(lax.ppermute(part, SHOT + RECV, perm))  13.2 us
    ppermute x4, starting transfers between devices, ring_blocks(): up = lax.ppermute(up, axis, right)  12.6 us
    ppermute x3, waiting for transfers between devices, stream_gather(): dn = lax.ppermute(dn, axis, perm(k, -1))  10.5 us
  transfers between devices with their start and end apart: 20, of which 12 were waited for; matrix products, arithmetic and copies ran while one was open for 7% of the time, Pallas kernels for 0%

profile of v11, /device:TPU:56, one launch (start us, length us, event | category | flops | bytes accessed | tf_op | source)
XLA Modules:
  0.0 251.5 jit_solution(1764338308238971876)
XLA Ops:
  9.5 7.8 %collective-permute-start.2 = (bf16[2,2,128,128]{3,2,1,0:T(8,128)(2,1)S(1)}, bf16[2,2,128,128]{3,2,1,0:T(8,128)(2,1)S(1)}, u32[]{:S(2)}, u32[]{:S(2)}) collective-permute-start(bf16[2,2,128,128]{3,2,1,0:T(8,128)(2,1)S(1)} %get-tuple-element.25), channel_id=1, source_target_pairs={{16,0},{17,32},{18,64},{19,96},{20,128},{21,160},{22,192},{23,224}... | collective-permute-start | bytes 393224 | tf_op jit(solution)/shard_map/ppermute | solution.py:96
  17.3 3.4 %collective-permute-start.3 = (bf16[2,2,128,128]{3,2,1,0:T(8,128)(2,1)S(1)}, bf16[2,2,128,128]{3,2,1,0:T(8,128)(2,1)S(1)}, u32[]{:S(2)}, u32[]{:S(2)}) collective-permute-start(bf16[2,2,128,128]{3,2,1,0:T(8,128)(2,1)S(1)} %get-tuple-element.24), channel_id=1, source_target_pairs={{16,16},{17,48},{18,80},{19,112},{20,144},{21,176},{22,208},{23,24... | collective-permute-start | bytes 393224 | tf_op jit(solution)/shard_map/ppermute | solution.py:96
  21.5 5.4 %collective-permute-done.3 = bf16[2,2,128,128]{3,2,1,0:T(8,128)(2,1)S(1)} collective-permute-done((bf16[2,2,128,128]{3,2,1,0:T(8,128)(2,1)S(1)}, bf16[2,2,128,128]{3,2,1,0:T(8,128)(2,1)S(1)}, u32[]{:S(2)}, u32[]{:S(2)}) %collective-permute-start.3) | collective-permute-done | bytes 131104 | tf_op jit(solution)/shard_map/ppermute | solution.py:96
  28.4 19.7 %collective-permute-start.16 = (bf16[2,2,128,256]{3,2,1,0:T(8,128)(2,1)S(1)}, bf16[2,2,128,256]{3,2,1,0:T(8,128)(2,1)S(1)}, u32[]{:S(2)}, u32[]{:S(2)}) collective-permute-start(bf16[2,2,128,256]{3,2,1,0:T(8,128)(2,1)S(1)} %get-tuple-element.10), channel_id=1, source_target_pairs={{0,8},{8,0},{1,9},{9,1},{2,10},{10,2},{3,11},{11,3},{4,12},{12,4},... | collective-permute-start | bytes 786440 | tf_op jit(solution)/shard_map/ppermute | solution.py:49
  48.1 9.5 %collective-permute-done.16 = bf16[2,2,128,256]{3,2,1,0:T(8,128)(2,1)S(1)} collective-permute-done((bf16[2,2,128,256]{3,2,1,0:T(8,128)(2,1)S(1)}, bf16[2,2,128,256]{3,2,1,0:T(8,128)(2,1)S(1)}, u32[]{:S(2)}, u32[]{:S(2)}) %collective-permute-start.16) | collective-permute-done | bytes 262176 | tf_op jit(solution)/shard_map/ppermute | solution.py:49
  59.2 7.8 %collective-permute-start.4 = (bf16[2,2,128,256]{3,2,1,0:T(8,128)(2,1)S(1)}, bf16[2,2,128,256]{3,2,1,0:T(8,128)(2,1)S(1)}, u32[]{:S(2)}, u32[]{:S(2)}) collective-permute-start(bf16[2,2,128,256]{3,2,1,0:T(8,128)(2,1)S(1)} %get-tuple-element.10), channel_id=1, source_target_pairs={{0,128},{128,256},{256,384},{1,129},{129,257},{257,385},{2,130},{1... | collective-permute-start | bytes 786440 | tf_op jit(solution)/shard_map/ppermute | solution.py:49
  68.4 4.5 %collective-permute-done.4 = bf16[2,2,128,256]{3,2,1,0:T(8,128)(2,1)S(1)} collective-permute-done((bf16[2,2,128,256]{3,2,1,0:T(8,128)(2,1)S(1)}, bf16[2,2,128,256]{3,2,1,0:T(8,128)(2,1)S(1)}, u32[]{:S(2)}, u32[]{:S(2)}) %collective-permute-start.4) | collective-permute-done | bytes 262176 | tf_op jit(solution)/shard_map/ppermute | solution.py:49
  73.6 3.4 %collective-permute-done.7 = bf16[2,2,128,256]{3,2,1,0:T(8,128)(2,1)S(1)} collective-permute-done((bf16[2,2,128,256]{3,2,1,0:T(8,128)(2,1)S(1)}, bf16[2,2,128,256]{3,2,1,0:T(8,128)(2,1)S(1)}, u32[]{:S(2)}, u32[]{:S(2)}) %collective-permute-start.7) | collective-permute-done | bytes 262176 | tf_op jit(solution)/shard_map/ppermute | solution.py:52
  79.1 7.0 %collective-permute-done.8 = bf16[2,2,128,256]{3,2,1,0:T(8,128)(2,1)S(1)} collective-permute-done((bf16[2,2,128,256]{3,2,1,0:T(8,128)(2,1)S(1)}, bf16[2,2,128,256]{3,2,1,0:T(8,128)(2,1)S(1)}, u32[]{:S(2)}, u32[]{:S(2)}) %collective-permute-start.8) | collective-permute-done | bytes 262176 | tf_op jit(solution)/shard_map/ppermute | solution.py:52
  87.4 15.7 %all-gather.4.cloned.1.call-done = bf16[2,4,2,2,128,256]{5,4,3,2,0,1:T(8,128)(2,1)} async-done(((bf16[2,1,2,2,128,256]{5,4,3,2,0,1:T(8,128)(2,1)}), bf16[2,4,2,2,128,256]{5,4,3,2,0,1:T(8,128)(2,1)}) %all-gather.4.cloned.1.call-update) | async-done | bytes 2097168 | tf_op jit(solution)/shard_map/all_gather | solution.py:109
  103.1 3.2 %copy.31 = bf16[2,4,2,2,128,256]{5,4,3,2,1,0:T(8,128)(2,1)} copy(bf16[2,4,2,2,128,256]{5,4,3,2,0,1:T(8,128)(2,1)} %all-gather.4.cloned.1.call-done) | data formatting | bytes 4194304 | tf_op jit(solution)/shard_map/all_gather | solution.py:109
  109.6 3.5 %collective-permute-start.13 = (bf16[2,2,4,128,256]{4,3,2,1,0:T(8,128)(2,1)S(1)}, bf16[2,2,4,128,256]{4,3,2,1,0:T(8,128)(2,1)S(1)}, u32[]{:S(2)}, u32[]{:S(2)}) collective-permute-start(bf16[2,2,4,128,256]{4,3,2,1,0:T(8,128)(2,1)S(1)} %fusion.34), channel_id=1, source_target_pairs={{16,0},{32,16},{48,32},{64,48},{80,64},{96,80},{112,96},{0,112},{1... | collective-permute-start | bytes 3145736 | tf_op jit(solution)/shard_map/ppermute | solution.py:75
  113.1 20.8 %collective-permute-done.10 = bf16[2,2,4,128,256]{4,3,2,1,0:T(8,128)(2,1)S(1)} collective-permute-done((bf16[2,2,4,128,256]{4,3,2,1,0:T(8,128)(2,1)S(1)}, bf16[2,2,4,128,256]{4,3,2,1,0:T(8,128)(2,1)S(1)}, u32[]{:S(2)}, u32[]{:S(2)}) %collective-permute-start.10) | collective-permute-done | bytes 1048608 | tf_op jit(solution)/shard_map/ppermute | solution.py:72
  134.9 3.5 %collective-permute-start.11 = (bf16[2,2,4,128,256]{4,3,2,1,0:T(8,128)(2,1)S(1)}, bf16[2,2,4,128,256]{4,3,2,1,0:T(8,128)(2,1)S(1)}, u32[]{:S(2)}, u32[]{:S(2)}) collective-permute-start(bf16[2,2,4,128,256]{4,3,2,1,0:T(8,128)(2,1)S(1)} %collective-permute-done.10), channel_id=1, source_target_pairs={{0,16},{16,32},{32,48},{48,64},{64,80},{80,96},{96,112},{112,0},{1... | collective-permute-start | bytes 3145736 | tf_op jit(solution)/shard_map/ppermute | solution.py:72
  140.8 19.9 %collective-permute-done.11 = bf16[2,2,4,128,256]{4,3,2,1,0:T(8,128)(2,1)S(1)} collective-permute-done((bf16[2,2,4,128,256]{4,3,2,1,0:T(8,128)(2,1)S(1)}, bf16[2,2,4,128,256]{4,3,2,1,0:T(8,128)(2,1)S(1)}, u32[]{:S(2)}, u32[]{:S(2)}) %collective-permute-start.11) | collective-permute-done | bytes 1048608 | tf_op jit(solution)/shard_map/ppermute | solution.py:72
  160.7 4.7 %collective-permute-start.12 = (bf16[2,2,4,128,256]{4,3,2,1,0:T(8,128)(2,1)S(1)}, bf16[2,2,4,128,256]{4,3,2,1,0:T(8,128)(2,1)}, u32[]{:S(2)}, u32[]{:S(2)}) collective-permute-start(bf16[2,2,4,128,256]{4,3,2,1,0:T(8,128)(2,1)S(1)} %collective-permute-done.11), channel_id=1, source_target_pairs={{0,16},{16,32},{32,48},{48,64},{64,80},{80,96},{96,112},{112,0},{1... | collective-permute-start | bytes 3145736 | tf_op jit(solution)/shard_map/ppermute | solution.py:72
  167.5 7.3 %copy.32 = bf16[2,2,128,2,4,2,256]{2,6,5,4,3,1,0:T(8,128)(2,1)} copy(bf16[2,2,128,2,4,2,256]{6,2,1,0,5,4,3:T(8,128)(2,1)} %bitcast.158) | data formatting | bytes 8388608 | tf_op jit(solution)/shard_map/transpose | solution.py:113
  174.8 11.1 %collective-permute-done.12 = bf16[2,2,4,128,256]{4,3,2,1,0:T(8,128)(2,1)} collective-permute-done((bf16[2,2,4,128,256]{4,3,2,1,0:T(8,128)(2,1)S(1)}, bf16[2,2,4,128,256]{4,3,2,1,0:T(8,128)(2,1)}, u32[]{:S(2)}, u32[]{:S(2)}) %collective-permute-start.12) | collective-permute-done | bytes 1048608 | tf_op jit(solution)/shard_map/ppermute | solution.py:72
  185.9 5.5 %collective-permute-done.15 = bf16[2,2,4,128,256]{4,3,2,1,0:T(8,128)(2,1)} collective-permute-done((bf16[2,2,4,128,256]{4,3,2,1,0:T(8,128)(2,1)S(1)}, bf16[2,2,4,128,256]{4,3,2,1,0:T(8,128)(2,1)}, u32[]{:S(2)}, u32[]{:S(2)}) %collective-permute-start.15) | collective-permute-done | bytes 1048608 | tf_op jit(solution)/shard_map/ppermute | solution.py:75
  191.4 2.8 %fusion.43 = (bf16[2,1,128,4,8,128]{2,5,4,3,1,0:T(8,128)(2,1)S(1)}, bf16[2,1,128,4,8,128]{2,5,4,3,1,0:T(8,128)(2,1)S(1)}, bf16[2,1,128,4,8,128]{2,5,4,3,1,0:T(8,128)(2,1)S(1)}) fusion(bf16[2,2,128,4,8,128]{2,5,4,3,1,0:T(8,128)(2,1)} %bitcast.157), kind=kLoop, calls=%fused_computation.108 | loop fusion | flops 1048576 | bytes 10485760 | tf_op jit(solution)/shard_map/slice | solution.py:117
  194.9 2.5 fusion.14
  210.0 3.0 %fusion.15 = (bf16[2,2,2,128,4,1,128]{3,6,5,4,2,0,1:T(8,128)(2,1)}, bf16[2,2,2,128,4,1,128]{3,6,5,4,2,0,1:T(8,128)(2,1)}) fusion(s32[]{:T(128)S(6)} %select_n.228, bf16[2,1,2,128,4,8,128]{3,6,5,4,2,0,1:T(8,128)(2,1)} %copy-done.1, bf16[2,1,2,128,4,8,128]{3,6,5,4,2,0,1:T(8,128)(2,1)} %copy-done, s32[]{:T(128)S(6)} %select_n.230), kind=kLoop, calls=%fused_computation.43 | loop fusion | flops 1048576 | bytes 10485768 | tf_op jit(solution)/shard_map/stack | solution.py:118
  228.0 13.7 %collective-permute-done.17 = bf16[2,2,4,128,256]{4,3,2,1,0:T(8,128)(2,1)S(1)} collective-permute-done((bf16[2,2,4,128,256]{4,3,2,1,0:T(8,128)(2,1)}, bf16[2,2,4,128,256]{4,3,2,1,0:T(8,128)(2,1)S(1)}, u32[]{:S(2)}, u32[]{:S(2)}) %collective-permute-start.17) | collective-permute-done | bytes 1048608 | tf_op jit(solution)/shard_map/ppermute | solution.py:72
  242.2 2.5 fusion.7
  (88 shorter events, 49.0 us)
Async XLA Ops:
  6.5 96.6 %all-gather.4.cloned.1.call-start = ((), (), s32[]{:S(2)}) async-start(), calls=%async_computation | async-start | bytes 2621440 | tf_op jit(solution)/shard_map/all_gather | solution.py:109
  7.5 13.3 %collective-permute-start = (bf16[2,2,128,128]{3,2,1,0:T(8,128)(2,1)S(1)}, bf16[2,2,128,128]{3,2,1,0:T(8,128)(2,1)S(1)}, u32[]{:S(2)}, u32[]{:S(2)}) collective-permute-start(bf16[2,2,128,128]{3,2,1,0:T(8,128)(2,1)S(1)} %get-tuple-element.25), channel_id=1, source_target_pairs={{0,0},{1,32},{2,64},{3,96},{4,128},{5,160},{6,192},{7,224},{8,256}... | collective-permute-start | bytes 393224 | tf_op jit(solution)/shard_map/ppermute | solution.py:96
  8.2 13.3 %collective-permute-start.1 = (bf16[2,2,128,128]{3,2,1,0:T(8,128)(2,1)S(1)}, bf16[2,2,128,128]{3,2,1,0:T(8,128)(2,1)S(1)}, u32[]{:S(2)}, u32[]{:S(2)}) collective-permute-start(bf16[2,2,128,128]{3,2,1,0:T(8,128)(2,1)S(1)} %get-tuple-element.24), channel_id=1, source_target_pairs={{0,16},{1,48},{2,80},{3,112},{4,144},{5,176},{6,208},{7,240},{8,27... | collective-permute-start | bytes 393224 | tf_op jit(solution)/shard_map/ppermute | solution.py:96
  9.5 12.0 %collective-permute-start.2 = (bf16[2,2,128,128]{3,2,1,0:T(8,128)(2,1)S(1)}, bf16[2,2,128,128]{3,2,1,0:T(8,128)(2,1)S(1)}, u32[]{:S(2)}, u32[]{:S(2)}) collective-permute-start(bf16[2,2,128,128]{3,2,1,0:T(8,128)(2,1)S(1)} %get-tuple-element.25), channel_id=1, source_target_pairs={{16,0},{17,32},{18,64},{19,96},{20,128},{21,160},{22,192},{23,224}... | collective-permute-start | bytes 393224 | tf_op jit(solution)/shard_map/ppermute | solution.py:96
  17.3 9.6 %collective-permute-start.3 = (bf16[2,2,128,128]{3,2,1,0:T(8,128)(2,1)S(1)}, bf16[2,2,128,128]{3,2,1,0:T(8,128)(2,1)S(1)}, u32[]{:S(2)}, u32[]{:S(2)}) collective-permute-start(bf16[2,2,128,128]{3,2,1,0:T(8,128)(2,1)S(1)} %get-tuple-element.24), channel_id=1, source_target_pairs={{16,16},{17,48},{18,80},{19,112},{20,144},{21,176},{22,208},{23,24... | collective-permute-start | bytes 393224 | tf_op jit(solution)/shard_map/ppermute | solution.py:96
  28.4 29.2 %collective-permute-start.16 = (bf16[2,2,128,256]{3,2,1,0:T(8,128)(2,1)S(1)}, bf16[2,2,128,256]{3,2,1,0:T(8,128)(2,1)S(1)}, u32[]{:S(2)}, u32[]{:S(2)}) collective-permute-start(bf16[2,2,128,256]{3,2,1,0:T(8,128)(2,1)S(1)} %get-tuple-element.10), channel_id=1, source_target_pairs={{0,8},{8,0},{1,9},{9,1},{2,10},{10,2},{3,11},{11,3},{4,12},{12,4},... | collective-permute-start | bytes 786440 | tf_op jit(solution)/shard_map/ppermute | solution.py:49
  59.2 108.3 %all-gather.6.cloned.1.call-start = ((), (), s32[]{:S(2)}) async-start(), calls=%async_computation.1 | async-start | bytes 6291456 | tf_op jit(solution)/shard_map/all_gather | solution.py:110
  59.2 13.7 %collective-permute-start.4 = (bf16[2,2,128,256]{3,2,1,0:T(8,128)(2,1)S(1)}, bf16[2,2,128,256]{3,2,1,0:T(8,128)(2,1)S(1)}, u32[]{:S(2)}, u32[]{:S(2)}) collective-permute-start(bf16[2,2,128,256]{3,2,1,0:T(8,128)(2,1)S(1)} %get-tuple-element.10), channel_id=1, source_target_pairs={{0,128},{128,256},{256,384},{1,129},{129,257},{257,385},{2,130},{1... | collective-permute-start | bytes 786440 | tf_op jit(solution)/shard_map/ppermute | solution.py:49
  67.1 9.9 %collective-permute-start.7 = (bf16[2,2,128,256]{3,2,1,0:T(8,128)(2,1)S(1)}, bf16[2,2,128,256]{3,2,1,0:T(8,128)(2,1)S(1)}, u32[]{:S(2)}, u32[]{:S(2)}) collective-permute-start(bf16[2,2,128,256]{3,2,1,0:T(8,128)(2,1)S(1)} %get-tuple-element.10), channel_id=1, source_target_pairs={{128,0},{256,128},{384,256},{129,1},{257,129},{385,257},{130,2},{2... | collective-permute-start | bytes 786440 | tf_op jit(solution)/shard_map/ppermute | solution.py:52
  72.9 5.4 %collective-permute-start.5 = (bf16[2,2,128,256]{3,2,1,0:T(8,128)(2,1)S(1)}, bf16[2,2,128,256]{3,2,1,0:T(8,128)(2,1)S(1)}, u32[]{:S(2)}, u32[]{:S(2)}) collective-permute-start(bf16[2,2,128,256]{3,2,1,0:T(8,128)(2,1)S(1)} %collective-permute-done.4), channel_id=1, source_target_pairs={{128,256},{256,384},{129,257},{257,385},{130,258},{258,386},{131,2... | collective-permute-start | bytes 786440 | tf_op jit(solution)/shard_map/ppermute | solution.py:49
  77.0 9.1 %collective-permute-start.8 = (bf16[2,2,128,256]{3,2,1,0:T(8,128)(2,1)S(1)}, bf16[2,2,128,256]{3,2,1,0:T(8,128)(2,1)S(1)}, u32[]{:S(2)}, u32[]{:S(2)}) collective-permute-start(bf16[2,2,128,256]{3,2,1,0:T(8,128)(2,1)S(1)} %collective-permute-done.7), channel_id=1, source_target_pairs={{128,0},{256,128},{129,1},{257,129},{130,2},{258,130},{131,3},{259... | collective-permute-start | bytes 786440 | tf_op jit(solution)/shard_map/ppermute | solution.py:52
  78.3 28.0 %collective-permute-start.6 = (bf16[2,2,128,256]{3,2,1,0:T(8,128)(2,1)S(1)}, bf16[2,2,128,256]{3,2,1,0:T(8,128)(2,1)S(1)}, u32[]{:S(2)}, u32[]{:S(2)}) collective-permute-start(bf16[2,2,128,256]{3,2,1,0:T(8,128)(2,1)S(1)} %collective-permute-done.5), channel_id=1, source_target_pairs={{256,384},{257,385},{258,386},{259,387},{260,388},{261,389},{262,3... | collective-permute-start | bytes 786440 | tf_op jit(solution)/shard_map/ppermute | solution.py:49
  86.1 20.4 %collective-permute-start.9 = (bf16[2,2,128,256]{3,2,1,0:T(8,128)(2,1)S(1)}, bf16[2,2,128,256]{3,2,1,0:T(8,128)(2,1)S(1)}, u32[]{:S(2)}, u32[]{:S(2)}) collective-permute-start(bf16[2,2,128,256]{3,2,1,0:T(8,128)(2,1)S(1)} %collective-permute-done.8), channel_id=1, source_target_pairs={{128,0},{129,1},{130,2},{131,3},{132,4},{133,5},{134,6},{135,7},{1... | collective-permute-start | bytes 786440 | tf_op jit(solution)/shard_map/ppermute | solution.py:52
  107.3 26.6 %collective-permute-start.10 = (bf16[2,2,4,128,256]{4,3,2,1,0:T(8,128)(2,1)S(1)}, bf16[2,2,4,128,256]{4,3,2,1,0:T(8,128)(2,1)S(1)}, u32[]{:S(2)}, u32[]{:S(2)}) collective-permute-start(bf16[2,2,4,128,256]{4,3,2,1,0:T(8,128)(2,1)S(1)} %fusion.34), channel_id=1, source_target_pairs={{0,16},{16,32},{32,48},{48,64},{64,80},{80,96},{96,112},{112,0},{1... | collective-permute-start | bytes 3145736 | tf_op jit(solution)/shard_map/ppermute | solution.py:72
  109.6 28.8 %collective-permute-start.13 = (bf16[2,2,4,128,256]{4,3,2,1,0:T(8,128)(2,1)S(1)}, bf16[2,2,4,128,256]{4,3,2,1,0:T(8,128)(2,1)S(1)}, u32[]{:S(2)}, u32[]{:S(2)}) collective-permute-start(bf16[2,2,4,128,256]{4,3,2,1,0:T(8,128)(2,1)S(1)} %fusion.34), channel_id=1, source_target_pairs={{16,0},{32,16},{48,32},{64,48},{80,64},{96,80},{112,96},{0,112},{1... | collective-permute-start | bytes 3145736 | tf_op jit(solution)/shard_map/ppermute | solution.py:75
  134.9 25.8 %collective-permute-start.11 = (bf16[2,2,4,128,256]{4,3,2,1,0:T(8,128)(2,1)S(1)}, bf16[2,2,4,128,256]{4,3,2,1,0:T(8,128)(2,1)S(1)}, u32[]{:S(2)}, u32[]{:S(2)}) collective-permute-start(bf16[2,2,4,128,256]{4,3,2,1,0:T(8,128)(2,1)S(1)} %collective-permute-done.10), channel_id=1, source_target_pairs={{0,16},{16,32},{32,48},{48,64},{64,80},{80,96},{96,112},{112,0},{1... | collective-permute-start | bytes 3145736 | tf_op jit(solution)/shard_map/ppermute | solution.py:72
  138.4 22.2 %copy-start.10 = (bf16[2,2,4,128,256]{4,3,2,1,0:T(8,128)(2,1)}, bf16[2,2,4,128,256]{4,3,2,1,0:T(8,128)(2,1)S(1)}, u32[]{:S(2)}) copy-start(bf16[2,2,4,128,256]{4,3,2,1,0:T(8,128)(2,1)S(1)} %collective-permute-done.13) | copy-start | bytes 3145732
  138.4 27.0 %collective-permute-start.14 = (bf16[2,2,4,128,256]{4,3,2,1,0:T(8,128)(2,1)S(1)}, bf16[2,2,4,128,256]{4,3,2,1,0:T(8,128)(2,1)S(1)}, u32[]{:S(2)}, u32[]{:S(2)}) collective-permute-start(bf16[2,2,4,128,256]{4,3,2,1,0:T(8,128)(2,1)S(1)} %collective-permute-done.13), channel_id=1, source_target_pairs={{16,0},{32,16},{48,32},{64,48},{80,64},{96,80},{112,96},{0,112},{1... | collective-permute-start | bytes 3145736 | tf_op jit(solution)/shard_map/ppermute | solution.py:75
  160.7 14.2 %copy-start.8 = (bf16[2,2,4,128,256]{4,3,2,1,0:T(8,128)(2,1)}, bf16[2,2,4,128,256]{4,3,2,1,0:T(8,128)(2,1)S(1)}, u32[]{:S(2)}) copy-start(bf16[2,2,4,128,256]{4,3,2,1,0:T(8,128)(2,1)S(1)} %collective-permute-done.11) | copy-start | bytes 3145732
  160.7 25.3 %collective-permute-start.12 = (bf16[2,2,4,128,256]{4,3,2,1,0:T(8,128)(2,1)S(1)}, bf16[2,2,4,128,256]{4,3,2,1,0:T(8,128)(2,1)}, u32[]{:S(2)}, u32[]{:S(2)}) collective-permute-start(bf16[2,2,4,128,256]{4,3,2,1,0:T(8,128)(2,1)S(1)} %collective-permute-done.11), channel_id=1, source_target_pairs={{0,16},{16,32},{32,48},{48,64},{64,80},{80,96},{96,112},{112,0},{1... | collective-permute-start | bytes 3145736 | tf_op jit(solution)/shard_map/ppermute | solution.py:72
  165.4 26.0 %collective-permute-start.15 = (bf16[2,2,4,128,256]{4,3,2,1,0:T(8,128)(2,1)S(1)}, bf16[2,2,4,128,256]{4,3,2,1,0:T(8,128)(2,1)}, u32[]{:S(2)}, u32[]{:S(2)}) collective-permute-start(bf16[2,2,4,128,256]{4,3,2,1,0:T(8,128)(2,1)S(1)} %collective-permute-done.14), channel_id=1, source_target_pairs={{16,0},{32,16},{48,32},{64,48},{80,64},{96,80},{112,96},{0,112},{1... | collective-permute-start | bytes 3145736 | tf_op jit(solution)/shard_map/ppermute | solution.py:75
  217.6 24.1 %collective-permute-start.17 = (bf16[2,2,4,128,256]{4,3,2,1,0:T(8,128)(2,1)}, bf16[2,2,4,128,256]{4,3,2,1,0:T(8,128)(2,1)S(1)}, u32[]{:S(2)}, u32[]{:S(2)}) collective-permute-start(bf16[2,2,4,128,256]{4,3,2,1,0:T(8,128)(2,1)} %collective-permute-done.12), channel_id=1, source_target_pairs={{0,16},{16,32},{32,48},{48,64},{64,80},{80,96},{96,112},{112,0},{1... | collective-permute-start | bytes 3145736 | tf_op jit(solution)/shard_map/ppermute | solution.py:72
  227.5 14.2 %copy-start.2 = (bf16[2,2,2,128,4,1,128]{6,3,4,2,1,0,5:T(8,128)(2,1)S(1)}, bf16[2,2,2,128,4,1,128]{6,3,4,2,1,0,5:T(8,128)(2,1)}, u32[]{:S(2)}) copy-start(bf16[2,2,2,128,4,1,128]{6,3,4,2,1,0,5:T(8,128)(2,1)} %copy.40) | copy-start | bytes 3145732
  228.0 14.2 %copy-start.5 = (bf16[2,2,2,128,4,1,128]{6,3,4,2,1,0,5:T(8,128)(2,1)S(1)}, bf16[2,2,2,128,4,1,128]{6,3,4,2,1,0,5:T(8,128)(2,1)}, u32[]{:S(2)}) copy-start(bf16[2,2,2,128,4,1,128]{6,3,4,2,1,0,5:T(8,128)(2,1)} %copy.38) | copy-start | bytes 3145732
  (9 other events, 34.0 us)
Sparse Core Ops, SparseCore 0:
  59.3 43.7 all-gather.3
  106.5 21.8 all-gather.5

commit v12 on v11

--- a/solution.py
+++ b/solution.py
@@ -74,7 +74,7 @@
         if k < n - n // 2:
             dn = lax.ppermute(dn, axis, left)
             got.append((-k, dn))
-        if k == 3:
+        if k == n // 2:
             up, dn, held = lax.optimization_barrier((up, dn, held))
     return got, held
 

time: 255 us -> 262 us (1.027)
  starting transfers between devices: 66.4 us -> 71.3 us
    all_gather x1, waiting for transfers between devices: 15.7 us -> 7.61 us  [per_device(): rows = lax.all_gather(rows, 'x', axis=1)]
    ppermute x3, waiting for transfers between devices: 10.5 us -> 17.3 us  [stream_gather(): dn = lax.ppermute(dn, axis, perm(k, -1))]
    ppermute x4, waiting for transfers between devices: 65.5 us -> 71.4 us  [ring_blocks(): up = lax.ppermute(up, axis, right)]
    ppermute x3, waiting for transfers between devices: 5.46 us -> 0.01 us  [ring_blocks(): dn = lax.ppermute(dn, axis, left)]
    ppermute x4, starting transfers between devices: 12.6 us -> 16.1 us  [ring_blocks(): up = lax.ppermute(up, axis, right)]
    ppermute x4, starting transfers between devices: 28.9 us -> 32.2 us  [stream_gather(): up = lax.ppermute(up, axis, perm(k, 1))]
    unnamed x31 -> x37, local copies, waits for them, and re-layouts: 4.7 us -> 7.52 us
  transfers between devices with their start and end apart: 20 -> 20, of which waited for: 12 -> 12; matrix products, arithmetic and copies ran while one was open for 7% -> 3% of each run, Pallas kernels for 0% -> 0%
where the time goes in v12:
time: 262 us; the launch traced here: 257 us
  waiting for transfers between devices  118 us (45%)
  starting transfers between devices  71.3 us (27%)
  local copies, waits for them, and re-layouts  33.9 us (13%)
  between operations  14.1 us (5%)
  other arithmetic  11 us (4%)
  matrix products  9.43 us (4%)
    ppermute x4, waiting for transfers between devices, ring_blocks(): up = lax.ppermute(up, axis, right)  71.4 us
    ppermute x4, starting transfers between devices, stream_gather(): up = lax.ppermute(up, axis, perm(k, 1))  32.2 us
    ppermute x3, waiting for transfers between devices, stream_gather(): dn = lax.ppermute(dn, axis, perm(k, -1))  17.3 us
    ppermute x4, starting transfers between devices, ring_blocks(): up = lax.ppermute(up, axis, right)  16.1 us
    ppermute x4, waiting for transfers between devices, stream_gather(): up = lax.ppermute(up, axis, perm(k, 1))  13.8 us
    dynamic_slice x8, local copies, waits for them, and re-layouts, per_device(): lax.dynamic_index_in_dim(paired, (me_y - offset) % y_n, axis=5, keepdims=...  13.4 us
    ppermute x4, starting transfers between devices, mirrored_pieces(): got.append(lax.ppermute(part, SHOT + RECV, perm))  11.3 us
    dot_general x8, matrix products, per_device(): jnp.einsum('fgcizk,fczkj->fgij', row_block, col_block, preferred_element_...  9.43 us
  transfers between devices with their start and end apart: 20, of which 12 were waited for; matrix products, arithmetic and copies ran while one was open for 3% of the time, Pallas kernels for 0%

profile of v12, /device:TPU:56, one launch (start us, length us, event | category | flops | bytes accessed | tf_op | source)
XLA Modules:
  0.0 257.3 jit_solution(1777814653229429749)
XLA Ops:
  9.6 7.3 %collective-permute-start.3 = (bf16[2,2,128,128]{3,2,1,0:T(8,128)(2,1)S(1)}, bf16[2,2,128,128]{3,2,1,0:T(8,128)(2,1)S(1)}, u32[]{:S(2)}, u32[]{:S(2)}) collective-permute-start(bf16[2,2,128,128]{3,2,1,0:T(8,128)(2,1)S(1)} %get-tuple-element.22), channel_id=1, source_target_pairs={{16,16},{17,48},{18,80},{19,112},{20,144},{21,176},{22,208},{23,24... | collective-permute-start | bytes 393224 | tf_op jit(solution)/shard_map/ppermute | solution.py:96
  19.5 6.8 %collective-permute-done.1 = bf16[2,2,128,128]{3,2,1,0:T(8,128)(2,1)S(1)} collective-permute-done((bf16[2,2,128,128]{3,2,1,0:T(8,128)(2,1)S(1)}, bf16[2,2,128,128]{3,2,1,0:T(8,128)(2,1)S(1)}, u32[]{:S(2)}, u32[]{:S(2)}) %collective-permute-start.1) | collective-permute-done | bytes 131104 | tf_op jit(solution)/shard_map/ppermute | solution.py:96
  27.7 22.9 %collective-permute-start.17 = (bf16[2,2,128,256]{3,2,1,0:T(8,128)(2,1)S(1)}, bf16[2,2,128,256]{3,2,1,0:T(8,128)(2,1)S(1)}, u32[]{:S(2)}, u32[]{:S(2)}) collective-permute-start(bf16[2,2,128,256]{3,2,1,0:T(8,128)(2,1)S(1)} %get-tuple-element.8), channel_id=1, source_target_pairs={{0,8},{8,0},{1,9},{9,1},{2,10},{10,2},{3,11},{11,3},{4,12},{12,4},... | collective-permute-start | bytes 786440 | tf_op jit(solution)/shard_map/ppermute | solution.py:49
  50.7 9.2 %collective-permute-done.17 = bf16[2,2,128,256]{3,2,1,0:T(8,128)(2,1)S(1)} collective-permute-done((bf16[2,2,128,256]{3,2,1,0:T(8,128)(2,1)S(1)}, bf16[2,2,128,256]{3,2,1,0:T(8,128)(2,1)S(1)}, u32[]{:S(2)}, u32[]{:S(2)}) %collective-permute-start.17) | collective-permute-done | bytes 262176 | tf_op jit(solution)/shard_map/ppermute | solution.py:49
  61.6 7.9 %collective-permute-start.4 = (bf16[2,2,128,256]{3,2,1,0:T(8,128)(2,1)S(1)}, bf16[2,2,128,256]{3,2,1,0:T(8,128)(2,1)S(1)}, u32[]{:S(2)}, u32[]{:S(2)}) collective-permute-start(bf16[2,2,128,256]{3,2,1,0:T(8,128)(2,1)S(1)} %get-tuple-element.8), channel_id=1, source_target_pairs={{0,128},{128,256},{256,384},{1,129},{129,257},{257,385},{2,130},{1... | collective-permute-start | bytes 786440 | tf_op jit(solution)/shard_map/ppermute | solution.py:49
  70.8 4.5 %collective-permute-done.4 = bf16[2,2,128,256]{3,2,1,0:T(8,128)(2,1)S(1)} collective-permute-done((bf16[2,2,128,256]{3,2,1,0:T(8,128)(2,1)S(1)}, bf16[2,2,128,256]{3,2,1,0:T(8,128)(2,1)S(1)}, u32[]{:S(2)}, u32[]{:S(2)}) %collective-permute-start.4) | collective-permute-done | bytes 262176 | tf_op jit(solution)/shard_map/ppermute | solution.py:49
  76.0 3.4 %collective-permute-done.7 = bf16[2,2,128,256]{3,2,1,0:T(8,128)(2,1)S(1)} collective-permute-done((bf16[2,2,128,256]{3,2,1,0:T(8,128)(2,1)S(1)}, bf16[2,2,128,256]{3,2,1,0:T(8,128)(2,1)S(1)}, u32[]{:S(2)}, u32[]{:S(2)}) %collective-permute-start.7) | collective-permute-done | bytes 262176 | tf_op jit(solution)/shard_map/ppermute | solution.py:52
  81.5 7.0 %collective-permute-done.8 = bf16[2,2,128,256]{3,2,1,0:T(8,128)(2,1)S(1)} collective-permute-done((bf16[2,2,128,256]{3,2,1,0:T(8,128)(2,1)S(1)}, bf16[2,2,128,256]{3,2,1,0:T(8,128)(2,1)S(1)}, u32[]{:S(2)}, u32[]{:S(2)}) %collective-permute-start.8) | collective-permute-done | bytes 262176 | tf_op jit(solution)/shard_map/ppermute | solution.py:52
  89.9 6.8 %collective-permute-done.9 = bf16[2,2,128,256]{3,2,1,0:T(8,128)(2,1)S(1)} collective-permute-done((bf16[2,2,128,256]{3,2,1,0:T(8,128)(2,1)S(1)}, bf16[2,2,128,256]{3,2,1,0:T(8,128)(2,1)S(1)}, u32[]{:S(2)}, u32[]{:S(2)}) %collective-permute-start.9) | collective-permute-done | bytes 262176 | tf_op jit(solution)/shard_map/ppermute | solution.py:52
  97.6 7.6 %all-gather.4.cloned.1.call-done = bf16[2,4,2,2,128,256]{5,4,3,2,0,1:T(8,128)(2,1)} async-done(((bf16[2,1,2,2,128,256]{5,4,3,2,0,1:T(8,128)(2,1)}), bf16[2,4,2,2,128,256]{5,4,3,2,0,1:T(8,128)(2,1)}) %all-gather.4.cloned.1.call-update) | async-done | bytes 2097168 | tf_op jit(solution)/shard_map/all_gather | solution.py:109
  105.2 3.2 %copy.31 = bf16[2,4,2,2,128,256]{5,4,3,2,1,0:T(8,128)(2,1)} copy(bf16[2,4,2,2,128,256]{5,4,3,2,0,1:T(8,128)(2,1)} %all-gather.4.cloned.1.call-done) | data formatting | bytes 4194304 | tf_op jit(solution)/shard_map/all_gather | solution.py:109
  110.7 3.5 %collective-permute-start.14 = (bf16[2,2,4,128,256]{4,3,2,1,0:T(8,128)(2,1)S(1)}, bf16[2,2,4,128,256]{4,3,2,1,0:T(8,128)(2,1)S(1)}, u32[]{:S(2)}, u32[]{:S(2)}) collective-permute-start(bf16[2,2,4,128,256]{4,3,2,1,0:T(8,128)(2,1)S(1)} %fusion.34), channel_id=1, source_target_pairs={{16,0},{32,16},{48,32},{64,48},{80,64},{96,80},{112,96},{0,112},{1... | collective-permute-start | bytes 3145736 | tf_op jit(solution)/shard_map/ppermute | solution.py:75
  114.2 20.8 %collective-permute-done.10 = bf16[2,2,4,128,256]{4,3,2,1,0:T(8,128)(2,1)S(1)} collective-permute-done((bf16[2,2,4,128,256]{4,3,2,1,0:T(8,128)(2,1)S(1)}, bf16[2,2,4,128,256]{4,3,2,1,0:T(8,128)(2,1)S(1)}, u32[]{:S(2)}, u32[]{:S(2)}) %collective-permute-start.10) | collective-permute-done | bytes 1048608 | tf_op jit(solution)/shard_map/ppermute | solution.py:72
  136.0 3.5 %collective-permute-start.11 = (bf16[2,2,4,128,256]{4,3,2,1,0:T(8,128)(2,1)S(1)}, bf16[2,2,4,128,256]{4,3,2,1,0:T(8,128)(2,1)S(1)}, u32[]{:S(2)}, u32[]{:S(2)}) collective-permute-start(bf16[2,2,4,128,256]{4,3,2,1,0:T(8,128)(2,1)S(1)} %collective-permute-done.10), channel_id=1, source_target_pairs={{0,16},{16,32},{32,48},{48,64},{64,80},{80,96},{96,112},{112,0},{1... | collective-permute-start | bytes 3145736 | tf_op jit(solution)/shard_map/ppermute | solution.py:72
  139.5 2.3 collective-permute-start.15
  141.9 19.9 %collective-permute-done.11 = bf16[2,2,4,128,256]{4,3,2,1,0:T(8,128)(2,1)S(1)} collective-permute-done((bf16[2,2,4,128,256]{4,3,2,1,0:T(8,128)(2,1)S(1)}, bf16[2,2,4,128,256]{4,3,2,1,0:T(8,128)(2,1)S(1)}, u32[]{:S(2)}, u32[]{:S(2)}) %collective-permute-start.11) | collective-permute-done | bytes 1048608 | tf_op jit(solution)/shard_map/ppermute | solution.py:72
  162.7 4.7 %collective-permute-start.12 = (bf16[2,2,4,128,256]{4,3,2,1,0:T(8,128)(2,1)S(1)}, bf16[2,2,4,128,256]{4,3,2,1,0:T(8,128)(2,1)S(1)}, u32[]{:S(2)}, u32[]{:S(2)}) collective-permute-start(bf16[2,2,4,128,256]{4,3,2,1,0:T(8,128)(2,1)S(1)} %collective-permute-done.11), channel_id=1, source_target_pairs={{0,16},{16,32},{32,48},{48,64},{64,80},{80,96},{96,112},{112,0},{1... | collective-permute-start | bytes 3145736 | tf_op jit(solution)/shard_map/ppermute | solution.py:72
  169.4 18.6 %collective-permute-done.12 = bf16[2,2,4,128,256]{4,3,2,1,0:T(8,128)(2,1)S(1)} collective-permute-done((bf16[2,2,4,128,256]{4,3,2,1,0:T(8,128)(2,1)S(1)}, bf16[2,2,4,128,256]{4,3,2,1,0:T(8,128)(2,1)S(1)}, u32[]{:S(2)}, u32[]{:S(2)}) %collective-permute-start.12) | collective-permute-done | bytes 1048608 | tf_op jit(solution)/shard_map/ppermute | solution.py:72
  188.0 5.6 %collective-permute-start.13 = (bf16[2,2,4,128,256]{4,3,2,1,0:T(8,128)(2,1)S(1)}, bf16[2,2,4,128,256]{4,3,2,1,0:T(8,128)(2,1)S(1)}, u32[]{:S(2)}, u32[]{:S(2)}) collective-permute-start(bf16[2,2,4,128,256]{4,3,2,1,0:T(8,128)(2,1)S(1)} %collective-permute-done.12), channel_id=1, source_target_pairs={{0,16},{16,32},{32,48},{48,64},{64,80},{80,96},{96,112},{112,0},{1... | collective-permute-start | bytes 3145736 | tf_op jit(solution)/shard_map/ppermute | solution.py:72
  193.7 7.3 %copy.32 = bf16[2,2,128,2,4,2,256]{2,6,5,4,3,1,0:T(8,128)(2,1)} copy(bf16[2,2,128,2,4,2,256]{6,2,1,0,5,4,3:T(8,128)(2,1)} %bitcast.158) | data formatting | bytes 8388608 | tf_op jit(solution)/shard_map/transpose | solution.py:113
  201.0 12.2 %collective-permute-done.13 = bf16[2,2,4,128,256]{4,3,2,1,0:T(8,128)(2,1)S(1)} collective-permute-done((bf16[2,2,4,128,256]{4,3,2,1,0:T(8,128)(2,1)S(1)}, bf16[2,2,4,128,256]{4,3,2,1,0:T(8,128)(2,1)S(1)}, u32[]{:S(2)}, u32[]{:S(2)}) %collective-permute-start.13) | collective-permute-done | bytes 1048608 | tf_op jit(solution)/shard_map/ppermute | solution.py:72
  213.2 3.1 %fusion.43 = (bf16[2,1,128,4,8,128]{2,5,4,3,1,0:T(8,128)(2,1)S(1)}, bf16[2,1,128,4,8,128]{2,5,4,3,1,0:T(8,128)(2,1)S(1)}, bf16[2,1,128,4,8,128]{2,5,4,3,1,0:T(8,128)(2,1)S(1)}) fusion(bf16[2,2,128,4,8,128]{2,5,4,3,1,0:T(8,128)(2,1)} %bitcast.157), kind=kLoop, calls=%fused_computation.108 | loop fusion | flops 1048576 | bytes 10485760 | tf_op jit(solution)/shard_map/slice | solution.py:117
  221.8 4.6 %fusion.8 = (bf16[2,2,2,128,4,1,128]{3,6,5,4,2,0,1:T(8,128)(2,1)}, bf16[2,2,2,128,4,1,128]{3,6,5,4,2,0,1:T(8,128)(2,1)}, bf16[2,2,2,128,4,1,128]{3,6,5,4,2,0,1:T...) fusion(s32[]{:T(128)S(6)} %select_n.230, ...), kind=kLoop, calls=%fused_computation.36 | loop fusion | flops 3145728 | bytes 14680088 | tf_op jit(solution)/shard_map/stack | solution.py:118
  233.3 2.5 convolution_bitcast_fusion.7
  (94 shorter events, 47.8 us)
Async XLA Ops:
  6.5 98.6 %all-gather.4.cloned.1.call-start = ((), (), s32[]{:S(2)}) async-start(), calls=%async_computation | async-start | bytes 2621440 | tf_op jit(solution)/shard_map/all_gather | solution.py:109
  7.5 11.4 %collective-permute-start.2 = (bf16[2,2,128,128]{3,2,1,0:T(8,128)(2,1)S(1)}, bf16[2,2,128,128]{3,2,1,0:T(8,128)(2,1)S(1)}, u32[]{:S(2)}, u32[]{:S(2)}) collective-permute-start(bf16[2,2,128,128]{3,2,1,0:T(8,128)(2,1)S(1)} %get-tuple-element.23), channel_id=1, source_target_pairs={{16,0},{17,32},{18,64},{19,96},{20,128},{21,160},{22,192},{23,224}... | collective-permute-start | bytes 393224 | tf_op jit(solution)/shard_map/ppermute | solution.py:96
  9.6 10.0 %collective-permute-start.3 = (bf16[2,2,128,128]{3,2,1,0:T(8,128)(2,1)S(1)}, bf16[2,2,128,128]{3,2,1,0:T(8,128)(2,1)S(1)}, u32[]{:S(2)}, u32[]{:S(2)}) collective-permute-start(bf16[2,2,128,128]{3,2,1,0:T(8,128)(2,1)S(1)} %get-tuple-element.22), channel_id=1, source_target_pairs={{16,16},{17,48},{18,80},{19,112},{20,144},{21,176},{22,208},{23,24... | collective-permute-start | bytes 393224 | tf_op jit(solution)/shard_map/ppermute | solution.py:96
  16.9 9.4 %collective-permute-start.1 = (bf16[2,2,128,128]{3,2,1,0:T(8,128)(2,1)S(1)}, bf16[2,2,128,128]{3,2,1,0:T(8,128)(2,1)S(1)}, u32[]{:S(2)}, u32[]{:S(2)}) collective-permute-start(bf16[2,2,128,128]{3,2,1,0:T(8,128)(2,1)S(1)} %get-tuple-element.22), channel_id=1, source_target_pairs={{0,16},{1,48},{2,80},{3,112},{4,144},{5,176},{6,208},{7,240},{8,27... | collective-permute-start | bytes 393224 | tf_op jit(solution)/shard_map/ppermute | solution.py:96
  18.2 8.1 %collective-permute-start = (bf16[2,2,128,128]{3,2,1,0:T(8,128)(2,1)S(1)}, bf16[2,2,128,128]{3,2,1,0:T(8,128)(2,1)S(1)}, u32[]{:S(2)}, u32[]{:S(2)}) collective-permute-start(bf16[2,2,128,128]{3,2,1,0:T(8,128)(2,1)S(1)} %get-tuple-element.23), channel_id=1, source_target_pairs={{0,0},{1,32},{2,64},{3,96},{4,128},{5,160},{6,192},{7,224},{8,256}... | collective-permute-start | bytes 393224 | tf_op jit(solution)/shard_map/ppermute | solution.py:96
  27.7 32.2 %collective-permute-start.17 = (bf16[2,2,128,256]{3,2,1,0:T(8,128)(2,1)S(1)}, bf16[2,2,128,256]{3,2,1,0:T(8,128)(2,1)S(1)}, u32[]{:S(2)}, u32[]{:S(2)}) collective-permute-start(bf16[2,2,128,256]{3,2,1,0:T(8,128)(2,1)S(1)} %get-tuple-element.8), channel_id=1, source_target_pairs={{0,8},{8,0},{1,9},{9,1},{2,10},{10,2},{3,11},{11,3},{4,12},{12,4},... | collective-permute-start | bytes 786440 | tf_op jit(solution)/shard_map/ppermute | solution.py:49
  61.5 132.2 %all-gather.6.cloned.1.call-start = ((), (), s32[]{:S(2)}) async-start(), calls=%async_computation.1 | async-start | bytes 6291456 | tf_op jit(solution)/shard_map/all_gather | solution.py:110
  61.6 13.7 %collective-permute-start.4 = (bf16[2,2,128,256]{3,2,1,0:T(8,128)(2,1)S(1)}, bf16[2,2,128,256]{3,2,1,0:T(8,128)(2,1)S(1)}, u32[]{:S(2)}, u32[]{:S(2)}) collective-permute-start(bf16[2,2,128,256]{3,2,1,0:T(8,128)(2,1)S(1)} %get-tuple-element.8), channel_id=1, source_target_pairs={{0,128},{128,256},{256,384},{1,129},{129,257},{257,385},{2,130},{1... | collective-permute-start | bytes 786440 | tf_op jit(solution)/shard_map/ppermute | solution.py:49
  69.5 9.9 %collective-permute-start.7 = (bf16[2,2,128,256]{3,2,1,0:T(8,128)(2,1)S(1)}, bf16[2,2,128,256]{3,2,1,0:T(8,128)(2,1)S(1)}, u32[]{:S(2)}, u32[]{:S(2)}) collective-permute-start(bf16[2,2,128,256]{3,2,1,0:T(8,128)(2,1)S(1)} %get-tuple-element.8), channel_id=1, source_target_pairs={{128,0},{256,128},{384,256},{129,1},{257,129},{385,257},{130,2},{2... | collective-permute-start | bytes 786440 | tf_op jit(solution)/shard_map/ppermute | solution.py:52
  75.3 5.4 %collective-permute-start.5 = (bf16[2,2,128,256]{3,2,1,0:T(8,128)(2,1)S(1)}, bf16[2,2,128,256]{3,2,1,0:T(8,128)(2,1)S(1)}, u32[]{:S(2)}, u32[]{:S(2)}) collective-permute-start(bf16[2,2,128,256]{3,2,1,0:T(8,128)(2,1)S(1)} %collective-permute-done.4), channel_id=1, source_target_pairs={{128,256},{256,384},{129,257},{257,385},{130,258},{258,386},{131,2... | collective-permute-start | bytes 786440 | tf_op jit(solution)/shard_map/ppermute | solution.py:49
  79.4 9.1 %collective-permute-start.8 = (bf16[2,2,128,256]{3,2,1,0:T(8,128)(2,1)S(1)}, bf16[2,2,128,256]{3,2,1,0:T(8,128)(2,1)S(1)}, u32[]{:S(2)}, u32[]{:S(2)}) collective-permute-start(bf16[2,2,128,256]{3,2,1,0:T(8,128)(2,1)S(1)} %collective-permute-done.7), channel_id=1, source_target_pairs={{128,0},{256,128},{129,1},{257,129},{130,2},{258,130},{131,3},{259... | collective-permute-start | bytes 786440 | tf_op jit(solution)/shard_map/ppermute | solution.py:52
  80.7 9.1 %collective-permute-start.6 = (bf16[2,2,128,256]{3,2,1,0:T(8,128)(2,1)S(1)}, bf16[2,2,128,256]{3,2,1,0:T(8,128)(2,1)S(1)}, u32[]{:S(2)}, u32[]{:S(2)}) collective-permute-start(bf16[2,2,128,256]{3,2,1,0:T(8,128)(2,1)S(1)} %collective-permute-done.5), channel_id=1, source_target_pairs={{256,384},{257,385},{258,386},{259,387},{260,388},{261,389},{262,3... | collective-permute-start | bytes 786440 | tf_op jit(solution)/shard_map/ppermute | solution.py:49
  88.5 8.3 %collective-permute-start.9 = (bf16[2,2,128,256]{3,2,1,0:T(8,128)(2,1)S(1)}, bf16[2,2,128,256]{3,2,1,0:T(8,128)(2,1)S(1)}, u32[]{:S(2)}, u32[]{:S(2)}) collective-permute-start(bf16[2,2,128,256]{3,2,1,0:T(8,128)(2,1)S(1)} %collective-permute-done.8), channel_id=1, source_target_pairs={{128,0},{129,1},{130,2},{131,3},{132,4},{133,5},{134,6},{135,7},{1... | collective-permute-start | bytes 786440 | tf_op jit(solution)/shard_map/ppermute | solution.py:52
  108.4 26.6 %collective-permute-start.10 = (bf16[2,2,4,128,256]{4,3,2,1,0:T(8,128)(2,1)S(1)}, bf16[2,2,4,128,256]{4,3,2,1,0:T(8,128)(2,1)S(1)}, u32[]{:S(2)}, u32[]{:S(2)}) collective-permute-start(bf16[2,2,4,128,256]{4,3,2,1,0:T(8,128)(2,1)S(1)} %fusion.34), channel_id=1, source_target_pairs={{0,16},{16,32},{32,48},{48,64},{64,80},{80,96},{96,112},{112,0},{1... | collective-permute-start | bytes 3145736 | tf_op jit(solution)/shard_map/ppermute | solution.py:72
  110.7 28.8 %collective-permute-start.14 = (bf16[2,2,4,128,256]{4,3,2,1,0:T(8,128)(2,1)S(1)}, bf16[2,2,4,128,256]{4,3,2,1,0:T(8,128)(2,1)S(1)}, u32[]{:S(2)}, u32[]{:S(2)}) collective-permute-start(bf16[2,2,4,128,256]{4,3,2,1,0:T(8,128)(2,1)S(1)} %fusion.34), channel_id=1, source_target_pairs={{16,0},{32,16},{48,32},{64,48},{80,64},{96,80},{112,96},{0,112},{1... | collective-permute-start | bytes 3145736 | tf_op jit(solution)/shard_map/ppermute | solution.py:75
  136.0 25.8 %collective-permute-start.11 = (bf16[2,2,4,128,256]{4,3,2,1,0:T(8,128)(2,1)S(1)}, bf16[2,2,4,128,256]{4,3,2,1,0:T(8,128)(2,1)S(1)}, u32[]{:S(2)}, u32[]{:S(2)}) collective-permute-start(bf16[2,2,4,128,256]{4,3,2,1,0:T(8,128)(2,1)S(1)} %collective-permute-done.10), channel_id=1, source_target_pairs={{0,16},{16,32},{32,48},{48,64},{64,80},{80,96},{96,112},{112,0},{1... | collective-permute-start | bytes 3145736 | tf_op jit(solution)/shard_map/ppermute | solution.py:72
  139.5 48.5 %copy-start.13 = (bf16[2,2,4,128,256]{4,3,2,1,0:T(8,128)(2,1)}, bf16[2,2,4,128,256]{4,3,2,1,0:T(8,128)(2,1)S(1)}, u32[]{:S(2)}) copy-start(bf16[2,2,4,128,256]{4,3,2,1,0:T(8,128)(2,1)S(1)} %collective-permute-done.14) | copy-start | bytes 3145732
  139.5 27.9 %collective-permute-start.15 = (bf16[2,2,4,128,256]{4,3,2,1,0:T(8,128)(2,1)S(1)}, bf16[2,2,4,128,256]{4,3,2,1,0:T(8,128)(2,1)}, u32[]{:S(2)}, u32[]{:S(2)}) collective-permute-start(bf16[2,2,4,128,256]{4,3,2,1,0:T(8,128)(2,1)S(1)} %collective-permute-done.14), channel_id=1, source_target_pairs={{16,0},{32,16},{48,32},{64,48},{80,64},{96,80},{112,96},{0,112},{1... | collective-permute-start | bytes 3145736 | tf_op jit(solution)/shard_map/ppermute | solution.py:75
  162.7 25.2 %collective-permute-start.12 = (bf16[2,2,4,128,256]{4,3,2,1,0:T(8,128)(2,1)S(1)}, bf16[2,2,4,128,256]{4,3,2,1,0:T(8,128)(2,1)S(1)}, u32[]{:S(2)}, u32[]{:S(2)}) collective-permute-start(bf16[2,2,4,128,256]{4,3,2,1,0:T(8,128)(2,1)S(1)} %collective-permute-done.11), channel_id=1, source_target_pairs={{0,16},{16,32},{32,48},{48,64},{64,80},{80,96},{96,112},{112,0},{1... | collective-permute-start | bytes 3145736 | tf_op jit(solution)/shard_map/ppermute | solution.py:72
  167.5 33.6 %collective-permute-start.16 = (bf16[2,2,4,128,256]{4,3,2,1,0:T(8,128)(2,1)}, bf16[2,2,4,128,256]{4,3,2,1,0:T(8,128)(2,1)}, u32[]{:S(2)}, u32[]{:S(2)}) collective-permute-start(bf16[2,2,4,128,256]{4,3,2,1,0:T(8,128)(2,1)} %collective-permute-done.15), channel_id=1, source_target_pairs={{16,0},{32,16},{48,32},{64,48},{80,64},{96,80},{112,96},{0,112},{1... | collective-permute-start | bytes 3145736 | tf_op jit(solution)/shard_map/ppermute | solution.py:75
  188.0 13.1 %copy-start.9 = (bf16[2,2,4,128,256]{4,3,2,1,0:T(8,128)(2,1)}, bf16[2,2,4,128,256]{4,3,2,1,0:T(8,128)(2,1)S(1)}, u32[]{:S(2)}) copy-start(bf16[2,2,4,128,256]{4,3,2,1,0:T(8,128)(2,1)S(1)} %collective-permute-done.12) | copy-start | bytes 3145732
  188.0 25.3 %collective-permute-start.13 = (bf16[2,2,4,128,256]{4,3,2,1,0:T(8,128)(2,1)S(1)}, bf16[2,2,4,128,256]{4,3,2,1,0:T(8,128)(2,1)S(1)}, u32[]{:S(2)}, u32[]{:S(2)}) collective-permute-start(bf16[2,2,4,128,256]{4,3,2,1,0:T(8,128)(2,1)S(1)} %collective-permute-done.12), channel_id=1, source_target_pairs={{0,16},{16,32},{32,48},{48,64},{64,80},{80,96},{96,112},{112,0},{1... | collective-permute-start | bytes 3145736 | tf_op jit(solution)/shard_map/ppermute | solution.py:72
  241.1 4.0 %copy-start.3 = (bf16[2,2,2,128,4,1,128]{6,3,4,2,1,0,5:T(8,128)(2,1)S(1)}, bf16[2,2,2,128,4,1,128]{6,3,4,2,1,0,5:T(8,128)(2,1)}, u32[]{:S(2)}) copy-start(bf16[2,2,2,128,4,1,128]{6,3,4,2,1,0,5:T(8,128)(2,1)} %copy.35) | copy-start | bytes 3145732
  241.1 4.0 %copy-start.14 = (bf16[2,2,4,128,256]{4,3,2,1,0:T(8,128)(2,1)S(1)}, bf16[2,2,4,128,256]{4,3,2,1,0:T(8,128)(2,1)}, u32[]{:S(2)}) copy-start(bf16[2,2,4,128,256]{4,3,2,1,0:T(8,128)(2,1)} %copy-done.13) | copy-start | bytes 3145732
  (12 other events, 23.2 us)
Sparse Core Ops, SparseCore 0:
  61.7 43.4 all-gather.3
  108.5 21.8 all-gather.5

commit v13 on v11

--- a/solution.py
+++ b/solution.py
@@ -116,10 +116,11 @@
     blocks, row_panel = ring_blocks(z_cols, "y", row_panel)
     real, imag = row_panel[:, 0], row_panel[:, 1]
     paired = jnp.stack((jnp.stack((real, -imag), axis=1), jnp.stack((imag, real), axis=1)), axis=1)
+    paired = jnp.transpose(paired, (5, 0, 1, 2, 4, 3, 6))
     product = None
     for offset, col_block in blocks:
-        row_block = lax.dynamic_index_in_dim(paired, (me_y - offset) % y_n, axis=5, keepdims=False)
-        part = jnp.einsum("fgcizk,fczkj->fgij", row_block, col_block, preferred_element_type=jnp.float32)
+        row_block = lax.dynamic_index_in_dim(paired, (me_y - offset) % y_n, axis=0, keepdims=False)
+        part = jnp.einsum("fgczik,fczkj->fgij", row_block, col_block, preferred_element_type=jnp.float32)
         product = part if product is None else product + part
     scale_factor = jnp.float32(float(NS) ** (-0.5))
     return product * scale_factor

time: 255 us -> 236 us (0.925)
  local copies, waits for them, and re-layouts: 32.7 us -> 20.2 us
  other arithmetic: 11.4 us -> 5.73 us
    dynamic_slice x8 -> x0, local copies, waits for them, and re-layouts: 15 us -> none  [per_device(): lax.dynamic_index_in_dim(paired, (me_y - offset) % y_n, axis=5, keepdims=...]
    optimization_barrier x0 -> x1, local copies, waits for them, and re-layouts: none -> 6.47 us  [ring_blocks(): up, dn, held = lax.optimization_barrier((up, dn, held))]
    another operation x3 -> x1, other arithmetic: 6.28 us -> 0.64 us  [per_device(): jnp.stack((jnp.stack((real, -imag), axis=1), jnp.stack((imag, real), axis...]
    unnamed x31 -> x9, local copies, waits for them, and re-layouts: 4.7 us -> 0.79 us
  transfers between devices with their start and end apart: 20 -> 20, of which waited for: 12 -> 12; matrix products, arithmetic and copies ran while one was open for 7% -> 8% of each run, Pallas kernels for 0% -> 0%
where the time goes in v13:
time: 236 us; the launch traced here: 232 us
  waiting for transfers between devices  118 us (50%)
  starting transfers between devices  66.2 us (28%)
  local copies, waits for them, and re-layouts  20.2 us (9%)
  between operations  14 us (6%)
  matrix products  8.13 us (3%)
  other arithmetic  5.73 us (2%)
    ppermute x4, waiting for transfers between devices, ring_blocks(): up = lax.ppermute(up, axis, right)  66.2 us
    ppermute x4, starting transfers between devices, stream_gather(): up = lax.ppermute(up, axis, perm(k, 1))  28.9 us
    all_gather x1, waiting for transfers between devices, per_device(): rows = lax.all_gather(rows, 'x', axis=1)  15.7 us
    ppermute x4, waiting for transfers between devices, stream_gather(): up = lax.ppermute(up, axis, perm(k, 1))  14 us
    ppermute x4, starting transfers between devices, mirrored_pieces(): got.append(lax.ppermute(part, SHOT + RECV, perm))  13.2 us
    ppermute x4, starting transfers between devices, ring_blocks(): up = lax.ppermute(up, axis, right)  12.5 us
    ppermute x3, waiting for transfers between devices, stream_gather(): dn = lax.ppermute(dn, axis, perm(k, -1))  10.5 us
    dot_general x8, matrix products, per_device(): jnp.einsum('fgczik,fczkj->fgij', row_block, col_block, preferred_element_...  8.13 us
  transfers between devices with their start and end apart: 20, of which 12 were waited for; matrix products, arithmetic and copies ran while one was open for 8% of the time, Pallas kernels for 0%

profile of v13, /device:TPU:56, one launch (start us, length us, event | category | flops | bytes accessed | tf_op | source)
XLA Modules:
  0.0 232.3 jit_solution(5799231508458998559)
XLA Ops:
  9.5 7.8 %collective-permute-start.2 = (bf16[2,2,128,128]{3,2,1,0:T(8,128)(2,1)S(1)}, bf16[2,2,128,128]{3,2,1,0:T(8,128)(2,1)S(1)}, u32[]{:S(2)}, u32[]{:S(2)}) collective-permute-start(bf16[2,2,128,128]{3,2,1,0:T(8,128)(2,1)S(1)} %get-tuple-element.17), channel_id=1, source_target_pairs={{16,0},{17,32},{18,64},{19,96},{20,128},{21,160},{22,192},{23,224}... | collective-permute-start | bytes 393224 | tf_op jit(solution)/shard_map/ppermute | solution.py:96
  17.3 3.4 %collective-permute-start.3 = (bf16[2,2,128,128]{3,2,1,0:T(8,128)(2,1)S(1)}, bf16[2,2,128,128]{3,2,1,0:T(8,128)(2,1)S(1)}, u32[]{:S(2)}, u32[]{:S(2)}) collective-permute-start(bf16[2,2,128,128]{3,2,1,0:T(8,128)(2,1)S(1)} %get-tuple-element.16), channel_id=1, source_target_pairs={{16,16},{17,48},{18,80},{19,112},{20,144},{21,176},{22,208},{23,24... | collective-permute-start | bytes 393224 | tf_op jit(solution)/shard_map/ppermute | solution.py:96
  21.5 5.4 %collective-permute-done.3 = bf16[2,2,128,128]{3,2,1,0:T(8,128)(2,1)S(1)} collective-permute-done((bf16[2,2,128,128]{3,2,1,0:T(8,128)(2,1)S(1)}, bf16[2,2,128,128]{3,2,1,0:T(8,128)(2,1)S(1)}, u32[]{:S(2)}, u32[]{:S(2)}) %collective-permute-start.3) | collective-permute-done | bytes 131104 | tf_op jit(solution)/shard_map/ppermute | solution.py:96
  28.4 19.7 %collective-permute-start.16 = (bf16[2,2,128,256]{3,2,1,0:T(8,128)(2,1)S(1)}, bf16[2,2,128,256]{3,2,1,0:T(8,128)(2,1)S(1)}, u32[]{:S(2)}, u32[]{:S(2)}) collective-permute-start(bf16[2,2,128,256]{3,2,1,0:T(8,128)(2,1)S(1)} %get-tuple-element.10), channel_id=1, source_target_pairs={{0,8},{8,0},{1,9},{9,1},{2,10},{10,2},{3,11},{11,3},{4,12},{12,4},... | collective-permute-start | bytes 786440 | tf_op jit(solution)/shard_map/ppermute | solution.py:49
  48.1 9.5 %collective-permute-done.16 = bf16[2,2,128,256]{3,2,1,0:T(8,128)(2,1)S(1)} collective-permute-done((bf16[2,2,128,256]{3,2,1,0:T(8,128)(2,1)S(1)}, bf16[2,2,128,256]{3,2,1,0:T(8,128)(2,1)S(1)}, u32[]{:S(2)}, u32[]{:S(2)}) %collective-permute-start.16) | collective-permute-done | bytes 262176 | tf_op jit(solution)/shard_map/ppermute | solution.py:49
  59.2 7.8 %collective-permute-start.4 = (bf16[2,2,128,256]{3,2,1,0:T(8,128)(2,1)S(1)}, bf16[2,2,128,256]{3,2,1,0:T(8,128)(2,1)S(1)}, u32[]{:S(2)}, u32[]{:S(2)}) collective-permute-start(bf16[2,2,128,256]{3,2,1,0:T(8,128)(2,1)S(1)} %get-tuple-element.10), channel_id=1, source_target_pairs={{0,128},{128,256},{256,384},{1,129},{129,257},{257,385},{2,130},{1... | collective-permute-start | bytes 786440 | tf_op jit(solution)/shard_map/ppermute | solution.py:49
  68.4 4.5 %collective-permute-done.4 = bf16[2,2,128,256]{3,2,1,0:T(8,128)(2,1)S(1)} collective-permute-done((bf16[2,2,128,256]{3,2,1,0:T(8,128)(2,1)S(1)}, bf16[2,2,128,256]{3,2,1,0:T(8,128)(2,1)S(1)}, u32[]{:S(2)}, u32[]{:S(2)}) %collective-permute-start.4) | collective-permute-done | bytes 262176 | tf_op jit(solution)/shard_map/ppermute | solution.py:49
  73.6 3.4 %collective-permute-done.7 = bf16[2,2,128,256]{3,2,1,0:T(8,128)(2,1)S(1)} collective-permute-done((bf16[2,2,128,256]{3,2,1,0:T(8,128)(2,1)S(1)}, bf16[2,2,128,256]{3,2,1,0:T(8,128)(2,1)S(1)}, u32[]{:S(2)}, u32[]{:S(2)}) %collective-permute-start.7) | collective-permute-done | bytes 262176 | tf_op jit(solution)/shard_map/ppermute | solution.py:52
  79.1 7.0 %collective-permute-done.8 = bf16[2,2,128,256]{3,2,1,0:T(8,128)(2,1)S(1)} collective-permute-done((bf16[2,2,128,256]{3,2,1,0:T(8,128)(2,1)S(1)}, bf16[2,2,128,256]{3,2,1,0:T(8,128)(2,1)S(1)}, u32[]{:S(2)}, u32[]{:S(2)}) %collective-permute-start.8) | collective-permute-done | bytes 262176 | tf_op jit(solution)/shard_map/ppermute | solution.py:52
  87.4 15.7 %all-gather.4.cloned.1.call-done = bf16[2,4,2,2,128,256]{5,4,3,2,0,1:T(8,128)(2,1)} async-done(((bf16[2,1,2,2,128,256]{5,4,3,2,0,1:T(8,128)(2,1)}), bf16[2,4,2,2,128,256]{5,4,3,2,0,1:T(8,128)(2,1)}) %all-gather.4.cloned.1.call-update) | async-done | bytes 2097168 | tf_op jit(solution)/shard_map/all_gather | solution.py:109
  103.1 3.2 %copy.21 = bf16[2,4,2,2,128,256]{5,4,3,2,1,0:T(8,128)(2,1)} copy(bf16[2,4,2,2,128,256]{5,4,3,2,0,1:T(8,128)(2,1)} %all-gather.4.cloned.1.call-done) | data formatting | bytes 4194304 | tf_op jit(solution)/shard_map/all_gather | solution.py:109
  107.3 2.3 collective-permute-start.10
  109.6 3.5 %collective-permute-start.13 = (bf16[2,2,4,128,256]{4,3,2,1,0:T(8,128)(2,1)S(1)}, bf16[2,2,4,128,256]{4,3,2,1,0:T(8,128)(2,1)S(1)}, u32[]{:S(2)}, u32[]{:S(2)}) collective-permute-start(bf16[2,2,4,128,256]{4,3,2,1,0:T(8,128)(2,1)S(1)} %fusion.42), channel_id=1, source_target_pairs={{16,0},{32,16},{48,32},{64,48},{80,64},{96,80},{112,96},{0,112},{1... | collective-permute-start | bytes 3145736 | tf_op jit(solution)/shard_map/ppermute | solution.py:75
  113.1 20.8 %collective-permute-done.10 = bf16[2,2,4,128,256]{4,3,2,1,0:T(8,128)(2,1)S(1)} collective-permute-done((bf16[2,2,4,128,256]{4,3,2,1,0:T(8,128)(2,1)S(1)}, bf16[2,2,4,128,256]{4,3,2,1,0:T(8,128)(2,1)S(1)}, u32[]{:S(2)}, u32[]{:S(2)}) %collective-permute-start.10) | collective-permute-done | bytes 1048608 | tf_op jit(solution)/shard_map/ppermute | solution.py:72
  133.9 3.5 %collective-permute-start.11 = (bf16[2,2,4,128,256]{4,3,2,1,0:T(8,128)(2,1)S(1)}, bf16[2,2,4,128,256]{4,3,2,1,0:T(8,128)(2,1)}, u32[]{:S(2)}, u32[]{:S(2)}) collective-permute-start(bf16[2,2,4,128,256]{4,3,2,1,0:T(8,128)(2,1)S(1)} %collective-permute-done.10), channel_id=1, source_target_pairs={{0,16},{16,32},{32,48},{48,64},{64,80},{80,96},{96,112},{112,0},{1... | collective-permute-start | bytes 3145736 | tf_op jit(solution)/shard_map/ppermute | solution.py:72
  137.4 2.3 collective-permute-start.14
  139.7 20.0 %collective-permute-done.11 = bf16[2,2,4,128,256]{4,3,2,1,0:T(8,128)(2,1)} collective-permute-done((bf16[2,2,4,128,256]{4,3,2,1,0:T(8,128)(2,1)S(1)}, bf16[2,2,4,128,256]{4,3,2,1,0:T(8,128)(2,1)}, u32[]{:S(2)}, u32[]{:S(2)}) %collective-permute-start.11) | collective-permute-done | bytes 1048608 | tf_op jit(solution)/shard_map/ppermute | solution.py:72
  159.8 4.7 %collective-permute-start.12 = (bf16[2,2,4,128,256]{4,3,2,1,0:T(8,128)(2,1)}, bf16[2,2,4,128,256]{4,3,2,1,0:T(8,128)(2,1)S(1)}, u32[]{:S(2)}, u32[]{:S(2)}) collective-permute-start(bf16[2,2,4,128,256]{4,3,2,1,0:T(8,128)(2,1)} %collective-permute-done.11), channel_id=1, source_target_pairs={{0,16},{16,32},{32,48},{48,64},{64,80},{80,96},{96,112},{112,0},{1... | collective-permute-start | bytes 3145736 | tf_op jit(solution)/shard_map/ppermute | solution.py:72
  166.6 7.4 %copy.22 = bf16[2,2,128,2,4,2,256]{2,6,5,4,3,1,0:T(8,128)(2,1)} copy(bf16[2,2,128,2,4,2,256]{6,2,1,0,5,4,3:T(8,128)(2,1)} %bitcast.176) | data formatting | bytes 8388608 | tf_op jit(solution)/shard_map/transpose | solution.py:113
  173.9 11.4 %collective-permute-done.12 = bf16[2,2,4,128,256]{4,3,2,1,0:T(8,128)(2,1)S(1)} collective-permute-done((bf16[2,2,4,128,256]{4,3,2,1,0:T(8,128)(2,1)}, bf16[2,2,4,128,256]{4,3,2,1,0:T(8,128)(2,1)S(1)}, u32[]{:S(2)}, u32[]{:S(2)}) %collective-permute-start.12) | collective-permute-done | bytes 1048608 | tf_op jit(solution)/shard_map/ppermute | solution.py:72
  185.3 5.3 %collective-permute-done.15 = bf16[2,2,4,128,256]{4,3,2,1,0:T(8,128)(2,1)} collective-permute-done((bf16[2,2,4,128,256]{4,3,2,1,0:T(8,128)(2,1)}, bf16[2,2,4,128,256]{4,3,2,1,0:T(8,128)(2,1)}, u32[]{:S(2)}, u32[]{:S(2)}) %collective-permute-start.15) | collective-permute-done | bytes 1048608 | tf_op jit(solution)/shard_map/ppermute | solution.py:75
  190.7 6.5 %copy.23 = bf16[2,2,128,4,8,128]{5,2,3,1,0,4:T(8,128)(2,1)} copy(bf16[2,2,128,4,8,128]{2,5,4,3,1,0:T(8,128)(2,1)} %bitcast.175) | data formatting | bytes 8388608 | tf_op jit(solution)/shard_map/optimization_barrier | solution.py:78
  197.1 2.8 %fusion.67 = (bf16[2,1,128,4,8,128]{5,2,3,1,0,4:T(8,128)(2,1)S(1)}, bf16[2,1,128,4,8,128]{5,2,3,1,0,4:T(8,128)(2,1)S(1)}, bf16[2,1,128,4,8,128]{5,2,3,1,0,4:T(8,128)(2,1)S(1)}) fusion(bf16[2,2,128,4,8,128]{5,2,3,1,0,4:T(8,128)(2,1)} %copy.23), kind=kLoop, calls=%fused_computation.124 | loop fusion | flops 1048576 | bytes 10485760 | tf_op jit(solution)/shard_map/slice | solution.py:117
  209.6 14.1 %collective-permute-done.17 = bf16[2,2,4,128,256]{4,3,2,1,0:T(8,128)(2,1)S(1)} collective-permute-done((bf16[2,2,4,128,256]{4,3,2,1,0:T(8,128)(2,1)S(1)}, bf16[2,2,4,128,256]{4,3,2,1,0:T(8,128)(2,1)S(1)}, u32[]{:S(2)}, u32[]{:S(2)}) %collective-permute-start.17) | collective-permute-done | bytes 1048608 | tf_op jit(solution)/shard_map/ppermute | solution.py:72
  (57 shorter events, 26.2 us)
Async XLA Ops:
  6.5 96.6 %all-gather.4.cloned.1.call-start = ((), (), s32[]{:S(2)}) async-start(), calls=%async_computation | async-start | bytes 2621440 | tf_op jit(solution)/shard_map/all_gather | solution.py:109
  7.5 13.3 %collective-permute-start = (bf16[2,2,128,128]{3,2,1,0:T(8,128)(2,1)S(1)}, bf16[2,2,128,128]{3,2,1,0:T(8,128)(2,1)S(1)}, u32[]{:S(2)}, u32[]{:S(2)}) collective-permute-start(bf16[2,2,128,128]{3,2,1,0:T(8,128)(2,1)S(1)} %get-tuple-element.17), channel_id=1, source_target_pairs={{0,0},{1,32},{2,64},{3,96},{4,128},{5,160},{6,192},{7,224},{8,256}... | collective-permute-start | bytes 393224 | tf_op jit(solution)/shard_map/ppermute | solution.py:96
  8.2 13.3 %collective-permute-start.1 = (bf16[2,2,128,128]{3,2,1,0:T(8,128)(2,1)S(1)}, bf16[2,2,128,128]{3,2,1,0:T(8,128)(2,1)S(1)}, u32[]{:S(2)}, u32[]{:S(2)}) collective-permute-start(bf16[2,2,128,128]{3,2,1,0:T(8,128)(2,1)S(1)} %get-tuple-element.16), channel_id=1, source_target_pairs={{0,16},{1,48},{2,80},{3,112},{4,144},{5,176},{6,208},{7,240},{8,27... | collective-permute-start | bytes 393224 | tf_op jit(solution)/shard_map/ppermute | solution.py:96
  9.5 12.0 %collective-permute-start.2 = (bf16[2,2,128,128]{3,2,1,0:T(8,128)(2,1)S(1)}, bf16[2,2,128,128]{3,2,1,0:T(8,128)(2,1)S(1)}, u32[]{:S(2)}, u32[]{:S(2)}) collective-permute-start(bf16[2,2,128,128]{3,2,1,0:T(8,128)(2,1)S(1)} %get-tuple-element.17), channel_id=1, source_target_pairs={{16,0},{17,32},{18,64},{19,96},{20,128},{21,160},{22,192},{23,224}... | collective-permute-start | bytes 393224 | tf_op jit(solution)/shard_map/ppermute | solution.py:96
  17.3 9.6 %collective-permute-start.3 = (bf16[2,2,128,128]{3,2,1,0:T(8,128)(2,1)S(1)}, bf16[2,2,128,128]{3,2,1,0:T(8,128)(2,1)S(1)}, u32[]{:S(2)}, u32[]{:S(2)}) collective-permute-start(bf16[2,2,128,128]{3,2,1,0:T(8,128)(2,1)S(1)} %get-tuple-element.16), channel_id=1, source_target_pairs={{16,16},{17,48},{18,80},{19,112},{20,144},{21,176},{22,208},{23,24... | collective-permute-start | bytes 393224 | tf_op jit(solution)/shard_map/ppermute | solution.py:96
  28.4 29.2 %collective-permute-start.16 = (bf16[2,2,128,256]{3,2,1,0:T(8,128)(2,1)S(1)}, bf16[2,2,128,256]{3,2,1,0:T(8,128)(2,1)S(1)}, u32[]{:S(2)}, u32[]{:S(2)}) collective-permute-start(bf16[2,2,128,256]{3,2,1,0:T(8,128)(2,1)S(1)} %get-tuple-element.10), channel_id=1, source_target_pairs={{0,8},{8,0},{1,9},{9,1},{2,10},{10,2},{3,11},{11,3},{4,12},{12,4},... | collective-permute-start | bytes 786440 | tf_op jit(solution)/shard_map/ppermute | solution.py:49
  59.2 107.4 %all-gather.6.cloned.1.call-start = ((), (), s32[]{:S(2)}) async-start(), calls=%async_computation.1 | async-start | bytes 6291456 | tf_op jit(solution)/shard_map/all_gather | solution.py:110
  59.2 13.7 %collective-permute-start.4 = (bf16[2,2,128,256]{3,2,1,0:T(8,128)(2,1)S(1)}, bf16[2,2,128,256]{3,2,1,0:T(8,128)(2,1)S(1)}, u32[]{:S(2)}, u32[]{:S(2)}) collective-permute-start(bf16[2,2,128,256]{3,2,1,0:T(8,128)(2,1)S(1)} %get-tuple-element.10), channel_id=1, source_target_pairs={{0,128},{128,256},{256,384},{1,129},{129,257},{257,385},{2,130},{1... | collective-permute-start | bytes 786440 | tf_op jit(solution)/shard_map/ppermute | solution.py:49
  67.1 9.9 %collective-permute-start.7 = (bf16[2,2,128,256]{3,2,1,0:T(8,128)(2,1)S(1)}, bf16[2,2,128,256]{3,2,1,0:T(8,128)(2,1)S(1)}, u32[]{:S(2)}, u32[]{:S(2)}) collective-permute-start(bf16[2,2,128,256]{3,2,1,0:T(8,128)(2,1)S(1)} %get-tuple-element.10), channel_id=1, source_target_pairs={{128,0},{256,128},{384,256},{129,1},{257,129},{385,257},{130,2},{2... | collective-permute-start | bytes 786440 | tf_op jit(solution)/shard_map/ppermute | solution.py:52
  72.9 5.4 %collective-permute-start.5 = (bf16[2,2,128,256]{3,2,1,0:T(8,128)(2,1)S(1)}, bf16[2,2,128,256]{3,2,1,0:T(8,128)(2,1)S(1)}, u32[]{:S(2)}, u32[]{:S(2)}) collective-permute-start(bf16[2,2,128,256]{3,2,1,0:T(8,128)(2,1)S(1)} %collective-permute-done.4), channel_id=1, source_target_pairs={{128,256},{256,384},{129,257},{257,385},{130,258},{258,386},{131,2... | collective-permute-start | bytes 786440 | tf_op jit(solution)/shard_map/ppermute | solution.py:49
  77.0 9.1 %collective-permute-start.8 = (bf16[2,2,128,256]{3,2,1,0:T(8,128)(2,1)S(1)}, bf16[2,2,128,256]{3,2,1,0:T(8,128)(2,1)S(1)}, u32[]{:S(2)}, u32[]{:S(2)}) collective-permute-start(bf16[2,2,128,256]{3,2,1,0:T(8,128)(2,1)S(1)} %collective-permute-done.7), channel_id=1, source_target_pairs={{128,0},{256,128},{129,1},{257,129},{130,2},{258,130},{131,3},{259... | collective-permute-start | bytes 786440 | tf_op jit(solution)/shard_map/ppermute | solution.py:52
  78.3 28.0 %collective-permute-start.6 = (bf16[2,2,128,256]{3,2,1,0:T(8,128)(2,1)S(1)}, bf16[2,2,128,256]{3,2,1,0:T(8,128)(2,1)S(1)}, u32[]{:S(2)}, u32[]{:S(2)}) collective-permute-start(bf16[2,2,128,256]{3,2,1,0:T(8,128)(2,1)S(1)} %collective-permute-done.5), channel_id=1, source_target_pairs={{256,384},{257,385},{258,386},{259,387},{260,388},{261,389},{262,3... | collective-permute-start | bytes 786440 | tf_op jit(solution)/shard_map/ppermute | solution.py:49
  86.1 20.3 %collective-permute-start.9 = (bf16[2,2,128,256]{3,2,1,0:T(8,128)(2,1)S(1)}, bf16[2,2,128,256]{3,2,1,0:T(8,128)(2,1)S(1)}, u32[]{:S(2)}, u32[]{:S(2)}) collective-permute-start(bf16[2,2,128,256]{3,2,1,0:T(8,128)(2,1)S(1)} %collective-permute-done.8), channel_id=1, source_target_pairs={{128,0},{129,1},{130,2},{131,3},{132,4},{133,5},{134,6},{135,7},{1... | collective-permute-start | bytes 786440 | tf_op jit(solution)/shard_map/ppermute | solution.py:52
  107.3 26.6 %collective-permute-start.10 = (bf16[2,2,4,128,256]{4,3,2,1,0:T(8,128)(2,1)S(1)}, bf16[2,2,4,128,256]{4,3,2,1,0:T(8,128)(2,1)S(1)}, u32[]{:S(2)}, u32[]{:S(2)}) collective-permute-start(bf16[2,2,4,128,256]{4,3,2,1,0:T(8,128)(2,1)S(1)} %fusion.42), channel_id=1, source_target_pairs={{0,16},{16,32},{32,48},{48,64},{64,80},{80,96},{96,112},{112,0},{1... | collective-permute-start | bytes 3145736 | tf_op jit(solution)/shard_map/ppermute | solution.py:72
  109.6 27.8 %collective-permute-start.13 = (bf16[2,2,4,128,256]{4,3,2,1,0:T(8,128)(2,1)S(1)}, bf16[2,2,4,128,256]{4,3,2,1,0:T(8,128)(2,1)S(1)}, u32[]{:S(2)}, u32[]{:S(2)}) collective-permute-start(bf16[2,2,4,128,256]{4,3,2,1,0:T(8,128)(2,1)S(1)} %fusion.42), channel_id=1, source_target_pairs={{16,0},{32,16},{48,32},{64,48},{80,64},{96,80},{112,96},{0,112},{1... | collective-permute-start | bytes 3145736 | tf_op jit(solution)/shard_map/ppermute | solution.py:75
  133.9 30.6 %copy-start = (bf16[2,2,4,128,256]{4,3,2,1,0:T(8,128)(2,1)}, bf16[2,2,4,128,256]{4,3,2,1,0:T(8,128)(2,1)S(1)}, u32[]{:S(2)}) copy-start(bf16[2,2,4,128,256]{4,3,2,1,0:T(8,128)(2,1)S(1)} %collective-permute-done.10) | copy-start | bytes 3145732
  133.9 25.9 %collective-permute-start.11 = (bf16[2,2,4,128,256]{4,3,2,1,0:T(8,128)(2,1)S(1)}, bf16[2,2,4,128,256]{4,3,2,1,0:T(8,128)(2,1)}, u32[]{:S(2)}, u32[]{:S(2)}) collective-permute-start(bf16[2,2,4,128,256]{4,3,2,1,0:T(8,128)(2,1)S(1)} %collective-permute-done.10), channel_id=1, source_target_pairs={{0,16},{16,32},{32,48},{48,64},{64,80},{80,96},{96,112},{112,0},{1... | collective-permute-start | bytes 3145736 | tf_op jit(solution)/shard_map/ppermute | solution.py:72
  137.4 27.1 %collective-permute-start.14 = (bf16[2,2,4,128,256]{4,3,2,1,0:T(8,128)(2,1)S(1)}, bf16[2,2,4,128,256]{4,3,2,1,0:T(8,128)(2,1)}, u32[]{:S(2)}, u32[]{:S(2)}) collective-permute-start(bf16[2,2,4,128,256]{4,3,2,1,0:T(8,128)(2,1)S(1)} %collective-permute-done.13), channel_id=1, source_target_pairs={{16,0},{32,16},{48,32},{64,48},{80,64},{96,80},{112,96},{0,112},{1... | collective-permute-start | bytes 3145736 | tf_op jit(solution)/shard_map/ppermute | solution.py:75
  159.8 25.6 %collective-permute-start.12 = (bf16[2,2,4,128,256]{4,3,2,1,0:T(8,128)(2,1)}, bf16[2,2,4,128,256]{4,3,2,1,0:T(8,128)(2,1)S(1)}, u32[]{:S(2)}, u32[]{:S(2)}) collective-permute-start(bf16[2,2,4,128,256]{4,3,2,1,0:T(8,128)(2,1)} %collective-permute-done.11), channel_id=1, source_target_pairs={{0,16},{16,32},{32,48},{48,64},{64,80},{80,96},{96,112},{112,0},{1... | collective-permute-start | bytes 3145736 | tf_op jit(solution)/shard_map/ppermute | solution.py:72
  164.5 26.2 %collective-permute-start.15 = (bf16[2,2,4,128,256]{4,3,2,1,0:T(8,128)(2,1)}, bf16[2,2,4,128,256]{4,3,2,1,0:T(8,128)(2,1)}, u32[]{:S(2)}, u32[]{:S(2)}) collective-permute-start(bf16[2,2,4,128,256]{4,3,2,1,0:T(8,128)(2,1)} %collective-permute-done.14), channel_id=1, source_target_pairs={{16,0},{32,16},{48,32},{64,48},{80,64},{96,80},{112,96},{0,112},{1... | collective-permute-start | bytes 3145736 | tf_op jit(solution)/shard_map/ppermute | solution.py:75
  199.9 23.8 %collective-permute-start.17 = (bf16[2,2,4,128,256]{4,3,2,1,0:T(8,128)(2,1)S(1)}, bf16[2,2,4,128,256]{4,3,2,1,0:T(8,128)(2,1)S(1)}, u32[]{:S(2)}, u32[]{:S(2)}) collective-permute-start(bf16[2,2,4,128,256]{4,3,2,1,0:T(8,128)(2,1)S(1)} %collective-permute-done.12), channel_id=1, source_target_pairs={{0,16},{16,32},{32,48},{48,64},{64,80},{80,96},{96,112},{112,0},{1... | collective-permute-start | bytes 3145736 | tf_op jit(solution)/shard_map/ppermute | solution.py:72
  206.3 1.2 copy-start.1
Sparse Core Ops, SparseCore 0:
  59.3 43.7 all-gather.3
  106.5 21.8 all-gather.5

commit v14 on v13

--- a/solution.py
+++ b/solution.py
@@ -74,7 +74,7 @@
         if k < n - n // 2:
             dn = lax.ppermute(dn, axis, left)
             got.append((-k, dn))
-        if k == 3:
+        if k == 0:
             up, dn, held = lax.optimization_barrier((up, dn, held))
     return got, held
 

time: 236 us -> 236 us (level)
  waiting for transfers between devices: 118 us -> 106 us
  local copies, waits for them, and re-layouts: 20.2 us -> 25.6 us
  starting transfers between devices: 66.2 us -> 70 us
    ppermute x4, waiting for transfers between devices: 66.2 us -> 59.1 us  [ring_blocks(): up = lax.ppermute(up, axis, right)]
    unnamed x9 -> x19, local copies, waits for them, and re-layouts: 0.79 us -> 7.86 us
    optimization_barrier x1 -> x0, local copies, waits for them, and re-layouts: 6.47 us -> none  [ring_blocks(): up, dn, held = lax.optimization_barrier((up, dn, held))]
    ppermute x3, waiting for transfers between devices: 5.35 us -> 0.01 us  [ring_blocks(): dn = lax.ppermute(dn, axis, left)]
    slice x0 -> x1, local copies, waits for them, and re-layouts: none -> 4.77 us  [per_device(): real, imag = (row_panel[:, 0], row_panel[:, 1])]
    ppermute x4, starting transfers between devices: 12.5 us -> 16.2 us  [ring_blocks(): up = lax.ppermute(up, axis, right)]
    slice x1 -> x0, other arithmetic: 2.76 us -> none  [per_device(): real, imag = (row_panel[:, 0], row_panel[:, 1])]
    another operation x1, other arithmetic: 0.64 us -> 3.3 us  [per_device(): jnp.stack((jnp.stack((real, -imag), axis=1), jnp.stack((imag, real), axis...]
  transfers between devices with their start and end apart: 20 -> 20, of which waited for: 12 -> 10; matrix products, arithmetic and copies ran while one was open for 8% -> 15% of each run, Pallas kernels for 0% -> 0%
where the time goes in v14:
time: 236 us; the launch traced here: 232 us
  waiting for transfers between devices  106 us (45%)
  starting transfers between devices  70 us (30%)
  local copies, waits for them, and re-layouts  25.6 us (11%)
  between operations  14 us (6%)
  matrix products  9.43 us (4%)
  other arithmetic  7.58 us (3%)
    ppermute x4, waiting for transfers between devices, ring_blocks(): up = lax.ppermute(up, axis, right)  59.1 us
    ppermute x4, starting transfers between devices, stream_gather(): up = lax.ppermute(up, axis, perm(k, 1))  28.9 us
    ppermute x4, starting transfers between devices, ring_blocks(): up = lax.ppermute(up, axis, right)  16.2 us
    all_gather x1, waiting for transfers between devices, per_device(): rows = lax.all_gather(rows, 'x', axis=1)  15.7 us
    ppermute x4, waiting for transfers between devices, stream_gather(): up = lax.ppermute(up, axis, perm(k, 1))  14 us
    ppermute x4, starting transfers between devices, mirrored_pieces(): got.append(lax.ppermute(part, SHOT + RECV, perm))  13.2 us
    ppermute x3, waiting for transfers between devices, stream_gather(): dn = lax.ppermute(dn, axis, perm(k, -1))  10.5 us
    dot_general x8, matrix products, per_device(): jnp.einsum('fgczik,fczkj->fgij', row_block, col_block, preferred_element_...  9.43 us
  transfers between devices with their start and end apart: 20, of which 10 were waited for; matrix products, arithmetic and copies ran while one was open for 15% of the time, Pallas kernels for 0%

profile of v14, /device:TPU:56, one launch (start us, length us, event | category | flops | bytes accessed | tf_op | source)
XLA Modules:
  0.0 232.2 jit_solution(9646220516476460367)
XLA Ops:
  9.5 7.8 %collective-permute-start.2 = (bf16[2,2,128,128]{3,2,1,0:T(8,128)(2,1)S(1)}, bf16[2,2,128,128]{3,2,1,0:T(8,128)(2,1)S(1)}, u32[]{:S(2)}, u32[]{:S(2)}) collective-permute-start(bf16[2,2,128,128]{3,2,1,0:T(8,128)(2,1)S(1)} %get-tuple-element.12), channel_id=1, source_target_pairs={{16,0},{17,32},{18,64},{19,96},{20,128},{21,160},{22,192},{23,224}... | collective-permute-start | bytes 393224 | tf_op jit(solution)/shard_map/ppermute | solution.py:96
  17.3 3.4 %collective-permute-start.3 = (bf16[2,2,128,128]{3,2,1,0:T(8,128)(2,1)S(1)}, bf16[2,2,128,128]{3,2,1,0:T(8,128)(2,1)S(1)}, u32[]{:S(2)}, u32[]{:S(2)}) collective-permute-start(bf16[2,2,128,128]{3,2,1,0:T(8,128)(2,1)S(1)} %get-tuple-element.11), channel_id=1, source_target_pairs={{16,16},{17,48},{18,80},{19,112},{20,144},{21,176},{22,208},{23,24... | collective-permute-start | bytes 393224 | tf_op jit(solution)/shard_map/ppermute | solution.py:96
  21.5 5.4 %collective-permute-done.3 = bf16[2,2,128,128]{3,2,1,0:T(8,128)(2,1)S(1)} collective-permute-done((bf16[2,2,128,128]{3,2,1,0:T(8,128)(2,1)S(1)}, bf16[2,2,128,128]{3,2,1,0:T(8,128)(2,1)S(1)}, u32[]{:S(2)}, u32[]{:S(2)}) %collective-permute-start.3) | collective-permute-done | bytes 131104 | tf_op jit(solution)/shard_map/ppermute | solution.py:96
  28.4 19.7 %collective-permute-start.4 = (bf16[2,2,128,256]{3,2,1,0:T(8,128)(2,1)S(1)}, bf16[2,2,128,256]{3,2,1,0:T(8,128)(2,1)S(1)}, u32[]{:S(2)}, u32[]{:S(2)}) collective-permute-start(bf16[2,2,128,256]{3,2,1,0:T(8,128)(2,1)S(1)} %get-tuple-element.6), channel_id=1, source_target_pairs={{0,8},{8,0},{1,9},{9,1},{2,10},{10,2},{3,11},{11,3},{4,12},{12,4},... | collective-permute-start | bytes 786440 | tf_op jit(solution)/shard_map/ppermute | solution.py:49
  48.1 9.5 %collective-permute-done.4 = bf16[2,2,128,256]{3,2,1,0:T(8,128)(2,1)S(1)} collective-permute-done((bf16[2,2,128,256]{3,2,1,0:T(8,128)(2,1)S(1)}, bf16[2,2,128,256]{3,2,1,0:T(8,128)(2,1)S(1)}, u32[]{:S(2)}, u32[]{:S(2)}) %collective-permute-start.4) | collective-permute-done | bytes 262176 | tf_op jit(solution)/shard_map/ppermute | solution.py:49
  59.2 7.8 %collective-permute-start.5 = (bf16[2,2,128,256]{3,2,1,0:T(8,128)(2,1)S(1)}, bf16[2,2,128,256]{3,2,1,0:T(8,128)(2,1)S(1)}, u32[]{:S(2)}, u32[]{:S(2)}) collective-permute-start(bf16[2,2,128,256]{3,2,1,0:T(8,128)(2,1)S(1)} %get-tuple-element.6), channel_id=1, source_target_pairs={{0,128},{128,256},{256,384},{1,129},{129,257},{257,385},{2,130},{1... | collective-permute-start | bytes 786440 | tf_op jit(solution)/shard_map/ppermute | solution.py:49
  68.4 4.5 %collective-permute-done.5 = bf16[2,2,128,256]{3,2,1,0:T(8,128)(2,1)S(1)} collective-permute-done((bf16[2,2,128,256]{3,2,1,0:T(8,128)(2,1)S(1)}, bf16[2,2,128,256]{3,2,1,0:T(8,128)(2,1)S(1)}, u32[]{:S(2)}, u32[]{:S(2)}) %collective-permute-start.5) | collective-permute-done | bytes 262176 | tf_op jit(solution)/shard_map/ppermute | solution.py:49
  73.6 3.4 %collective-permute-done.8 = bf16[2,2,128,256]{3,2,1,0:T(8,128)(2,1)S(1)} collective-permute-done((bf16[2,2,128,256]{3,2,1,0:T(8,128)(2,1)S(1)}, bf16[2,2,128,256]{3,2,1,0:T(8,128)(2,1)S(1)}, u32[]{:S(2)}, u32[]{:S(2)}) %collective-permute-start.8) | collective-permute-done | bytes 262176 | tf_op jit(solution)/shard_map/ppermute | solution.py:52
  79.1 7.0 %collective-permute-done.9 = bf16[2,2,128,256]{3,2,1,0:T(8,128)(2,1)S(1)} collective-permute-done((bf16[2,2,128,256]{3,2,1,0:T(8,128)(2,1)S(1)}, bf16[2,2,128,256]{3,2,1,0:T(8,128)(2,1)S(1)}, u32[]{:S(2)}, u32[]{:S(2)}) %collective-permute-start.9) | collective-permute-done | bytes 262176 | tf_op jit(solution)/shard_map/ppermute | solution.py:52
  87.4 15.7 %all-gather.4.cloned.1.call-done = bf16[2,4,2,2,128,256]{5,4,3,2,0,1:T(8,128)(2,1)} async-done(((bf16[2,1,2,2,128,256]{5,4,3,2,0,1:T(8,128)(2,1)}), bf16[2,4,2,2,128,256]{5,4,3,2,0,1:T(8,128)(2,1)}) %all-gather.4.cloned.1.call-update) | async-done | bytes 2097168 | tf_op jit(solution)/shard_map/all_gather | solution.py:109
  103.1 3.2 %copy.20 = bf16[2,4,2,2,128,256]{5,4,3,2,1,0:T(8,128)(2,1)} copy(bf16[2,4,2,2,128,256]{5,4,3,2,0,1:T(8,128)(2,1)} %all-gather.4.cloned.1.call-done) | data formatting | bytes 4194304 | tf_op jit(solution)/shard_map/all_gather | solution.py:109
  109.6 3.5 %collective-permute-start.12 = (bf16[2,2,4,128,256]{4,3,2,1,0:T(8,128)(2,1)S(1)}, bf16[2,2,4,128,256]{4,3,2,1,0:T(8,128)(2,1)S(1)}, u32[]{:S(2)}, u32[]{:S(2)}) collective-permute-start(bf16[2,2,4,128,256]{4,3,2,1,0:T(8,128)(2,1)S(1)} %fusion.42), channel_id=1, source_target_pairs={{16,0},{32,16},{48,32},{64,48},{80,64},{96,80},{112,96},{0,112},{1... | collective-permute-start | bytes 3145736 | tf_op jit(solution)/shard_map/ppermute | solution.py:75
  113.1 20.8 %collective-permute-done.11 = bf16[2,2,4,128,256]{4,3,2,1,0:T(8,128)(2,1)S(1)} collective-permute-done((bf16[2,2,4,128,256]{4,3,2,1,0:T(8,128)(2,1)S(1)}, bf16[2,2,4,128,256]{4,3,2,1,0:T(8,128)(2,1)S(1)}, u32[]{:S(2)}, u32[]{:S(2)}) %collective-permute-start.11) | collective-permute-done | bytes 1048608 | tf_op jit(solution)/shard_map/ppermute | solution.py:72
  133.9 3.5 %collective-permute-start.13 = (bf16[2,2,4,128,256]{4,3,2,1,0:T(8,128)(2,1)S(1)}, bf16[2,2,4,128,256]{4,3,2,1,0:T(8,128)(2,1)S(1)}, u32[]{:S(2)}, u32[]{:S(2)}) collective-permute-start(bf16[2,2,4,128,256]{4,3,2,1,0:T(8,128)(2,1)S(1)} %collective-permute-done.11), channel_id=1, source_target_pairs={{0,16},{16,32},{32,48},{48,64},{64,80},{80,96},{96,112},{112,0},{1... | collective-permute-start | bytes 3145736 | tf_op jit(solution)/shard_map/ppermute | solution.py:72
  139.8 19.9 %collective-permute-done.13 = bf16[2,2,4,128,256]{4,3,2,1,0:T(8,128)(2,1)S(1)} collective-permute-done((bf16[2,2,4,128,256]{4,3,2,1,0:T(8,128)(2,1)S(1)}, bf16[2,2,4,128,256]{4,3,2,1,0:T(8,128)(2,1)S(1)}, u32[]{:S(2)}, u32[]{:S(2)}) %collective-permute-start.13) | collective-permute-done | bytes 1048608 | tf_op jit(solution)/shard_map/ppermute | solution.py:72
  159.7 4.7 %collective-permute-start.15 = (bf16[2,2,4,128,256]{4,3,2,1,0:T(8,128)(2,1)S(1)}, bf16[2,2,4,128,256]{4,3,2,1,0:T(8,128)(2,1)}, u32[]{:S(2)}, u32[]{:S(2)}) collective-permute-start(bf16[2,2,4,128,256]{4,3,2,1,0:T(8,128)(2,1)S(1)} %collective-permute-done.13), channel_id=1, source_target_pairs={{0,16},{16,32},{32,48},{48,64},{64,80},{80,96},{96,112},{112,0},{1... | collective-permute-start | bytes 3145736 | tf_op jit(solution)/shard_map/ppermute | solution.py:72
  166.5 18.4 %collective-permute-done.15 = bf16[2,2,4,128,256]{4,3,2,1,0:T(8,128)(2,1)} collective-permute-done((bf16[2,2,4,128,256]{4,3,2,1,0:T(8,128)(2,1)S(1)}, bf16[2,2,4,128,256]{4,3,2,1,0:T(8,128)(2,1)}, u32[]{:S(2)}, u32[]{:S(2)}) %collective-permute-start.15) | collective-permute-done | bytes 1048608 | tf_op jit(solution)/shard_map/ppermute | solution.py:72
  184.9 5.7 %collective-permute-start.17 = (bf16[2,2,4,128,256]{4,3,2,1,0:T(8,128)(2,1)}, bf16[2,2,4,128,256]{4,3,2,1,0:T(8,128)(2,1)}, u32[]{:S(2)}, u32[]{:S(2)}) collective-permute-start(bf16[2,2,4,128,256]{4,3,2,1,0:T(8,128)(2,1)} %collective-permute-done.15), channel_id=1, source_target_pairs={{0,16},{16,32},{32,48},{48,64},{64,80},{80,96},{96,112},{112,0},{1... | collective-permute-start | bytes 3145736 | tf_op jit(solution)/shard_map/ppermute | solution.py:72
  190.7 7.3 %copy.21 = bf16[2,2,128,2,4,2,256]{2,6,5,4,3,1,0:T(8,128)(2,1)} copy(bf16[2,2,128,2,4,2,256]{6,2,1,0,5,4,3:T(8,128)(2,1)} %bitcast.176) | data formatting | bytes 8388608 | tf_op jit(solution)/shard_map/transpose | solution.py:113
  198.0 4.8 %fusion.67 = (bf16[2,1,128,4,8,128]{2,5,4,3,1,0:T(8,128)(2,1)}, bf16[2,1,128,4,8,128]{2,5,4,3,1,0:T(8,128)(2,1)}) fusion(bf16[2,2,128,4,8,128]{2,5,4,3,1,0:T(8,128)(2,1)} %bitcast.175), kind=kLoop, calls=%fused_computation.123 | loop fusion | bytes 8388608 | tf_op jit(solution)/shard_map/slice | solution.py:117
  202.8 3.0 %copy.43 = bf16[2,1,128,4,8,128]{5,2,3,1,0,4:T(8,128)(2,1)S(1)} copy(bf16[2,1,128,4,8,128]{2,5,4,3,1,0:T(8,128)(2,1)} %get-tuple-element.8) | data formatting | bytes 4194304
  207.8 3.9 %copy.42 = bf16[2,1,128,4,8,128]{5,2,3,1,0,4:T(8,128)(2,1)} copy(bf16[2,1,128,4,8,128]{2,5,4,3,1,0:T(8,128)(2,1)} %get-tuple-element.7) | data formatting | bytes 4194304
  211.7 3.3 %maximum_bitcast_fusion.1 = (bf16[2,1,2,128,4,8,128]{6,3,4,2,1,0,5:T(8,128)(2,1)S(1)}, bf16[2,1,2,128,4,8,128]{6,3,4,2,1,0,5:T(8,128)(2,1)S(1)}) fusion(bf16[2,1,128,4,8,128]{5,2,3,1,0,4:T(8,128)(2,1)} %copy.42, bf16[2,1,128,4,8,128]{5,2,3,1,0,4:T(8,128)(2,1)S(1)} %copy.43, bf16[2,1,128,4,8,128]{5,2,3,1,0,4:T(8,128)(2,1)} %neg.4), kind=kLoop, calls=%fused_computation.19 | loop fusion | flops 4194304 | bytes 14680064 | tf_op jit(solution)/shard_map/stack | solution.py:118
  222.8 2.5 %fusion.7 = f32[2,2,128,256]{3,2,1,0:T(8,128)} fusion(f32[2,2,128,256]{3,2,1,0:T(8,128)S(1)} %fusion.5, bf16[2,2,4,128,256]{4,3,2,1,0:T(8,128)(2,1)} %collective-permute-done.17, s32[]{:T(128)S(6)} %select_n.230, bf16[2,1,2,128,4,8,128]{6,3,4,2,1,0,5:T(8,128)(2,1)S(1)} %get-tuple-element.10, bf16[2,1,2,128,4,8,128]{6,3,4,2,1,0,5:T(8,128)(2,1)S(1)} %get-tuple-element.9), kind=kOutput, calls=%fused_computation.35 | convolution fusion | flops 269221888 | bytes 10485764 | tf_op jit(solution)/shard_map/fgczik,fczkj->fgij/dot_general | solution.py:123
  (67 shorter events, 29.1 us)
Async XLA Ops:
  6.5 96.6 %all-gather.4.cloned.1.call-start = ((), (), s32[]{:S(2)}) async-start(), calls=%async_computation | async-start | bytes 2621440 | tf_op jit(solution)/shard_map/all_gather | solution.py:109
  7.5 13.3 %collective-permute-start = (bf16[2,2,128,128]{3,2,1,0:T(8,128)(2,1)S(1)}, bf16[2,2,128,128]{3,2,1,0:T(8,128)(2,1)S(1)}, u32[]{:S(2)}, u32[]{:S(2)}) collective-permute-start(bf16[2,2,128,128]{3,2,1,0:T(8,128)(2,1)S(1)} %get-tuple-element.12), channel_id=1, source_target_pairs={{0,0},{1,32},{2,64},{3,96},{4,128},{5,160},{6,192},{7,224},{8,256}... | collective-permute-start | bytes 393224 | tf_op jit(solution)/shard_map/ppermute | solution.py:96
  8.2 13.3 %collective-permute-start.1 = (bf16[2,2,128,128]{3,2,1,0:T(8,128)(2,1)S(1)}, bf16[2,2,128,128]{3,2,1,0:T(8,128)(2,1)S(1)}, u32[]{:S(2)}, u32[]{:S(2)}) collective-permute-start(bf16[2,2,128,128]{3,2,1,0:T(8,128)(2,1)S(1)} %get-tuple-element.11), channel_id=1, source_target_pairs={{0,16},{1,48},{2,80},{3,112},{4,144},{5,176},{6,208},{7,240},{8,27... | collective-permute-start | bytes 393224 | tf_op jit(solution)/shard_map/ppermute | solution.py:96
  9.5 12.0 %collective-permute-start.2 = (bf16[2,2,128,128]{3,2,1,0:T(8,128)(2,1)S(1)}, bf16[2,2,128,128]{3,2,1,0:T(8,128)(2,1)S(1)}, u32[]{:S(2)}, u32[]{:S(2)}) collective-permute-start(bf16[2,2,128,128]{3,2,1,0:T(8,128)(2,1)S(1)} %get-tuple-element.12), channel_id=1, source_target_pairs={{16,0},{17,32},{18,64},{19,96},{20,128},{21,160},{22,192},{23,224}... | collective-permute-start | bytes 393224 | tf_op jit(solution)/shard_map/ppermute | solution.py:96
  17.3 9.6 %collective-permute-start.3 = (bf16[2,2,128,128]{3,2,1,0:T(8,128)(2,1)S(1)}, bf16[2,2,128,128]{3,2,1,0:T(8,128)(2,1)S(1)}, u32[]{:S(2)}, u32[]{:S(2)}) collective-permute-start(bf16[2,2,128,128]{3,2,1,0:T(8,128)(2,1)S(1)} %get-tuple-element.11), channel_id=1, source_target_pairs={{16,16},{17,48},{18,80},{19,112},{20,144},{21,176},{22,208},{23,24... | collective-permute-start | bytes 393224 | tf_op jit(solution)/shard_map/ppermute | solution.py:96
  28.4 29.2 %collective-permute-start.4 = (bf16[2,2,128,256]{3,2,1,0:T(8,128)(2,1)S(1)}, bf16[2,2,128,256]{3,2,1,0:T(8,128)(2,1)S(1)}, u32[]{:S(2)}, u32[]{:S(2)}) collective-permute-start(bf16[2,2,128,256]{3,2,1,0:T(8,128)(2,1)S(1)} %get-tuple-element.6), channel_id=1, source_target_pairs={{0,8},{8,0},{1,9},{9,1},{2,10},{10,2},{3,11},{11,3},{4,12},{12,4},... | collective-permute-start | bytes 786440 | tf_op jit(solution)/shard_map/ppermute | solution.py:49
  59.2 131.5 %all-gather.6.cloned.1.call-start = ((), (), s32[]{:S(2)}) async-start(), calls=%async_computation.1 | async-start | bytes 6291456 | tf_op jit(solution)/shard_map/all_gather | solution.py:110
  59.2 13.7 %collective-permute-start.5 = (bf16[2,2,128,256]{3,2,1,0:T(8,128)(2,1)S(1)}, bf16[2,2,128,256]{3,2,1,0:T(8,128)(2,1)S(1)}, u32[]{:S(2)}, u32[]{:S(2)}) collective-permute-start(bf16[2,2,128,256]{3,2,1,0:T(8,128)(2,1)S(1)} %get-tuple-element.6), channel_id=1, source_target_pairs={{0,128},{128,256},{256,384},{1,129},{129,257},{257,385},{2,130},{1... | collective-permute-start | bytes 786440 | tf_op jit(solution)/shard_map/ppermute | solution.py:49
  67.1 9.9 %collective-permute-start.8 = (bf16[2,2,128,256]{3,2,1,0:T(8,128)(2,1)S(1)}, bf16[2,2,128,256]{3,2,1,0:T(8,128)(2,1)S(1)}, u32[]{:S(2)}, u32[]{:S(2)}) collective-permute-start(bf16[2,2,128,256]{3,2,1,0:T(8,128)(2,1)S(1)} %get-tuple-element.6), channel_id=1, source_target_pairs={{128,0},{256,128},{384,256},{129,1},{257,129},{385,257},{130,2},{2... | collective-permute-start | bytes 786440 | tf_op jit(solution)/shard_map/ppermute | solution.py:52
  72.9 5.4 %collective-permute-start.6 = (bf16[2,2,128,256]{3,2,1,0:T(8,128)(2,1)S(1)}, bf16[2,2,128,256]{3,2,1,0:T(8,128)(2,1)S(1)}, u32[]{:S(2)}, u32[]{:S(2)}) collective-permute-start(bf16[2,2,128,256]{3,2,1,0:T(8,128)(2,1)S(1)} %collective-permute-done.5), channel_id=1, source_target_pairs={{128,256},{256,384},{129,257},{257,385},{130,258},{258,386},{131,2... | collective-permute-start | bytes 786440 | tf_op jit(solution)/shard_map/ppermute | solution.py:49
  77.0 9.1 %collective-permute-start.9 = (bf16[2,2,128,256]{3,2,1,0:T(8,128)(2,1)S(1)}, bf16[2,2,128,256]{3,2,1,0:T(8,128)(2,1)S(1)}, u32[]{:S(2)}, u32[]{:S(2)}) collective-permute-start(bf16[2,2,128,256]{3,2,1,0:T(8,128)(2,1)S(1)} %collective-permute-done.8), channel_id=1, source_target_pairs={{128,0},{256,128},{129,1},{257,129},{130,2},{258,130},{131,3},{259... | collective-permute-start | bytes 786440 | tf_op jit(solution)/shard_map/ppermute | solution.py:52
  78.3 28.0 %collective-permute-start.7 = (bf16[2,2,128,256]{3,2,1,0:T(8,128)(2,1)S(1)}, bf16[2,2,128,256]{3,2,1,0:T(8,128)(2,1)S(1)}, u32[]{:S(2)}, u32[]{:S(2)}) collective-permute-start(bf16[2,2,128,256]{3,2,1,0:T(8,128)(2,1)S(1)} %collective-permute-done.6), channel_id=1, source_target_pairs={{256,384},{257,385},{258,386},{259,387},{260,388},{261,389},{262,3... | collective-permute-start | bytes 786440 | tf_op jit(solution)/shard_map/ppermute | solution.py:49
  86.1 20.3 %collective-permute-start.10 = (bf16[2,2,128,256]{3,2,1,0:T(8,128)(2,1)S(1)}, bf16[2,2,128,256]{3,2,1,0:T(8,128)(2,1)S(1)}, u32[]{:S(2)}, u32[]{:S(2)}) collective-permute-start(bf16[2,2,128,256]{3,2,1,0:T(8,128)(2,1)S(1)} %collective-permute-done.9), channel_id=1, source_target_pairs={{128,0},{129,1},{130,2},{131,3},{132,4},{133,5},{134,6},{135,7},{1... | collective-permute-start | bytes 786440 | tf_op jit(solution)/shard_map/ppermute | solution.py:52
  107.3 26.6 %collective-permute-start.11 = (bf16[2,2,4,128,256]{4,3,2,1,0:T(8,128)(2,1)S(1)}, bf16[2,2,4,128,256]{4,3,2,1,0:T(8,128)(2,1)S(1)}, u32[]{:S(2)}, u32[]{:S(2)}) collective-permute-start(bf16[2,2,4,128,256]{4,3,2,1,0:T(8,128)(2,1)S(1)} %fusion.42), channel_id=1, source_target_pairs={{0,16},{16,32},{32,48},{48,64},{64,80},{80,96},{96,112},{112,0},{1... | collective-permute-start | bytes 3145736 | tf_op jit(solution)/shard_map/ppermute | solution.py:72
  109.6 27.8 %collective-permute-start.12 = (bf16[2,2,4,128,256]{4,3,2,1,0:T(8,128)(2,1)S(1)}, bf16[2,2,4,128,256]{4,3,2,1,0:T(8,128)(2,1)S(1)}, u32[]{:S(2)}, u32[]{:S(2)}) collective-permute-start(bf16[2,2,4,128,256]{4,3,2,1,0:T(8,128)(2,1)S(1)} %fusion.42), channel_id=1, source_target_pairs={{16,0},{32,16},{48,32},{64,48},{80,64},{96,80},{112,96},{0,112},{1... | collective-permute-start | bytes 3145736 | tf_op jit(solution)/shard_map/ppermute | solution.py:75
  133.9 3.5 %copy-start.2 = (bf16[2,2,4,128,256]{4,3,2,1,0:T(8,128)(2,1)}, bf16[2,2,4,128,256]{4,3,2,1,0:T(8,128)(2,1)S(1)}, u32[]{:S(2)}) copy-start(bf16[2,2,4,128,256]{4,3,2,1,0:T(8,128)(2,1)S(1)} %collective-permute-done.11) | copy-start | bytes 3145732
  133.9 25.8 %collective-permute-start.13 = (bf16[2,2,4,128,256]{4,3,2,1,0:T(8,128)(2,1)S(1)}, bf16[2,2,4,128,256]{4,3,2,1,0:T(8,128)(2,1)S(1)}, u32[]{:S(2)}, u32[]{:S(2)}) collective-permute-start(bf16[2,2,4,128,256]{4,3,2,1,0:T(8,128)(2,1)S(1)} %collective-permute-done.11), channel_id=1, source_target_pairs={{0,16},{16,32},{32,48},{48,64},{64,80},{80,96},{96,112},{112,0},{1... | collective-permute-start | bytes 3145736 | tf_op jit(solution)/shard_map/ppermute | solution.py:72
  137.4 60.5 %copy-start = (bf16[2,2,4,128,256]{4,3,2,1,0:T(8,128)(2,1)}, bf16[2,2,4,128,256]{4,3,2,1,0:T(8,128)(2,1)S(1)}, u32[]{:S(2)}) copy-start(bf16[2,2,4,128,256]{4,3,2,1,0:T(8,128)(2,1)S(1)} %collective-permute-done.12) | copy-start | bytes 3145732
  137.5 27.1 %collective-permute-start.14 = (bf16[2,2,4,128,256]{4,3,2,1,0:T(8,128)(2,1)S(1)}, bf16[2,2,4,128,256]{4,3,2,1,0:T(8,128)(2,1)}, u32[]{:S(2)}, u32[]{:S(2)}) collective-permute-start(bf16[2,2,4,128,256]{4,3,2,1,0:T(8,128)(2,1)S(1)} %collective-permute-done.12), channel_id=1, source_target_pairs={{16,0},{32,16},{48,32},{64,48},{80,64},{96,80},{112,96},{0,112},{1... | collective-permute-start | bytes 3145736 | tf_op jit(solution)/shard_map/ppermute | solution.py:75
  159.7 38.3 %copy-start.4 = (bf16[2,2,4,128,256]{4,3,2,1,0:T(8,128)(2,1)}, bf16[2,2,4,128,256]{4,3,2,1,0:T(8,128)(2,1)S(1)}, u32[]{:S(2)}) copy-start(bf16[2,2,4,128,256]{4,3,2,1,0:T(8,128)(2,1)S(1)} %collective-permute-done.13) | copy-start | bytes 3145732
  159.7 25.2 %collective-permute-start.15 = (bf16[2,2,4,128,256]{4,3,2,1,0:T(8,128)(2,1)S(1)}, bf16[2,2,4,128,256]{4,3,2,1,0:T(8,128)(2,1)}, u32[]{:S(2)}, u32[]{:S(2)}) collective-permute-start(bf16[2,2,4,128,256]{4,3,2,1,0:T(8,128)(2,1)S(1)} %collective-permute-done.13), channel_id=1, source_target_pairs={{0,16},{16,32},{32,48},{48,64},{64,80},{80,96},{96,112},{112,0},{1... | collective-permute-start | bytes 3145736 | tf_op jit(solution)/shard_map/ppermute | solution.py:72
  164.5 53.1 %collective-permute-start.16 = (bf16[2,2,4,128,256]{4,3,2,1,0:T(8,128)(2,1)}, bf16[2,2,4,128,256]{4,3,2,1,0:T(8,128)(2,1)}, u32[]{:S(2)}, u32[]{:S(2)}) collective-permute-start(bf16[2,2,4,128,256]{4,3,2,1,0:T(8,128)(2,1)} %collective-permute-done.14), channel_id=1, source_target_pairs={{16,0},{32,16},{48,32},{64,48},{80,64},{96,80},{112,96},{0,112},{1... | collective-permute-start | bytes 3145736 | tf_op jit(solution)/shard_map/ppermute | solution.py:75
  184.9 37.9 %collective-permute-start.17 = (bf16[2,2,4,128,256]{4,3,2,1,0:T(8,128)(2,1)}, bf16[2,2,4,128,256]{4,3,2,1,0:T(8,128)(2,1)}, u32[]{:S(2)}, u32[]{:S(2)}) collective-permute-start(bf16[2,2,4,128,256]{4,3,2,1,0:T(8,128)(2,1)} %collective-permute-done.15), channel_id=1, source_target_pairs={{0,16},{16,32},{32,48},{48,64},{64,80},{80,96},{96,112},{112,0},{1... | collective-permute-start | bytes 3145736 | tf_op jit(solution)/shard_map/ppermute | solution.py:72
  211.7 3.3 %copy-start.1 = (bf16[2,2,4,128,256]{4,3,2,1,0:T(8,128)(2,1)S(1)}, bf16[2,2,4,128,256]{4,3,2,1,0:T(8,128)(2,1)}, u32[]{:S(2)}) copy-start(bf16[2,2,4,128,256]{4,3,2,1,0:T(8,128)(2,1)} %copy-done) | copy-start | bytes 3145732
  (2 other events, 3.0 us)
Sparse Core Ops, SparseCore 0:
  59.3 43.7 all-gather.3
  106.5 21.8 all-gather.5

commit v15 on v14

--- a/solution.py
+++ b/solution.py
@@ -62,7 +62,7 @@
     return jnp.take(stacked, sel, axis=0)
 
 
-def ring_blocks(block, axis, held):
+def ring_blocks(block, axis):
     n = lax.axis_size(axis)
     right = [(i, (i + 1) % n) for i in range(n)]
     left = [(d, s) for s, d in right]
@@ -74,9 +74,7 @@
         if k < n - n // 2:
             dn = lax.ppermute(dn, axis, left)
             got.append((-k, dn))
-        if k == 0:
-            up, dn, held = lax.optimization_barrier((up, dn, held))
-    return got, held
+    return got
 
 
 def mirrored_pieces(traces, shot_count, recv_count):
@@ -113,7 +111,7 @@
     row_panel = jnp.transpose(rows, (3, 4, 5, 0, 1, 2, 6)).reshape(freqs, 2, block_rows, z_n, y_n, block_rows)
     me_y = lax.axis_index("y")
     z_cols = jnp.moveaxis(stream_gather(averaged, "z_lo", False), 0, 2)
-    blocks, row_panel = ring_blocks(z_cols, "y", row_panel)
+    blocks = ring_blocks(z_cols, "y")
     real, imag = row_panel[:, 0], row_panel[:, 1]
     paired = jnp.stack((jnp.stack((real, -imag), axis=1), jnp.stack((imag, real), axis=1)), axis=1)
     paired = jnp.transpose(paired, (5, 0, 1, 2, 4, 3, 6))

time: 236 us -> 236 us (level)
  no operation moved by 1% of the time
where the time goes in v15:
time: 236 us; the launch traced here: 232 us
  waiting for transfers between devices  106 us (45%)
  starting transfers between devices  70 us (30%)
  local copies, waits for them, and re-layouts  25.6 us (11%)
  between operations  14 us (6%)
  matrix products  9.43 us (4%)
  other arithmetic  7.58 us (3%)
    ppermute x4, waiting for transfers between devices, ring_blocks(): up = lax.ppermute(up, axis, right)  59.1 us
    ppermute x4, starting transfers between devices, stream_gather(): up = lax.ppermute(up, axis, perm(k, 1))  28.9 us
    ppermute x4, starting transfers between devices, ring_blocks(): up = lax.ppermute(up, axis, right)  16.2 us
    all_gather x1, waiting for transfers between devices, per_device(): rows = lax.all_gather(rows, 'x', axis=1)  15.7 us
    ppermute x4, waiting for transfers between devices, stream_gather(): up = lax.ppermute(up, axis, perm(k, 1))  14 us
    ppermute x4, starting transfers between devices, mirrored_pieces(): got.append(lax.ppermute(part, SHOT + RECV, perm))  13.2 us
    ppermute x3, waiting for transfers between devices, stream_gather(): dn = lax.ppermute(dn, axis, perm(k, -1))  10.5 us
    dot_general x8, matrix products, per_device(): jnp.einsum('fgczik,fczkj->fgij', row_block, col_block, preferred_element_...  9.43 us
  transfers between devices with their start and end apart: 20, of which 10 were waited for; matrix products, arithmetic and copies ran while one was open for 15% of the time, Pallas kernels for 0%

profile of v15, /device:TPU:56, one launch (start us, length us, event | category | flops | bytes accessed | tf_op | source)
XLA Modules:
  0.0 232.2 jit_solution(9646220516476460367)
XLA Ops:
  9.5 7.8 %collective-permute-start.2 = (bf16[2,2,128,128]{3,2,1,0:T(8,128)(2,1)S(1)}, bf16[2,2,128,128]{3,2,1,0:T(8,128)(2,1)S(1)}, u32[]{:S(2)}, u32[]{:S(2)}) collective-permute-start(bf16[2,2,128,128]{3,2,1,0:T(8,128)(2,1)S(1)} %get-tuple-element.12), channel_id=1, source_target_pairs={{16,0},{17,32},{18,64},{19,96},{20,128},{21,160},{22,192},{23,224}... | collective-permute-start | bytes 393224 | tf_op jit(solution)/shard_map/ppermute | solution.py:94
  17.3 3.4 %collective-permute-start.3 = (bf16[2,2,128,128]{3,2,1,0:T(8,128)(2,1)S(1)}, bf16[2,2,128,128]{3,2,1,0:T(8,128)(2,1)S(1)}, u32[]{:S(2)}, u32[]{:S(2)}) collective-permute-start(bf16[2,2,128,128]{3,2,1,0:T(8,128)(2,1)S(1)} %get-tuple-element.11), channel_id=1, source_target_pairs={{16,16},{17,48},{18,80},{19,112},{20,144},{21,176},{22,208},{23,24... | collective-permute-start | bytes 393224 | tf_op jit(solution)/shard_map/ppermute | solution.py:94
  21.5 5.4 %collective-permute-done.3 = bf16[2,2,128,128]{3,2,1,0:T(8,128)(2,1)S(1)} collective-permute-done((bf16[2,2,128,128]{3,2,1,0:T(8,128)(2,1)S(1)}, bf16[2,2,128,128]{3,2,1,0:T(8,128)(2,1)S(1)}, u32[]{:S(2)}, u32[]{:S(2)}) %collective-permute-start.3) | collective-permute-done | bytes 131104 | tf_op jit(solution)/shard_map/ppermute | solution.py:94
  28.4 19.7 %collective-permute-start.4 = (bf16[2,2,128,256]{3,2,1,0:T(8,128)(2,1)S(1)}, bf16[2,2,128,256]{3,2,1,0:T(8,128)(2,1)S(1)}, u32[]{:S(2)}, u32[]{:S(2)}) collective-permute-start(bf16[2,2,128,256]{3,2,1,0:T(8,128)(2,1)S(1)} %get-tuple-element.6), channel_id=1, source_target_pairs={{0,8},{8,0},{1,9},{9,1},{2,10},{10,2},{3,11},{11,3},{4,12},{12,4},... | collective-permute-start | bytes 786440 | tf_op jit(solution)/shard_map/ppermute | solution.py:49
  48.1 9.5 %collective-permute-done.4 = bf16[2,2,128,256]{3,2,1,0:T(8,128)(2,1)S(1)} collective-permute-done((bf16[2,2,128,256]{3,2,1,0:T(8,128)(2,1)S(1)}, bf16[2,2,128,256]{3,2,1,0:T(8,128)(2,1)S(1)}, u32[]{:S(2)}, u32[]{:S(2)}) %collective-permute-start.4) | collective-permute-done | bytes 262176 | tf_op jit(solution)/shard_map/ppermute | solution.py:49
  59.2 7.8 %collective-permute-start.5 = (bf16[2,2,128,256]{3,2,1,0:T(8,128)(2,1)S(1)}, bf16[2,2,128,256]{3,2,1,0:T(8,128)(2,1)S(1)}, u32[]{:S(2)}, u32[]{:S(2)}) collective-permute-start(bf16[2,2,128,256]{3,2,1,0:T(8,128)(2,1)S(1)} %get-tuple-element.6), channel_id=1, source_target_pairs={{0,128},{128,256},{256,384},{1,129},{129,257},{257,385},{2,130},{1... | collective-permute-start | bytes 786440 | tf_op jit(solution)/shard_map/ppermute | solution.py:49
  68.4 4.5 %collective-permute-done.5 = bf16[2,2,128,256]{3,2,1,0:T(8,128)(2,1)S(1)} collective-permute-done((bf16[2,2,128,256]{3,2,1,0:T(8,128)(2,1)S(1)}, bf16[2,2,128,256]{3,2,1,0:T(8,128)(2,1)S(1)}, u32[]{:S(2)}, u32[]{:S(2)}) %collective-permute-start.5) | collective-permute-done | bytes 262176 | tf_op jit(solution)/shard_map/ppermute | solution.py:49
  73.6 3.4 %collective-permute-done.8 = bf16[2,2,128,256]{3,2,1,0:T(8,128)(2,1)S(1)} collective-permute-done((bf16[2,2,128,256]{3,2,1,0:T(8,128)(2,1)S(1)}, bf16[2,2,128,256]{3,2,1,0:T(8,128)(2,1)S(1)}, u32[]{:S(2)}, u32[]{:S(2)}) %collective-permute-start.8) | collective-permute-done | bytes 262176 | tf_op jit(solution)/shard_map/ppermute | solution.py:52
  79.1 7.0 %collective-permute-done.9 = bf16[2,2,128,256]{3,2,1,0:T(8,128)(2,1)S(1)} collective-permute-done((bf16[2,2,128,256]{3,2,1,0:T(8,128)(2,1)S(1)}, bf16[2,2,128,256]{3,2,1,0:T(8,128)(2,1)S(1)}, u32[]{:S(2)}, u32[]{:S(2)}) %collective-permute-start.9) | collective-permute-done | bytes 262176 | tf_op jit(solution)/shard_map/ppermute | solution.py:52
  87.4 15.7 %all-gather.4.cloned.1.call-done = bf16[2,4,2,2,128,256]{5,4,3,2,0,1:T(8,128)(2,1)} async-done(((bf16[2,1,2,2,128,256]{5,4,3,2,0,1:T(8,128)(2,1)}), bf16[2,4,2,2,128,256]{5,4,3,2,0,1:T(8,128)(2,1)}) %all-gather.4.cloned.1.call-update) | async-done | bytes 2097168 | tf_op jit(solution)/shard_map/all_gather | solution.py:107
  103.1 3.2 %copy.20 = bf16[2,4,2,2,128,256]{5,4,3,2,1,0:T(8,128)(2,1)} copy(bf16[2,4,2,2,128,256]{5,4,3,2,0,1:T(8,128)(2,1)} %all-gather.4.cloned.1.call-done) | data formatting | bytes 4194304 | tf_op jit(solution)/shard_map/all_gather | solution.py:107
  109.6 3.5 %collective-permute-start.12 = (bf16[2,2,4,128,256]{4,3,2,1,0:T(8,128)(2,1)S(1)}, bf16[2,2,4,128,256]{4,3,2,1,0:T(8,128)(2,1)S(1)}, u32[]{:S(2)}, u32[]{:S(2)}) collective-permute-start(bf16[2,2,4,128,256]{4,3,2,1,0:T(8,128)(2,1)S(1)} %fusion.42), channel_id=1, source_target_pairs={{16,0},{32,16},{48,32},{64,48},{80,64},{96,80},{112,96},{0,112},{1... | collective-permute-start | bytes 3145736 | tf_op jit(solution)/shard_map/ppermute | solution.py:75
  113.1 20.8 %collective-permute-done.11 = bf16[2,2,4,128,256]{4,3,2,1,0:T(8,128)(2,1)S(1)} collective-permute-done((bf16[2,2,4,128,256]{4,3,2,1,0:T(8,128)(2,1)S(1)}, bf16[2,2,4,128,256]{4,3,2,1,0:T(8,128)(2,1)S(1)}, u32[]{:S(2)}, u32[]{:S(2)}) %collective-permute-start.11) | collective-permute-done | bytes 1048608 | tf_op jit(solution)/shard_map/ppermute | solution.py:72
  133.9 3.5 %collective-permute-start.13 = (bf16[2,2,4,128,256]{4,3,2,1,0:T(8,128)(2,1)S(1)}, bf16[2,2,4,128,256]{4,3,2,1,0:T(8,128)(2,1)S(1)}, u32[]{:S(2)}, u32[]{:S(2)}) collective-permute-start(bf16[2,2,4,128,256]{4,3,2,1,0:T(8,128)(2,1)S(1)} %collective-permute-done.11), channel_id=1, source_target_pairs={{0,16},{16,32},{32,48},{48,64},{64,80},{80,96},{96,112},{112,0},{1... | collective-permute-start | bytes 3145736 | tf_op jit(solution)/shard_map/ppermute | solution.py:72
  139.8 19.9 %collective-permute-done.13 = bf16[2,2,4,128,256]{4,3,2,1,0:T(8,128)(2,1)S(1)} collective-permute-done((bf16[2,2,4,128,256]{4,3,2,1,0:T(8,128)(2,1)S(1)}, bf16[2,2,4,128,256]{4,3,2,1,0:T(8,128)(2,1)S(1)}, u32[]{:S(2)}, u32[]{:S(2)}) %collective-permute-start.13) | collective-permute-done | bytes 1048608 | tf_op jit(solution)/shard_map/ppermute | solution.py:72
  159.7 4.7 %collective-permute-start.15 = (bf16[2,2,4,128,256]{4,3,2,1,0:T(8,128)(2,1)S(1)}, bf16[2,2,4,128,256]{4,3,2,1,0:T(8,128)(2,1)}, u32[]{:S(2)}, u32[]{:S(2)}) collective-permute-start(bf16[2,2,4,128,256]{4,3,2,1,0:T(8,128)(2,1)S(1)} %collective-permute-done.13), channel_id=1, source_target_pairs={{0,16},{16,32},{32,48},{48,64},{64,80},{80,96},{96,112},{112,0},{1... | collective-permute-start | bytes 3145736 | tf_op jit(solution)/shard_map/ppermute | solution.py:72
  166.5 18.4 %collective-permute-done.15 = bf16[2,2,4,128,256]{4,3,2,1,0:T(8,128)(2,1)} collective-permute-done((bf16[2,2,4,128,256]{4,3,2,1,0:T(8,128)(2,1)S(1)}, bf16[2,2,4,128,256]{4,3,2,1,0:T(8,128)(2,1)}, u32[]{:S(2)}, u32[]{:S(2)}) %collective-permute-start.15) | collective-permute-done | bytes 1048608 | tf_op jit(solution)/shard_map/ppermute | solution.py:72
  184.9 5.7 %collective-permute-start.17 = (bf16[2,2,4,128,256]{4,3,2,1,0:T(8,128)(2,1)}, bf16[2,2,4,128,256]{4,3,2,1,0:T(8,128)(2,1)}, u32[]{:S(2)}, u32[]{:S(2)}) collective-permute-start(bf16[2,2,4,128,256]{4,3,2,1,0:T(8,128)(2,1)} %collective-permute-done.15), channel_id=1, source_target_pairs={{0,16},{16,32},{32,48},{48,64},{64,80},{80,96},{96,112},{112,0},{1... | collective-permute-start | bytes 3145736 | tf_op jit(solution)/shard_map/ppermute | solution.py:72
  190.7 7.3 %copy.21 = bf16[2,2,128,2,4,2,256]{2,6,5,4,3,1,0:T(8,128)(2,1)} copy(bf16[2,2,128,2,4,2,256]{6,2,1,0,5,4,3:T(8,128)(2,1)} %bitcast.176) | data formatting | bytes 8388608 | tf_op jit(solution)/shard_map/transpose | solution.py:111
  198.0 4.8 %fusion.67 = (bf16[2,1,128,4,8,128]{2,5,4,3,1,0:T(8,128)(2,1)}, bf16[2,1,128,4,8,128]{2,5,4,3,1,0:T(8,128)(2,1)}) fusion(bf16[2,2,128,4,8,128]{2,5,4,3,1,0:T(8,128)(2,1)} %bitcast.175), kind=kLoop, calls=%fused_computation.123 | loop fusion | bytes 8388608 | tf_op jit(solution)/shard_map/slice | solution.py:115
  202.8 3.0 %copy.43 = bf16[2,1,128,4,8,128]{5,2,3,1,0,4:T(8,128)(2,1)S(1)} copy(bf16[2,1,128,4,8,128]{2,5,4,3,1,0:T(8,128)(2,1)} %get-tuple-element.8) | data formatting | bytes 4194304
  207.8 3.9 %copy.42 = bf16[2,1,128,4,8,128]{5,2,3,1,0,4:T(8,128)(2,1)} copy(bf16[2,1,128,4,8,128]{2,5,4,3,1,0:T(8,128)(2,1)} %get-tuple-element.7) | data formatting | bytes 4194304
  211.7 3.3 %maximum_bitcast_fusion.1 = (bf16[2,1,2,128,4,8,128]{6,3,4,2,1,0,5:T(8,128)(2,1)S(1)}, bf16[2,1,2,128,4,8,128]{6,3,4,2,1,0,5:T(8,128)(2,1)S(1)}) fusion(bf16[2,1,128,4,8,128]{5,2,3,1,0,4:T(8,128)(2,1)} %copy.42, bf16[2,1,128,4,8,128]{5,2,3,1,0,4:T(8,128)(2,1)S(1)} %copy.43, bf16[2,1,128,4,8,128]{5,2,3,1,0,4:T(8,128)(2,1)} %neg.4), kind=kLoop, calls=%fused_computation.19 | loop fusion | flops 4194304 | bytes 14680064 | tf_op jit(solution)/shard_map/stack | solution.py:116
  222.8 2.5 %fusion.7 = f32[2,2,128,256]{3,2,1,0:T(8,128)} fusion(f32[2,2,128,256]{3,2,1,0:T(8,128)S(1)} %fusion.5, bf16[2,2,4,128,256]{4,3,2,1,0:T(8,128)(2,1)} %collective-permute-done.17, s32[]{:T(128)S(6)} %select_n.230, bf16[2,1,2,128,4,8,128]{6,3,4,2,1,0,5:T(8,128)(2,1)S(1)} %get-tuple-element.10, bf16[2,1,2,128,4,8,128]{6,3,4,2,1,0,5:T(8,128)(2,1)S(1)} %get-tuple-element.9), kind=kOutput, calls=%fused_computation.35 | convolution fusion | flops 269221888 | bytes 10485764 | tf_op jit(solution)/shard_map/fgczik,fczkj->fgij/dot_general | solution.py:121
  (67 shorter events, 29.1 us)
Async XLA Ops:
  6.5 96.6 %all-gather.4.cloned.1.call-start = ((), (), s32[]{:S(2)}) async-start(), calls=%async_computation | async-start | bytes 2621440 | tf_op jit(solution)/shard_map/all_gather | solution.py:107
  7.5 13.3 %collective-permute-start = (bf16[2,2,128,128]{3,2,1,0:T(8,128)(2,1)S(1)}, bf16[2,2,128,128]{3,2,1,0:T(8,128)(2,1)S(1)}, u32[]{:S(2)}, u32[]{:S(2)}) collective-permute-start(bf16[2,2,128,128]{3,2,1,0:T(8,128)(2,1)S(1)} %get-tuple-element.12), channel_id=1, source_target_pairs={{0,0},{1,32},{2,64},{3,96},{4,128},{5,160},{6,192},{7,224},{8,256}... | collective-permute-start | bytes 393224 | tf_op jit(solution)/shard_map/ppermute | solution.py:94
  8.2 13.3 %collective-permute-start.1 = (bf16[2,2,128,128]{3,2,1,0:T(8,128)(2,1)S(1)}, bf16[2,2,128,128]{3,2,1,0:T(8,128)(2,1)S(1)}, u32[]{:S(2)}, u32[]{:S(2)}) collective-permute-start(bf16[2,2,128,128]{3,2,1,0:T(8,128)(2,1)S(1)} %get-tuple-element.11), channel_id=1, source_target_pairs={{0,16},{1,48},{2,80},{3,112},{4,144},{5,176},{6,208},{7,240},{8,27... | collective-permute-start | bytes 393224 | tf_op jit(solution)/shard_map/ppermute | solution.py:94
  9.5 12.0 %collective-permute-start.2 = (bf16[2,2,128,128]{3,2,1,0:T(8,128)(2,1)S(1)}, bf16[2,2,128,128]{3,2,1,0:T(8,128)(2,1)S(1)}, u32[]{:S(2)}, u32[]{:S(2)}) collective-permute-start(bf16[2,2,128,128]{3,2,1,0:T(8,128)(2,1)S(1)} %get-tuple-element.12), channel_id=1, source_target_pairs={{16,0},{17,32},{18,64},{19,96},{20,128},{21,160},{22,192},{23,224}... | collective-permute-start | bytes 393224 | tf_op jit(solution)/shard_map/ppermute | solution.py:94
  17.3 9.6 %collective-permute-start.3 = (bf16[2,2,128,128]{3,2,1,0:T(8,128)(2,1)S(1)}, bf16[2,2,128,128]{3,2,1,0:T(8,128)(2,1)S(1)}, u32[]{:S(2)}, u32[]{:S(2)}) collective-permute-start(bf16[2,2,128,128]{3,2,1,0:T(8,128)(2,1)S(1)} %get-tuple-element.11), channel_id=1, source_target_pairs={{16,16},{17,48},{18,80},{19,112},{20,144},{21,176},{22,208},{23,24... | collective-permute-start | bytes 393224 | tf_op jit(solution)/shard_map/ppermute | solution.py:94
  28.4 29.2 %collective-permute-start.4 = (bf16[2,2,128,256]{3,2,1,0:T(8,128)(2,1)S(1)}, bf16[2,2,128,256]{3,2,1,0:T(8,128)(2,1)S(1)}, u32[]{:S(2)}, u32[]{:S(2)}) collective-permute-start(bf16[2,2,128,256]{3,2,1,0:T(8,128)(2,1)S(1)} %get-tuple-element.6), channel_id=1, source_target_pairs={{0,8},{8,0},{1,9},{9,1},{2,10},{10,2},{3,11},{11,3},{4,12},{12,4},... | collective-permute-start | bytes 786440 | tf_op jit(solution)/shard_map/ppermute | solution.py:49
  59.2 131.5 %all-gather.6.cloned.1.call-start = ((), (), s32[]{:S(2)}) async-start(), calls=%async_computation.1 | async-start | bytes 6291456 | tf_op jit(solution)/shard_map/all_gather | solution.py:108
  59.2 13.7 %collective-permute-start.5 = (bf16[2,2,128,256]{3,2,1,0:T(8,128)(2,1)S(1)}, bf16[2,2,128,256]{3,2,1,0:T(8,128)(2,1)S(1)}, u32[]{:S(2)}, u32[]{:S(2)}) collective-permute-start(bf16[2,2,128,256]{3,2,1,0:T(8,128)(2,1)S(1)} %get-tuple-element.6), channel_id=1, source_target_pairs={{0,128},{128,256},{256,384},{1,129},{129,257},{257,385},{2,130},{1... | collective-permute-start | bytes 786440 | tf_op jit(solution)/shard_map/ppermute | solution.py:49
  67.1 9.9 %collective-permute-start.8 = (bf16[2,2,128,256]{3,2,1,0:T(8,128)(2,1)S(1)}, bf16[2,2,128,256]{3,2,1,0:T(8,128)(2,1)S(1)}, u32[]{:S(2)}, u32[]{:S(2)}) collective-permute-start(bf16[2,2,128,256]{3,2,1,0:T(8,128)(2,1)S(1)} %get-tuple-element.6), channel_id=1, source_target_pairs={{128,0},{256,128},{384,256},{129,1},{257,129},{385,257},{130,2},{2... | collective-permute-start | bytes 786440 | tf_op jit(solution)/shard_map/ppermute | solution.py:52
  72.9 5.4 %collective-permute-start.6 = (bf16[2,2,128,256]{3,2,1,0:T(8,128)(2,1)S(1)}, bf16[2,2,128,256]{3,2,1,0:T(8,128)(2,1)S(1)}, u32[]{:S(2)}, u32[]{:S(2)}) collective-permute-start(bf16[2,2,128,256]{3,2,1,0:T(8,128)(2,1)S(1)} %collective-permute-done.5), channel_id=1, source_target_pairs={{128,256},{256,384},{129,257},{257,385},{130,258},{258,386},{131,2... | collective-permute-start | bytes 786440 | tf_op jit(solution)/shard_map/ppermute | solution.py:49
  77.0 9.1 %collective-permute-start.9 = (bf16[2,2,128,256]{3,2,1,0:T(8,128)(2,1)S(1)}, bf16[2,2,128,256]{3,2,1,0:T(8,128)(2,1)S(1)}, u32[]{:S(2)}, u32[]{:S(2)}) collective-permute-start(bf16[2,2,128,256]{3,2,1,0:T(8,128)(2,1)S(1)} %collective-permute-done.8), channel_id=1, source_target_pairs={{128,0},{256,128},{129,1},{257,129},{130,2},{258,130},{131,3},{259... | collective-permute-start | bytes 786440 | tf_op jit(solution)/shard_map/ppermute | solution.py:52
  78.3 28.0 %collective-permute-start.7 = (bf16[2,2,128,256]{3,2,1,0:T(8,128)(2,1)S(1)}, bf16[2,2,128,256]{3,2,1,0:T(8,128)(2,1)S(1)}, u32[]{:S(2)}, u32[]{:S(2)}) collective-permute-start(bf16[2,2,128,256]{3,2,1,0:T(8,128)(2,1)S(1)} %collective-permute-done.6), channel_id=1, source_target_pairs={{256,384},{257,385},{258,386},{259,387},{260,388},{261,389},{262,3... | collective-permute-start | bytes 786440 | tf_op jit(solution)/shard_map/ppermute | solution.py:49
  86.1 20.3 %collective-permute-start.10 = (bf16[2,2,128,256]{3,2,1,0:T(8,128)(2,1)S(1)}, bf16[2,2,128,256]{3,2,1,0:T(8,128)(2,1)S(1)}, u32[]{:S(2)}, u32[]{:S(2)}) collective-permute-start(bf16[2,2,128,256]{3,2,1,0:T(8,128)(2,1)S(1)} %collective-permute-done.9), channel_id=1, source_target_pairs={{128,0},{129,1},{130,2},{131,3},{132,4},{133,5},{134,6},{135,7},{1... | collective-permute-start | bytes 786440 | tf_op jit(solution)/shard_map/ppermute | solution.py:52
  107.3 26.6 %collective-permute-start.11 = (bf16[2,2,4,128,256]{4,3,2,1,0:T(8,128)(2,1)S(1)}, bf16[2,2,4,128,256]{4,3,2,1,0:T(8,128)(2,1)S(1)}, u32[]{:S(2)}, u32[]{:S(2)}) collective-permute-start(bf16[2,2,4,128,256]{4,3,2,1,0:T(8,128)(2,1)S(1)} %fusion.42), channel_id=1, source_target_pairs={{0,16},{16,32},{32,48},{48,64},{64,80},{80,96},{96,112},{112,0},{1... | collective-permute-start | bytes 3145736 | tf_op jit(solution)/shard_map/ppermute | solution.py:72
  109.6 27.8 %collective-permute-start.12 = (bf16[2,2,4,128,256]{4,3,2,1,0:T(8,128)(2,1)S(1)}, bf16[2,2,4,128,256]{4,3,2,1,0:T(8,128)(2,1)S(1)}, u32[]{:S(2)}, u32[]{:S(2)}) collective-permute-start(bf16[2,2,4,128,256]{4,3,2,1,0:T(8,128)(2,1)S(1)} %fusion.42), channel_id=1, source_target_pairs={{16,0},{32,16},{48,32},{64,48},{80,64},{96,80},{112,96},{0,112},{1... | collective-permute-start | bytes 3145736 | tf_op jit(solution)/shard_map/ppermute | solution.py:75
  133.9 3.5 %copy-start.2 = (bf16[2,2,4,128,256]{4,3,2,1,0:T(8,128)(2,1)}, bf16[2,2,4,128,256]{4,3,2,1,0:T(8,128)(2,1)S(1)}, u32[]{:S(2)}) copy-start(bf16[2,2,4,128,256]{4,3,2,1,0:T(8,128)(2,1)S(1)} %collective-permute-done.11) | copy-start | bytes 3145732
  133.9 25.8 %collective-permute-start.13 = (bf16[2,2,4,128,256]{4,3,2,1,0:T(8,128)(2,1)S(1)}, bf16[2,2,4,128,256]{4,3,2,1,0:T(8,128)(2,1)S(1)}, u32[]{:S(2)}, u32[]{:S(2)}) collective-permute-start(bf16[2,2,4,128,256]{4,3,2,1,0:T(8,128)(2,1)S(1)} %collective-permute-done.11), channel_id=1, source_target_pairs={{0,16},{16,32},{32,48},{48,64},{64,80},{80,96},{96,112},{112,0},{1... | collective-permute-start | bytes 3145736 | tf_op jit(solution)/shard_map/ppermute | solution.py:72
  137.4 60.5 %copy-start = (bf16[2,2,4,128,256]{4,3,2,1,0:T(8,128)(2,1)}, bf16[2,2,4,128,256]{4,3,2,1,0:T(8,128)(2,1)S(1)}, u32[]{:S(2)}) copy-start(bf16[2,2,4,128,256]{4,3,2,1,0:T(8,128)(2,1)S(1)} %collective-permute-done.12) | copy-start | bytes 3145732
  137.5 27.1 %collective-permute-start.14 = (bf16[2,2,4,128,256]{4,3,2,1,0:T(8,128)(2,1)S(1)}, bf16[2,2,4,128,256]{4,3,2,1,0:T(8,128)(2,1)}, u32[]{:S(2)}, u32[]{:S(2)}) collective-permute-start(bf16[2,2,4,128,256]{4,3,2,1,0:T(8,128)(2,1)S(1)} %collective-permute-done.12), channel_id=1, source_target_pairs={{16,0},{32,16},{48,32},{64,48},{80,64},{96,80},{112,96},{0,112},{1... | collective-permute-start | bytes 3145736 | tf_op jit(solution)/shard_map/ppermute | solution.py:75
  159.7 38.3 %copy-start.4 = (bf16[2,2,4,128,256]{4,3,2,1,0:T(8,128)(2,1)}, bf16[2,2,4,128,256]{4,3,2,1,0:T(8,128)(2,1)S(1)}, u32[]{:S(2)}) copy-start(bf16[2,2,4,128,256]{4,3,2,1,0:T(8,128)(2,1)S(1)} %collective-permute-done.13) | copy-start | bytes 3145732
  159.7 25.2 %collective-permute-start.15 = (bf16[2,2,4,128,256]{4,3,2,1,0:T(8,128)(2,1)S(1)}, bf16[2,2,4,128,256]{4,3,2,1,0:T(8,128)(2,1)}, u32[]{:S(2)}, u32[]{:S(2)}) collective-permute-start(bf16[2,2,4,128,256]{4,3,2,1,0:T(8,128)(2,1)S(1)} %collective-permute-done.13), channel_id=1, source_target_pairs={{0,16},{16,32},{32,48},{48,64},{64,80},{80,96},{96,112},{112,0},{1... | collective-permute-start | bytes 3145736 | tf_op jit(solution)/shard_map/ppermute | solution.py:72
  164.5 53.1 %collective-permute-start.16 = (bf16[2,2,4,128,256]{4,3,2,1,0:T(8,128)(2,1)}, bf16[2,2,4,128,256]{4,3,2,1,0:T(8,128)(2,1)}, u32[]{:S(2)}, u32[]{:S(2)}) collective-permute-start(bf16[2,2,4,128,256]{4,3,2,1,0:T(8,128)(2,1)} %collective-permute-done.14), channel_id=1, source_target_pairs={{16,0},{32,16},{48,32},{64,48},{80,64},{96,80},{112,96},{0,112},{1... | collective-permute-start | bytes 3145736 | tf_op jit(solution)/shard_map/ppermute | solution.py:75
  184.9 37.9 %collective-permute-start.17 = (bf16[2,2,4,128,256]{4,3,2,1,0:T(8,128)(2,1)}, bf16[2,2,4,128,256]{4,3,2,1,0:T(8,128)(2,1)}, u32[]{:S(2)}, u32[]{:S(2)}) collective-permute-start(bf16[2,2,4,128,256]{4,3,2,1,0:T(8,128)(2,1)} %collective-permute-done.15), channel_id=1, source_target_pairs={{0,16},{16,32},{32,48},{48,64},{64,80},{80,96},{96,112},{112,0},{1... | collective-permute-start | bytes 3145736 | tf_op jit(solution)/shard_map/ppermute | solution.py:72
  211.7 3.3 %copy-start.1 = (bf16[2,2,4,128,256]{4,3,2,1,0:T(8,128)(2,1)S(1)}, bf16[2,2,4,128,256]{4,3,2,1,0:T(8,128)(2,1)}, u32[]{:S(2)}) copy-start(bf16[2,2,4,128,256]{4,3,2,1,0:T(8,128)(2,1)} %copy-done) | copy-start | bytes 3145732
  (2 other events, 3.0 us)
Sparse Core Ops, SparseCore 0:
  59.3 43.7 all-gather.3
  106.5 21.8 all-gather.5
